TPU v7x, 256 devices: a whole 4x4x8 slice. The times are simulated.
256 devices in a mesh: tm: 32 (over y_hi, z, core), space: 8 (over y_lo, x).
Axes of the slice: x: 4, y: 4 (y_hi: 2, y_lo: 2; y = y_hi * 2 + y_lo), z: 8, core: 2. Of those that a mesh axis runs over, the one named last changes fastest.
Arguments:
- start_state: float32 [32, 64, 8192], P('tm', None, 'space'), may hold values from -1.2 to 1.2
- stiffness: float32 [64, 64], replicated, may hold values from -0.75 to 0.75
- lifting: float32 [64, 96], replicated, may hold values from -0.625 to 0.625
- coarse: float32 [64, 64], replicated
- neighbor: int32 [6, 8192], P(None, 'space'), may hold values from 0 to 2047, as said below
- orientation: int32 [6, 8192], P(None, 'space'), may hold values from 0 to 7
- send_low: int32 [4096], P('space'), may hold values from 0 to 1023, as said below
- send_high: int32 [4096], P('space'), may hold values from 0 to 1023, as said below
Outputs:
- end_state: float32 [32, 64, 8192], P('tm', None, 'space')
Inputs may be any that keep to these rules, and one draw needn't show every extreme that they name: `send_low`: distinct local slots of one partition, 512 per partition; the lower boundary elements of a partition are the upper neighbours, across face 1, of the upper boundary elements of the partition below, in the same order. `send_high`: distinct local slots of one partition, 512 per partition. `neighbor`: values of 1024 or more occur only for face 0 (first 512 halo slots) and face 1 (next 512 halo slots); each halo slot is named by exactly one element.
All inputs are finite; a program needn't handle non-finite values.
Results may differ from a plain program's by a relative error of at most 0.00015.
Values sent between devices are 32-bit elements; how exact they have to be, the bound alone decides.
No kernel may reach another device: no remote copies, remote signals or barrier semaphores. Data moves between devices by JAX's collectives and lax.ppermute only.
A program may use at most 64 MiB of HBM per device.

v0:
```python
import jax
import jax.numpy as jnp
from jax import lax
from jax.sharding import PartitionSpec as P

STEPS = 3


time_step = 0.05


def with_halo(shard, sides, width):
    for axis, dim in sides:
        peers, length = (lax.axis_size(axis), shard.shape[dim])
        up = [(i, (i + 1) % peers) for i in range(peers)]
        down = [(j, i) for i, j in up]
        last = lax.slice_in_dim(shard, length - width, length, axis=dim)
        initial = lax.slice_in_dim(shard, 0, width, axis=dim)
        before = lax.ppermute(last, axis, up)
        after = lax.ppermute(initial, axis, down)
        shard = jnp.concatenate([before, shard, after], axis=dim)
    return shard


def from_behind(shard, axis, by):
    peers = lax.axis_size(axis)
    pairs = [(i, i + by) for i in range(peers) if 0 <= i + by < peers]
    return lax.ppermute(shard, axis, pairs)


def product(matrix, vector):
    return jnp.dot(
        matrix, vector, precision=lax.Precision.HIGHEST, preferred_element_type=jnp.float32
    )


def face_traces(state_now):
    elements = state_now.shape[1]
    cube_view = state_now.reshape(4, 4, 4, elements)
    return [
        cube_view[0],
        cube_view[3],
        cube_view[:, 0],
        cube_view[:, 3],
        cube_view[:, :, 0],
        cube_view[:, :, 3],
    ]


def oriented_all(traces, codes):
    summed = jnp.zeros_like(traces)
    for variant in range(8):
        turned = traces
        if variant & 4:
            turned = jnp.swapaxes(turned, 1, 2)
        if variant & 1:
            turned = turned[:, ::-1]
        if variant & 2:
            turned = turned[:, :, ::-1]
        summed = summed + jnp.where(codes[:, None, None, :] == variant, turned, 0.0)
    return summed


def fine_step(state_now, stiffness, lifting, neighbor, orientation, send_low, send_high):
    elements = state_now.shape[1]
    own_list = face_traces(state_now)
    own_stack = jnp.stack(own_list)
    flat_stack = own_stack.reshape(6, 16, elements)
    outgoing = jnp.stack(
        [jnp.take(flat_stack[0], send_low, axis=1), jnp.take(flat_stack[1], send_high, axis=1)]
    )
    received = with_halo(outgoing, (("space", 0),), 1)
    opposite = flat_stack[jnp.array([1, 0, 3, 2, 5, 4])]
    halo_part = jnp.concatenate([received[0], received[3]], axis=1)
    bound = halo_part.shape[1]
    extended = jnp.concatenate(
        [opposite, jnp.broadcast_to(halo_part[None], (6, 16, bound))], axis=2
    )
    beside = jnp.take_along_axis(extended, neighbor[:, None, :], axis=2).reshape(6, 4, 4, elements)
    jumps = oriented_all(beside, orientation) - own_stack
    stacked = jumps.reshape(96, elements)
    rate = (
        product(stiffness, state_now)
        + product(lifting, stacked)
        + state_now
        - state_now * state_now * state_now
    )
    return state_now + time_step * rate


def shards(start_state, stiffness, lifting, coarse, neighbor, orientation, send_low, send_high):
    state_start = start_state[0]
    fine_state = state_start
    for step_id in range(STEPS):
        fine_state = fine_step(
            fine_state, stiffness, lifting, neighbor, orientation, send_low, send_high
        )
    defect = fine_state - product(coarse, state_start)
    is_first = lax.axis_index("tm") == 0

    def turn(turn_id, current):
        advanced = product(coarse, current) + defect
        arrived = from_behind(advanced, "tm", 1)
        return jnp.where(is_first, state_start, arrived)

    current = lax.fori_loop(0, lax.axis_size("tm") - 1, turn, state_start)
    end_now = product(coarse, current) + defect
    return end_now[None]


def solution(mesh):
    return jax.shard_map(
        shards,
        mesh=mesh,
        in_specs=(
            P("tm", None, "space"),
            P(),
            P(),
            P(),
            P(None, "space"),
            P(None, "space"),
            P("space"),
            P("space"),
        ),
        out_specs=P("tm", None, "space"),
        check_vma=False,
    )
```

profile of v0, /device:TPU:22, one launch (start us, length us, event | category | flops | bytes accessed | tf_op | source)
XLA Modules:
  0.0 722.0 jit_solution(2814056200024691211)
XLA Ops:
  13.5 5.2 collective-permute-done.2
  19.8 4.0 copy.89
  23.9 89.6 %gather_fusion.5 = f32[6144,16]{1,0:T(8,128)} fusion(f32[6,16,2048]{1,2,0:T(8,128)} %copy.89, s32[6144]{0:T(1024)S(1)} %reshape.255), kind=kCustom, calls=%fused_computation.1.clone | custom fusion | bytes 835584 | tf_op jit(solution)/shard_map/jit(take_along_axis)/gather | solution.py:79
  113.5 4.7 select_bitcast_fusion.2
  118.1 2.7 copy.90
  126.8 4.4 collective-permute-start.3
  135.8 4.0 copy.101
  139.8 89.6 %gather_fusion.8 = f32[6144,16]{1,0:T(8,128)} fusion(f32[6,16,2048]{1,2,0:T(8,128)} %copy.101, s32[6144]{0:T(1024)S(1)} %reshape.255), kind=kCustom, calls=%fused_computation.7.clone | custom fusion | bytes 835584 | tf_op jit(solution)/shard_map/jit(take_along_axis)/gather | solution.py:79
  229.4 4.7 select_bitcast_fusion.1
  234.1 2.7 copy.102
  240.6 4.2 collective-permute-start.5
  249.7 5.0 collective-permute-done.6
  254.9 4.0 copy.113
  258.9 89.6 %gather_fusion.11 = f32[6144,16]{1,0:T(8,128)} fusion(f32[6,16,2048]{1,2,0:T(8,128)} %copy.113, s32[6144]{0:T(1024)S(1)} %reshape.255), kind=kCustom, calls=%fused_computation.8.clone | custom fusion | bytes 835584 | tf_op jit(solution)/shard_map/jit(take_along_axis)/gather | solution.py:79
  348.6 4.7 select_bitcast_fusion
  353.2 2.7 copy.114
  357.6 363.4 %while.10 = (s32[]{:T(128)}, f32[64,1024]{1,0:T(8,128)S(1)}, pred[]{:T(512)}, f32[64,64]{1,0:T(8,128)S(1)}, f32[64,1024]{1,0:T(8,128)S(1)}, /*index=5*/f32[64,1024]{1,0:T(8,128)S(1)}, s32[]{:T(128)}) while((s32[]{:T(128)}, f32[64,1024]{1,0:T(8,128)S(1)}, pred[]{:T(512)}, f32[64,64]{1,0:T(8,128)S(1)}, f32[64,1024]{1,0:T(8,128)S(1)}, ...), condition=%wide.region_1.0_spmd, body=%wide.region_0.3_spmd.sunk | while | flops 50462720 | bytes 2637942 | solution.py:106
  359.9 9.4 %collective-permute-done = f32[64,1024]{1,0:T(8,128)S(1)} collective-permute-done((f32[64,1024]{1,0:T(8,128)S(1)}, f32[64,1024]{1,0:T(8,128)S(1)}, u32[]{:S(2)}, u32[]{:S(2)}) %collective-permute-start) | collective-permute-done | bytes 262176 | tf_op jit(solution)/shard_map/while/body/eval_jaxpr/ppermute | solution.py:28
  371.6 9.4 %collective-permute-done = f32[64,1024]{1,0:T(8,128)S(1)} collective-permute-done((f32[64,1024]{1,0:T(8,128)S(1)}, f32[64,1024]{1,0:T(8,128)S(1)}, u32[]{:S(2)}, u32[]{:S(2)}) %collective-permute-start) | collective-permute-done | bytes 262176 | tf_op jit(solution)/shard_map/while/body/eval_jaxpr/ppermute | solution.py:28
  383.3 9.4 %collective-permute-done = f32[64,1024]{1,0:T(8,128)S(1)} collective-permute-done((f32[64,1024]{1,0:T(8,128)S(1)}, f32[64,1024]{1,0:T(8,128)S(1)}, u32[]{:S(2)}, u32[]{:S(2)}) %collective-permute-start) | collective-permute-done | bytes 262176 | tf_op jit(solution)/shard_map/while/body/eval_jaxpr/ppermute | solution.py:28
  395.1 9.4 %collective-permute-done = f32[64,1024]{1,0:T(8,128)S(1)} collective-permute-done((f32[64,1024]{1,0:T(8,128)S(1)}, f32[64,1024]{1,0:T(8,128)S(1)}, u32[]{:S(2)}, u32[]{:S(2)}) %collective-permute-start) | collective-permute-done | bytes 262176 | tf_op jit(solution)/shard_map/while/body/eval_jaxpr/ppermute | solution.py:28
  406.8 9.4 %collective-permute-done = f32[64,1024]{1,0:T(8,128)S(1)} collective-permute-done((f32[64,1024]{1,0:T(8,128)S(1)}, f32[64,1024]{1,0:T(8,128)S(1)}, u32[]{:S(2)}, u32[]{:S(2)}) %collective-permute-start) | collective-permute-done | bytes 262176 | tf_op jit(solution)/shard_map/while/body/eval_jaxpr/ppermute | solution.py:28
  418.5 9.4 %collective-permute-done = f32[64,1024]{1,0:T(8,128)S(1)} collective-permute-done((f32[64,1024]{1,0:T(8,128)S(1)}, f32[64,1024]{1,0:T(8,128)S(1)}, u32[]{:S(2)}, u32[]{:S(2)}) %collective-permute-start) | collective-permute-done | bytes 262176 | tf_op jit(solution)/shard_map/while/body/eval_jaxpr/ppermute | solution.py:28
  430.2 9.4 %collective-permute-done = f32[64,1024]{1,0:T(8,128)S(1)} collective-permute-done((f32[64,1024]{1,0:T(8,128)S(1)}, f32[64,1024]{1,0:T(8,128)S(1)}, u32[]{:S(2)}, u32[]{:S(2)}) %collective-permute-start) | collective-permute-done | bytes 262176 | tf_op jit(solution)/shard_map/while/body/eval_jaxpr/ppermute | solution.py:28
  441.9 9.4 %collective-permute-done = f32[64,1024]{1,0:T(8,128)S(1)} collective-permute-done((f32[64,1024]{1,0:T(8,128)S(1)}, f32[64,1024]{1,0:T(8,128)S(1)}, u32[]{:S(2)}, u32[]{:S(2)}) %collective-permute-start) | collective-permute-done | bytes 262176 | tf_op jit(solution)/shard_map/while/body/eval_jaxpr/ppermute | solution.py:28
  453.7 9.4 %collective-permute-done = f32[64,1024]{1,0:T(8,128)S(1)} collective-permute-done((f32[64,1024]{1,0:T(8,128)S(1)}, f32[64,1024]{1,0:T(8,128)S(1)}, u32[]{:S(2)}, u32[]{:S(2)}) %collective-permute-start) | collective-permute-done | bytes 262176 | tf_op jit(solution)/shard_map/while/body/eval_jaxpr/ppermute | solution.py:28
  465.4 9.4 %collective-permute-done = f32[64,1024]{1,0:T(8,128)S(1)} collective-permute-done((f32[64,1024]{1,0:T(8,128)S(1)}, f32[64,1024]{1,0:T(8,128)S(1)}, u32[]{:S(2)}, u32[]{:S(2)}) %collective-permute-start) | collective-permute-done | bytes 262176 | tf_op jit(solution)/shard_map/while/body/eval_jaxpr/ppermute | solution.py:28
  477.1 9.4 %collective-permute-done = f32[64,1024]{1,0:T(8,128)S(1)} collective-permute-done((f32[64,1024]{1,0:T(8,128)S(1)}, f32[64,1024]{1,0:T(8,128)S(1)}, u32[]{:S(2)}, u32[]{:S(2)}) %collective-permute-start) | collective-permute-done | bytes 262176 | tf_op jit(solution)/shard_map/while/body/eval_jaxpr/ppermute | solution.py:28
  488.8 9.4 %collective-permute-done = f32[64,1024]{1,0:T(8,128)S(1)} collective-permute-done((f32[64,1024]{1,0:T(8,128)S(1)}, f32[64,1024]{1,0:T(8,128)S(1)}, u32[]{:S(2)}, u32[]{:S(2)}) %collective-permute-start) | collective-permute-done | bytes 262176 | tf_op jit(solution)/shard_map/while/body/eval_jaxpr/ppermute | solution.py:28
  500.6 9.4 %collective-permute-done = f32[64,1024]{1,0:T(8,128)S(1)} collective-permute-done((f32[64,1024]{1,0:T(8,128)S(1)}, f32[64,1024]{1,0:T(8,128)S(1)}, u32[]{:S(2)}, u32[]{:S(2)}) %collective-permute-start) | collective-permute-done | bytes 262176 | tf_op jit(solution)/shard_map/while/body/eval_jaxpr/ppermute | solution.py:28
  512.3 9.4 %collective-permute-done = f32[64,1024]{1,0:T(8,128)S(1)} collective-permute-done((f32[64,1024]{1,0:T(8,128)S(1)}, f32[64,1024]{1,0:T(8,128)S(1)}, u32[]{:S(2)}, u32[]{:S(2)}) %collective-permute-start) | collective-permute-done | bytes 262176 | tf_op jit(solution)/shard_map/while/body/eval_jaxpr/ppermute | solution.py:28
  524.0 9.4 %collective-permute-done = f32[64,1024]{1,0:T(8,128)S(1)} collective-permute-done((f32[64,1024]{1,0:T(8,128)S(1)}, f32[64,1024]{1,0:T(8,128)S(1)}, u32[]{:S(2)}, u32[]{:S(2)}) %collective-permute-start) | collective-permute-done | bytes 262176 | tf_op jit(solution)/shard_map/while/body/eval_jaxpr/ppermute | solution.py:28
  535.7 9.4 %collective-permute-done = f32[64,1024]{1,0:T(8,128)S(1)} collective-permute-done((f32[64,1024]{1,0:T(8,128)S(1)}, f32[64,1024]{1,0:T(8,128)S(1)}, u32[]{:S(2)}, u32[]{:S(2)}) %collective-permute-start) | collective-permute-done | bytes 262176 | tf_op jit(solution)/shard_map/while/body/eval_jaxpr/ppermute | solution.py:28
  547.4 9.4 %collective-permute-done = f32[64,1024]{1,0:T(8,128)S(1)} collective-permute-done((f32[64,1024]{1,0:T(8,128)S(1)}, f32[64,1024]{1,0:T(8,128)S(1)}, u32[]{:S(2)}, u32[]{:S(2)}) %collective-permute-start) | collective-permute-done | bytes 262176 | tf_op jit(solution)/shard_map/while/body/eval_jaxpr/ppermute | solution.py:28
  559.2 9.4 %collective-permute-done = f32[64,1024]{1,0:T(8,128)S(1)} collective-permute-done((f32[64,1024]{1,0:T(8,128)S(1)}, f32[64,1024]{1,0:T(8,128)S(1)}, u32[]{:S(2)}, u32[]{:S(2)}) %collective-permute-start) | collective-permute-done | bytes 262176 | tf_op jit(solution)/shard_map/while/body/eval_jaxpr/ppermute | solution.py:28
  570.9 9.4 %collective-permute-done = f32[64,1024]{1,0:T(8,128)S(1)} collective-permute-done((f32[64,1024]{1,0:T(8,128)S(1)}, f32[64,1024]{1,0:T(8,128)S(1)}, u32[]{:S(2)}, u32[]{:S(2)}) %collective-permute-start) | collective-permute-done | bytes 262176 | tf_op jit(solution)/shard_map/while/body/eval_jaxpr/ppermute | solution.py:28
  582.6 9.4 %collective-permute-done = f32[64,1024]{1,0:T(8,128)S(1)} collective-permute-done((f32[64,1024]{1,0:T(8,128)S(1)}, f32[64,1024]{1,0:T(8,128)S(1)}, u32[]{:S(2)}, u32[]{:S(2)}) %collective-permute-start) | collective-permute-done | bytes 262176 | tf_op jit(solution)/shard_map/while/body/eval_jaxpr/ppermute | solution.py:28
  594.3 9.4 %collective-permute-done = f32[64,1024]{1,0:T(8,128)S(1)} collective-permute-done((f32[64,1024]{1,0:T(8,128)S(1)}, f32[64,1024]{1,0:T(8,128)S(1)}, u32[]{:S(2)}, u32[]{:S(2)}) %collective-permute-start) | collective-permute-done | bytes 262176 | tf_op jit(solution)/shard_map/while/body/eval_jaxpr/ppermute | solution.py:28
  606.0 9.4 %collective-permute-done = f32[64,1024]{1,0:T(8,128)S(1)} collective-permute-done((f32[64,1024]{1,0:T(8,128)S(1)}, f32[64,1024]{1,0:T(8,128)S(1)}, u32[]{:S(2)}, u32[]{:S(2)}) %collective-permute-start) | collective-permute-done | bytes 262176 | tf_op jit(solution)/shard_map/while/body/eval_jaxpr/ppermute | solution.py:28
  617.8 9.4 %collective-permute-done = f32[64,1024]{1,0:T(8,128)S(1)} collective-permute-done((f32[64,1024]{1,0:T(8,128)S(1)}, f32[64,1024]{1,0:T(8,128)S(1)}, u32[]{:S(2)}, u32[]{:S(2)}) %collective-permute-start) | collective-permute-done | bytes 262176 | tf_op jit(solution)/shard_map/while/body/eval_jaxpr/ppermute | solution.py:28
  629.5 9.4 %collective-permute-done = f32[64,1024]{1,0:T(8,128)S(1)} collective-permute-done((f32[64,1024]{1,0:T(8,128)S(1)}, f32[64,1024]{1,0:T(8,128)S(1)}, u32[]{:S(2)}, u32[]{:S(2)}) %collective-permute-start) | collective-permute-done | bytes 262176 | tf_op jit(solution)/shard_map/while/body/eval_jaxpr/ppermute | solution.py:28
  641.2 9.4 %collective-permute-done = f32[64,1024]{1,0:T(8,128)S(1)} collective-permute-done((f32[64,1024]{1,0:T(8,128)S(1)}, f32[64,1024]{1,0:T(8,128)S(1)}, u32[]{:S(2)}, u32[]{:S(2)}) %collective-permute-start) | collective-permute-done | bytes 262176 | tf_op jit(solution)/shard_map/while/body/eval_jaxpr/ppermute | solution.py:28
  652.9 9.4 %collective-permute-done = f32[64,1024]{1,0:T(8,128)S(1)} collective-permute-done((f32[64,1024]{1,0:T(8,128)S(1)}, f32[64,1024]{1,0:T(8,128)S(1)}, u32[]{:S(2)}, u32[]{:S(2)}) %collective-permute-start) | collective-permute-done | bytes 262176 | tf_op jit(solution)/shard_map/while/body/eval_jaxpr/ppermute | solution.py:28
  664.7 9.4 %collective-permute-done = f32[64,1024]{1,0:T(8,128)S(1)} collective-permute-done((f32[64,1024]{1,0:T(8,128)S(1)}, f32[64,1024]{1,0:T(8,128)S(1)}, u32[]{:S(2)}, u32[]{:S(2)}) %collective-permute-start) | collective-permute-done | bytes 262176 | tf_op jit(solution)/shard_map/while/body/eval_jaxpr/ppermute | solution.py:28
  676.4 9.4 %collective-permute-done = f32[64,1024]{1,0:T(8,128)S(1)} collective-permute-done((f32[64,1024]{1,0:T(8,128)S(1)}, f32[64,1024]{1,0:T(8,128)S(1)}, u32[]{:S(2)}, u32[]{:S(2)}) %collective-permute-start) | collective-permute-done | bytes 262176 | tf_op jit(solution)/shard_map/while/body/eval_jaxpr/ppermute | solution.py:28
  688.1 9.4 %collective-permute-done = f32[64,1024]{1,0:T(8,128)S(1)} collective-permute-done((f32[64,1024]{1,0:T(8,128)S(1)}, f32[64,1024]{1,0:T(8,128)S(1)}, u32[]{:S(2)}, u32[]{:S(2)}) %collective-permute-start) | collective-permute-done | bytes 262176 | tf_op jit(solution)/shard_map/while/body/eval_jaxpr/ppermute | solution.py:28
  699.8 9.4 %collective-permute-done = f32[64,1024]{1,0:T(8,128)S(1)} collective-permute-done((f32[64,1024]{1,0:T(8,128)S(1)}, f32[64,1024]{1,0:T(8,128)S(1)}, u32[]{:S(2)}, u32[]{:S(2)}) %collective-permute-start) | collective-permute-done | bytes 262176 | tf_op jit(solution)/shard_map/while/body/eval_jaxpr/ppermute | solution.py:28
  711.6 9.4 %collective-permute-done = f32[64,1024]{1,0:T(8,128)S(1)} collective-permute-done((f32[64,1024]{1,0:T(8,128)S(1)}, f32[64,1024]{1,0:T(8,128)S(1)}, u32[]{:S(2)}, u32[]{:S(2)}) %collective-permute-start) | collective-permute-done | bytes 262176 | tf_op jit(solution)/shard_map/while/body/eval_jaxpr/ppermute | solution.py:28
  (272 shorter events, 107.5 us)
Async XLA Ops:
  0.0 10.0 %copy-start = (f32[64,64]{1,0:T(8,128)S(1)}, f32[64,64]{1,0:T(8,128)}, u32[]{:S(2)}) copy-start(f32[64,64]{1,0:T(8,128)} %param.18) | copy-start | bytes 49156
  0.0 10.5 %copy-start.24 = (s32[6]{0:T(128)S(1)}, s32[6]{0:T(128)}, u32[]{:S(2)}) copy-start(s32[6]{0:T(128)} %constant.100) | copy-start | bytes 76
  0.0 9.5 %copy-start.1 = (f32[1,64,1024]{2,1,0:T(8,128)S(1)}, f32[1,64,1024]{2,1,0:T(8,128)}, u32[]{:S(2)}) copy-start(f32[1,64,1024]{2,1,0:T(8,128)} %param.17) | copy-start | bytes 786436
  0.0 9.8 %copy-start.10 = (s32[6,1024]{1,0:T(8,128)S(1)}, s32[6,1024]{1,0:T(8,128)}, u32[]{:S(2)}) copy-start(s32[6,1024]{1,0:T(8,128)} %param.21) | copy-start | bytes 73732
  0.0 9.9 %copy-start.11 = (s32[6,1024]{1,0:T(8,128)S(1)}, s32[6,1024]{1,0:T(8,128)}, u32[]{:S(2)}) copy-start(s32[6,1024]{1,0:T(8,128)} %param.22) | copy-start | bytes 73732
  1.4 9.2 %copy-start.17 = (pred[512]{0:T(512)(128)(4,1)}, pred[512]{0:T(512)(128)(4,1)S(1)}, u32[]{:S(2)}) copy-start(pred[512]{0:T(512)(128)(4,1)S(1)} %compare_and_fusion.1) | copy-start | bytes 1540
  4.1 120.0 %copy-start.12 = (s32[1024]{0:T(1024)}, s32[1024]{0:T(1024)S(1)}, u32[]{:S(2)}) copy-start(s32[1024]{0:T(1024)S(1)} %get-tuple-element.91) | copy-start | bytes 12292
  5.3 8.1 %collective-permute-start.1 = (f32[1,16,512]{1,2,0:T(8,128)S(1)}, f32[1,16,512]{1,2,0:T(8,128)S(1)}, u32[]{:S(2)}, u32[]{:S(2)}) collective-permute-start(f32[1,16,512]{1,2,0:T(8,128)S(1)} %select_bitcast_fusion.8), channel_id=1, source_target_pairs={{0,1},{1,2},{2,3},{3,4},{4,5},{5,6},{6,7},{7,0},{8,9},{9,10},{10,1... | collective-permute-start | bytes 98312 | tf_op jit(solution)/shard_map/ppermute | solution.py:19
  8.6 10.1 %collective-permute-start.2 = (f32[1,16,512]{1,2,0:T(8,128)S(1)}, f32[1,16,512]{1,2,0:T(8,128)}, u32[]{:S(2)}, u32[]{:S(2)}) collective-permute-start(f32[1,16,512]{1,2,0:T(8,128)S(1)} %select_bitcast_fusion.7), channel_id=1, source_target_pairs={{1,0},{2,1},{3,2},{4,3},{5,4},{6,5},{7,6},{0,7},{9,8},{10,9},{11,1... | collective-permute-start | bytes 98312 | tf_op jit(solution)/shard_map/ppermute | solution.py:20
  10.0 110.9 %copy-start.4 = (pred[6,1024]{1,0:T(8,128)(4,1)}, pred[6,1024]{1,0:T(8,128)(4,1)S(1)}, u32[]{:S(2)}) copy-start(pred[6,1024]{1,0:T(8,128)(4,1)S(1)} %get-tuple-element.89) | copy-start | bytes 18436
  10.0 110.9 %copy-start.7 = (pred[6,1024]{1,0:T(8,128)(4,1)}, pred[6,1024]{1,0:T(8,128)(4,1)S(1)}, u32[]{:S(2)}) copy-start(pred[6,1024]{1,0:T(8,128)(4,1)S(1)} %get-tuple-element.90) | copy-start | bytes 18436
  125.3 9.3 %collective-permute-start.4 = (f32[1,16,512]{1,2,0:T(8,128)S(1)}, f32[1,16,512]{1,2,0:T(8,128)}, u32[]{:S(2)}, u32[]{:S(2)}) collective-permute-start(f32[1,16,512]{1,2,0:T(8,128)S(1)} %select_bitcast_fusion.5), channel_id=1, source_target_pairs={{1,0},{2,1},{3,2},{4,3},{5,4},{6,5},{7,6},{0,7},{9,8},{10,9},{11,1... | collective-permute-start | bytes 98312 | tf_op jit(solution)/shard_map/ppermute | solution.py:20
  126.8 8.8 %collective-permute-start.3 = (f32[1,16,512]{1,2,0:T(8,128)S(1)}, f32[1,16,512]{1,2,0:T(8,128)S(1)}, u32[]{:S(2)}, u32[]{:S(2)}) collective-permute-start(f32[1,16,512]{1,2,0:T(8,128)S(1)} %select_bitcast_fusion.6), channel_id=1, source_target_pairs={{0,1},{1,2},{2,3},{3,4},{4,5},{5,6},{6,7},{7,0},{8,9},{9,10},{10,1... | collective-permute-start | bytes 98312 | tf_op jit(solution)/shard_map/ppermute | solution.py:19
  237.6 7.3 %copy-start.13 = (s32[1024]{0:T(1024)S(1)}, s32[1024]{0:T(1024)}, u32[]{:S(2)}) copy-start(s32[1024]{0:T(1024)} %copy-done.12) | copy-start | bytes 12292
  237.6 8.4 %copy-start.22 = (pred[512]{0:T(512)(128)(4,1)S(1)}, pred[512]{0:T(512)(128)(4,1)}, u32[]{:S(2)}) copy-start(pred[512]{0:T(512)(128)(4,1)} %copy-done.20) | copy-start | bytes 1540
  240.6 8.1 %collective-permute-start.5 = (f32[1,16,512]{1,2,0:T(8,128)S(1)}, f32[1,16,512]{1,2,0:T(8,128)}, u32[]{:S(2)}, u32[]{:S(2)}) collective-permute-start(f32[1,16,512]{1,2,0:T(8,128)S(1)} %select_bitcast_fusion.4), channel_id=1, source_target_pairs={{0,1},{1,2},{2,3},{3,4},{4,5},{5,6},{6,7},{7,0},{8,9},{9,10},{10,1... | collective-permute-start | bytes 98312 | tf_op jit(solution)/shard_map/ppermute | solution.py:19
  246.2 8.6 %collective-permute-start.6 = (f32[1,16,512]{1,2,0:T(8,128)S(1)}, f32[1,16,512]{1,2,0:T(8,128)S(1)}, u32[]{:S(2)}, u32[]{:S(2)}) collective-permute-start(f32[1,16,512]{1,2,0:T(8,128)S(1)} %select_bitcast_fusion.3), channel_id=1, source_target_pairs={{1,0},{2,1},{3,2},{4,3},{5,4},{6,5},{7,6},{0,7},{9,8},{10,9},{11,1... | collective-permute-start | bytes 98312 | tf_op jit(solution)/shard_map/ppermute | solution.py:20
  358.0 11.3 %collective-permute-start = (f32[64,1024]{1,0:T(8,128)S(1)}, f32[64,1024]{1,0:T(8,128)S(1)}, u32[]{:S(2)}, u32[]{:S(2)}) collective-permute-start(f32[64,1024]{1,0:T(8,128)S(1)} %convolution_add_fusion.4), channel_id=1, source_target_pairs={{0,8},{8,16},{16,24},{24,32},{32,40},{40,48},{48,56},{56,64},{64,7... | collective-permute-start | bytes 786440 | tf_op jit(solution)/shard_map/while/body/eval_jaxpr/ppermute | solution.py:28
  369.7 11.3 %collective-permute-start = (f32[64,1024]{1,0:T(8,128)S(1)}, f32[64,1024]{1,0:T(8,128)S(1)}, u32[]{:S(2)}, u32[]{:S(2)}) collective-permute-start(f32[64,1024]{1,0:T(8,128)S(1)} %convolution_add_fusion.4), channel_id=1, source_target_pairs={{0,8},{8,16},{16,24},{24,32},{32,40},{40,48},{48,56},{56,64},{64,7... | collective-permute-start | bytes 786440 | tf_op jit(solution)/shard_map/while/body/eval_jaxpr/ppermute | solution.py:28
  381.4 11.3 %collective-permute-start = (f32[64,1024]{1,0:T(8,128)S(1)}, f32[64,1024]{1,0:T(8,128)S(1)}, u32[]{:S(2)}, u32[]{:S(2)}) collective-permute-start(f32[64,1024]{1,0:T(8,128)S(1)} %convolution_add_fusion.4), channel_id=1, source_target_pairs={{0,8},{8,16},{16,24},{24,32},{32,40},{40,48},{48,56},{56,64},{64,7... | collective-permute-start | bytes 786440 | tf_op jit(solution)/shard_map/while/body/eval_jaxpr/ppermute | solution.py:28
  393.1 11.3 %collective-permute-start = (f32[64,1024]{1,0:T(8,128)S(1)}, f32[64,1024]{1,0:T(8,128)S(1)}, u32[]{:S(2)}, u32[]{:S(2)}) collective-permute-start(f32[64,1024]{1,0:T(8,128)S(1)} %convolution_add_fusion.4), channel_id=1, source_target_pairs={{0,8},{8,16},{16,24},{24,32},{32,40},{40,48},{48,56},{56,64},{64,7... | collective-permute-start | bytes 786440 | tf_op jit(solution)/shard_map/while/body/eval_jaxpr/ppermute | solution.py:28
  404.8 11.3 %collective-permute-start = (f32[64,1024]{1,0:T(8,128)S(1)}, f32[64,1024]{1,0:T(8,128)S(1)}, u32[]{:S(2)}, u32[]{:S(2)}) collective-permute-start(f32[64,1024]{1,0:T(8,128)S(1)} %convolution_add_fusion.4), channel_id=1, source_target_pairs={{0,8},{8,16},{16,24},{24,32},{32,40},{40,48},{48,56},{56,64},{64,7... | collective-permute-start | bytes 786440 | tf_op jit(solution)/shard_map/while/body/eval_jaxpr/ppermute | solution.py:28
  416.6 11.3 %collective-permute-start = (f32[64,1024]{1,0:T(8,128)S(1)}, f32[64,1024]{1,0:T(8,128)S(1)}, u32[]{:S(2)}, u32[]{:S(2)}) collective-permute-start(f32[64,1024]{1,0:T(8,128)S(1)} %convolution_add_fusion.4), channel_id=1, source_target_pairs={{0,8},{8,16},{16,24},{24,32},{32,40},{40,48},{48,56},{56,64},{64,7... | collective-permute-start | bytes 786440 | tf_op jit(solution)/shard_map/while/body/eval_jaxpr/ppermute | solution.py:28
  428.3 11.3 %collective-permute-start = (f32[64,1024]{1,0:T(8,128)S(1)}, f32[64,1024]{1,0:T(8,128)S(1)}, u32[]{:S(2)}, u32[]{:S(2)}) collective-permute-start(f32[64,1024]{1,0:T(8,128)S(1)} %convolution_add_fusion.4), channel_id=1, source_target_pairs={{0,8},{8,16},{16,24},{24,32},{32,40},{40,48},{48,56},{56,64},{64,7... | collective-permute-start | bytes 786440 | tf_op jit(solution)/shard_map/while/body/eval_jaxpr/ppermute | solution.py:28
  440.0 11.3 %collective-permute-start = (f32[64,1024]{1,0:T(8,128)S(1)}, f32[64,1024]{1,0:T(8,128)S(1)}, u32[]{:S(2)}, u32[]{:S(2)}) collective-permute-start(f32[64,1024]{1,0:T(8,128)S(1)} %convolution_add_fusion.4), channel_id=1, source_target_pairs={{0,8},{8,16},{16,24},{24,32},{32,40},{40,48},{48,56},{56,64},{64,7... | collective-permute-start | bytes 786440 | tf_op jit(solution)/shard_map/while/body/eval_jaxpr/ppermute | solution.py:28
  451.7 11.3 %collective-permute-start = (f32[64,1024]{1,0:T(8,128)S(1)}, f32[64,1024]{1,0:T(8,128)S(1)}, u32[]{:S(2)}, u32[]{:S(2)}) collective-permute-start(f32[64,1024]{1,0:T(8,128)S(1)} %convolution_add_fusion.4), channel_id=1, source_target_pairs={{0,8},{8,16},{16,24},{24,32},{32,40},{40,48},{48,56},{56,64},{64,7... | collective-permute-start | bytes 786440 | tf_op jit(solution)/shard_map/while/body/eval_jaxpr/ppermute | solution.py:28
  463.5 11.3 %collective-permute-start = (f32[64,1024]{1,0:T(8,128)S(1)}, f32[64,1024]{1,0:T(8,128)S(1)}, u32[]{:S(2)}, u32[]{:S(2)}) collective-permute-start(f32[64,1024]{1,0:T(8,128)S(1)} %convolution_add_fusion.4), channel_id=1, source_target_pairs={{0,8},{8,16},{16,24},{24,32},{32,40},{40,48},{48,56},{56,64},{64,7... | collective-permute-start | bytes 786440 | tf_op jit(solution)/shard_map/while/body/eval_jaxpr/ppermute | solution.py:28
  475.2 11.3 %collective-permute-start = (f32[64,1024]{1,0:T(8,128)S(1)}, f32[64,1024]{1,0:T(8,128)S(1)}, u32[]{:S(2)}, u32[]{:S(2)}) collective-permute-start(f32[64,1024]{1,0:T(8,128)S(1)} %convolution_add_fusion.4), channel_id=1, source_target_pairs={{0,8},{8,16},{16,24},{24,32},{32,40},{40,48},{48,56},{56,64},{64,7... | collective-permute-start | bytes 786440 | tf_op jit(solution)/shard_map/while/body/eval_jaxpr/ppermute | solution.py:28
  486.9 11.3 %collective-permute-start = (f32[64,1024]{1,0:T(8,128)S(1)}, f32[64,1024]{1,0:T(8,128)S(1)}, u32[]{:S(2)}, u32[]{:S(2)}) collective-permute-start(f32[64,1024]{1,0:T(8,128)S(1)} %convolution_add_fusion.4), channel_id=1, source_target_pairs={{0,8},{8,16},{16,24},{24,32},{32,40},{40,48},{48,56},{56,64},{64,7... | collective-permute-start | bytes 786440 | tf_op jit(solution)/shard_map/while/body/eval_jaxpr/ppermute | solution.py:28
  498.6 11.3 %collective-permute-start = (f32[64,1024]{1,0:T(8,128)S(1)}, f32[64,1024]{1,0:T(8,128)S(1)}, u32[]{:S(2)}, u32[]{:S(2)}) collective-permute-start(f32[64,1024]{1,0:T(8,128)S(1)} %convolution_add_fusion.4), channel_id=1, source_target_pairs={{0,8},{8,16},{16,24},{24,32},{32,40},{40,48},{48,56},{56,64},{64,7... | collective-permute-start | bytes 786440 | tf_op jit(solution)/shard_map/while/body/eval_jaxpr/ppermute | solution.py:28
  510.3 11.3 %collective-permute-start = (f32[64,1024]{1,0:T(8,128)S(1)}, f32[64,1024]{1,0:T(8,128)S(1)}, u32[]{:S(2)}, u32[]{:S(2)}) collective-permute-start(f32[64,1024]{1,0:T(8,128)S(1)} %convolution_add_fusion.4), channel_id=1, source_target_pairs={{0,8},{8,16},{16,24},{24,32},{32,40},{40,48},{48,56},{56,64},{64,7... | collective-permute-start | bytes 786440 | tf_op jit(solution)/shard_map/while/body/eval_jaxpr/ppermute | solution.py:28
  522.1 11.3 %collective-permute-start = (f32[64,1024]{1,0:T(8,128)S(1)}, f32[64,1024]{1,0:T(8,128)S(1)}, u32[]{:S(2)}, u32[]{:S(2)}) collective-permute-start(f32[64,1024]{1,0:T(8,128)S(1)} %convolution_add_fusion.4), channel_id=1, source_target_pairs={{0,8},{8,16},{16,24},{24,32},{32,40},{40,48},{48,56},{56,64},{64,7... | collective-permute-start | bytes 786440 | tf_op jit(solution)/shard_map/while/body/eval_jaxpr/ppermute | solution.py:28
  533.8 11.3 %collective-permute-start = (f32[64,1024]{1,0:T(8,128)S(1)}, f32[64,1024]{1,0:T(8,128)S(1)}, u32[]{:S(2)}, u32[]{:S(2)}) collective-permute-start(f32[64,1024]{1,0:T(8,128)S(1)} %convolution_add_fusion.4), channel_id=1, source_target_pairs={{0,8},{8,16},{16,24},{24,32},{32,40},{40,48},{48,56},{56,64},{64,7... | collective-permute-start | bytes 786440 | tf_op jit(solution)/shard_map/while/body/eval_jaxpr/ppermute | solution.py:28
  545.5 11.3 %collective-permute-start = (f32[64,1024]{1,0:T(8,128)S(1)}, f32[64,1024]{1,0:T(8,128)S(1)}, u32[]{:S(2)}, u32[]{:S(2)}) collective-permute-start(f32[64,1024]{1,0:T(8,128)S(1)} %convolution_add_fusion.4), channel_id=1, source_target_pairs={{0,8},{8,16},{16,24},{24,32},{32,40},{40,48},{48,56},{56,64},{64,7... | collective-permute-start | bytes 786440 | tf_op jit(solution)/shard_map/while/body/eval_jaxpr/ppermute | solution.py:28
  557.2 11.3 %collective-permute-start = (f32[64,1024]{1,0:T(8,128)S(1)}, f32[64,1024]{1,0:T(8,128)S(1)}, u32[]{:S(2)}, u32[]{:S(2)}) collective-permute-start(f32[64,1024]{1,0:T(8,128)S(1)} %convolution_add_fusion.4), channel_id=1, source_target_pairs={{0,8},{8,16},{16,24},{24,32},{32,40},{40,48},{48,56},{56,64},{64,7... | collective-permute-start | bytes 786440 | tf_op jit(solution)/shard_map/while/body/eval_jaxpr/ppermute | solution.py:28
  569.0 11.3 %collective-permute-start = (f32[64,1024]{1,0:T(8,128)S(1)}, f32[64,1024]{1,0:T(8,128)S(1)}, u32[]{:S(2)}, u32[]{:S(2)}) collective-permute-start(f32[64,1024]{1,0:T(8,128)S(1)} %convolution_add_fusion.4), channel_id=1, source_target_pairs={{0,8},{8,16},{16,24},{24,32},{32,40},{40,48},{48,56},{56,64},{64,7... | collective-permute-start | bytes 786440 | tf_op jit(solution)/shard_map/while/body/eval_jaxpr/ppermute | solution.py:28
  580.7 11.3 %collective-permute-start = (f32[64,1024]{1,0:T(8,128)S(1)}, f32[64,1024]{1,0:T(8,128)S(1)}, u32[]{:S(2)}, u32[]{:S(2)}) collective-permute-start(f32[64,1024]{1,0:T(8,128)S(1)} %convolution_add_fusion.4), channel_id=1, source_target_pairs={{0,8},{8,16},{16,24},{24,32},{32,40},{40,48},{48,56},{56,64},{64,7... | collective-permute-start | bytes 786440 | tf_op jit(solution)/shard_map/while/body/eval_jaxpr/ppermute | solution.py:28
  592.4 11.3 %collective-permute-start = (f32[64,1024]{1,0:T(8,128)S(1)}, f32[64,1024]{1,0:T(8,128)S(1)}, u32[]{:S(2)}, u32[]{:S(2)}) collective-permute-start(f32[64,1024]{1,0:T(8,128)S(1)} %convolution_add_fusion.4), channel_id=1, source_target_pairs={{0,8},{8,16},{16,24},{24,32},{32,40},{40,48},{48,56},{56,64},{64,7... | collective-permute-start | bytes 786440 | tf_op jit(solution)/shard_map/while/body/eval_jaxpr/ppermute | solution.py:28
  604.1 11.3 %collective-permute-start = (f32[64,1024]{1,0:T(8,128)S(1)}, f32[64,1024]{1,0:T(8,128)S(1)}, u32[]{:S(2)}, u32[]{:S(2)}) collective-permute-start(f32[64,1024]{1,0:T(8,128)S(1)} %convolution_add_fusion.4), channel_id=1, source_target_pairs={{0,8},{8,16},{16,24},{24,32},{32,40},{40,48},{48,56},{56,64},{64,7... | collective-permute-start | bytes 786440 | tf_op jit(solution)/shard_map/while/body/eval_jaxpr/ppermute | solution.py:28
  615.8 11.3 %collective-permute-start = (f32[64,1024]{1,0:T(8,128)S(1)}, f32[64,1024]{1,0:T(8,128)S(1)}, u32[]{:S(2)}, u32[]{:S(2)}) collective-permute-start(f32[64,1024]{1,0:T(8,128)S(1)} %convolution_add_fusion.4), channel_id=1, source_target_pairs={{0,8},{8,16},{16,24},{24,32},{32,40},{40,48},{48,56},{56,64},{64,7... | collective-permute-start | bytes 786440 | tf_op jit(solution)/shard_map/while/body/eval_jaxpr/ppermute | solution.py:28
  627.6 11.3 %collective-permute-start = (f32[64,1024]{1,0:T(8,128)S(1)}, f32[64,1024]{1,0:T(8,128)S(1)}, u32[]{:S(2)}, u32[]{:S(2)}) collective-permute-start(f32[64,1024]{1,0:T(8,128)S(1)} %convolution_add_fusion.4), channel_id=1, source_target_pairs={{0,8},{8,16},{16,24},{24,32},{32,40},{40,48},{48,56},{56,64},{64,7... | collective-permute-start | bytes 786440 | tf_op jit(solution)/shard_map/while/body/eval_jaxpr/ppermute | solution.py:28
  639.3 11.3 %collective-permute-start = (f32[64,1024]{1,0:T(8,128)S(1)}, f32[64,1024]{1,0:T(8,128)S(1)}, u32[]{:S(2)}, u32[]{:S(2)}) collective-permute-start(f32[64,1024]{1,0:T(8,128)S(1)} %convolution_add_fusion.4), channel_id=1, source_target_pairs={{0,8},{8,16},{16,24},{24,32},{32,40},{40,48},{48,56},{56,64},{64,7... | collective-permute-start | bytes 786440 | tf_op jit(solution)/shard_map/while/body/eval_jaxpr/ppermute | solution.py:28
  651.0 11.3 %collective-permute-start = (f32[64,1024]{1,0:T(8,128)S(1)}, f32[64,1024]{1,0:T(8,128)S(1)}, u32[]{:S(2)}, u32[]{:S(2)}) collective-permute-start(f32[64,1024]{1,0:T(8,128)S(1)} %convolution_add_fusion.4), channel_id=1, source_target_pairs={{0,8},{8,16},{16,24},{24,32},{32,40},{40,48},{48,56},{56,64},{64,7... | collective-permute-start | bytes 786440 | tf_op jit(solution)/shard_map/while/body/eval_jaxpr/ppermute | solution.py:28
  662.7 11.3 %collective-permute-start = (f32[64,1024]{1,0:T(8,128)S(1)}, f32[64,1024]{1,0:T(8,128)S(1)}, u32[]{:S(2)}, u32[]{:S(2)}) collective-permute-start(f32[64,1024]{1,0:T(8,128)S(1)} %convolution_add_fusion.4), channel_id=1, source_target_pairs={{0,8},{8,16},{16,24},{24,32},{32,40},{40,48},{48,56},{56,64},{64,7... | collective-permute-start | bytes 786440 | tf_op jit(solution)/shard_map/while/body/eval_jaxpr/ppermute | solution.py:28
  674.5 11.3 %collective-permute-start = (f32[64,1024]{1,0:T(8,128)S(1)}, f32[64,1024]{1,0:T(8,128)S(1)}, u32[]{:S(2)}, u32[]{:S(2)}) collective-permute-start(f32[64,1024]{1,0:T(8,128)S(1)} %convolution_add_fusion.4), channel_id=1, source_target_pairs={{0,8},{8,16},{16,24},{24,32},{32,40},{40,48},{48,56},{56,64},{64,7... | collective-permute-start | bytes 786440 | tf_op jit(solution)/shard_map/while/body/eval_jaxpr/ppermute | solution.py:28
  686.2 11.3 %collective-permute-start = (f32[64,1024]{1,0:T(8,128)S(1)}, f32[64,1024]{1,0:T(8,128)S(1)}, u32[]{:S(2)}, u32[]{:S(2)}) collective-permute-start(f32[64,1024]{1,0:T(8,128)S(1)} %convolution_add_fusion.4), channel_id=1, source_target_pairs={{0,8},{8,16},{16,24},{24,32},{32,40},{40,48},{48,56},{56,64},{64,7... | collective-permute-start | bytes 786440 | tf_op jit(solution)/shard_map/while/body/eval_jaxpr/ppermute | solution.py:28
  697.9 11.3 %collective-permute-start = (f32[64,1024]{1,0:T(8,128)S(1)}, f32[64,1024]{1,0:T(8,128)S(1)}, u32[]{:S(2)}, u32[]{:S(2)}) collective-permute-start(f32[64,1024]{1,0:T(8,128)S(1)} %convolution_add_fusion.4), channel_id=1, source_target_pairs={{0,8},{8,16},{16,24},{24,32},{32,40},{40,48},{48,56},{56,64},{64,7... | collective-permute-start | bytes 786440 | tf_op jit(solution)/shard_map/while/body/eval_jaxpr/ppermute | solution.py:28
  709.6 11.3 %collective-permute-start = (f32[64,1024]{1,0:T(8,128)S(1)}, f32[64,1024]{1,0:T(8,128)S(1)}, u32[]{:S(2)}, u32[]{:S(2)}) collective-permute-start(f32[64,1024]{1,0:T(8,128)S(1)} %convolution_add_fusion.4), channel_id=1, source_target_pairs={{0,8},{8,16},{16,24},{24,32},{32,40},{40,48},{48,56},{56,64},{64,7... | collective-permute-start | bytes 786440 | tf_op jit(solution)/shard_map/while/body/eval_jaxpr/ppermute | solution.py:28
  (14 other events, 44.3 us)
where the time goes:
time: 725 us; the launch traced here: 722 us
  local copies, waits for them, and re-layouts  312 us (43%)
  waiting for transfers between devices  303 us (42%)
  starting transfers between devices  70.4 us (10%)
  other arithmetic  19.8 us (3%)
  matrix products  15 us (2%)
    ppermute x31, waiting for transfers between devices, from_behind(): return lax.ppermute(shard, axis, pairs)  291 us
    gather x4, local copies, waits for them, and re-layouts, fine_step(): jnp.take_along_axis(extended, neighbor[:, None, :], axis=2)  269 us
    ppermute x31, starting transfers between devices, from_behind(): return lax.ppermute(shard, axis, pairs)  59.5 us
    dot_general x39, matrix products, product(): jnp.dot(matrix, vector, precision=lax.Precision.HIGHEST, preferred_elemen...  15 us
  transfers between devices with their start and end apart: 37, of which 35 were waited for; matrix products, arithmetic and copies ran while one was open for 2% of the time, Pallas kernels for 0%

commit v1 on v0

--- a/solution.py
+++ b/solution.py
@@ -95,17 +95,20 @@
         fine_state = fine_step(
             fine_state, stiffness, lifting, neighbor, orientation, send_low, send_high
         )
-    defect = fine_state - product(coarse, state_start)
+    coarse_start = product(coarse, state_start)
+    defect = fine_state - coarse_start
     is_first = lax.axis_index("tm") == 0
-
-    def turn(turn_id, current):
-        advanced = product(coarse, current) + defect
-        arrived = from_behind(advanced, "tm", 1)
-        return jnp.where(is_first, state_start, arrived)
-
-    current = lax.fori_loop(0, lax.axis_size("tm") - 1, turn, state_start)
-    end_now = product(coarse, current) + defect
-    return end_now[None]
+    total = jnp.where(is_first, coarse_start + defect, defect)
+    power = coarse
+    offset = 1
+    peers = lax.axis_size("tm")
+    while offset < peers:
+        arrived = from_behind(total, "tm", offset)
+        total = total + product(power, arrived)
+        offset *= 2
+        if offset < peers:
+            power = product(power, power)
+    return total[None]
 
 
 def solution(mesh):

time: 725 us -> 432 us (0.60)
  waiting for transfers between devices: 303 us -> 57.9 us
  starting transfers between devices: 70.4 us -> 28.1 us
  matrix products: 15 us -> 7.35 us
    ppermute x31 -> x5, waiting for transfers between devices: 291 us -> 46.2 us  [from_behind(): return lax.ppermute(shard, axis, pairs)]
    ppermute x31 -> x5, starting transfers between devices: 59.5 us -> 16.9 us  [from_behind(): return lax.ppermute(shard, axis, pairs)]
    dot_general x39 -> x16, matrix products: 15 us -> 7.35 us  [product(): jnp.dot(matrix, vector, precision=lax.Precision.HIGHEST, preferred_elemen...]
  transfers between devices with their start and end apart: 37 -> 11, of which waited for: 35 -> 9; matrix products, arithmetic and copies ran while one was open for 2% -> 4% of each run, Pallas kernels for 0% -> 0%
where the time goes in v1:
time: 432 us; the launch traced here: 425 us
  local copies, waits for them, and re-layouts  309 us (72%)
  waiting for transfers between devices  57.9 us (13%)
  starting transfers between devices  28.1 us (7%)
  other arithmetic  21.2 us (5%)
  matrix products  7.35 us (2%)
    gather x4, local copies, waits for them, and re-layouts, fine_step(): jnp.take_along_axis(extended, neighbor[:, None, :], axis=2)  268 us
    ppermute x5, waiting for transfers between devices, from_behind(): return lax.ppermute(shard, axis, pairs)  46.2 us
    ppermute x5, starting transfers between devices, from_behind(): return lax.ppermute(shard, axis, pairs)  16.9 us
    concatenate x3, local copies, waits for them, and re-layouts, fine_step(): jnp.concatenate([opposite, jnp.broadcast_to(halo_part[None], (6, 16, boun...  12.1 us
    ppermute x3, waiting for transfers between devices, with_halo(): after = lax.ppermute(initial, axis, down)  10.9 us
    ppermute x3, starting transfers between devices, with_halo(): before = lax.ppermute(last, axis, up)  10.2 us
    select_n x3, other arithmetic, fine_step(): jnp.take_along_axis(extended, neighbor[:, None, :], axis=2)  9.57 us
  transfers between devices with their start and end apart: 11, of which 9 were waited for; matrix products, arithmetic and copies ran while one was open for 4% of the time, Pallas kernels for 0%

profile of v1, /device:TPU:22, one launch (start us, length us, event | category | flops | bytes accessed | tf_op | source)
XLA Modules:
  0.0 425.0 jit_solution(17068669644850856846)
XLA Ops:
  1.4 0.8 constant_dynamic-update-slice_fusion.3
  2.3 0.9 constant_dynamic-update-slice_fusion.2
  4.1 1.0 gather_fusion.3
  5.3 1.3 collective-permute-start
  7.5 1.0 gather_fusion.4
  8.6 0.9 collective-permute-start.1
  11.0 1.1 fusion.20
  13.1 1.3 stack.72
  14.5 4.1 collective-permute-done.1
  18.8 4.0 copy.89
  22.8 89.2 %gather_fusion.5 = f32[6144,16]{1,0:T(8,128)} fusion(f32[6,16,2048]{1,2,0:T(8,128)} %copy.89, s32[6144]{0:T(1024)S(1)} %reshape.255), kind=kCustom, calls=%fused_computation.1.clone | custom fusion | bytes 835584 | tf_op jit(solution)/shard_map/jit(take_along_axis)/gather | solution.py:79
  112.1 3.2 select_bitcast_fusion.2
  115.3 2.2 copy.90
  117.4 1.1 copy.136
  118.6 2.4 add_subtract_fusion.2
  122.4 1.1 fusion.28
  123.9 1.0 gather_fusion.7
  125.4 1.0 gather_fusion.6
  126.6 4.4 %collective-permute-start.2 = (f32[1,16,512]{1,2,0:T(8,128)S(1)}, f32[1,16,512]{1,2,0:T(8,128)S(1)}, u32[]{:S(2)}, u32[]{:S(2)}) collective-permute-start(f32[1,16,512]{1,2,0:T(8,128)S(1)} %select_bitcast_fusion.6), channel_id=1, source_target_pairs={{0,1},{1,2},{2,3},{3,4},{4,5},{5,6},{6,7},{7,0},{8,9},{9,10},{10,1... | collective-permute-start | bytes 98312 | tf_op jit(solution)/shard_map/ppermute | solution.py:19
  132.0 1.3 stack.82
  135.2 4.0 copy.101
  139.3 89.2 %gather_fusion.8 = f32[6144,16]{1,0:T(8,128)} fusion(f32[6,16,2048]{1,2,0:T(8,128)} %copy.101, s32[6144]{0:T(1024)S(1)} %reshape.255), kind=kCustom, calls=%fused_computation.7.clone | custom fusion | bytes 835584 | tf_op jit(solution)/shard_map/jit(take_along_axis)/gather | solution.py:79
  228.5 3.2 select_bitcast_fusion.1
  231.7 2.2 copy.102
  233.9 1.1 copy.135
  235.0 2.4 add_subtract_fusion.1
  239.6 1.0 gather_fusion.9
  240.8 4.6 %collective-permute-start.4 = (f32[1,16,512]{1,2,0:T(8,128)S(1)}, f32[1,16,512]{1,2,0:T(8,128)S(1)}, u32[]{:S(2)}, u32[]{:S(2)}) collective-permute-start(f32[1,16,512]{1,2,0:T(8,128)S(1)} %select_bitcast_fusion.4), channel_id=1, source_target_pairs={{0,1},{1,2},{2,3},{3,4},{4,5},{5,6},{6,7},{7,0},{8,9},{9,10},{10,1... | collective-permute-start | bytes 98312 | tf_op jit(solution)/shard_map/ppermute | solution.py:19
  245.6 1.0 gather_fusion.10
  248.0 1.3 stack.92
  249.3 6.0 %collective-permute-done.5 = f32[1,16,512]{1,2,0:T(8,128)S(1)} collective-permute-done((f32[1,16,512]{1,2,0:T(8,128)S(1)}, f32[1,16,512]{1,2,0:T(8,128)S(1)}, u32[]{:S(2)}, u32[]{:S(2)}) %collective-permute-start.5) | collective-permute-done | bytes 32800 | tf_op jit(solution)/shard_map/ppermute | solution.py:20
  255.5 4.0 copy.113
  259.6 89.2 %gather_fusion.11 = f32[6144,16]{1,0:T(8,128)} fusion(f32[6,16,2048]{1,2,0:T(8,128)} %copy.113, s32[6144]{0:T(1024)S(1)} %reshape.255), kind=kCustom, calls=%fused_computation.8.clone | custom fusion | bytes 835584 | tf_op jit(solution)/shard_map/jit(take_along_axis)/gather | solution.py:79
  348.8 3.2 select_bitcast_fusion
  352.0 2.2 copy.114
  354.2 1.1 copy.134
  355.4 2.4 add_subtract_fusion
  358.7 1.9 collective-permute-start.6
  360.6 9.4 %collective-permute-done.6 = f32[64,1024]{1,0:T(8,128)S(1)} collective-permute-done((f32[64,1024]{1,0:T(8,128)S(1)}, f32[64,1024]{1,0:T(8,128)S(1)}, u32[]{:S(2)}, u32[]{:S(2)}) %collective-permute-start.6) | collective-permute-done | bytes 262176 | tf_op jit(solution)/shard_map/ppermute | solution.py:28
  370.4 1.9 collective-permute-start.7
  372.5 9.8 %collective-permute-done.7 = f32[64,1024]{1,0:T(8,128)S(1)} collective-permute-done((f32[64,1024]{1,0:T(8,128)S(1)}, f32[64,1024]{1,0:T(8,128)S(1)}, u32[]{:S(2)}, u32[]{:S(2)}) %collective-permute-start.7) | collective-permute-done | bytes 262176 | tf_op jit(solution)/shard_map/ppermute | solution.py:28
  382.6 1.9 collective-permute-start.8
  384.7 11.5 %collective-permute-done.8 = f32[64,1024]{1,0:T(8,128)S(1)} collective-permute-done((f32[64,1024]{1,0:T(8,128)S(1)}, f32[64,1024]{1,0:T(8,128)S(1)}, u32[]{:S(2)}, u32[]{:S(2)}) %collective-permute-start.8) | collective-permute-done | bytes 262176 | tf_op jit(solution)/shard_map/ppermute | solution.py:28
  396.6 9.8 %collective-permute-start.9 = (f32[64,1024]{1,0:T(8,128)S(1)}, f32[64,1024]{1,0:T(8,128)S(1)}, u32[]{:S(2)}, u32[]{:S(2)}) collective-permute-start(f32[64,1024]{1,0:T(8,128)S(1)} %convolution_add_fusion.2), channel_id=1, source_target_pairs={{0,64},{8,72},{16,80},{24,88},{32,96},{40,104},{48,112},{56,120},{... | collective-permute-start | bytes 786440 | tf_op jit(solution)/shard_map/ppermute | solution.py:28
  406.5 7.2 %collective-permute-done.9 = f32[64,1024]{1,0:T(8,128)S(1)} collective-permute-done((f32[64,1024]{1,0:T(8,128)S(1)}, f32[64,1024]{1,0:T(8,128)S(1)}, u32[]{:S(2)}, u32[]{:S(2)}) %collective-permute-start.9) | collective-permute-done | bytes 262176 | tf_op jit(solution)/shard_map/ppermute | solution.py:28
  414.1 1.3 collective-permute-start.10
  415.6 8.3 %collective-permute-done.10 = f32[64,1024]{1,0:T(8,128)S(1)} collective-permute-done((f32[64,1024]{1,0:T(8,128)S(1)}, f32[64,1024]{1,0:T(8,128)S(1)}, u32[]{:S(2)}, u32[]{:S(2)}) %collective-permute-start.10) | collective-permute-done | bytes 262176 | tf_op jit(solution)/shard_map/ppermute | solution.py:28
  423.9 1.1 fusion
  (172 shorter events, 18.1 us)
Async XLA Ops:
  0.0 10.6 %copy-start = (f32[64,64]{1,0:T(8,128)S(1)}, f32[64,64]{1,0:T(8,128)}, u32[]{:S(2)}) copy-start(f32[64,64]{1,0:T(8,128)} %param.16) | copy-start | bytes 49156
  0.0 9.5 %copy-start.3 = (f32[1,64,1024]{2,1,0:T(8,128)S(1)}, f32[1,64,1024]{2,1,0:T(8,128)}, u32[]{:S(2)}) copy-start(f32[1,64,1024]{2,1,0:T(8,128)} %param.15) | copy-start | bytes 786436
  0.0 9.9 %copy-start.13 = (s32[6,1024]{1,0:T(8,128)S(1)}, s32[6,1024]{1,0:T(8,128)}, u32[]{:S(2)}) copy-start(s32[6,1024]{1,0:T(8,128)} %param.19) | copy-start | bytes 73732
  0.0 10.0 %copy-start.14 = (s32[6,1024]{1,0:T(8,128)S(1)}, s32[6,1024]{1,0:T(8,128)}, u32[]{:S(2)}) copy-start(s32[6,1024]{1,0:T(8,128)} %param.20) | copy-start | bytes 73732
  0.0 11.0 %copy-start.7 = (f32[64,64]{1,0:T(8,128)S(1)}, f32[64,64]{1,0:T(8,128)}, u32[]{:S(2)}) copy-start(f32[64,64]{1,0:T(8,128)} %param.18) | copy-start | bytes 49156
  1.4 10.6 %copy-start.21 = (pred[512]{0:T(512)(128)(4,1)}, pred[512]{0:T(512)(128)(4,1)S(1)}, u32[]{:S(2)}) copy-start(pred[512]{0:T(512)(128)(4,1)S(1)} %compare_and_fusion.1) | copy-start | bytes 1540
  3.2 9.0 %copy-start.28 = (s32[6]{0:T(128)S(1)}, s32[6]{0:T(128)}, u32[]{:S(2)}) copy-start(s32[6]{0:T(128)} %constant.96) | copy-start | bytes 76
  4.1 8.2 %copy-start.15 = (s32[1024]{0:T(1024)}, s32[1024]{0:T(1024)S(1)}, u32[]{:S(2)}) copy-start(s32[1024]{0:T(1024)S(1)} %get-tuple-element.46) | copy-start | bytes 12292
  4.1 8.2 %copy-start.18 = (s32[1024]{0:T(1024)}, s32[1024]{0:T(1024)S(1)}, u32[]{:S(2)}) copy-start(s32[1024]{0:T(1024)S(1)} %get-tuple-element.47) | copy-start | bytes 12292
  5.3 9.1 %collective-permute-start = (f32[1,16,512]{1,2,0:T(8,128)S(1)}, f32[1,16,512]{1,2,0:T(8,128)S(1)}, u32[]{:S(2)}, u32[]{:S(2)}) collective-permute-start(f32[1,16,512]{1,2,0:T(8,128)S(1)} %select_bitcast_fusion.8), channel_id=1, source_target_pairs={{0,1},{1,2},{2,3},{3,4},{4,5},{5,6},{6,7},{7,0},{8,9},{9,10},{10,1... | collective-permute-start | bytes 98312 | tf_op jit(solution)/shard_map/ppermute | solution.py:19
  7.3 5.1 %copy-start.24 = (pred[512]{0:T(512)(128)(4,1)}, pred[512]{0:T(512)(128)(4,1)S(1)}, u32[]{:S(2)}) copy-start(pred[512]{0:T(512)(128)(4,1)S(1)} %compare_and_fusion) | copy-start | bytes 1540
  8.6 10.0 %collective-permute-start.1 = (f32[1,16,512]{1,2,0:T(8,128)S(1)}, f32[1,16,512]{1,2,0:T(8,128)S(1)}, u32[]{:S(2)}, u32[]{:S(2)}) collective-permute-start(f32[1,16,512]{1,2,0:T(8,128)S(1)} %select_bitcast_fusion.7), channel_id=1, source_target_pairs={{1,0},{2,1},{3,2},{4,3},{5,4},{6,5},{7,6},{0,7},{9,8},{10,9},{11,1... | collective-permute-start | bytes 98312 | tf_op jit(solution)/shard_map/ppermute | solution.py:20
  12.2 2.3 copy-start.27
  117.4 4.0 copy-start.4
  117.4 4.0 copy-start.8
  121.0 2.9 copy-start.16
  121.0 3.9 copy-start.25
  121.4 3.9 copy-start.19
  121.4 5.0 %copy-start.22 = (pred[512]{0:T(512)(128)(4,1)S(1)}, pred[512]{0:T(512)(128)(4,1)}, u32[]{:S(2)}) copy-start(pred[512]{0:T(512)(128)(4,1)} %copy-done.21) | copy-start | bytes 1540
  125.1 9.0 %collective-permute-start.3 = (f32[1,16,512]{1,2,0:T(8,128)S(1)}, f32[1,16,512]{1,2,0:T(8,128)S(1)}, u32[]{:S(2)}, u32[]{:S(2)}) collective-permute-start(f32[1,16,512]{1,2,0:T(8,128)S(1)} %select_bitcast_fusion.5), channel_id=1, source_target_pairs={{1,0},{2,1},{3,2},{4,3},{5,4},{6,5},{7,6},{0,7},{9,8},{10,9},{11,1... | collective-permute-start | bytes 98312 | tf_op jit(solution)/shard_map/ppermute | solution.py:20
  126.6 8.5 %collective-permute-start.2 = (f32[1,16,512]{1,2,0:T(8,128)S(1)}, f32[1,16,512]{1,2,0:T(8,128)S(1)}, u32[]{:S(2)}, u32[]{:S(2)}) collective-permute-start(f32[1,16,512]{1,2,0:T(8,128)S(1)} %select_bitcast_fusion.6), channel_id=1, source_target_pairs={{0,1},{1,2},{2,3},{3,4},{4,5},{5,6},{6,7},{7,0},{8,9},{9,10},{10,1... | collective-permute-start | bytes 98312 | tf_op jit(solution)/shard_map/ppermute | solution.py:19
  233.9 4.0 copy-start.5
  237.4 2.2 copy-start.20
  237.4 3.2 copy-start.23
  237.8 7.7 %copy-start.17 = (s32[1024]{0:T(1024)S(1)}, s32[1024]{0:T(1024)}, u32[]{:S(2)}) copy-start(s32[1024]{0:T(1024)} %copy-done.15) | copy-start | bytes 12292
  237.8 8.8 %copy-start.26 = (pred[512]{0:T(512)(128)(4,1)S(1)}, pred[512]{0:T(512)(128)(4,1)}, u32[]{:S(2)}) copy-start(pred[512]{0:T(512)(128)(4,1)} %copy-done.24) | copy-start | bytes 1540
  238.3 8.7 %copy-start.1 = (f32[64,1024]{1,0:T(8,128)}, f32[64,1024]{1,0:T(8,128)S(1)}, u32[]{:S(2)}) copy-start(f32[64,1024]{1,0:T(8,128)S(1)} %fusion.15) | copy-start | bytes 786436
  240.8 8.4 %collective-permute-start.4 = (f32[1,16,512]{1,2,0:T(8,128)S(1)}, f32[1,16,512]{1,2,0:T(8,128)S(1)}, u32[]{:S(2)}, u32[]{:S(2)}) collective-permute-start(f32[1,16,512]{1,2,0:T(8,128)S(1)} %select_bitcast_fusion.4), channel_id=1, source_target_pairs={{0,1},{1,2},{2,3},{3,4},{4,5},{5,6},{6,7},{7,0},{8,9},{9,10},{10,1... | collective-permute-start | bytes 98312 | tf_op jit(solution)/shard_map/ppermute | solution.py:19
  246.8 8.6 %collective-permute-start.5 = (f32[1,16,512]{1,2,0:T(8,128)S(1)}, f32[1,16,512]{1,2,0:T(8,128)S(1)}, u32[]{:S(2)}, u32[]{:S(2)}) collective-permute-start(f32[1,16,512]{1,2,0:T(8,128)S(1)} %select_bitcast_fusion.3), channel_id=1, source_target_pairs={{1,0},{2,1},{3,2},{4,3},{5,4},{6,5},{7,6},{0,7},{9,8},{10,9},{11,1... | collective-permute-start | bytes 98312 | tf_op jit(solution)/shard_map/ppermute | solution.py:20
  352.0 3.4 copy-start.9
  352.0 3.4 copy-start.10
  352.0 3.4 copy-start.11
  352.0 3.4 copy-start.12
  354.2 4.0 copy-start.2
  354.2 4.0 copy-start.6
  358.7 11.3 %collective-permute-start.6 = (f32[64,1024]{1,0:T(8,128)S(1)}, f32[64,1024]{1,0:T(8,128)S(1)}, u32[]{:S(2)}, u32[]{:S(2)}) collective-permute-start(f32[64,1024]{1,0:T(8,128)S(1)} %add_select_fusion), channel_id=1, source_target_pairs={{0,8},{8,16},{16,24},{24,32},{32,40},{40,48},{48,56},{56,64},{64,7... | collective-permute-start | bytes 786440 | tf_op jit(solution)/shard_map/ppermute | solution.py:28
  370.4 11.9 %collective-permute-start.7 = (f32[64,1024]{1,0:T(8,128)S(1)}, f32[64,1024]{1,0:T(8,128)S(1)}, u32[]{:S(2)}, u32[]{:S(2)}) collective-permute-start(f32[64,1024]{1,0:T(8,128)S(1)} %fusion.10), channel_id=1, source_target_pairs={{0,16},{8,24},{16,32},{24,40},{32,48},{40,56},{48,64},{56,72},{64,... | collective-permute-start | bytes 786440 | tf_op jit(solution)/shard_map/ppermute | solution.py:28
  382.6 13.6 %collective-permute-start.8 = (f32[64,1024]{1,0:T(8,128)S(1)}, f32[64,1024]{1,0:T(8,128)S(1)}, u32[]{:S(2)}, u32[]{:S(2)}) collective-permute-start(f32[64,1024]{1,0:T(8,128)S(1)} %convolution_add_fusion.3), channel_id=1, source_target_pairs={{0,32},{8,40},{16,48},{24,56},{32,64},{40,72},{48,80},{56,88},{64,... | collective-permute-start | bytes 786440 | tf_op jit(solution)/shard_map/ppermute | solution.py:28
  396.6 17.2 %collective-permute-start.9 = (f32[64,1024]{1,0:T(8,128)S(1)}, f32[64,1024]{1,0:T(8,128)S(1)}, u32[]{:S(2)}, u32[]{:S(2)}) collective-permute-start(f32[64,1024]{1,0:T(8,128)S(1)} %convolution_add_fusion.2), channel_id=1, source_target_pairs={{0,64},{8,72},{16,80},{24,88},{32,96},{40,104},{48,112},{56,120},{... | collective-permute-start | bytes 786440 | tf_op jit(solution)/shard_map/ppermute | solution.py:28
  414.1 9.8 %collective-permute-start.10 = (f32[64,1024]{1,0:T(8,128)S(1)}, f32[64,1024]{1,0:T(8,128)S(1)}, u32[]{:S(2)}, u32[]{:S(2)}) collective-permute-start(f32[64,1024]{1,0:T(8,128)S(1)} %convolution_add_fusion.1), channel_id=1, source_target_pairs={{0,128},{8,136},{16,144},{24,152},{32,160},{40,168},{48,176},{56,1... | collective-permute-start | bytes 786440 | tf_op jit(solution)/shard_map/ppermute | solution.py:28

commit v2 on v1

v2 whole, which is shorter than its diff:
```python
import functools

import numpy as np
import jax
import jax.numpy as jnp
from jax import lax
from jax.experimental import pallas as pl
from jax.experimental.pallas import tpu as pltpu
from jax.sharding import PartitionSpec as P

STEPS = 3
LANES = 128
UNROLL = 8


time_step = 0.05


def from_behind(shard, axis, by):
    peers = lax.axis_size(axis)
    pairs = [(i, i + by) for i in range(peers) if 0 <= i + by < peers]
    return lax.ppermute(shard, axis, pairs)


def ring(shard, axis, by):
    peers = lax.axis_size(axis)
    return lax.ppermute(shard, axis, [(i, (i + by) % peers) for i in range(peers)])


def product(matrix, vector):
    return jnp.dot(
        matrix, vector, precision=lax.Precision.HIGHEST, preferred_element_type=jnp.float32
    )


def face_nodes():
    i, j, k = np.meshgrid(np.arange(4), np.arange(4), np.arange(4), indexing="ij")
    node = 16 * i + 4 * j + k
    return [
        node[0].ravel(), node[3].ravel(),
        node[:, 0].ravel(), node[:, 3].ravel(),
        node[:, :, 0].ravel(), node[:, :, 3].ravel(),
    ]


def orientations():
    base = np.arange(16).reshape(4, 4)
    out = []
    for code in range(8):
        turned = base
        if code & 4:
            turned = turned.T
        if code & 1:
            turned = turned[::-1]
        if code & 2:
            turned = turned[:, ::-1]
        out.append(turned.ravel())
    return out


def selection_tables():
    nodes, perms = face_nodes(), orientations()
    pick = np.zeros((6, LANES, LANES), np.float32)
    own = np.zeros((64, 96), np.float32)
    for f in range(6):
        for code in range(8):
            for q in range(16):
                pick[f, nodes[f ^ 1][perms[code][q]], 16 * code + q] = 1.0
        for m in range(16):
            own[nodes[f][m], 16 * f + m] = 1.0
    return pick, own


def gather_kernel(idx_ref, table_ref, out_ref):
    def body(step, carry):
        for u in range(UNROLL):
            row = step * UNROLL + u
            out_ref[pl.ds(row, 1), :] = table_ref[pl.ds(idx_ref[row], 1), :]
        return carry

    lax.fori_loop(0, out_ref.shape[0] // UNROLL, body, 0)


def gather_rows(table, idx):
    return pl.pallas_call(
        gather_kernel,
        out_shape=jax.ShapeDtypeStruct((idx.shape[0], table.shape[1]), table.dtype),
        in_specs=[
            pl.BlockSpec(memory_space=pltpu.SMEM),
            pl.BlockSpec(memory_space=pltpu.VMEM),
        ],
        out_specs=pl.BlockSpec(memory_space=pltpu.VMEM),
    )(idx, table)


def fine_step(state, folded, pick, spread, mask, nbr_rows, send_rows):
    elements = state.shape[0]
    padded = jnp.pad(state, ((0, 0), (0, LANES - state.shape[1])))
    sent = gather_rows(padded, send_rows)
    half = sent.shape[0] // 2
    low_trace = sent[:half, 0:16].T
    high_trace = sent[half:, 48:64].T
    before = ring(high_trace, "space", 1)
    after = ring(low_trace, "space", -1)
    halo_low = jnp.pad(before.T, ((0, 0), (48, LANES - 64)))
    halo_high = jnp.pad(after.T, ((0, 0), (0, LANES - 16)))
    table = jnp.concatenate([padded, halo_low, halo_high], axis=0)
    beside = gather_rows(table, nbr_rows).reshape(6, elements, LANES)
    turned = jnp.einsum(
        "fer,frq->feq", beside, pick, precision=lax.Precision.HIGHEST,
        preferred_element_type=jnp.float32,
    )
    chosen = jnp.where(mask, turned, 0.0)
    lifted = jnp.einsum(
        "feq,fqn->en", chosen, spread, precision=lax.Precision.HIGHEST,
        preferred_element_type=jnp.float32,
    )
    rate = product(state, folded) + lifted + state - state * state * state
    return state + time_step * rate


def shards(start_state, stiffness, lifting, coarse, neighbor, orientation, send_low, send_high):
    pick_np, own_np = selection_tables()
    pick = jnp.asarray(pick_np)
    own = jnp.asarray(own_np)
    lift_t = lifting.T.reshape(6, 16, 64)
    spread = jnp.broadcast_to(lift_t[:, None], (6, 8, 16, 64)).reshape(6, LANES, 64)
    folded = stiffness.T - product(own, lifting.T)
    lane_code = jnp.arange(LANES, dtype=jnp.int32) // 16
    mask = orientation[:, :, None] == lane_code[None, None, :]
    nbr_rows = neighbor.reshape(-1)
    send_rows = jnp.concatenate([send_low, send_high])

    state_start = start_state[0]
    fine_state = state_start.T
    for step_id in range(STEPS):
        fine_state = fine_step(fine_state, folded, pick, spread, mask, nbr_rows, send_rows)
    fine_state = fine_state.T
    coarse_start = product(coarse, state_start)
    defect = fine_state - coarse_start
    is_first = lax.axis_index("tm") == 0
    total = jnp.where(is_first, coarse_start + defect, defect)
    power = coarse
    offset = 1
    peers = lax.axis_size("tm")
    while offset < peers:
        arrived = from_behind(total, "tm", offset)
        total = total + product(power, arrived)
        offset *= 2
        if offset < peers:
            power = product(power, power)
    return total[None]


def solution(mesh):
    return jax.shard_map(
        shards,
        mesh=mesh,
        in_specs=(
            P("tm", None, "space"),
            P(),
            P(),
            P(),
            P(None, "space"),
            P(None, "space"),
            P("space"),
            P("space"),
        ),
        out_specs=P("tm", None, "space"),
        check_vma=False,
    )
```

time: 432 us -> 240 us (0.56)
  the two profiles are of different devices: /device:TPU:22 before, /device:TPU:54 now
where the time goes in v2:
time: 240 us; the launch traced here: 239 us
  waiting for transfers between devices  123 us (51%)
  Pallas kernels  43.9 us (18%)
  matrix products  31.7 us (13%)
  starting transfers between devices  21.6 us (9%)
  local copies, waits for them, and re-layouts  12.2 us (5%)
  other arithmetic  6.58 us (3%)
    ppermute x5, waiting for transfers between devices, from_behind(): return lax.ppermute(shard, axis, pairs)  102 us
    pallas_call x6, Pallas kernels, gather_rows(): pl.pallas_call(gather_kernel, out_shape=jax.ShapeDtypeStruct((idx.shape[0...  43.9 us
    ppermute x6, waiting for transfers between devices, ring(): lax.ppermute(shard, axis, [(i, (i + by) % peers) for i in range(peers)])  20.4 us
    ppermute x5, starting transfers between devices, from_behind(): return lax.ppermute(shard, axis, pairs)  15.3 us
    dot_general x3, matrix products, fine_step(): jnp.einsum('fer,frq->feq', beside, pick, precision=lax.Precision.HIGHEST,...  14.5 us
    dot_general x3, matrix products, fine_step(): jnp.einsum('feq,fqn->en', chosen, spread, precision=lax.Precision.HIGHEST...  8.96 us
    dot_general x14, matrix products, product(): jnp.dot(matrix, vector, precision=lax.Precision.HIGHEST, preferred_elemen...  8.22 us
    concatenate x3, other arithmetic, fine_step(): table = jnp.concatenate([padded, halo_low, halo_high], axis=0)  6.45 us
  transfers between devices with their start and end apart: 11, of which 11 were waited for; matrix products, arithmetic and copies ran while one was open for 2% of the time, Pallas kernels for 0%

profile of v2, /device:TPU:54, one launch (start us, length us, event | category | flops | bytes accessed | tf_op | source)
XLA Modules:
  0.0 238.9 jit_solution(11773048380912627398)
XLA Ops:
  0.0 1.2 copy.52
  1.2 0.9 pad.30.table_ref
  2.1 0.7 constant_dynamic-update-slice_fusion.1
  2.8 0.7 constant_dynamic-update-slice_fusion.idx_ref
  4.0 3.3 %shard_map.100 = f32[1024,128]{1,0:T(8,128)} custom-call(s32[1024]{0:T(1024)} %copy-done.8, f32[1024,128]{1,0:T(8,128)} %pad.30.table_ref), custom_call_target="tpu_custom_call" | custom-call | tf_op jit(solution)/shard_map/pallas_call | solution.py:85
  7.3 1.2 slice_bitcast_fusion.5
  8.5 1.3 collective-permute-start
  9.8 0.8 collective-permute-start.1
  11.6 5.0 %collective-permute-done = f32[16,512]{0,1:T(8,128)S(1)} collective-permute-done((f32[16,512]{0,1:T(8,128)S(1)}, f32[16,512]{0,1:T(8,128)S(1)}, u32[]{:S(2)}, u32[]{:S(2)}) %collective-permute-start) | collective-permute-done | bytes 32800 | tf_op jit(solution)/shard_map/ppermute | solution.py:27
  16.6 3.0 %collective-permute-done.1 = f32[16,512]{0,1:T(8,128)S(1)} collective-permute-done((f32[16,512]{0,1:T(8,128)S(1)}, f32[16,512]{0,1:T(8,128)S(1)}, u32[]{:S(2)}, u32[]{:S(2)}) %collective-permute-start.1) | collective-permute-done | bytes 32800 | tf_op jit(solution)/shard_map/ppermute | solution.py:27
  19.6 2.2 select_maximum_fusion.4.table_ref
  21.8 11.4 %shard_map.101 = f32[6144,128]{1,0:T(8,128)} custom-call(s32[6144]{0:T(1024)} %reshape.30.idx_ref, f32[2048,128]{1,0:T(8,128)} %select_maximum_fusion.4.table_ref), custom_call_target="tpu_custom_call" | custom-call | tf_op jit(solution)/shard_map/pallas_call | solution.py:85
  33.2 4.9 %fusion.43 = f32[6,1024,128]{2,1,0:T(8,128)S(1)} fusion(f32[6,1024,128]{2,1,0:T(8,128)} %bitcast.104, f32[6,128,128]{2,1,0:T(8,128)S(1)} %copy-done.2), kind=kOutput, calls=%fused_computation.84 | convolution fusion | flops 1207959552 | bytes 6684672 | tf_op jit(solution)/shard_map/fer,frq->feq/dot_general | solution.py:109
  38.1 3.6 %fusion = f32[1024,64,1]{0,1,2:T(8,128)S(1)} fusion(f32[6,128,64]{2,1,0:T(8,128)S(1)} %bitcast.106, f32[6,1024,128]{2,1,0:T(8,128)S(1)} %fusion.43, s32[128]{0:T(128)S(1)} %and_select_fusion, s32[6,1024]{1,0:T(8,128)S(1)} %copy-done.6), kind=kOutput, calls=%fused_computation.3 | convolution fusion | flops 605552640 | bytes 3629568 | tf_op jit(solution)/shard_map/feq,fqn->en/dot_general | solution.py:114
  42.7 0.9 pad.33.table_ref
  43.5 3.3 %shard_map.102 = f32[1024,128]{1,0:T(8,128)} custom-call(s32[1024]{0:T(1024)} %copy-done.8, f32[1024,128]{1,0:T(8,128)} %pad.33.table_ref), custom_call_target="tpu_custom_call" | custom-call | tf_op jit(solution)/shard_map/pallas_call | solution.py:85
  46.8 1.2 slice_bitcast_fusion.3
  48.3 1.7 collective-permute-start.3
  50.1 4.8 %collective-permute-done.2 = f32[16,512]{0,1:T(8,128)S(1)} collective-permute-done((f32[16,512]{0,1:T(8,128)S(1)}, f32[16,512]{0,1:T(8,128)S(1)}, u32[]{:S(2)}, u32[]{:S(2)}) %collective-permute-start.2) | collective-permute-done | bytes 32800 | tf_op jit(solution)/shard_map/ppermute | solution.py:27
  54.9 2.4 %collective-permute-done.3 = f32[16,512]{0,1:T(8,128)S(1)} collective-permute-done((f32[16,512]{0,1:T(8,128)S(1)}, f32[16,512]{0,1:T(8,128)S(1)}, u32[]{:S(2)}, u32[]{:S(2)}) %collective-permute-start.3) | collective-permute-done | bytes 32800 | tf_op jit(solution)/shard_map/ppermute | solution.py:27
  57.3 2.1 select_maximum_fusion.2.table_ref
  59.5 11.4 %shard_map.103 = f32[6144,128]{1,0:T(8,128)} custom-call(s32[6144]{0:T(1024)} %reshape.30.idx_ref, f32[2048,128]{1,0:T(8,128)} %select_maximum_fusion.2.table_ref), custom_call_target="tpu_custom_call" | custom-call | tf_op jit(solution)/shard_map/pallas_call | solution.py:85
  70.8 4.8 %fusion.44 = f32[6,1024,128]{2,1,0:T(8,128)S(1)} fusion(f32[6,1024,128]{2,1,0:T(8,128)} %bitcast.105, f32[6,128,128]{2,1,0:T(8,128)S(1)} %copy-done.2), kind=kOutput, calls=%fused_computation.85 | convolution fusion | flops 1207959552 | bytes 6684672 | tf_op jit(solution)/shard_map/fer,frq->feq/dot_general | solution.py:109
  75.7 2.7 %fusion.13 = f32[1024,64]{1,0:T(8,128)S(1)} fusion(f32[6,128,64]{2,1,0:T(8,128)S(1)} %bitcast.107, f32[6,1024,128]{2,1,0:T(8,128)S(1)} %fusion.44, s32[128]{0:T(128)S(1)} %and_select_fusion, s32[6,1024]{1,0:T(8,128)S(1)} %copy-done.6), kind=kOutput, calls=%fused_computation.18 | convolution fusion | flops 605552640 | bytes 3629568 | tf_op jit(solution)/shard_map/feq,fqn->en/dot_general | solution.py:114
  78.4 1.4 fusion.33
  79.8 0.8 pad.36.table_ref
  80.6 3.3 %shard_map.104 = f32[1024,128]{1,0:T(8,128)} custom-call(s32[1024]{0:T(1024)} %copy-done.8, f32[1024,128]{1,0:T(8,128)} %pad.36.table_ref), custom_call_target="tpu_custom_call" | custom-call | tf_op jit(solution)/shard_map/pallas_call | solution.py:85
  84.0 1.9 slice_bitcast_fusion.1
  86.1 1.7 collective-permute-start.5
  87.9 1.8 fusion.37
  89.9 2.7 %collective-permute-done.4 = f32[16,512]{0,1:T(8,128)} collective-permute-done((f32[16,512]{0,1:T(8,128)}, f32[16,512]{0,1:T(8,128)}, u32[]{:S(2)}, u32[]{:S(2)}) %collective-permute-start.4) | collective-permute-done | bytes 32800 | tf_op jit(solution)/shard_map/ppermute | solution.py:27
  92.5 2.4 %collective-permute-done.5 = f32[16,512]{0,1:T(8,128)} collective-permute-done((f32[16,512]{0,1:T(8,128)}, f32[16,512]{0,1:T(8,128)}, u32[]{:S(2)}, u32[]{:S(2)}) %collective-permute-start.5) | collective-permute-done | bytes 32800 | tf_op jit(solution)/shard_map/ppermute | solution.py:27
  94.9 2.1 select_maximum_fusion.table_ref
  97.1 11.4 %shard_map.105 = f32[6144,128]{1,0:T(8,128)} custom-call(s32[6144]{0:T(1024)} %reshape.30.idx_ref, f32[2048,128]{1,0:T(8,128)} %select_maximum_fusion.table_ref), custom_call_target="tpu_custom_call" | custom-call | tf_op jit(solution)/shard_map/pallas_call | solution.py:85
  108.4 4.8 %fusion.45 = f32[6,1024,128]{2,1,0:T(8,128)S(1)} fusion(f32[6,1024,128]{2,1,0:T(8,128)} %bitcast.103, f32[6,128,128]{2,1,0:T(8,128)S(1)} %copy-done.2), kind=kOutput, calls=%fused_computation.86 | convolution fusion | flops 1207959552 | bytes 6684672 | tf_op jit(solution)/shard_map/fer,frq->feq/dot_general | solution.py:109
  113.3 2.7 %fusion.12 = f32[64,1024]{0,1:T(8,128)S(1)} fusion(f32[6,128,64]{2,1,0:T(8,128)S(1)} %bitcast.108, f32[6,1024,128]{2,1,0:T(8,128)S(1)} %fusion.45, s32[128]{0:T(128)S(1)} %and_select_fusion, s32[6,1024]{1,0:T(8,128)S(1)} %copy-done.6), kind=kOutput, calls=%fused_computation.17 | convolution fusion | flops 605552640 | bytes 3629568 | tf_op jit(solution)/shard_map/feq,fqn->en/dot_general | solution.py:114
  116.0 0.9 add_select_fusion
  116.9 1.9 collective-permute-start.6
  118.8 8.6 %collective-permute-done.6 = f32[64,1024]{0,1:T(8,128)S(1)} collective-permute-done((f32[64,1024]{0,1:T(8,128)S(1)}, f32[64,1024]{0,1:T(8,128)S(1)}, u32[]{:S(2)}, u32[]{:S(2)}) %collective-permute-start.6) | collective-permute-done | bytes 262176 | tf_op jit(solution)/shard_map/ppermute | solution.py:22
  127.9 3.8 %collective-permute-start.7 = (f32[64,1024]{0,1:T(8,128)S(1)}, f32[64,1024]{0,1:T(8,128)S(1)}, u32[]{:S(2)}, u32[]{:S(2)}) collective-permute-start(f32[64,1024]{0,1:T(8,128)S(1)} %fusion.14), channel_id=1, source_target_pairs={{0,16},{8,24},{16,32},{24,40},{32,48},{40,56},{48,64},{56,72},{64,... | collective-permute-start | bytes 786440 | tf_op jit(solution)/shard_map/ppermute | solution.py:22
  131.9 11.3 %collective-permute-done.7 = f32[64,1024]{0,1:T(8,128)S(1)} collective-permute-done((f32[64,1024]{0,1:T(8,128)S(1)}, f32[64,1024]{0,1:T(8,128)S(1)}, u32[]{:S(2)}, u32[]{:S(2)}) %collective-permute-start.7) | collective-permute-done | bytes 262176 | tf_op jit(solution)/shard_map/ppermute | solution.py:22
  143.8 6.4 %collective-permute-start.8 = (f32[64,1024]{0,1:T(8,128)S(1)}, f32[64,1024]{0,1:T(8,128)S(1)}, u32[]{:S(2)}, u32[]{:S(2)}) collective-permute-start(f32[64,1024]{0,1:T(8,128)S(1)} %convolution_add_fusion.3), channel_id=1, source_target_pairs={{0,32},{8,40},{16,48},{24,56},{32,64},{40,72},{48,80},{56,88},{64,... | collective-permute-start | bytes 786440 | tf_op jit(solution)/shard_map/ppermute | solution.py:22
  150.4 37.9 %collective-permute-done.8 = f32[64,1024]{0,1:T(8,128)S(1)} collective-permute-done((f32[64,1024]{0,1:T(8,128)S(1)}, f32[64,1024]{0,1:T(8,128)S(1)}, u32[]{:S(2)}, u32[]{:S(2)}) %collective-permute-start.8) | collective-permute-done | bytes 262176 | tf_op jit(solution)/shard_map/ppermute | solution.py:22
  188.9 1.9 collective-permute-start.9
  191.0 28.6 %collective-permute-done.9 = f32[64,1024]{0,1:T(8,128)S(1)} collective-permute-done((f32[64,1024]{0,1:T(8,128)S(1)}, f32[64,1024]{0,1:T(8,128)S(1)}, u32[]{:S(2)}, u32[]{:S(2)}) %collective-permute-start.9) | collective-permute-done | bytes 262176 | tf_op jit(solution)/shard_map/ppermute | solution.py:22
  220.2 1.3 collective-permute-start.10
  221.7 15.8 %collective-permute-done.10 = f32[64,1024]{0,1:T(8,128)S(1)} collective-permute-done((f32[64,1024]{0,1:T(8,128)S(1)}, f32[64,1024]{0,1:T(8,128)S(1)}, u32[]{:S(2)}, u32[]{:S(2)}) %collective-permute-start.10) | collective-permute-done | bytes 262176 | tf_op jit(solution)/shard_map/ppermute | solution.py:22
  238.0 0.9 copy.72
  (47 shorter events, 6.9 us)
Async XLA Ops:
  0.0 87.9 %copy-start = (f32[64,64]{1,0:T(8,128)S(1)}, f32[64,64]{1,0:T(8,128)}, u32[]{:S(2)}) copy-start(f32[64,64]{1,0:T(8,128)} %param.13) | copy-start | bytes 49156
  0.0 10.7 %copy-start.11 = (f32[64,96]{1,0:T(8,128)S(1)}, f32[64,96]{1,0:T(8,128)}, u32[]{:S(2)}) copy-start(f32[64,96]{1,0:T(8,128)} %constant.35.clone) | copy-start | bytes 73732
  0.0 10.6 %copy-start.10 = (f32[64,64]{1,0:T(8,128)S(1)}, f32[64,64]{1,0:T(8,128)}, u32[]{:S(2)}) copy-start(f32[64,64]{1,0:T(8,128)} %param.11) | copy-start | bytes 49156
  0.0 10.7 %copy-start.7 = (f32[64,96]{1,0:T(8,128)S(1)}, f32[64,96]{1,0:T(8,128)}, u32[]{:S(2)}) copy-start(f32[64,96]{1,0:T(8,128)} %param.12) | copy-start | bytes 73732
  0.0 11.0 %copy-start.9 = (s32[6,1024]{1,0:T(8,128)S(1)}, s32[6,1024]{1,0:T(8,128)}, u32[]{:S(2)}) copy-start(s32[6,1024]{1,0:T(8,128)} %param.14) | copy-start | bytes 73732
  3.5 0.6 copy-start.8
  8.5 8.1 %collective-permute-start = (f32[16,512]{0,1:T(8,128)S(1)}, f32[16,512]{0,1:T(8,128)S(1)}, u32[]{:S(2)}, u32[]{:S(2)}) collective-permute-start(f32[16,512]{0,1:T(8,128)S(1)} %get-tuple-element.9), channel_id=1, source_target_pairs={{0,1},{1,2},{2,3},{3,4},{4,5},{5,6},{6,7},{7,0},{8,9},{9,10},{10,1... | collective-permute-start | bytes 98312 | tf_op jit(solution)/shard_map/ppermute | solution.py:27
  9.8 9.9 %collective-permute-start.1 = (f32[16,512]{0,1:T(8,128)S(1)}, f32[16,512]{0,1:T(8,128)S(1)}, u32[]{:S(2)}, u32[]{:S(2)}) collective-permute-start(f32[16,512]{0,1:T(8,128)S(1)} %get-tuple-element.10), channel_id=1, source_target_pairs={{0,7},{1,0},{2,1},{3,2},{4,3},{5,4},{6,5},{7,6},{8,15},{9,8},{10,9... | collective-permute-start | bytes 98312 | tf_op jit(solution)/shard_map/ppermute | solution.py:27
  19.6 13.5 %copy-start.2 = (f32[6,128,128]{2,1,0:T(8,128)S(1)}, f32[6,128,128]{2,1,0:T(8,128)}, u32[]{:S(2)}) copy-start(f32[6,128,128]{2,1,0:T(8,128)} %constant.34.clone) | copy-start | bytes 1179652
  33.2 4.9 %copy-start.6 = (s32[6,1024]{1,0:T(8,128)S(1)}, s32[6,1024]{1,0:T(8,128)}, u32[]{:S(2)}) copy-start(s32[6,1024]{1,0:T(8,128)} %param.15) | copy-start | bytes 73732
  38.0 3.7 %copy-start.3 = (f32[1,64,1024]{2,1,0:T(8,128)S(1)}, f32[1,64,1024]{2,1,0:T(8,128)}, u32[]{:S(2)}) copy-start(f32[1,64,1024]{2,1,0:T(8,128)} %param.10) | copy-start | bytes 786436
  48.0 6.9 %collective-permute-start.2 = (f32[16,512]{0,1:T(8,128)S(1)}, f32[16,512]{0,1:T(8,128)S(1)}, u32[]{:S(2)}, u32[]{:S(2)}) collective-permute-start(f32[16,512]{0,1:T(8,128)S(1)} %get-tuple-element.7), channel_id=1, source_target_pairs={{0,1},{1,2},{2,3},{3,4},{4,5},{5,6},{6,7},{7,0},{8,9},{9,10},{10,1... | collective-permute-start | bytes 98312 | tf_op jit(solution)/shard_map/ppermute | solution.py:27
  48.3 9.0 %collective-permute-start.3 = (f32[16,512]{0,1:T(8,128)S(1)}, f32[16,512]{0,1:T(8,128)S(1)}, u32[]{:S(2)}, u32[]{:S(2)}) collective-permute-start(f32[16,512]{0,1:T(8,128)S(1)} %get-tuple-element.8), channel_id=1, source_target_pairs={{0,7},{1,0},{2,1},{3,2},{4,3},{5,4},{6,5},{7,6},{8,15},{9,8},{10,9... | collective-permute-start | bytes 98312 | tf_op jit(solution)/shard_map/ppermute | solution.py:27
  80.6 14.3 %copy-start.1 = (f32[1024,128]{1,0:T(8,128)S(1)}, f32[1024,128]{1,0:T(8,128)}, u32[]{:S(2)}) copy-start(f32[1024,128]{1,0:T(8,128)} %pad.36.table_ref) | copy-start | bytes 1572868
  85.8 6.7 %collective-permute-start.4 = (f32[16,512]{0,1:T(8,128)}, f32[16,512]{0,1:T(8,128)}, u32[]{:S(2)}, u32[]{:S(2)}) collective-permute-start(f32[16,512]{0,1:T(8,128)} %get-tuple-element.5), channel_id=1, source_target_pairs={{0,1},{1,2},{2,3},{3,4},{4,5},{5,6},{6,7},{7,0},{8,9},{9,10},{10,1... | collective-permute-start | bytes 98312 | tf_op jit(solution)/shard_map/ppermute | solution.py:27
  86.1 8.8 %collective-permute-start.5 = (f32[16,512]{0,1:T(8,128)}, f32[16,512]{0,1:T(8,128)}, u32[]{:S(2)}, u32[]{:S(2)}) collective-permute-start(f32[16,512]{0,1:T(8,128)} %get-tuple-element.6), channel_id=1, source_target_pairs={{0,7},{1,0},{2,1},{3,2},{4,3},{5,4},{6,5},{7,6},{8,15},{9,8},{10,9... | collective-permute-start | bytes 98312 | tf_op jit(solution)/shard_map/ppermute | solution.py:27
  113.3 2.7 %copy-start.4 = (f32[64,1024]{0,1:T(8,128)S(1)}, f32[64,1024]{0,1:T(8,128)}, u32[]{:S(2)}) copy-start(f32[64,1024]{0,1:T(8,128)} %fusion.37) | copy-start | bytes 786436
  113.3 2.7 %copy-start.5 = (f32[1024,64]{1,0:T(8,128)S(1)}, f32[1024,64]{1,0:T(8,128)}, u32[]{:S(2)}) copy-start(f32[1024,64]{1,0:T(8,128)} %get-tuple-element.12) | copy-start | bytes 786436
  116.9 10.5 %collective-permute-start.6 = (f32[64,1024]{0,1:T(8,128)S(1)}, f32[64,1024]{0,1:T(8,128)S(1)}, u32[]{:S(2)}, u32[]{:S(2)}) collective-permute-start(f32[64,1024]{0,1:T(8,128)S(1)} %add_select_fusion), channel_id=1, source_target_pairs={{0,8},{8,16},{16,24},{24,32},{32,40},{40,48},{48,56},{56,64},{64,7... | collective-permute-start | bytes 786440 | tf_op jit(solution)/shard_map/ppermute | solution.py:22
  127.9 15.3 %collective-permute-start.7 = (f32[64,1024]{0,1:T(8,128)S(1)}, f32[64,1024]{0,1:T(8,128)S(1)}, u32[]{:S(2)}, u32[]{:S(2)}) collective-permute-start(f32[64,1024]{0,1:T(8,128)S(1)} %fusion.14), channel_id=1, source_target_pairs={{0,16},{8,24},{16,32},{24,40},{32,48},{40,56},{48,64},{56,72},{64,... | collective-permute-start | bytes 786440 | tf_op jit(solution)/shard_map/ppermute | solution.py:22
  143.8 44.5 %collective-permute-start.8 = (f32[64,1024]{0,1:T(8,128)S(1)}, f32[64,1024]{0,1:T(8,128)S(1)}, u32[]{:S(2)}, u32[]{:S(2)}) collective-permute-start(f32[64,1024]{0,1:T(8,128)S(1)} %convolution_add_fusion.3), channel_id=1, source_target_pairs={{0,32},{8,40},{16,48},{24,56},{32,64},{40,72},{48,80},{56,88},{64,... | collective-permute-start | bytes 786440 | tf_op jit(solution)/shard_map/ppermute | solution.py:22
  188.9 30.7 %collective-permute-start.9 = (f32[64,1024]{0,1:T(8,128)S(1)}, f32[64,1024]{0,1:T(8,128)S(1)}, u32[]{:S(2)}, u32[]{:S(2)}) collective-permute-start(f32[64,1024]{0,1:T(8,128)S(1)} %convolution_add_fusion.2), channel_id=1, source_target_pairs={{0,64},{8,72},{16,80},{24,88},{32,96},{40,104},{48,112},{56,120},{... | collective-permute-start | bytes 786440 | tf_op jit(solution)/shard_map/ppermute | solution.py:22
  220.2 17.2 %collective-permute-start.10 = (f32[64,1024]{0,1:T(8,128)S(1)}, f32[64,1024]{0,1:T(8,128)S(1)}, u32[]{:S(2)}, u32[]{:S(2)}) collective-permute-start(f32[64,1024]{0,1:T(8,128)S(1)} %convolution_add_fusion.1), channel_id=1, source_target_pairs={{0,128},{8,136},{16,144},{24,152},{32,160},{40,168},{48,176},{56,1... | collective-permute-start | bytes 786440 | tf_op jit(solution)/shard_map/ppermute | solution.py:22

commit v3 on v2

--- a/solution.py
+++ b/solution.py
@@ -11,6 +11,7 @@
 STEPS = 3
 LANES = 128
 UNROLL = 8
+SCAN_PIECES = 4
 
 
 time_step = 0.05
@@ -144,8 +145,11 @@
     offset = 1
     peers = lax.axis_size("tm")
     while offset < peers:
-        arrived = from_behind(total, "tm", offset)
-        total = total + product(power, arrived)
+        pieces = jnp.split(total, SCAN_PIECES, axis=1)
+        arrived = [from_behind(piece, "tm", offset) for piece in pieces]
+        total = jnp.concatenate(
+            [piece + product(power, got) for piece, got in zip(pieces, arrived)], axis=1
+        )
         offset *= 2
         if offset < peers:
             power = product(power, power)

time: 240 us -> 209 us (0.87)
  the two profiles are of different devices: /device:TPU:54 before, /device:TPU:22 now
where the time goes in v3:
time: 209 us; the launch traced here: 208 us
  starting transfers between devices  73.6 us (35%)
  Pallas kernels  44.1 us (21%)
  waiting for transfers between devices  37.2 us (18%)
  matrix products  34.1 us (16%)
  local copies, waits for them, and re-layouts  12.3 us (6%)
  other arithmetic  5.58 us (3%)
    ppermute x20, starting transfers between devices, from_behind(): return lax.ppermute(shard, axis, pairs)  67.3 us
    pallas_call x6, Pallas kernels, gather_rows(): pl.pallas_call(gather_kernel, out_shape=jax.ShapeDtypeStruct((idx.shape[0...  44.1 us
    ppermute x6, waiting for transfers between devices, ring(): lax.ppermute(shard, axis, [(i, (i + by) % peers) for i in range(peers)])  18.8 us
    ppermute x20, waiting for transfers between devices, from_behind(): return lax.ppermute(shard, axis, pairs)  18.4 us
    dot_general x3, matrix products, fine_step(): jnp.einsum('fer,frq->feq', beside, pick, precision=lax.Precision.HIGHEST,...  14.5 us
    dot_general x29, matrix products, product(): jnp.dot(matrix, vector, precision=lax.Precision.HIGHEST, preferred_elemen...  10.6 us
    dot_general x3, matrix products, fine_step(): jnp.einsum('feq,fqn->en', chosen, spread, precision=lax.Precision.HIGHEST...  8.96 us
    ppermute x6, starting transfers between devices, ring(): lax.ppermute(shard, axis, [(i, (i + by) % peers) for i in range(peers)])  6.31 us
  transfers between devices with their start and end apart: 26, of which 15 were waited for; matrix products, arithmetic and copies ran while one was open for 5% of the time, Pallas kernels for 0%

profile of v3, /device:TPU:22, one launch (start us, length us, event | category | flops | bytes accessed | tf_op | source)
XLA Modules:
  0.0 207.7 jit_solution(6259330117160535107)
XLA Ops:
  4.1 3.3 %shard_map.100 = f32[1024,128]{1,0:T(8,128)} custom-call(s32[1024]{0:T(1024)} %copy-done.10, f32[1024,128]{1,0:T(8,128)} %pad.30.table_ref), custom_call_target="tpu_custom_call" | custom-call | tf_op jit(solution)/shard_map/pallas_call | solution.py:86
  10.7 1.8 fusion.39
  13.7 3.0 %collective-permute-done = f32[16,512]{0,1:T(8,128)S(1)} collective-permute-done((f32[16,512]{0,1:T(8,128)S(1)}, f32[16,512]{0,1:T(8,128)S(1)}, u32[]{:S(2)}, u32[]{:S(2)}) %collective-permute-start) | collective-permute-done | bytes 32800 | tf_op jit(solution)/shard_map/ppermute | solution.py:28
  16.7 3.0 %collective-permute-done.1 = f32[16,512]{0,1:T(8,128)S(1)} collective-permute-done((f32[16,512]{0,1:T(8,128)S(1)}, f32[16,512]{0,1:T(8,128)S(1)}, u32[]{:S(2)}, u32[]{:S(2)}) %collective-permute-start.1) | collective-permute-done | bytes 32800 | tf_op jit(solution)/shard_map/ppermute | solution.py:28
  20.8 11.4 %shard_map.101 = f32[6144,128]{1,0:T(8,128)} custom-call(s32[6144]{0:T(1024)} %reshape.30.idx_ref, f32[2048,128]{1,0:T(8,128)} %select_maximum_fusion.4.table_ref), custom_call_target="tpu_custom_call" | custom-call | tf_op jit(solution)/shard_map/pallas_call | solution.py:86
  32.2 4.9 %fusion.46 = f32[6,1024,128]{2,1,0:T(8,128)S(1)} fusion(f32[6,1024,128]{2,1,0:T(8,128)} %bitcast.146, f32[6,128,128]{2,1,0:T(8,128)S(1)} %copy-done.3), kind=kOutput, calls=%fused_computation.103 | convolution fusion | flops 1207959552 | bytes 6684672 | tf_op jit(solution)/shard_map/fer,frq->feq/dot_general | solution.py:110
  37.1 3.6 %fusion = f32[1024,64,1]{0,1,2:T(8,128)S(1)} fusion(f32[6,128,64]{2,1,0:T(8,128)S(1)} %bitcast.148, f32[6,1024,128]{2,1,0:T(8,128)S(1)} %fusion.46, s32[128]{0:T(128)S(1)} %and_select_fusion, s32[6,1024]{1,0:T(8,128)S(1)} %copy-done.8), kind=kOutput, calls=%fused_computation.3 | convolution fusion | flops 605552640 | bytes 3629568 | tf_op jit(solution)/shard_map/feq,fqn->en/dot_general | solution.py:115
  42.5 3.3 %shard_map.102 = f32[1024,128]{1,0:T(8,128)} custom-call(s32[1024]{0:T(1024)} %copy-done.10, f32[1024,128]{1,0:T(8,128)} %pad.33.table_ref), custom_call_target="tpu_custom_call" | custom-call | tf_op jit(solution)/shard_map/pallas_call | solution.py:86
  47.4 1.7 collective-permute-start.3
  49.3 4.7 %collective-permute-done.2 = f32[16,512]{0,1:T(8,128)S(1)} collective-permute-done((f32[16,512]{0,1:T(8,128)S(1)}, f32[16,512]{0,1:T(8,128)S(1)}, u32[]{:S(2)}, u32[]{:S(2)}) %collective-permute-start.2) | collective-permute-done | bytes 32800 | tf_op jit(solution)/shard_map/ppermute | solution.py:28
  53.9 2.4 %collective-permute-done.3 = f32[16,512]{0,1:T(8,128)S(1)} collective-permute-done((f32[16,512]{0,1:T(8,128)S(1)}, f32[16,512]{0,1:T(8,128)S(1)}, u32[]{:S(2)}, u32[]{:S(2)}) %collective-permute-start.3) | collective-permute-done | bytes 32800 | tf_op jit(solution)/shard_map/ppermute | solution.py:28
  56.4 2.2 %select_maximum_fusion.2.table_ref = f32[2048,128]{1,0:T(8,128)} fusion(f32[512,16]{1,0:T(8,128)S(1)} %bitcast.156, f32[512,16]{1,0:T(8,128)S(1)} %bitcast.155, f32[1024,128]{1,0:T(8,128)} %pad.33.table_ref), kind=kLoop, calls=%fused_computation.53 | loop fusion | flops 2097152 | bytes 1638400 | tf_op jit(solution)/shard_map/concatenate | solution.py:108
  58.5 11.4 %shard_map.103 = f32[6144,128]{1,0:T(8,128)} custom-call(s32[6144]{0:T(1024)} %reshape.30.idx_ref, f32[2048,128]{1,0:T(8,128)} %select_maximum_fusion.2.table_ref), custom_call_target="tpu_custom_call" | custom-call | tf_op jit(solution)/shard_map/pallas_call | solution.py:86
  69.9 4.8 %fusion.47 = f32[6,1024,128]{2,1,0:T(8,128)S(1)} fusion(f32[6,1024,128]{2,1,0:T(8,128)} %bitcast.147, f32[6,128,128]{2,1,0:T(8,128)S(1)} %copy-done.3), kind=kOutput, calls=%fused_computation.104 | convolution fusion | flops 1207959552 | bytes 6684672 | tf_op jit(solution)/shard_map/fer,frq->feq/dot_general | solution.py:110
  74.7 2.7 %fusion.13 = f32[1024,64]{1,0:T(8,128)S(1)} fusion(f32[6,128,64]{2,1,0:T(8,128)S(1)} %bitcast.149, f32[6,1024,128]{2,1,0:T(8,128)S(1)} %fusion.47, s32[128]{0:T(128)S(1)} %and_select_fusion, s32[6,1024]{1,0:T(8,128)S(1)} %copy-done.8), kind=kOutput, calls=%fused_computation.18 | convolution fusion | flops 605552640 | bytes 3629568 | tf_op jit(solution)/shard_map/feq,fqn->en/dot_general | solution.py:115
  77.4 1.4 fusion.35
  79.7 3.4 %shard_map.104 = f32[1024,128]{1,0:T(8,128)} custom-call(s32[1024]{0:T(1024)} %copy-done.10, f32[1024,128]{1,0:T(8,128)} %pad.36.table_ref), custom_call_target="tpu_custom_call" | custom-call | tf_op jit(solution)/shard_map/pallas_call | solution.py:86
  84.6 1.7 collective-permute-start.5
  87.5 3.3 %collective-permute-done.4 = f32[16,512]{0,1:T(8,128)} collective-permute-done((f32[16,512]{0,1:T(8,128)S(1)}, f32[16,512]{0,1:T(8,128)}, u32[]{:S(2)}, u32[]{:S(2)}) %collective-permute-start.4) | collective-permute-done | bytes 32800 | tf_op jit(solution)/shard_map/ppermute | solution.py:28
  90.8 2.4 %collective-permute-done.5 = f32[16,512]{0,1:T(8,128)} collective-permute-done((f32[16,512]{0,1:T(8,128)S(1)}, f32[16,512]{0,1:T(8,128)}, u32[]{:S(2)}, u32[]{:S(2)}) %collective-permute-start.5) | collective-permute-done | bytes 32800 | tf_op jit(solution)/shard_map/ppermute | solution.py:28
  93.2 2.1 %select_maximum_fusion.table_ref = f32[2048,128]{1,0:T(8,128)} fusion(f32[512,16]{1,0:T(8,128)} %bitcast.25, f32[512,16]{1,0:T(8,128)} %bitcast.23, f32[1024,128]{1,0:T(8,128)S(1)} %copy-done.1), kind=kLoop, calls=%fused_computation.51 | loop fusion | flops 2097152 | bytes 1638400 | tf_op jit(solution)/shard_map/concatenate | solution.py:108
  95.3 11.4 %shard_map.105 = f32[6144,128]{1,0:T(8,128)} custom-call(s32[6144]{0:T(1024)} %reshape.30.idx_ref, f32[2048,128]{1,0:T(8,128)} %select_maximum_fusion.table_ref), custom_call_target="tpu_custom_call" | custom-call | tf_op jit(solution)/shard_map/pallas_call | solution.py:86
  106.7 4.8 %fusion.48 = f32[6,1024,128]{2,1,0:T(8,128)S(1)} fusion(f32[6,1024,128]{2,1,0:T(8,128)} %bitcast.145, f32[6,128,128]{2,1,0:T(8,128)S(1)} %copy-done.3), kind=kOutput, calls=%fused_computation.105 | convolution fusion | flops 1207959552 | bytes 6684672 | tf_op jit(solution)/shard_map/fer,frq->feq/dot_general | solution.py:110
  111.6 2.7 %fusion.12 = f32[64,1024]{0,1:T(8,128)S(1)} fusion(f32[6,128,64]{2,1,0:T(8,128)S(1)} %bitcast.150, f32[6,1024,128]{2,1,0:T(8,128)S(1)} %fusion.48, s32[128]{0:T(128)S(1)} %and_select_fusion, s32[6,1024]{1,0:T(8,128)S(1)} %copy-done.8), kind=kOutput, calls=%fused_computation.17 | convolution fusion | flops 605552640 | bytes 3629568 | tf_op jit(solution)/shard_map/feq,fqn->en/dot_general | solution.py:115
  115.2 1.9 collective-permute-start.6
  117.3 3.9 %collective-permute-start.11 = (f32[64,256]{0,1:T(8,128)S(1)}, f32[64,256]{0,1:T(8,128)S(1)}, u32[]{:S(2)}, u32[]{:S(2)}) collective-permute-start(f32[64,256]{0,1:T(8,128)S(1)} %get-tuple-element.8), channel_id=1, source_target_pairs={{0,8},{8,16},{16,24},{24,32},{32,40},{40,48},{48,56},{56,64},{64,7... | collective-permute-start | bytes 196616 | tf_op jit(solution)/shard_map/ppermute | solution.py:23
  121.2 1.9 collective-permute-start.16
  123.2 3.9 %collective-permute-start.21 = (f32[64,256]{0,1:T(8,128)S(1)}, f32[64,256]{0,1:T(8,128)S(1)}, u32[]{:S(2)}, u32[]{:S(2)}) collective-permute-start(f32[64,256]{0,1:T(8,128)S(1)} %get-tuple-element.6), channel_id=1, source_target_pairs={{0,8},{8,16},{16,24},{24,32},{32,40},{40,48},{48,56},{56,64},{64,7... | collective-permute-start | bytes 196616 | tf_op jit(solution)/shard_map/ppermute | solution.py:23
  127.4 3.8 %collective-permute-start.7 = (f32[64,256]{0,1:T(8,128)S(1)}, f32[64,256]{0,1:T(8,128)S(1)}, u32[]{:S(2)}, u32[]{:S(2)}) collective-permute-start(f32[64,256]{0,1:T(8,128)S(1)} %fusion.22), channel_id=1, source_target_pairs={{0,16},{8,24},{16,32},{24,40},{32,48},{40,56},{48,64},{56,72},{64,... | collective-permute-start | bytes 196616 | tf_op jit(solution)/shard_map/ppermute | solution.py:23
  131.5 5.0 %collective-permute-start.12 = (f32[64,256]{0,1:T(8,128)S(1)}, f32[64,256]{0,1:T(8,128)S(1)}, u32[]{:S(2)}, u32[]{:S(2)}) collective-permute-start(f32[64,256]{0,1:T(8,128)S(1)} %fusion.21), channel_id=1, source_target_pairs={{0,16},{8,24},{16,32},{24,40},{32,48},{40,56},{48,64},{56,72},{64,... | collective-permute-start | bytes 196616 | tf_op jit(solution)/shard_map/ppermute | solution.py:23
  136.8 2.9 %collective-permute-start.17 = (f32[64,256]{0,1:T(8,128)S(1)}, f32[64,256]{0,1:T(8,128)S(1)}, u32[]{:S(2)}, u32[]{:S(2)}) collective-permute-start(f32[64,256]{0,1:T(8,128)S(1)} %fusion.20), channel_id=1, source_target_pairs={{0,16},{8,24},{16,32},{24,40},{32,48},{40,56},{48,64},{56,72},{64,... | collective-permute-start | bytes 196616 | tf_op jit(solution)/shard_map/ppermute | solution.py:23
  140.0 2.9 %collective-permute-start.22 = (f32[64,256]{0,1:T(8,128)S(1)}, f32[64,256]{0,1:T(8,128)S(1)}, u32[]{:S(2)}, u32[]{:S(2)}) collective-permute-start(f32[64,256]{0,1:T(8,128)S(1)} %fusion.19), channel_id=1, source_target_pairs={{0,16},{8,24},{16,32},{24,40},{32,48},{40,56},{48,64},{56,72},{64,... | collective-permute-start | bytes 196616 | tf_op jit(solution)/shard_map/ppermute | solution.py:23
  143.3 2.4 %collective-permute-start.8 = (f32[64,256]{0,1:T(8,128)S(1)}, f32[64,256]{0,1:T(8,128)S(1)}, u32[]{:S(2)}, u32[]{:S(2)}) collective-permute-start(f32[64,256]{0,1:T(8,128)S(1)} %convolution_add_fusion.17), channel_id=1, source_target_pairs={{0,32},{8,40},{16,48},{24,56},{32,64},{40,72},{48,80},{56,88},{64,... | collective-permute-start | bytes 196616 | tf_op jit(solution)/shard_map/ppermute | solution.py:23
  145.9 1.9 collective-permute-start.13
  148.1 1.9 collective-permute-start.18
  150.8 12.1 %collective-permute-start.23 = (f32[64,256]{0,1:T(8,128)S(1)}, f32[64,256]{0,1:T(8,128)S(1)}, u32[]{:S(2)}, u32[]{:S(2)}) collective-permute-start(f32[64,256]{0,1:T(8,128)S(1)} %convolution_add_fusion.5), channel_id=1, source_target_pairs={{0,32},{8,40},{16,48},{24,56},{32,64},{40,72},{48,80},{56,88},{64,... | collective-permute-start | bytes 196616 | tf_op jit(solution)/shard_map/ppermute | solution.py:23
  163.2 1.9 collective-permute-start.9
  165.1 4.0 %collective-permute-done.13 = f32[64,256]{0,1:T(8,128)S(1)} collective-permute-done((f32[64,256]{0,1:T(8,128)S(1)}, f32[64,256]{0,1:T(8,128)S(1)}, u32[]{:S(2)}, u32[]{:S(2)}) %collective-permute-start.13) | collective-permute-done | bytes 65568 | tf_op jit(solution)/shard_map/ppermute | solution.py:23
  169.4 1.9 collective-permute-start.14
  172.2 1.9 collective-permute-start.19
  174.1 1.3 collective-permute-done.23
  175.7 11.7 %collective-permute-start.24 = (f32[64,256]{0,1:T(8,128)S(1)}, f32[64,256]{0,1:T(8,128)S(1)}, u32[]{:S(2)}, u32[]{:S(2)}) collective-permute-start(f32[64,256]{0,1:T(8,128)S(1)} %convolution_add_fusion.4), channel_id=1, source_target_pairs={{0,64},{8,72},{16,80},{24,88},{32,96},{40,104},{48,112},{56,120},{... | collective-permute-start | bytes 196616 | tf_op jit(solution)/shard_map/ppermute | solution.py:23
  187.7 1.3 collective-permute-start.10
  189.2 1.3 collective-permute-start.15
  190.5 5.1 %collective-permute-done.19 = f32[64,256]{0,1:T(8,128)S(1)} collective-permute-done((f32[64,256]{0,1:T(8,128)S(1)}, f32[64,256]{0,1:T(8,128)S(1)}, u32[]{:S(2)}, u32[]{:S(2)}) %collective-permute-start.19) | collective-permute-done | bytes 65568 | tf_op jit(solution)/shard_map/ppermute | solution.py:23
  195.9 1.3 collective-permute-start.20
  199.5 1.4 collective-permute-done.15
  201.2 3.9 %collective-permute-done.20 = f32[64,256]{0,1:T(8,128)S(1)} collective-permute-done((f32[64,256]{0,1:T(8,128)S(1)}, f32[64,256]{0,1:T(8,128)S(1)}, u32[]{:S(2)}, u32[]{:S(2)}) %collective-permute-start.20) | collective-permute-done | bytes 65568 | tf_op jit(solution)/shard_map/ppermute | solution.py:23
  (98 shorter events, 27.8 us)
Async XLA Ops:
  0.0 10.7 %copy-start = (f32[64,64]{1,0:T(8,128)S(1)}, f32[64,64]{1,0:T(8,128)}, u32[]{:S(2)}) copy-start(f32[64,64]{1,0:T(8,128)} %param.13) | copy-start | bytes 49156
  0.0 12.7 %copy-start.13 = (f32[64,96]{1,0:T(8,128)S(1)}, f32[64,96]{1,0:T(8,128)}, u32[]{:S(2)}) copy-start(f32[64,96]{1,0:T(8,128)} %constant.35.clone) | copy-start | bytes 73732
  0.0 10.7 %copy-start.4 = (f32[1,64,1024]{2,1,0:T(8,128)S(1)}, f32[1,64,1024]{2,1,0:T(8,128)}, u32[]{:S(2)}) copy-start(f32[1,64,1024]{2,1,0:T(8,128)} %param.10) | copy-start | bytes 786436
  0.0 12.6 %copy-start.12 = (f32[64,64]{1,0:T(8,128)S(1)}, f32[64,64]{1,0:T(8,128)}, u32[]{:S(2)}) copy-start(f32[64,64]{1,0:T(8,128)} %param.11) | copy-start | bytes 49156
  0.0 12.7 %copy-start.9 = (f32[64,96]{1,0:T(8,128)S(1)}, f32[64,96]{1,0:T(8,128)}, u32[]{:S(2)}) copy-start(f32[64,96]{1,0:T(8,128)} %param.12) | copy-start | bytes 73732
  0.0 13.0 %copy-start.11 = (s32[6,1024]{1,0:T(8,128)S(1)}, s32[6,1024]{1,0:T(8,128)}, u32[]{:S(2)}) copy-start(s32[6,1024]{1,0:T(8,128)} %param.14) | copy-start | bytes 73732
  2.1 17.6 %copy-start.2 = (f32[1024,128]{1,0:T(8,128)S(1)}, f32[1024,128]{1,0:T(8,128)}, u32[]{:S(2)}) copy-start(f32[1024,128]{1,0:T(8,128)} %pad.30.table_ref) | copy-start | bytes 1572868
  3.5 0.6 copy-start.10
  8.6 8.1 %collective-permute-start = (f32[16,512]{0,1:T(8,128)S(1)}, f32[16,512]{0,1:T(8,128)S(1)}, u32[]{:S(2)}, u32[]{:S(2)}) collective-permute-start(f32[16,512]{0,1:T(8,128)S(1)} %get-tuple-element.13), channel_id=1, source_target_pairs={{0,1},{1,2},{2,3},{3,4},{4,5},{5,6},{6,7},{7,0},{8,9},{9,10},{10,1... | collective-permute-start | bytes 98312 | tf_op jit(solution)/shard_map/ppermute | solution.py:28
  9.8 9.9 %collective-permute-start.1 = (f32[16,512]{0,1:T(8,128)S(1)}, f32[16,512]{0,1:T(8,128)S(1)}, u32[]{:S(2)}, u32[]{:S(2)}) collective-permute-start(f32[16,512]{0,1:T(8,128)S(1)} %get-tuple-element.14), channel_id=1, source_target_pairs={{0,7},{1,0},{2,1},{3,2},{4,3},{5,4},{6,5},{7,6},{8,15},{9,8},{10,9... | collective-permute-start | bytes 98312 | tf_op jit(solution)/shard_map/ppermute | solution.py:28
  19.7 12.5 %copy-start.3 = (f32[6,128,128]{2,1,0:T(8,128)S(1)}, f32[6,128,128]{2,1,0:T(8,128)}, u32[]{:S(2)}) copy-start(f32[6,128,128]{2,1,0:T(8,128)} %constant.34.clone) | copy-start | bytes 1179652
  32.2 4.9 %copy-start.8 = (s32[6,1024]{1,0:T(8,128)S(1)}, s32[6,1024]{1,0:T(8,128)}, u32[]{:S(2)}) copy-start(s32[6,1024]{1,0:T(8,128)} %param.15) | copy-start | bytes 73732
  47.0 6.9 %collective-permute-start.2 = (f32[16,512]{0,1:T(8,128)S(1)}, f32[16,512]{0,1:T(8,128)S(1)}, u32[]{:S(2)}, u32[]{:S(2)}) collective-permute-start(f32[16,512]{0,1:T(8,128)S(1)} %get-tuple-element.11), channel_id=1, source_target_pairs={{0,1},{1,2},{2,3},{3,4},{4,5},{5,6},{6,7},{7,0},{8,9},{9,10},{10,1... | collective-permute-start | bytes 98312 | tf_op jit(solution)/shard_map/ppermute | solution.py:28
  47.4 9.0 %collective-permute-start.3 = (f32[16,512]{0,1:T(8,128)S(1)}, f32[16,512]{0,1:T(8,128)S(1)}, u32[]{:S(2)}, u32[]{:S(2)}) collective-permute-start(f32[16,512]{0,1:T(8,128)S(1)} %get-tuple-element.12), channel_id=1, source_target_pairs={{0,7},{1,0},{2,1},{3,2},{4,3},{5,4},{6,5},{7,6},{8,15},{9,8},{10,9... | collective-permute-start | bytes 98312 | tf_op jit(solution)/shard_map/ppermute | solution.py:28
  79.7 13.5 %copy-start.1 = (f32[1024,128]{1,0:T(8,128)S(1)}, f32[1024,128]{1,0:T(8,128)}, u32[]{:S(2)}) copy-start(f32[1024,128]{1,0:T(8,128)} %pad.36.table_ref) | copy-start | bytes 1572868
  84.2 6.6 %collective-permute-start.4 = (f32[16,512]{0,1:T(8,128)S(1)}, f32[16,512]{0,1:T(8,128)}, u32[]{:S(2)}, u32[]{:S(2)}) collective-permute-start(f32[16,512]{0,1:T(8,128)S(1)} %get-tuple-element.9), channel_id=1, source_target_pairs={{0,1},{1,2},{2,3},{3,4},{4,5},{5,6},{6,7},{7,0},{8,9},{9,10},{10,1... | collective-permute-start | bytes 98312 | tf_op jit(solution)/shard_map/ppermute | solution.py:28
  84.6 8.6 %collective-permute-start.5 = (f32[16,512]{0,1:T(8,128)S(1)}, f32[16,512]{0,1:T(8,128)}, u32[]{:S(2)}, u32[]{:S(2)}) collective-permute-start(f32[16,512]{0,1:T(8,128)S(1)} %get-tuple-element.10), channel_id=1, source_target_pairs={{0,7},{1,0},{2,1},{3,2},{4,3},{5,4},{6,5},{7,6},{8,15},{9,8},{10,9... | collective-permute-start | bytes 98312 | tf_op jit(solution)/shard_map/ppermute | solution.py:28
  111.6 2.7 %copy-start.5 = (f32[64,1024]{0,1:T(8,128)S(1)}, f32[64,1024]{0,1:T(8,128)}, u32[]{:S(2)}) copy-start(f32[64,1024]{0,1:T(8,128)} %copy.86) | copy-start | bytes 786436
  111.6 2.7 %copy-start.6 = (f32[64,1024]{0,1:T(8,128)S(1)}, f32[64,1024]{0,1:T(8,128)}, u32[]{:S(2)}) copy-start(f32[64,1024]{0,1:T(8,128)} %fusion.39) | copy-start | bytes 786436
  111.6 2.7 %copy-start.7 = (f32[1024,64]{1,0:T(8,128)S(1)}, f32[1024,64]{1,0:T(8,128)}, u32[]{:S(2)}) copy-start(f32[1024,64]{1,0:T(8,128)} %get-tuple-element.16) | copy-start | bytes 786436
  115.2 11.9 %collective-permute-start.6 = (f32[64,256]{0,1:T(8,128)S(1)}, f32[64,256]{0,1:T(8,128)S(1)}, u32[]{:S(2)}, u32[]{:S(2)}) collective-permute-start(f32[64,256]{0,1:T(8,128)S(1)} %get-tuple-element.5), channel_id=1, source_target_pairs={{0,8},{8,16},{16,24},{24,32},{32,40},{40,48},{48,56},{56,64},{64,7... | collective-permute-start | bytes 196616 | tf_op jit(solution)/shard_map/ppermute | solution.py:23
  117.3 13.9 %collective-permute-start.11 = (f32[64,256]{0,1:T(8,128)S(1)}, f32[64,256]{0,1:T(8,128)S(1)}, u32[]{:S(2)}, u32[]{:S(2)}) collective-permute-start(f32[64,256]{0,1:T(8,128)S(1)} %get-tuple-element.8), channel_id=1, source_target_pairs={{0,8},{8,16},{16,24},{24,32},{32,40},{40,48},{48,56},{56,64},{64,7... | collective-permute-start | bytes 196616 | tf_op jit(solution)/shard_map/ppermute | solution.py:23
  121.2 15.3 %collective-permute-start.16 = (f32[64,256]{0,1:T(8,128)S(1)}, f32[64,256]{0,1:T(8,128)S(1)}, u32[]{:S(2)}, u32[]{:S(2)}) collective-permute-start(f32[64,256]{0,1:T(8,128)S(1)} %get-tuple-element.7), channel_id=1, source_target_pairs={{0,8},{8,16},{16,24},{24,32},{32,40},{40,48},{48,56},{56,64},{64,7... | collective-permute-start | bytes 196616 | tf_op jit(solution)/shard_map/ppermute | solution.py:23
  123.2 16.6 %collective-permute-start.21 = (f32[64,256]{0,1:T(8,128)S(1)}, f32[64,256]{0,1:T(8,128)S(1)}, u32[]{:S(2)}, u32[]{:S(2)}) collective-permute-start(f32[64,256]{0,1:T(8,128)S(1)} %get-tuple-element.6), channel_id=1, source_target_pairs={{0,8},{8,16},{16,24},{24,32},{32,40},{40,48},{48,56},{56,64},{64,7... | collective-permute-start | bytes 196616 | tf_op jit(solution)/shard_map/ppermute | solution.py:23
  127.4 15.6 %collective-permute-start.7 = (f32[64,256]{0,1:T(8,128)S(1)}, f32[64,256]{0,1:T(8,128)S(1)}, u32[]{:S(2)}, u32[]{:S(2)}) collective-permute-start(f32[64,256]{0,1:T(8,128)S(1)} %fusion.22), channel_id=1, source_target_pairs={{0,16},{8,24},{16,32},{24,40},{32,48},{40,56},{48,64},{56,72},{64,... | collective-permute-start | bytes 196616 | tf_op jit(solution)/shard_map/ppermute | solution.py:23
  131.5 14.1 %collective-permute-start.12 = (f32[64,256]{0,1:T(8,128)S(1)}, f32[64,256]{0,1:T(8,128)S(1)}, u32[]{:S(2)}, u32[]{:S(2)}) collective-permute-start(f32[64,256]{0,1:T(8,128)S(1)} %fusion.21), channel_id=1, source_target_pairs={{0,16},{8,24},{16,32},{24,40},{32,48},{40,56},{48,64},{56,72},{64,... | collective-permute-start | bytes 196616 | tf_op jit(solution)/shard_map/ppermute | solution.py:23
  136.8 11.0 %collective-permute-start.17 = (f32[64,256]{0,1:T(8,128)S(1)}, f32[64,256]{0,1:T(8,128)S(1)}, u32[]{:S(2)}, u32[]{:S(2)}) collective-permute-start(f32[64,256]{0,1:T(8,128)S(1)} %fusion.20), channel_id=1, source_target_pairs={{0,16},{8,24},{16,32},{24,40},{32,48},{40,56},{48,64},{56,72},{64,... | collective-permute-start | bytes 196616 | tf_op jit(solution)/shard_map/ppermute | solution.py:23
  140.0 10.5 %collective-permute-start.22 = (f32[64,256]{0,1:T(8,128)S(1)}, f32[64,256]{0,1:T(8,128)S(1)}, u32[]{:S(2)}, u32[]{:S(2)}) collective-permute-start(f32[64,256]{0,1:T(8,128)S(1)} %fusion.19), channel_id=1, source_target_pairs={{0,16},{8,24},{16,32},{24,40},{32,48},{40,56},{48,64},{56,72},{64,... | collective-permute-start | bytes 196616 | tf_op jit(solution)/shard_map/ppermute | solution.py:23
  143.3 19.7 %collective-permute-start.8 = (f32[64,256]{0,1:T(8,128)S(1)}, f32[64,256]{0,1:T(8,128)S(1)}, u32[]{:S(2)}, u32[]{:S(2)}) collective-permute-start(f32[64,256]{0,1:T(8,128)S(1)} %convolution_add_fusion.17), channel_id=1, source_target_pairs={{0,32},{8,40},{16,48},{24,56},{32,64},{40,72},{48,80},{56,88},{64,... | collective-permute-start | bytes 196616 | tf_op jit(solution)/shard_map/ppermute | solution.py:23
  145.9 23.2 %collective-permute-start.13 = (f32[64,256]{0,1:T(8,128)S(1)}, f32[64,256]{0,1:T(8,128)S(1)}, u32[]{:S(2)}, u32[]{:S(2)}) collective-permute-start(f32[64,256]{0,1:T(8,128)S(1)} %convolution_add_fusion.13), channel_id=1, source_target_pairs={{0,32},{8,40},{16,48},{24,56},{32,64},{40,72},{48,80},{56,88},{64,... | collective-permute-start | bytes 196616 | tf_op jit(solution)/shard_map/ppermute | solution.py:23
  148.1 23.8 %collective-permute-start.18 = (f32[64,256]{0,1:T(8,128)S(1)}, f32[64,256]{0,1:T(8,128)S(1)}, u32[]{:S(2)}, u32[]{:S(2)}) collective-permute-start(f32[64,256]{0,1:T(8,128)S(1)} %convolution_add_fusion.9), channel_id=1, source_target_pairs={{0,32},{8,40},{16,48},{24,56},{32,64},{40,72},{48,80},{56,88},{64,... | collective-permute-start | bytes 196616 | tf_op jit(solution)/shard_map/ppermute | solution.py:23
  150.8 24.7 %collective-permute-start.23 = (f32[64,256]{0,1:T(8,128)S(1)}, f32[64,256]{0,1:T(8,128)S(1)}, u32[]{:S(2)}, u32[]{:S(2)}) collective-permute-start(f32[64,256]{0,1:T(8,128)S(1)} %convolution_add_fusion.5), channel_id=1, source_target_pairs={{0,32},{8,40},{16,48},{24,56},{32,64},{40,72},{48,80},{56,88},{64,... | collective-permute-start | bytes 196616 | tf_op jit(solution)/shard_map/ppermute | solution.py:23
  163.2 24.2 %collective-permute-start.9 = (f32[64,256]{0,1:T(8,128)S(1)}, f32[64,256]{0,1:T(8,128)S(1)}, u32[]{:S(2)}, u32[]{:S(2)}) collective-permute-start(f32[64,256]{0,1:T(8,128)S(1)} %convolution_add_fusion.16), channel_id=1, source_target_pairs={{0,64},{8,72},{16,80},{24,88},{32,96},{40,104},{48,112},{56,120},{... | collective-permute-start | bytes 196616 | tf_op jit(solution)/shard_map/ppermute | solution.py:23
  169.4 19.6 %collective-permute-start.14 = (f32[64,256]{0,1:T(8,128)S(1)}, f32[64,256]{0,1:T(8,128)S(1)}, u32[]{:S(2)}, u32[]{:S(2)}) collective-permute-start(f32[64,256]{0,1:T(8,128)S(1)} %convolution_add_fusion.12), channel_id=1, source_target_pairs={{0,64},{8,72},{16,80},{24,88},{32,96},{40,104},{48,112},{56,120},{... | collective-permute-start | bytes 196616 | tf_op jit(solution)/shard_map/ppermute | solution.py:23
  172.2 23.4 %collective-permute-start.19 = (f32[64,256]{0,1:T(8,128)S(1)}, f32[64,256]{0,1:T(8,128)S(1)}, u32[]{:S(2)}, u32[]{:S(2)}) collective-permute-start(f32[64,256]{0,1:T(8,128)S(1)} %convolution_add_fusion.8), channel_id=1, source_target_pairs={{0,64},{8,72},{16,80},{24,88},{32,96},{40,104},{48,112},{56,120},{... | collective-permute-start | bytes 196616 | tf_op jit(solution)/shard_map/ppermute | solution.py:23
  175.7 21.5 %collective-permute-start.24 = (f32[64,256]{0,1:T(8,128)S(1)}, f32[64,256]{0,1:T(8,128)S(1)}, u32[]{:S(2)}, u32[]{:S(2)}) collective-permute-start(f32[64,256]{0,1:T(8,128)S(1)} %convolution_add_fusion.4), channel_id=1, source_target_pairs={{0,64},{8,72},{16,80},{24,88},{32,96},{40,104},{48,112},{56,120},{... | collective-permute-start | bytes 196616 | tf_op jit(solution)/shard_map/ppermute | solution.py:23
  187.7 11.6 %collective-permute-start.10 = (f32[64,256]{0,1:T(8,128)S(1)}, f32[64,256]{0,1:T(8,128)S(1)}, u32[]{:S(2)}, u32[]{:S(2)}) collective-permute-start(f32[64,256]{0,1:T(8,128)S(1)} %convolution_add_fusion.15), channel_id=1, source_target_pairs={{0,128},{8,136},{16,144},{24,152},{32,160},{40,168},{48,176},{56,1... | collective-permute-start | bytes 196616 | tf_op jit(solution)/shard_map/ppermute | solution.py:23
  189.2 11.7 %collective-permute-start.15 = (f32[64,256]{0,1:T(8,128)S(1)}, f32[64,256]{0,1:T(8,128)S(1)}, u32[]{:S(2)}, u32[]{:S(2)}) collective-permute-start(f32[64,256]{0,1:T(8,128)S(1)} %convolution_add_fusion.11), channel_id=1, source_target_pairs={{0,128},{8,136},{16,144},{24,152},{32,160},{40,168},{48,176},{56,1... | collective-permute-start | bytes 196616 | tf_op jit(solution)/shard_map/ppermute | solution.py:23
  195.9 9.2 %collective-permute-start.20 = (f32[64,256]{0,1:T(8,128)S(1)}, f32[64,256]{0,1:T(8,128)S(1)}, u32[]{:S(2)}, u32[]{:S(2)}) collective-permute-start(f32[64,256]{0,1:T(8,128)S(1)} %convolution_add_fusion.7), channel_id=1, source_target_pairs={{0,128},{8,136},{16,144},{24,152},{32,160},{40,168},{48,176},{56,1... | collective-permute-start | bytes 196616 | tf_op jit(solution)/shard_map/ppermute | solution.py:23
  197.5 9.0 %collective-permute-start.25 = (f32[64,256]{0,1:T(8,128)S(1)}, f32[64,256]{0,1:T(8,128)S(1)}, u32[]{:S(2)}, u32[]{:S(2)}) collective-permute-start(f32[64,256]{0,1:T(8,128)S(1)} %convolution_add_fusion.3), channel_id=1, source_target_pairs={{0,128},{8,136},{16,144},{24,152},{32,160},{40,168},{48,176},{56,1... | collective-permute-start | bytes 196616 | tf_op jit(solution)/shard_map/ppermute | solution.py:23

commit v4 on v3

--- a/solution.py
+++ b/solution.py
@@ -83,9 +83,11 @@
 
 
 def gather_rows(table, idx):
+    moved = 4 * table.shape[1] * (2 * idx.shape[0] + table.shape[0])
     return pl.pallas_call(
         gather_kernel,
         out_shape=jax.ShapeDtypeStruct((idx.shape[0], table.shape[1]), table.dtype),
+        cost_estimate=pl.CostEstimate(flops=0, transcendentals=0, bytes_accessed=moved),
         in_specs=[
             pl.BlockSpec(memory_space=pltpu.SMEM),
             pl.BlockSpec(memory_space=pltpu.VMEM),
@@ -94,7 +96,7 @@
     )(idx, table)
 
 
-def fine_step(state, folded, pick, spread, mask, nbr_rows, send_rows):
+def fine_step(state, folded, pick, spread, mask, near_rows, far_rows, send_rows):
     elements = state.shape[0]
     padded = jnp.pad(state, ((0, 0), (0, LANES - state.shape[1])))
     sent = gather_rows(padded, send_rows)
@@ -103,19 +105,22 @@
     high_trace = sent[half:, 48:64].T
     before = ring(high_trace, "space", 1)
     after = ring(low_trace, "space", -1)
+    beside_near = gather_rows(padded, near_rows).reshape(4, elements, LANES)
     halo_low = jnp.pad(before.T, ((0, 0), (48, LANES - 64)))
     halo_high = jnp.pad(after.T, ((0, 0), (0, LANES - 16)))
     table = jnp.concatenate([padded, halo_low, halo_high], axis=0)
-    beside = gather_rows(table, nbr_rows).reshape(6, elements, LANES)
-    turned = jnp.einsum(
-        "fer,frq->feq", beside, pick, precision=lax.Precision.HIGHEST,
-        preferred_element_type=jnp.float32,
-    )
-    chosen = jnp.where(mask, turned, 0.0)
-    lifted = jnp.einsum(
-        "feq,fqn->en", chosen, spread, precision=lax.Precision.HIGHEST,
-        preferred_element_type=jnp.float32,
-    )
+    beside_far = gather_rows(table, far_rows).reshape(2, elements, LANES)
+    lifted = 0.0
+    for beside, faces in ((beside_far, slice(0, 2)), (beside_near, slice(2, 6))):
+        turned = jnp.einsum(
+            "fer,frq->feq", beside, pick[faces], precision=lax.Precision.HIGHEST,
+            preferred_element_type=jnp.float32,
+        )
+        chosen = jnp.where(mask[faces], turned, 0.0)
+        lifted = lifted + jnp.einsum(
+            "feq,fqn->en", chosen, spread[faces], precision=lax.Precision.HIGHEST,
+            preferred_element_type=jnp.float32,
+        )
     rate = product(state, folded) + lifted + state - state * state * state
     return state + time_step * rate
 
@@ -129,13 +134,16 @@
     folded = stiffness.T - product(own, lifting.T)
     lane_code = jnp.arange(LANES, dtype=jnp.int32) // 16
     mask = orientation[:, :, None] == lane_code[None, None, :]
-    nbr_rows = neighbor.reshape(-1)
+    far_rows = neighbor[:2].reshape(-1)
+    near_rows = neighbor[2:].reshape(-1)
     send_rows = jnp.concatenate([send_low, send_high])
 
     state_start = start_state[0]
     fine_state = state_start.T
     for step_id in range(STEPS):
-        fine_state = fine_step(fine_state, folded, pick, spread, mask, nbr_rows, send_rows)
+        fine_state = fine_step(
+            fine_state, folded, pick, spread, mask, near_rows, far_rows, send_rows
+        )
     fine_state = fine_state.T
     coarse_start = product(coarse, state_start)
     defect = fine_state - coarse_start

time: 209 us -> 211 us (level)
  waiting for transfers between devices: 37.2 us -> 23.3 us
  matrix products: 34.1 us -> 39.8 us
  Pallas kernels: 44.1 us -> 49.1 us
  local copies, waits for them, and re-layouts: 12.3 us -> 15.1 us
    ppermute x6, waiting for transfers between devices: 18.8 us -> 4.96 us  [ring(): lax.ppermute(shard, axis, [(i, (i + by) % peers) for i in range(peers)])]
    pallas_call x6 -> x9, Pallas kernels: 44.1 us -> 49.1 us  [gather_rows(): pl.pallas_call(gather_kernel, out_shape=jax.ShapeDtypeStruct((idx.shape[0...]
    dot_general x6 -> x12, matrix products: 23.5 us -> 27.3 us  [the longest x6 17.4 us: fine_step(): jnp.einsum('fer,frq->feq', beside, pick[faces], precision=lax.Precision.H...]
    unnamed x32 -> x52, local copies, waits for them, and re-layouts: 2.73 us -> 4.58 us
  transfers between devices with their start and end apart: 26 -> 26, of which waited for: 15 -> 11; matrix products, arithmetic and copies ran while one was open for 5% -> 14% of each run, Pallas kernels for 0% -> 4%
where the time goes in v4:
time: 211 us; the launch traced here: 210 us
  starting transfers between devices  74.7 us (35%)
  Pallas kernels  49.1 us (23%)
  matrix products  39.8 us (19%)
  waiting for transfers between devices  23.3 us (11%)
  local copies, waits for them, and re-layouts  15.1 us (7%)
  other arithmetic  6.81 us (3%)
    ppermute x20, starting transfers between devices, from_behind(): return lax.ppermute(shard, axis, pairs)  67.3 us
    pallas_call x9, Pallas kernels, gather_rows(): pl.pallas_call(gather_kernel, out_shape=jax.ShapeDtypeStruct((idx.shape[0...  49.1 us
    ppermute x20, waiting for transfers between devices, from_behind(): return lax.ppermute(shard, axis, pairs)  18.4 us
    dot_general x6, matrix products, fine_step(): jnp.einsum('fer,frq->feq', beside, pick[faces], precision=lax.Precision.H...  17.4 us
    dot_general x29, matrix products, product(): jnp.dot(matrix, vector, precision=lax.Precision.HIGHEST, preferred_elemen...  12.5 us
    dot_general x6, matrix products, fine_step(): jnp.einsum('feq,fqn->en', chosen, spread[faces], precision=lax.Precision....  9.92 us
    ppermute x6, starting transfers between devices, ring(): lax.ppermute(shard, axis, [(i, (i + by) % peers) for i in range(peers)])  7.44 us
    concatenate x3, other arithmetic, fine_step(): table = jnp.concatenate([padded, halo_low, halo_high], axis=0)  5.5 us
  transfers between devices with their start and end apart: 26, of which 11 were waited for; matrix products, arithmetic and copies ran while one was open for 14% of the time, Pallas kernels for 4%

profile of v4, /device:TPU:22, one launch (start us, length us, event | category | flops | bytes accessed | tf_op | source)
XLA Modules:
  0.0 209.8 jit_solution(4370572123521060679)
XLA Ops:
  4.0 3.3 %shard_map.100 = f32[1024,128]{1,0:T(8,128)} custom-call(s32[1024]{0:T(1024)} %copy-done.17, f32[1024,128]{1,0:T(8,128)} %pad.30.table_ref), custom_call_target="tpu_custom_call" | custom-call | bytes 1572864 | tf_op jit(solution)/shard_map/pallas_call | solution.py:87
  7.3 1.9 slice_bitcast_fusion.5
  11.2 1.8 fusion.49
  13.8 8.0 %shard_map.102 = f32[4096,128]{1,0:T(8,128)} custom-call(s32[4096]{0:T(1024)} %bitcast.196, f32[1024,128]{1,0:T(8,128)} %pad.30.table_ref), custom_call_target="tpu_custom_call" | custom-call | bytes 4718592 | tf_op jit(solution)/shard_map/pallas_call | solution.py:87
  23.5 3.5 %fusion.56 = f32[4,1024,128]{2,1,0:T(8,128)S(1)} fusion(f32[4,1024,128]{2,1,0:T(8,128)} %bitcast.185, f32[4,128,128]{2,1,0:T(8,128)S(1)} %copy-done.4), kind=kOutput, calls=%fused_computation.115 | convolution fusion | flops 805306368 | bytes 4456448 | tf_op jit(solution)/shard_map/fer,frq->feq/dot_general | solution.py:115
  27.3 2.4 %fusion.15 = f32[1024,64]{0,1:T(8,128)S(1)} fusion(f32[4,128,64]{2,1,0:T(8,128)S(1)} %bitcast.190, f32[4,1024,128]{2,1,0:T(8,128)S(1)} %fusion.56, pred[6,1024,128]{2,1,0:T(32,128)(4,1)S(1)} %broadcast_compare_fusion), kind=kOutput, calls=%fused_computation.22 | convolution fusion | flops 403177472 | bytes 3145728 | tf_op jit(solution)/shard_map/feq,fqn->en/dot_general | solution.py:120
  30.4 2.2 %select_maximum_fusion.4.table_ref = f32[2048,128]{1,0:T(8,128)} fusion(f32[512,16]{1,0:T(8,128)} %bitcast.6, f32[512,16]{1,0:T(8,128)} %bitcast.4, f32[1024,128]{1,0:T(8,128)S(1)} %copy-done.1), kind=kLoop, calls=%fused_computation.60 | loop fusion | flops 2097152 | bytes 1638400 | tf_op jit(solution)/shard_map/concatenate | solution.py:111
  32.6 5.0 %shard_map.101 = f32[2048,128]{1,0:T(8,128)} custom-call(s32[2048]{0:T(1024)} %bitcast.203, f32[2048,128]{1,0:T(8,128)} %select_maximum_fusion.4.table_ref), custom_call_target="tpu_custom_call" | custom-call | bytes 3145728 | tf_op jit(solution)/shard_map/pallas_call | solution.py:87
  37.6 2.3 %convolution_select_fusion.2 = f32[2,1024,128]{2,1,0:T(8,128)S(1)} fusion(f32[2,1024,128]{2,1,0:T(8,128)} %bitcast.188, f32[2,128,128]{2,1,0:T(8,128)S(1)} %copy-done.10, pred[6,1024,128]{2,1,0:T(32,128)(4,1)S(1)} %broadcast_compare_fusion), kind=kOutput, calls=%fused_computation.11 | convolution fusion | flops 402915328 | bytes 2490368 | tf_op jit(solution)/shard_map/fer,frq->feq/dot_general | solution.py:115
  45.2 3.2 %shard_map.103 = f32[1024,128]{1,0:T(8,128)} custom-call(s32[1024]{0:T(1024)} %copy-done.17, f32[1024,128]{1,0:T(8,128)} %pad.33.table_ref), custom_call_target="tpu_custom_call" | custom-call | bytes 1572864 | tf_op jit(solution)/shard_map/pallas_call | solution.py:87
  48.5 8.1 %shard_map.105 = f32[4096,128]{1,0:T(8,128)} custom-call(s32[4096]{0:T(1024)} %bitcast.197, f32[1024,128]{1,0:T(8,128)} %pad.33.table_ref), custom_call_target="tpu_custom_call" | custom-call | bytes 4718592 | tf_op jit(solution)/shard_map/pallas_call | solution.py:87
  57.5 3.3 %collective-permute-start.2 = (f32[16,512]{0,1:T(8,128)}, f32[16,512]{0,1:T(8,128)}, u32[]{:S(2)}, u32[]{:S(2)}) collective-permute-start(f32[16,512]{0,1:T(8,128)} %get-tuple-element.11), channel_id=1, source_target_pairs={{0,1},{1,2},{2,3},{3,4},{4,5},{5,6},{6,7},{7,0},{8,9},{9,10},{10,1... | collective-permute-start | bytes 98312 | tf_op jit(solution)/shard_map/ppermute | solution.py:28
  60.8 3.5 %fusion.57 = f32[4,1024,128]{2,1,0:T(8,128)S(1)} fusion(f32[4,1024,128]{2,1,0:T(8,128)} %bitcast.184, f32[4,128,128]{2,1,0:T(8,128)S(1)} %copy-done.4), kind=kOutput, calls=%fused_computation.116 | convolution fusion | flops 805306368 | bytes 4456448 | tf_op jit(solution)/shard_map/fer,frq->feq/dot_general | solution.py:115
  64.3 1.8 fusion.6
  66.1 1.9 copy.95
  68.1 2.3 %collective-permute-done.3 = f32[16,512]{0,1:T(8,128)} collective-permute-done((f32[16,512]{0,1:T(8,128)}, f32[16,512]{0,1:T(8,128)}, u32[]{:S(2)}, u32[]{:S(2)}) %collective-permute-start.3) | collective-permute-done | bytes 32800 | tf_op jit(solution)/shard_map/ppermute | solution.py:28
  70.4 2.2 %select_maximum_fusion.2.table_ref = f32[2048,128]{1,0:T(8,128)} fusion(f32[512,16]{1,0:T(8,128)} %bitcast.22, f32[512,16]{1,0:T(8,128)} %bitcast.20, f32[1024,128]{1,0:T(8,128)S(1)} %copy-done.3), kind=kLoop, calls=%fused_computation.58 | loop fusion | flops 2097152 | bytes 1638400 | tf_op jit(solution)/shard_map/concatenate | solution.py:111
  72.6 5.1 %shard_map.104 = f32[2048,128]{1,0:T(8,128)} custom-call(s32[2048]{0:T(1024)} %bitcast.204, f32[2048,128]{1,0:T(8,128)} %select_maximum_fusion.2.table_ref), custom_call_target="tpu_custom_call" | custom-call | bytes 3145728 | tf_op jit(solution)/shard_map/pallas_call | solution.py:87
  77.7 2.3 %convolution_select_fusion.1 = f32[2,1024,128]{2,1,0:T(8,128)S(1)} fusion(f32[2,1024,128]{2,1,0:T(8,128)} %bitcast.189, f32[2,128,128]{2,1,0:T(8,128)S(1)} %copy-done.11, pred[6,1024,128]{2,1,0:T(32,128)(4,1)S(1)} %broadcast_compare_fusion), kind=kOutput, calls=%fused_computation.10 | convolution fusion | flops 402915328 | bytes 2490368 | tf_op jit(solution)/shard_map/fer,frq->feq/dot_general | solution.py:115
  81.0 1.4 fusion.45
  83.2 3.2 %shard_map.106 = f32[1024,128]{1,0:T(8,128)} custom-call(s32[1024]{0:T(1024)} %copy-done.17, f32[1024,128]{1,0:T(8,128)} %pad.36.table_ref), custom_call_target="tpu_custom_call" | custom-call | bytes 1572864 | tf_op jit(solution)/shard_map/pallas_call | solution.py:87
  86.4 8.1 %shard_map.108 = f32[4096,128]{1,0:T(8,128)} custom-call(s32[4096]{0:T(1024)} %bitcast.198, f32[1024,128]{1,0:T(8,128)} %pad.36.table_ref), custom_call_target="tpu_custom_call" | custom-call | bytes 4718592 | tf_op jit(solution)/shard_map/pallas_call | solution.py:87
  94.7 1.9 collective-permute-start.4
  96.8 3.5 %fusion.58 = f32[4,1024,128]{2,1,0:T(8,128)S(1)} fusion(f32[4,1024,128]{2,1,0:T(8,128)} %bitcast.183, f32[4,128,128]{2,1,0:T(8,128)S(1)} %copy-done.4), kind=kOutput, calls=%fused_computation.117 | convolution fusion | flops 805306368 | bytes 4456448 | tf_op jit(solution)/shard_map/fer,frq->feq/dot_general | solution.py:115
  100.3 2.4 %fusion.18 = f32[1024,64]{0,1:T(8,128)S(1)} fusion(f32[4,128,64]{2,1,0:T(8,128)S(1)} %bitcast.192, f32[4,1024,128]{2,1,0:T(8,128)S(1)} %fusion.58, pred[6,1024,128]{2,1,0:T(32,128)(4,1)S(1)} %broadcast_compare_fusion), kind=kOutput, calls=%fused_computation.23 | convolution fusion | flops 403177472 | bytes 3145728 | tf_op jit(solution)/shard_map/feq,fqn->en/dot_general | solution.py:120
  102.7 2.6 %collective-permute-done.5 = f32[16,512]{0,1:T(8,128)S(1)} collective-permute-done((f32[16,512]{0,1:T(8,128)S(1)}, f32[16,512]{0,1:T(8,128)S(1)}, u32[]{:S(2)}, u32[]{:S(2)}) %collective-permute-start.5) | collective-permute-done | bytes 32800 | tf_op jit(solution)/shard_map/ppermute | solution.py:28
  106.4 5.0 %shard_map.107 = f32[2048,128]{1,0:T(8,128)} custom-call(s32[2048]{0:T(1024)} %bitcast.205, f32[2048,128]{1,0:T(8,128)} %select_maximum_fusion.table_ref), custom_call_target="tpu_custom_call" | custom-call | bytes 3145728 | tf_op jit(solution)/shard_map/pallas_call | solution.py:87
  111.5 2.3 %convolution_select_fusion = f32[2,1024,128]{2,1,0:T(8,128)S(1)} fusion(f32[2,1024,128]{2,1,0:T(8,128)} %bitcast.187, f32[2,128,128]{2,1,0:T(8,128)S(1)} %copy-done.11, pred[6,1024,128]{2,1,0:T(32,128)(4,1)S(1)} %broadcast_compare_fusion), kind=kOutput, calls=%fused_computation.9 | convolution fusion | flops 402915328 | bytes 2490368 | tf_op jit(solution)/shard_map/fer,frq->feq/dot_general | solution.py:115
  115.2 2.1 add_select_fusion
  117.3 1.9 collective-permute-start.6
  119.4 3.9 %collective-permute-start.11 = (f32[64,256]{0,1:T(8,128)S(1)}, f32[64,256]{0,1:T(8,128)S(1)}, u32[]{:S(2)}, u32[]{:S(2)}) collective-permute-start(f32[64,256]{0,1:T(8,128)S(1)} %get-tuple-element.8), channel_id=1, source_target_pairs={{0,8},{8,16},{16,24},{24,32},{32,40},{40,48},{48,56},{56,64},{64,7... | collective-permute-start | bytes 196616 | tf_op jit(solution)/shard_map/ppermute | solution.py:23
  123.4 1.9 collective-permute-start.16
  125.3 3.9 %collective-permute-start.21 = (f32[64,256]{0,1:T(8,128)S(1)}, f32[64,256]{0,1:T(8,128)S(1)}, u32[]{:S(2)}, u32[]{:S(2)}) collective-permute-start(f32[64,256]{0,1:T(8,128)S(1)} %get-tuple-element.6), channel_id=1, source_target_pairs={{0,8},{8,16},{16,24},{24,32},{32,40},{40,48},{48,56},{56,64},{64,7... | collective-permute-start | bytes 196616 | tf_op jit(solution)/shard_map/ppermute | solution.py:23
  129.5 3.8 %collective-permute-start.7 = (f32[64,256]{0,1:T(8,128)S(1)}, f32[64,256]{0,1:T(8,128)S(1)}, u32[]{:S(2)}, u32[]{:S(2)}) collective-permute-start(f32[64,256]{0,1:T(8,128)S(1)} %fusion.26), channel_id=1, source_target_pairs={{0,16},{8,24},{16,32},{24,40},{32,48},{40,56},{48,64},{56,72},{64,... | collective-permute-start | bytes 196616 | tf_op jit(solution)/shard_map/ppermute | solution.py:23
  133.6 5.0 %collective-permute-start.12 = (f32[64,256]{0,1:T(8,128)S(1)}, f32[64,256]{0,1:T(8,128)S(1)}, u32[]{:S(2)}, u32[]{:S(2)}) collective-permute-start(f32[64,256]{0,1:T(8,128)S(1)} %fusion.25), channel_id=1, source_target_pairs={{0,16},{8,24},{16,32},{24,40},{32,48},{40,56},{48,64},{56,72},{64,... | collective-permute-start | bytes 196616 | tf_op jit(solution)/shard_map/ppermute | solution.py:23
  138.9 2.9 %collective-permute-start.17 = (f32[64,256]{0,1:T(8,128)S(1)}, f32[64,256]{0,1:T(8,128)S(1)}, u32[]{:S(2)}, u32[]{:S(2)}) collective-permute-start(f32[64,256]{0,1:T(8,128)S(1)} %fusion.24), channel_id=1, source_target_pairs={{0,16},{8,24},{16,32},{24,40},{32,48},{40,56},{48,64},{56,72},{64,... | collective-permute-start | bytes 196616 | tf_op jit(solution)/shard_map/ppermute | solution.py:23
  142.2 2.9 %collective-permute-start.22 = (f32[64,256]{0,1:T(8,128)S(1)}, f32[64,256]{0,1:T(8,128)S(1)}, u32[]{:S(2)}, u32[]{:S(2)}) collective-permute-start(f32[64,256]{0,1:T(8,128)S(1)} %fusion.23), channel_id=1, source_target_pairs={{0,16},{8,24},{16,32},{24,40},{32,48},{40,56},{48,64},{56,72},{64,... | collective-permute-start | bytes 196616 | tf_op jit(solution)/shard_map/ppermute | solution.py:23
  145.4 2.4 %collective-permute-start.8 = (f32[64,256]{0,1:T(8,128)S(1)}, f32[64,256]{0,1:T(8,128)S(1)}, u32[]{:S(2)}, u32[]{:S(2)}) collective-permute-start(f32[64,256]{0,1:T(8,128)S(1)} %convolution_add_fusion.17), channel_id=1, source_target_pairs={{0,32},{8,40},{16,48},{24,56},{32,64},{40,72},{48,80},{56,88},{64,... | collective-permute-start | bytes 196616 | tf_op jit(solution)/shard_map/ppermute | solution.py:23
  148.0 1.9 collective-permute-start.13
  150.2 1.9 collective-permute-start.18
  152.9 12.1 %collective-permute-start.23 = (f32[64,256]{0,1:T(8,128)S(1)}, f32[64,256]{0,1:T(8,128)S(1)}, u32[]{:S(2)}, u32[]{:S(2)}) collective-permute-start(f32[64,256]{0,1:T(8,128)S(1)} %convolution_add_fusion.5), channel_id=1, source_target_pairs={{0,32},{8,40},{16,48},{24,56},{32,64},{40,72},{48,80},{56,88},{64,... | collective-permute-start | bytes 196616 | tf_op jit(solution)/shard_map/ppermute | solution.py:23
  165.3 1.9 collective-permute-start.9
  167.2 4.0 %collective-permute-done.13 = f32[64,256]{0,1:T(8,128)S(1)} collective-permute-done((f32[64,256]{0,1:T(8,128)S(1)}, f32[64,256]{0,1:T(8,128)S(1)}, u32[]{:S(2)}, u32[]{:S(2)}) %collective-permute-start.13) | collective-permute-done | bytes 65568 | tf_op jit(solution)/shard_map/ppermute | solution.py:23
  171.5 1.9 collective-permute-start.14
  174.3 1.9 collective-permute-start.19
  177.9 11.6 %collective-permute-start.24 = (f32[64,256]{0,1:T(8,128)S(1)}, f32[64,256]{0,1:T(8,128)S(1)}, u32[]{:S(2)}, u32[]{:S(2)}) collective-permute-start(f32[64,256]{0,1:T(8,128)S(1)} %convolution_add_fusion.4), channel_id=1, source_target_pairs={{0,64},{8,72},{16,80},{24,88},{32,96},{40,104},{48,112},{56,120},{... | collective-permute-start | bytes 196616 | tf_op jit(solution)/shard_map/ppermute | solution.py:23
  192.7 5.1 %collective-permute-done.19 = f32[64,256]{0,1:T(8,128)S(1)} collective-permute-done((f32[64,256]{0,1:T(8,128)S(1)}, f32[64,256]{0,1:T(8,128)S(1)}, u32[]{:S(2)}, u32[]{:S(2)}) %collective-permute-start.19) | collective-permute-done | bytes 65568 | tf_op jit(solution)/shard_map/ppermute | solution.py:23
  203.3 3.9 %collective-permute-done.20 = f32[64,256]{0,1:T(8,128)S(1)} collective-permute-done((f32[64,256]{0,1:T(8,128)S(1)}, f32[64,256]{0,1:T(8,128)S(1)}, u32[]{:S(2)}, u32[]{:S(2)}) %collective-permute-start.20) | collective-permute-done | bytes 65568 | tf_op jit(solution)/shard_map/ppermute | solution.py:23
  (131 shorter events, 37.1 us)
Async XLA Ops:
  0.0 11.2 %copy-start = (f32[64,64]{1,0:T(8,128)S(1)}, f32[64,64]{1,0:T(8,128)}, u32[]{:S(2)}) copy-start(f32[64,64]{1,0:T(8,128)} %param.13) | copy-start | bytes 49156
  0.0 11.2 %copy-start.5 = (f32[1,64,1024]{2,1,0:T(8,128)S(1)}, f32[1,64,1024]{2,1,0:T(8,128)}, u32[]{:S(2)}) copy-start(f32[1,64,1024]{2,1,0:T(8,128)} %param.10) | copy-start | bytes 786436
  1.2 11.9 %copy-start.21 = (s32[6,1024]{1,0:T(8,128)S(1)}, s32[6,1024]{1,0:T(8,128)}, u32[]{:S(2)}) copy-start(s32[6,1024]{1,0:T(8,128)} %param.14) | copy-start | bytes 73732
  3.4 0.6 copy-start.17
  7.3 14.6 %copy-start.16 = (f32[64,96]{1,0:T(8,128)S(1)}, f32[64,96]{1,0:T(8,128)}, u32[]{:S(2)}) copy-start(f32[64,96]{1,0:T(8,128)} %param.12) | copy-start | bytes 73732
  9.2 12.8 %copy-start.19 = (f32[64,64]{1,0:T(8,128)S(1)}, f32[64,64]{1,0:T(8,128)}, u32[]{:S(2)}) copy-start(f32[64,64]{1,0:T(8,128)} %param.11) | copy-start | bytes 49156
  9.2 13.2 %copy-start.18 = (s32[6,1024]{1,0:T(8,128)S(1)}, s32[6,1024]{1,0:T(8,128)}, u32[]{:S(2)}) copy-start(s32[6,1024]{1,0:T(8,128)} %param.15) | copy-start | bytes 73732
  9.2 21.2 %collective-permute-start = (f32[16,512]{0,1:T(8,128)}, f32[16,512]{0,1:T(8,128)}, u32[]{:S(2)}, u32[]{:S(2)}) collective-permute-start(f32[16,512]{0,1:T(8,128)} %get-tuple-element.13), channel_id=1, source_target_pairs={{0,1},{1,2},{2,3},{3,4},{4,5},{5,6},{6,7},{7,0},{8,9},{9,10},{10,1... | collective-permute-start | bytes 98312 | tf_op jit(solution)/shard_map/ppermute | solution.py:28
  10.4 20.0 %collective-permute-start.1 = (f32[16,512]{0,1:T(8,128)S(1)}, f32[16,512]{0,1:T(8,128)}, u32[]{:S(2)}, u32[]{:S(2)}) collective-permute-start(f32[16,512]{0,1:T(8,128)S(1)} %get-tuple-element.14), channel_id=1, source_target_pairs={{0,7},{1,0},{2,1},{3,2},{4,3},{5,4},{6,5},{7,6},{8,15},{9,8},{10,9... | collective-permute-start | bytes 98312 | tf_op jit(solution)/shard_map/ppermute | solution.py:28
  13.0 10.5 %copy-start.4 = (f32[4,128,128]{2,1,0:T(8,128)S(1)}, f32[4,128,128]{2,1,0:T(8,128)}, u32[]{:S(2)}) copy-start(f32[4,128,128]{2,1,0:T(8,128)} %constant.56) | copy-start | bytes 786436
  23.5 3.5 %copy-start.20 = (f32[64,96]{1,0:T(8,128)S(1)}, f32[64,96]{1,0:T(8,128)}, u32[]{:S(2)}) copy-start(f32[64,96]{1,0:T(8,128)} %constant.35.clone) | copy-start | bytes 73732
  27.1 3.3 %copy-start.1 = (f32[1024,128]{1,0:T(8,128)S(1)}, f32[1024,128]{1,0:T(8,128)}, u32[]{:S(2)}) copy-start(f32[1024,128]{1,0:T(8,128)} %pad.30.table_ref) | copy-start | bytes 1572868
  27.3 14.6 %copy-start.14 = (f32[64,64]{1,0:T(8,128)}, f32[64,64]{1,0:T(8,128)S(1)}, u32[]{:S(2)}) copy-start(f32[64,64]{1,0:T(8,128)S(1)} %convolution_subtract_fusion) | copy-start | bytes 49156
  30.3 7.3 %copy-start.10 = (f32[2,128,128]{2,1,0:T(8,128)S(1)}, f32[2,128,128]{2,1,0:T(8,128)}, u32[]{:S(2)}) copy-start(f32[2,128,128]{2,1,0:T(8,128)} %constant.55) | copy-start | bytes 393220
  39.9 0.7 copy-start.8
  48.5 8.1 %copy-start.7 = (f32[1024,128]{1,0:T(8,128)S(1)}, f32[1024,128]{1,0:T(8,128)}, u32[]{:S(2)}) copy-start(f32[1024,128]{1,0:T(8,128)} %shard_map.103) | copy-start | bytes 1572868
  57.5 10.6 %collective-permute-start.2 = (f32[16,512]{0,1:T(8,128)}, f32[16,512]{0,1:T(8,128)}, u32[]{:S(2)}, u32[]{:S(2)}) collective-permute-start(f32[16,512]{0,1:T(8,128)} %get-tuple-element.11), channel_id=1, source_target_pairs={{0,1},{1,2},{2,3},{3,4},{4,5},{5,6},{6,7},{7,0},{8,9},{9,10},{10,1... | collective-permute-start | bytes 98312 | tf_op jit(solution)/shard_map/ppermute | solution.py:28
  60.8 9.6 %collective-permute-start.3 = (f32[16,512]{0,1:T(8,128)}, f32[16,512]{0,1:T(8,128)}, u32[]{:S(2)}, u32[]{:S(2)}) collective-permute-start(f32[16,512]{0,1:T(8,128)} %get-tuple-element.12), channel_id=1, source_target_pairs={{0,7},{1,0},{2,1},{3,2},{4,3},{5,4},{6,5},{7,6},{8,15},{9,8},{10,9... | collective-permute-start | bytes 98312 | tf_op jit(solution)/shard_map/ppermute | solution.py:28
  64.3 6.1 %copy-start.3 = (f32[1024,128]{1,0:T(8,128)S(1)}, f32[1024,128]{1,0:T(8,128)}, u32[]{:S(2)}) copy-start(f32[1024,128]{1,0:T(8,128)} %pad.33.table_ref) | copy-start | bytes 1572868
  72.6 5.1 %copy-start.11 = (f32[2,128,128]{2,1,0:T(8,128)S(1)}, f32[2,128,128]{2,1,0:T(8,128)}, u32[]{:S(2)}) copy-start(f32[2,128,128]{2,1,0:T(8,128)} %constant.55) | copy-start | bytes 393220
  72.6 7.4 %copy-start.9 = (f32[2,8,16,64]{3,2,1,0:T(8,128)S(1)}, f32[2,8,16,64]{3,2,1,0:T(8,128)}, u32[]{:S(2)}) copy-start(f32[2,8,16,64]{3,2,1,0:T(8,128)} %copy-done.8) | copy-start | bytes 196612
  77.7 3.3 %copy-start.15 = (f32[64,64]{1,0:T(8,128)S(1)}, f32[64,64]{1,0:T(8,128)}, u32[]{:S(2)}) copy-start(f32[64,64]{1,0:T(8,128)} %copy-done.14) | copy-start | bytes 49156
  86.4 8.1 %copy-start.6 = (f32[1024,128]{1,0:T(8,128)S(1)}, f32[1024,128]{1,0:T(8,128)}, u32[]{:S(2)}) copy-start(f32[1024,128]{1,0:T(8,128)} %shard_map.106) | copy-start | bytes 1572868
  94.7 8.0 %collective-permute-start.4 = (f32[16,512]{0,1:T(8,128)S(1)}, f32[16,512]{0,1:T(8,128)S(1)}, u32[]{:S(2)}, u32[]{:S(2)}) collective-permute-start(f32[16,512]{0,1:T(8,128)S(1)} %get-tuple-element.9), channel_id=1, source_target_pairs={{0,1},{1,2},{2,3},{3,4},{4,5},{5,6},{6,7},{7,0},{8,9},{9,10},{10,1... | collective-permute-start | bytes 98312 | tf_op jit(solution)/shard_map/ppermute | solution.py:28
  96.5 8.8 %collective-permute-start.5 = (f32[16,512]{0,1:T(8,128)S(1)}, f32[16,512]{0,1:T(8,128)S(1)}, u32[]{:S(2)}, u32[]{:S(2)}) collective-permute-start(f32[16,512]{0,1:T(8,128)S(1)} %get-tuple-element.10), channel_id=1, source_target_pairs={{0,7},{1,0},{2,1},{3,2},{4,3},{5,4},{6,5},{7,6},{8,15},{9,8},{10,9... | collective-permute-start | bytes 98312 | tf_op jit(solution)/shard_map/ppermute | solution.py:28
  100.3 5.0 %copy-start.2 = (f32[1024,128]{1,0:T(8,128)S(1)}, f32[1024,128]{1,0:T(8,128)}, u32[]{:S(2)}) copy-start(f32[1024,128]{1,0:T(8,128)} %pad.36.table_ref) | copy-start | bytes 1572868
  111.5 3.7 %copy-start.12 = (f32[64,1024]{0,1:T(8,128)S(1)}, f32[64,1024]{0,1:T(8,128)}, u32[]{:S(2)}) copy-start(f32[64,1024]{0,1:T(8,128)} %copy.95) | copy-start | bytes 786436
  113.8 1.4 copy-start.13
  117.3 11.9 %collective-permute-start.6 = (f32[64,256]{0,1:T(8,128)S(1)}, f32[64,256]{0,1:T(8,128)S(1)}, u32[]{:S(2)}, u32[]{:S(2)}) collective-permute-start(f32[64,256]{0,1:T(8,128)S(1)} %get-tuple-element.5), channel_id=1, source_target_pairs={{0,8},{8,16},{16,24},{24,32},{32,40},{40,48},{48,56},{56,64},{64,7... | collective-permute-start | bytes 196616 | tf_op jit(solution)/shard_map/ppermute | solution.py:23
  119.4 13.9 %collective-permute-start.11 = (f32[64,256]{0,1:T(8,128)S(1)}, f32[64,256]{0,1:T(8,128)S(1)}, u32[]{:S(2)}, u32[]{:S(2)}) collective-permute-start(f32[64,256]{0,1:T(8,128)S(1)} %get-tuple-element.8), channel_id=1, source_target_pairs={{0,8},{8,16},{16,24},{24,32},{32,40},{40,48},{48,56},{56,64},{64,7... | collective-permute-start | bytes 196616 | tf_op jit(solution)/shard_map/ppermute | solution.py:23
  123.4 15.3 %collective-permute-start.16 = (f32[64,256]{0,1:T(8,128)S(1)}, f32[64,256]{0,1:T(8,128)S(1)}, u32[]{:S(2)}, u32[]{:S(2)}) collective-permute-start(f32[64,256]{0,1:T(8,128)S(1)} %get-tuple-element.7), channel_id=1, source_target_pairs={{0,8},{8,16},{16,24},{24,32},{32,40},{40,48},{48,56},{56,64},{64,7... | collective-permute-start | bytes 196616 | tf_op jit(solution)/shard_map/ppermute | solution.py:23
  125.3 16.6 %collective-permute-start.21 = (f32[64,256]{0,1:T(8,128)S(1)}, f32[64,256]{0,1:T(8,128)S(1)}, u32[]{:S(2)}, u32[]{:S(2)}) collective-permute-start(f32[64,256]{0,1:T(8,128)S(1)} %get-tuple-element.6), channel_id=1, source_target_pairs={{0,8},{8,16},{16,24},{24,32},{32,40},{40,48},{48,56},{56,64},{64,7... | collective-permute-start | bytes 196616 | tf_op jit(solution)/shard_map/ppermute | solution.py:23
  129.5 15.6 %collective-permute-start.7 = (f32[64,256]{0,1:T(8,128)S(1)}, f32[64,256]{0,1:T(8,128)S(1)}, u32[]{:S(2)}, u32[]{:S(2)}) collective-permute-start(f32[64,256]{0,1:T(8,128)S(1)} %fusion.26), channel_id=1, source_target_pairs={{0,16},{8,24},{16,32},{24,40},{32,48},{40,56},{48,64},{56,72},{64,... | collective-permute-start | bytes 196616 | tf_op jit(solution)/shard_map/ppermute | solution.py:23
  133.6 14.1 %collective-permute-start.12 = (f32[64,256]{0,1:T(8,128)S(1)}, f32[64,256]{0,1:T(8,128)S(1)}, u32[]{:S(2)}, u32[]{:S(2)}) collective-permute-start(f32[64,256]{0,1:T(8,128)S(1)} %fusion.25), channel_id=1, source_target_pairs={{0,16},{8,24},{16,32},{24,40},{32,48},{40,56},{48,64},{56,72},{64,... | collective-permute-start | bytes 196616 | tf_op jit(solution)/shard_map/ppermute | solution.py:23
  138.9 11.0 %collective-permute-start.17 = (f32[64,256]{0,1:T(8,128)S(1)}, f32[64,256]{0,1:T(8,128)S(1)}, u32[]{:S(2)}, u32[]{:S(2)}) collective-permute-start(f32[64,256]{0,1:T(8,128)S(1)} %fusion.24), channel_id=1, source_target_pairs={{0,16},{8,24},{16,32},{24,40},{32,48},{40,56},{48,64},{56,72},{64,... | collective-permute-start | bytes 196616 | tf_op jit(solution)/shard_map/ppermute | solution.py:23
  142.2 10.5 %collective-permute-start.22 = (f32[64,256]{0,1:T(8,128)S(1)}, f32[64,256]{0,1:T(8,128)S(1)}, u32[]{:S(2)}, u32[]{:S(2)}) collective-permute-start(f32[64,256]{0,1:T(8,128)S(1)} %fusion.23), channel_id=1, source_target_pairs={{0,16},{8,24},{16,32},{24,40},{32,48},{40,56},{48,64},{56,72},{64,... | collective-permute-start | bytes 196616 | tf_op jit(solution)/shard_map/ppermute | solution.py:23
  145.4 19.7 %collective-permute-start.8 = (f32[64,256]{0,1:T(8,128)S(1)}, f32[64,256]{0,1:T(8,128)S(1)}, u32[]{:S(2)}, u32[]{:S(2)}) collective-permute-start(f32[64,256]{0,1:T(8,128)S(1)} %convolution_add_fusion.17), channel_id=1, source_target_pairs={{0,32},{8,40},{16,48},{24,56},{32,64},{40,72},{48,80},{56,88},{64,... | collective-permute-start | bytes 196616 | tf_op jit(solution)/shard_map/ppermute | solution.py:23
  148.0 23.2 %collective-permute-start.13 = (f32[64,256]{0,1:T(8,128)S(1)}, f32[64,256]{0,1:T(8,128)S(1)}, u32[]{:S(2)}, u32[]{:S(2)}) collective-permute-start(f32[64,256]{0,1:T(8,128)S(1)} %convolution_add_fusion.13), channel_id=1, source_target_pairs={{0,32},{8,40},{16,48},{24,56},{32,64},{40,72},{48,80},{56,88},{64,... | collective-permute-start | bytes 196616 | tf_op jit(solution)/shard_map/ppermute | solution.py:23
  150.2 23.8 %collective-permute-start.18 = (f32[64,256]{0,1:T(8,128)S(1)}, f32[64,256]{0,1:T(8,128)S(1)}, u32[]{:S(2)}, u32[]{:S(2)}) collective-permute-start(f32[64,256]{0,1:T(8,128)S(1)} %convolution_add_fusion.9), channel_id=1, source_target_pairs={{0,32},{8,40},{16,48},{24,56},{32,64},{40,72},{48,80},{56,88},{64,... | collective-permute-start | bytes 196616 | tf_op jit(solution)/shard_map/ppermute | solution.py:23
  152.9 24.7 %collective-permute-start.23 = (f32[64,256]{0,1:T(8,128)S(1)}, f32[64,256]{0,1:T(8,128)S(1)}, u32[]{:S(2)}, u32[]{:S(2)}) collective-permute-start(f32[64,256]{0,1:T(8,128)S(1)} %convolution_add_fusion.5), channel_id=1, source_target_pairs={{0,32},{8,40},{16,48},{24,56},{32,64},{40,72},{48,80},{56,88},{64,... | collective-permute-start | bytes 196616 | tf_op jit(solution)/shard_map/ppermute | solution.py:23
  165.3 24.2 %collective-permute-start.9 = (f32[64,256]{0,1:T(8,128)S(1)}, f32[64,256]{0,1:T(8,128)S(1)}, u32[]{:S(2)}, u32[]{:S(2)}) collective-permute-start(f32[64,256]{0,1:T(8,128)S(1)} %convolution_add_fusion.16), channel_id=1, source_target_pairs={{0,64},{8,72},{16,80},{24,88},{32,96},{40,104},{48,112},{56,120},{... | collective-permute-start | bytes 196616 | tf_op jit(solution)/shard_map/ppermute | solution.py:23
  171.5 19.5 %collective-permute-start.14 = (f32[64,256]{0,1:T(8,128)S(1)}, f32[64,256]{0,1:T(8,128)S(1)}, u32[]{:S(2)}, u32[]{:S(2)}) collective-permute-start(f32[64,256]{0,1:T(8,128)S(1)} %convolution_add_fusion.12), channel_id=1, source_target_pairs={{0,64},{8,72},{16,80},{24,88},{32,96},{40,104},{48,112},{56,120},{... | collective-permute-start | bytes 196616 | tf_op jit(solution)/shard_map/ppermute | solution.py:23
  174.3 23.4 %collective-permute-start.19 = (f32[64,256]{0,1:T(8,128)S(1)}, f32[64,256]{0,1:T(8,128)S(1)}, u32[]{:S(2)}, u32[]{:S(2)}) collective-permute-start(f32[64,256]{0,1:T(8,128)S(1)} %convolution_add_fusion.8), channel_id=1, source_target_pairs={{0,64},{8,72},{16,80},{24,88},{32,96},{40,104},{48,112},{56,120},{... | collective-permute-start | bytes 196616 | tf_op jit(solution)/shard_map/ppermute | solution.py:23
  177.9 21.5 %collective-permute-start.24 = (f32[64,256]{0,1:T(8,128)S(1)}, f32[64,256]{0,1:T(8,128)S(1)}, u32[]{:S(2)}, u32[]{:S(2)}) collective-permute-start(f32[64,256]{0,1:T(8,128)S(1)} %convolution_add_fusion.4), channel_id=1, source_target_pairs={{0,64},{8,72},{16,80},{24,88},{32,96},{40,104},{48,112},{56,120},{... | collective-permute-start | bytes 196616 | tf_op jit(solution)/shard_map/ppermute | solution.py:23
  189.8 11.7 %collective-permute-start.10 = (f32[64,256]{0,1:T(8,128)S(1)}, f32[64,256]{0,1:T(8,128)S(1)}, u32[]{:S(2)}, u32[]{:S(2)}) collective-permute-start(f32[64,256]{0,1:T(8,128)S(1)} %convolution_add_fusion.15), channel_id=1, source_target_pairs={{0,128},{8,136},{16,144},{24,152},{32,160},{40,168},{48,176},{56,1... | collective-permute-start | bytes 196616 | tf_op jit(solution)/shard_map/ppermute | solution.py:23
  191.4 11.7 %collective-permute-start.15 = (f32[64,256]{0,1:T(8,128)S(1)}, f32[64,256]{0,1:T(8,128)S(1)}, u32[]{:S(2)}, u32[]{:S(2)}) collective-permute-start(f32[64,256]{0,1:T(8,128)S(1)} %convolution_add_fusion.11), channel_id=1, source_target_pairs={{0,128},{8,136},{16,144},{24,152},{32,160},{40,168},{48,176},{56,1... | collective-permute-start | bytes 196616 | tf_op jit(solution)/shard_map/ppermute | solution.py:23
  198.0 9.1 %collective-permute-start.20 = (f32[64,256]{0,1:T(8,128)S(1)}, f32[64,256]{0,1:T(8,128)S(1)}, u32[]{:S(2)}, u32[]{:S(2)}) collective-permute-start(f32[64,256]{0,1:T(8,128)S(1)} %convolution_add_fusion.7), channel_id=1, source_target_pairs={{0,128},{8,136},{16,144},{24,152},{32,160},{40,168},{48,176},{56,1... | collective-permute-start | bytes 196616 | tf_op jit(solution)/shard_map/ppermute | solution.py:23
  199.6 8.9 %collective-permute-start.25 = (f32[64,256]{0,1:T(8,128)S(1)}, f32[64,256]{0,1:T(8,128)S(1)}, u32[]{:S(2)}, u32[]{:S(2)}) collective-permute-start(f32[64,256]{0,1:T(8,128)S(1)} %convolution_add_fusion.3), channel_id=1, source_target_pairs={{0,128},{8,136},{16,144},{24,152},{32,160},{40,168},{48,176},{56,1... | collective-permute-start | bytes 196616 | tf_op jit(solution)/shard_map/ppermute | solution.py:23

commit v5 on v3

--- a/solution.py
+++ b/solution.py
@@ -94,30 +94,73 @@
     )(idx, table)
 
 
-def fine_step(state, folded, pick, spread, mask, nbr_rows, send_rows):
-    elements = state.shape[0]
-    padded = jnp.pad(state, ((0, 0), (0, LANES - state.shape[1])))
-    sent = gather_rows(padded, send_rows)
-    half = sent.shape[0] // 2
-    low_trace = sent[:half, 0:16].T
-    high_trace = sent[half:, 48:64].T
-    before = ring(high_trace, "space", 1)
-    after = ring(low_trace, "space", -1)
-    halo_low = jnp.pad(before.T, ((0, 0), (48, LANES - 64)))
-    halo_high = jnp.pad(after.T, ((0, 0), (0, LANES - 16)))
-    table = jnp.concatenate([padded, halo_low, halo_high], axis=0)
-    beside = gather_rows(table, nbr_rows).reshape(6, elements, LANES)
-    turned = jnp.einsum(
-        "fer,frq->feq", beside, pick, precision=lax.Precision.HIGHEST,
+def fused_kernel(with_send, idx_ref, send_ref, state_ref, halo_ref, mask_ref, pick_ref,
+                 spread_ref, folded_ref, out_ref, *rest):
+    if with_send:
+        sent_ref, table, beside = rest
+    else:
+        table, beside = rest
+    elements = state_ref.shape[0]
+    table[0:elements, :] = state_ref[...]
+    table[elements:, :] = halo_ref[...]
+
+    def gather(step, carry):
+        for u in range(UNROLL):
+            row = step * UNROLL + u
+            beside[pl.ds(row, 1), :] = table[pl.ds(idx_ref[row], 1), :]
+        return carry
+
+    lax.fori_loop(0, beside.shape[0] // UNROLL, gather, 0)
+    state = state_ref[...]
+    lifted = jnp.zeros_like(state)
+    for face in range(6):
+        turned = jnp.dot(
+            beside[face * elements:(face + 1) * elements, :], pick_ref[face],
+            precision=lax.Precision.HIGHEST, preferred_element_type=jnp.float32,
+        )
+        chosen = jnp.where(mask_ref[face] > 0.5, turned, 0.0)
+        lifted = lifted + jnp.dot(
+            chosen, spread_ref[face],
+            precision=lax.Precision.HIGHEST, preferred_element_type=jnp.float32,
+        )
+    own = jnp.dot(
+        state, folded_ref[...], precision=lax.Precision.HIGHEST,
         preferred_element_type=jnp.float32,
     )
-    chosen = jnp.where(mask, turned, 0.0)
-    lifted = jnp.einsum(
-        "feq,fqn->en", chosen, spread, precision=lax.Precision.HIGHEST,
-        preferred_element_type=jnp.float32,
-    )
-    rate = product(state, folded) + lifted + state - state * state * state
-    return state + time_step * rate
+    rate = own + lifted + state - state * state * state
+    out_ref[...] = state + time_step * rate
+    if with_send:
+        def send(step, carry):
+            for u in range(UNROLL):
+                row = step * UNROLL + u
+                sent_ref[pl.ds(row, 1), :] = out_ref[pl.ds(send_ref[row], 1), :]
+            return carry
+
+        lax.fori_loop(0, sent_ref.shape[0] // UNROLL, send, 0)
+
+
+def fused_step(state, halo, mask, pick, spread, folded, nbr_rows, send_rows, with_send):
+    elements, lanes = state.shape
+    block = jax.ShapeDtypeStruct((elements, lanes), state.dtype)
+    shapes = [block]
+    if with_send:
+        shapes.append(jax.ShapeDtypeStruct((send_rows.shape[0], lanes), state.dtype))
+    vmem = pl.BlockSpec(memory_space=pltpu.VMEM)
+    smem = pl.BlockSpec(memory_space=pltpu.SMEM)
+    flops = 2 * 6 * 6 * elements * lanes * (2 * lanes) + 2 * 6 * elements * lanes * lanes
+    moved = 4 * (4 * elements * lanes + mask.size + pick.size + spread.size)
+    result = pl.pallas_call(
+        functools.partial(fused_kernel, with_send),
+        out_shape=tuple(shapes),
+        in_specs=[smem, smem] + [vmem] * 6,
+        out_specs=tuple([vmem] * len(shapes)),
+        scratch_shapes=[
+            pltpu.VMEM((elements + halo.shape[0], lanes), jnp.float32),
+            pltpu.VMEM((nbr_rows.shape[0], lanes), jnp.float32),
+        ],
+        cost_estimate=pl.CostEstimate(flops=flops, transcendentals=0, bytes_accessed=moved),
+    )(nbr_rows, send_rows, state, halo, mask, pick, spread, folded)
+    return result
 
 
 def shards(start_state, stiffness, lifting, coarse, neighbor, orientation, send_low, send_high):
@@ -131,12 +174,32 @@
     mask = orientation[:, :, None] == lane_code[None, None, :]
     nbr_rows = neighbor.reshape(-1)
     send_rows = jnp.concatenate([send_low, send_high])
+    spread = jnp.pad(spread, ((0, 0), (0, 0), (0, LANES - 64)))
+    folded = jnp.pad(folded, ((0, LANES - 64), (0, LANES - 64)))
+    mask = mask.astype(jnp.float32)
 
     state_start = start_state[0]
-    fine_state = state_start.T
+    state = jnp.pad(state_start.T, ((0, 0), (0, LANES - state_start.shape[0])))
+    sent = gather_rows(state, send_rows)
+    half = send_low.shape[0]
     for step_id in range(STEPS):
-        fine_state = fine_step(fine_state, folded, pick, spread, mask, nbr_rows, send_rows)
-    fine_state = fine_state.T
+        before = ring(sent[half:, 48:64].T, "space", 1)
+        after = ring(sent[:half, 0:16].T, "space", -1)
+        halo = jnp.concatenate(
+            [
+                jnp.pad(before.T, ((0, 0), (48, LANES - 64))),
+                jnp.pad(after.T, ((0, 0), (0, LANES - 16))),
+            ],
+            axis=0,
+        )
+        with_send = step_id < STEPS - 1
+        result = fused_step(
+            state, halo, mask, pick, spread, folded, nbr_rows, send_rows, with_send
+        )
+        state = result[0]
+        if with_send:
+            sent = result[1]
+    fine_state = state[:, : state_start.shape[0]].T
     coarse_start = product(coarse, state_start)
     defect = fine_state - coarse_start
     is_first = lax.axis_index("tm") == 0

time: 209 us -> 197 us (0.943)
  matrix products: 34.1 us -> 8.12 us
  Pallas kernels: 44.1 us -> 62.2 us
  local copies, waits for them, and re-layouts: 12.3 us -> 9.99 us
    pallas_call x0 -> x3, Pallas kernels: none -> 58.9 us  [fused_step(): pl.pallas_call(functools.partial(fused_kernel, with_send), out_shape=tupl...]
    pallas_call x6 -> x1, Pallas kernels: 44.1 us -> 3.25 us  [gather_rows(): pl.pallas_call(gather_kernel, out_shape=jax.ShapeDtypeStruct((idx.shape[0...]
    dot_general x6 -> x0, matrix products: 23.5 us -> none  [the longest x3 14.5 us: fine_step(): jnp.einsum('fer,frq->feq', beside, pick, precision=lax.Precision.HIGHEST,...]
    convert_element_type x0 -> x1, other arithmetic: none -> 2.62 us  [shards(): mask = mask.astype(jnp.float32)]
    concatenate x3, other arithmetic: 5.42 us -> 2.81 us  [shards(): jnp.concatenate([jnp.pad(before.T, ((0, 0), (48, LANES - 64))), jnp.pad(a...]
    dot_general x29 -> x26, matrix products: 10.6 us -> 8.12 us  [product(): jnp.dot(matrix, vector, precision=lax.Precision.HIGHEST, preferred_elemen...]
where the time goes in v5:
time: 197 us; the launch traced here: 196 us
  starting transfers between devices  73.6 us (37%)
  Pallas kernels  62.2 us (32%)
  waiting for transfers between devices  35.9 us (18%)
  local copies, waits for them, and re-layouts  9.99 us (5%)
  matrix products  8.12 us (4%)
  other arithmetic  5.47 us (3%)
    ppermute x20, starting transfers between devices, from_behind(): return lax.ppermute(shard, axis, pairs)  67.3 us
    pallas_call x3, Pallas kernels, fused_step(): pl.pallas_call(functools.partial(fused_kernel, with_send), out_shape=tupl...  58.9 us
    ppermute x20, waiting for transfers between devices, from_behind(): return lax.ppermute(shard, axis, pairs)  18.4 us
    ppermute x6, waiting for transfers between devices, ring(): lax.ppermute(shard, axis, [(i, (i + by) % peers) for i in range(peers)])  17.5 us
    dot_general x26, matrix products, product(): jnp.dot(matrix, vector, precision=lax.Precision.HIGHEST, preferred_elemen...  8.12 us
    ppermute x6, starting transfers between devices, ring(): lax.ppermute(shard, axis, [(i, (i + by) % peers) for i in range(peers)])  6.31 us
  transfers between devices with their start and end apart: 26, of which 15 were waited for; matrix products, arithmetic and copies ran while one was open for 5% of the time, Pallas kernels for 0%

profile of v5, /device:TPU:22, one launch (start us, length us, event | category | flops | bytes accessed | tf_op | source)
XLA Modules:
  0.0 195.8 jit_solution(5020737136590413466)
XLA Ops:
  0.0 1.2 copy.37
  3.4 3.3 %shard_map.100 = f32[1024,128]{1,0:T(8,128)} custom-call(s32[1024]{0:T(1024)} %copy-done.7, f32[1024,128]{1,0:T(8,128)} %pad.32.table_ref.state_ref), custom_call_target="tpu_custom_call" | custom-call | tf_op jit(solution)/shard_map/pallas_call | solution.py:86
  6.7 1.2 slice_bitcast_fusion.2
  7.8 1.3 collective-permute-start
  10.0 2.6 %compare_convert_fusion.mask_ref = f32[6,1024,128]{2,1,0:T(8,128)} fusion(s32[128]{0:T(128)S(1)} %and_select_fusion, s32[6,1024]{1,0:T(8,128)S(1)} %copy-done.3), kind=kLoop, calls=%fused_computation | loop fusion | flops 1572864 | bytes 3170816 | tf_op jit(solution)/shard_map/convert_element_type | solution.py:179
  16.0 3.0 %collective-permute-done.1 = f32[16,512]{0,1:T(8,128)S(1)} collective-permute-done((f32[16,512]{0,1:T(8,128)S(1)}, f32[16,512]{0,1:T(8,128)S(1)}, u32[]{:S(2)}, u32[]{:S(2)}) %collective-permute-start.1) | collective-permute-done | bytes 32800 | tf_op jit(solution)/shard_map/ppermute | solution.py:28
  19.0 0.9 select_maximum_fusion.2.halo_ref
  19.9 20.2 %shard_map.101 = (f32[1024,128]{1,0:T(8,128)}, f32[1024,128]{1,0:T(8,128)}) custom-call(s32[6144]{0:T(1024)} %reshape.21.idx_ref, s32[1024]{0:T(1024)} %copy-done.7, f32[1024,128]{1,0:T(8,128)} %pad.32.table_ref.state_ref, f32[1024,128]{1,0:T(8,128)} %select_maximum_fusion.2.halo_ref, f32[6,1024,128]{2,1,0:T(8,128)} %compare_convert_fusion.mask_ref, ...), custom_call_target="tpu_custom_call" | custom-call | flops 2617245696 | bytes 6029312 | tf_op jit(solution)/shard_map/pallas_call | solution.py:152
  40.1 1.2 slice_bitcast_fusion.6
  41.6 1.7 collective-permute-start.3
  43.5 4.7 %collective-permute-done.2 = f32[16,512]{0,1:T(8,128)S(1)} collective-permute-done((f32[16,512]{0,1:T(8,128)S(1)}, f32[16,512]{0,1:T(8,128)S(1)}, u32[]{:S(2)}, u32[]{:S(2)}) %collective-permute-start.2) | collective-permute-done | bytes 32800 | tf_op jit(solution)/shard_map/ppermute | solution.py:28
  48.2 2.4 %collective-permute-done.3 = f32[16,512]{0,1:T(8,128)S(1)} collective-permute-done((f32[16,512]{0,1:T(8,128)S(1)}, f32[16,512]{0,1:T(8,128)S(1)}, u32[]{:S(2)}, u32[]{:S(2)}) %collective-permute-start.3) | collective-permute-done | bytes 32800 | tf_op jit(solution)/shard_map/ppermute | solution.py:28
  50.6 0.9 select_maximum_fusion.1.halo_ref
  51.5 20.2 %shard_map.102 = (f32[1024,128]{1,0:T(8,128)}, f32[1024,128]{1,0:T(8,128)}) custom-call(s32[6144]{0:T(1024)} %reshape.21.idx_ref, s32[1024]{0:T(1024)} %copy-done.7, f32[1024,128]{1,0:T(8,128)} %get-tuple-element.9.state_ref, f32[1024,128]{1,0:T(8,128)} %select_maximum_fusion.1.halo_ref, f32[6,1024,128]{2,1,0:T(8,128)} %compare_convert_fusion.mask_ref, ...), custom_call_target="tpu_custom_call" | custom-call | flops 2617245696 | bytes 6029312 | tf_op jit(solution)/shard_map/pallas_call | solution.py:152
  71.7 1.2 slice_bitcast_fusion.4
  73.2 1.7 collective-permute-start.5
  75.1 4.2 %collective-permute-done.4 = f32[16,512]{0,1:T(8,128)S(1)} collective-permute-done((f32[16,512]{0,1:T(8,128)S(1)}, f32[16,512]{0,1:T(8,128)S(1)}, u32[]{:S(2)}, u32[]{:S(2)}) %collective-permute-start.4) | collective-permute-done | bytes 32800 | tf_op jit(solution)/shard_map/ppermute | solution.py:28
  79.3 2.4 %collective-permute-done.5 = f32[16,512]{0,1:T(8,128)S(1)} collective-permute-done((f32[16,512]{0,1:T(8,128)S(1)}, f32[16,512]{0,1:T(8,128)S(1)}, u32[]{:S(2)}, u32[]{:S(2)}) %collective-permute-start.5) | collective-permute-done | bytes 32800 | tf_op jit(solution)/shard_map/ppermute | solution.py:28
  81.7 0.9 select_maximum_fusion.halo_ref
  82.7 18.6 %shard_map.103 = f32[1024,128]{1,0:T(8,128)} custom-call(s32[6144]{0:T(1024)} %reshape.21.idx_ref, s32[1024]{0:T(1024)} %copy-done.7, f32[1024,128]{1,0:T(8,128)} %get-tuple-element.11.state_ref, f32[1024,128]{1,0:T(8,128)} %select_maximum_fusion.halo_ref, f32[6,1024,128]{2,1,0:T(8,128)} %compare_convert_fusion.mask_ref, ...), custom_call_target="tpu_custom_call" | custom-call | flops 2617245696 | bytes 6029312 | tf_op jit(solution)/shard_map/pallas_call | solution.py:152
  101.3 2.0 %add_select_fusion = f32[64,1024]{0,1:T(8,128)S(1)} fusion(f32[1024,128]{1,0:T(8,128)} %shard_map.103, f32[64,64]{1,0:T(8,128)S(1)} %copy-done, f32[1,64,1024]{2,1,0:T(8,128)S(1)} %copy-done.1, pred[]{:T(512)S(6)} %eq.16), kind=kOutput, calls=%fused_computation.26 | convolution fusion | flops 50528256 | bytes 802817 | tf_op jit(solution)/shard_map/dot_general | solution.py:32
  103.4 1.9 collective-permute-start.6
  105.5 3.9 %collective-permute-start.11 = (f32[64,256]{0,1:T(8,128)S(1)}, f32[64,256]{0,1:T(8,128)S(1)}, u32[]{:S(2)}, u32[]{:S(2)}) collective-permute-start(f32[64,256]{0,1:T(8,128)S(1)} %get-tuple-element.16), channel_id=1, source_target_pairs={{0,8},{8,16},{16,24},{24,32},{32,40},{40,48},{48,56},{56,64},{64,7... | collective-permute-start | bytes 196616 | tf_op jit(solution)/shard_map/ppermute | solution.py:23
  109.4 1.9 collective-permute-start.16
  111.3 3.9 %collective-permute-start.21 = (f32[64,256]{0,1:T(8,128)S(1)}, f32[64,256]{0,1:T(8,128)S(1)}, u32[]{:S(2)}, u32[]{:S(2)}) collective-permute-start(f32[64,256]{0,1:T(8,128)S(1)} %get-tuple-element.14), channel_id=1, source_target_pairs={{0,8},{8,16},{16,24},{24,32},{32,40},{40,48},{48,56},{56,64},{64,7... | collective-permute-start | bytes 196616 | tf_op jit(solution)/shard_map/ppermute | solution.py:23
  115.5 3.8 %collective-permute-start.7 = (f32[64,256]{0,1:T(8,128)S(1)}, f32[64,256]{0,1:T(8,128)S(1)}, u32[]{:S(2)}, u32[]{:S(2)}) collective-permute-start(f32[64,256]{0,1:T(8,128)S(1)} %fusion.3), channel_id=1, source_target_pairs={{0,16},{8,24},{16,32},{24,40},{32,48},{40,56},{48,64},{56,72},{64,... | collective-permute-start | bytes 196616 | tf_op jit(solution)/shard_map/ppermute | solution.py:23
  119.7 5.0 %collective-permute-start.12 = (f32[64,256]{0,1:T(8,128)S(1)}, f32[64,256]{0,1:T(8,128)S(1)}, u32[]{:S(2)}, u32[]{:S(2)}) collective-permute-start(f32[64,256]{0,1:T(8,128)S(1)} %fusion.2), channel_id=1, source_target_pairs={{0,16},{8,24},{16,32},{24,40},{32,48},{40,56},{48,64},{56,72},{64,... | collective-permute-start | bytes 196616 | tf_op jit(solution)/shard_map/ppermute | solution.py:23
  125.0 2.9 %collective-permute-start.17 = (f32[64,256]{0,1:T(8,128)S(1)}, f32[64,256]{0,1:T(8,128)S(1)}, u32[]{:S(2)}, u32[]{:S(2)}) collective-permute-start(f32[64,256]{0,1:T(8,128)S(1)} %fusion.1), channel_id=1, source_target_pairs={{0,16},{8,24},{16,32},{24,40},{32,48},{40,56},{48,64},{56,72},{64,... | collective-permute-start | bytes 196616 | tf_op jit(solution)/shard_map/ppermute | solution.py:23
  128.2 2.9 %collective-permute-start.22 = (f32[64,256]{0,1:T(8,128)S(1)}, f32[64,256]{0,1:T(8,128)S(1)}, u32[]{:S(2)}, u32[]{:S(2)}) collective-permute-start(f32[64,256]{0,1:T(8,128)S(1)} %fusion), channel_id=1, source_target_pairs={{0,16},{8,24},{16,32},{24,40},{32,48},{40,56},{48,64},{56,72},{64,... | collective-permute-start | bytes 196616 | tf_op jit(solution)/shard_map/ppermute | solution.py:23
  131.4 2.4 %collective-permute-start.8 = (f32[64,256]{0,1:T(8,128)S(1)}, f32[64,256]{0,1:T(8,128)S(1)}, u32[]{:S(2)}, u32[]{:S(2)}) collective-permute-start(f32[64,256]{0,1:T(8,128)S(1)} %convolution_add_fusion.15), channel_id=1, source_target_pairs={{0,32},{8,40},{16,48},{24,56},{32,64},{40,72},{48,80},{56,88},{64,... | collective-permute-start | bytes 196616 | tf_op jit(solution)/shard_map/ppermute | solution.py:23
  134.1 1.9 collective-permute-start.13
  136.3 1.9 collective-permute-start.18
  138.9 12.1 %collective-permute-start.23 = (f32[64,256]{0,1:T(8,128)S(1)}, f32[64,256]{0,1:T(8,128)S(1)}, u32[]{:S(2)}, u32[]{:S(2)}) collective-permute-start(f32[64,256]{0,1:T(8,128)S(1)} %convolution_add_fusion.3), channel_id=1, source_target_pairs={{0,32},{8,40},{16,48},{24,56},{32,64},{40,72},{48,80},{56,88},{64,... | collective-permute-start | bytes 196616 | tf_op jit(solution)/shard_map/ppermute | solution.py:23
  151.3 1.9 collective-permute-start.9
  153.3 4.0 %collective-permute-done.13 = f32[64,256]{0,1:T(8,128)S(1)} collective-permute-done((f32[64,256]{0,1:T(8,128)S(1)}, f32[64,256]{0,1:T(8,128)S(1)}, u32[]{:S(2)}, u32[]{:S(2)}) %collective-permute-start.13) | collective-permute-done | bytes 65568 | tf_op jit(solution)/shard_map/ppermute | solution.py:23
  157.6 1.9 collective-permute-start.14
  160.4 1.9 collective-permute-start.19
  162.3 1.3 collective-permute-done.23
  163.9 11.7 %collective-permute-start.24 = (f32[64,256]{0,1:T(8,128)S(1)}, f32[64,256]{0,1:T(8,128)S(1)}, u32[]{:S(2)}, u32[]{:S(2)}) collective-permute-start(f32[64,256]{0,1:T(8,128)S(1)} %convolution_add_fusion.2), channel_id=1, source_target_pairs={{0,64},{8,72},{16,80},{24,88},{32,96},{40,104},{48,112},{56,120},{... | collective-permute-start | bytes 196616 | tf_op jit(solution)/shard_map/ppermute | solution.py:23
  175.8 1.3 collective-permute-start.10
  177.4 1.3 collective-permute-start.15
  178.7 5.1 %collective-permute-done.19 = f32[64,256]{0,1:T(8,128)S(1)} collective-permute-done((f32[64,256]{0,1:T(8,128)S(1)}, f32[64,256]{0,1:T(8,128)S(1)}, u32[]{:S(2)}, u32[]{:S(2)}) %collective-permute-start.19) | collective-permute-done | bytes 65568 | tf_op jit(solution)/shard_map/ppermute | solution.py:23
  184.0 1.3 collective-permute-start.20
  185.6 1.3 collective-permute-start.25
  187.7 1.4 collective-permute-done.15
  189.3 3.9 %collective-permute-done.20 = f32[64,256]{0,1:T(8,128)S(1)} collective-permute-done((f32[64,256]{0,1:T(8,128)S(1)}, f32[64,256]{0,1:T(8,128)S(1)}, u32[]{:S(2)}, u32[]{:S(2)}) %collective-permute-start.20) | collective-permute-done | bytes 65568 | tf_op jit(solution)/shard_map/ppermute | solution.py:23
  193.5 1.1 collective-permute-done.25
  194.9 0.9 copy.62
  (72 shorter events, 14.5 us)
Async XLA Ops:
  0.0 12.8 %copy-start = (f32[64,64]{1,0:T(8,128)S(1)}, f32[64,64]{1,0:T(8,128)}, u32[]{:S(2)}) copy-start(f32[64,64]{1,0:T(8,128)} %param.13) | copy-start | bytes 49156
  0.0 9.9 %copy-start.5 = (f32[64,64]{1,0:T(8,128)S(1)}, f32[64,64]{1,0:T(8,128)}, u32[]{:S(2)}) copy-start(f32[64,64]{1,0:T(8,128)} %param.11) | copy-start | bytes 49156
  0.0 10.0 %copy-start.3 = (s32[6,1024]{1,0:T(8,128)S(1)}, s32[6,1024]{1,0:T(8,128)}, u32[]{:S(2)}) copy-start(s32[6,1024]{1,0:T(8,128)} %param.15) | copy-start | bytes 73732
  2.6 0.8 copy-start.7
  2.6 10.1 %copy-start.2 = (f32[64,96]{1,0:T(8,128)S(1)}, f32[64,96]{1,0:T(8,128)}, u32[]{:S(2)}) copy-start(f32[64,96]{1,0:T(8,128)} %param.12) | copy-start | bytes 73732
  2.6 10.1 %copy-start.6 = (f32[64,96]{1,0:T(8,128)S(1)}, f32[64,96]{1,0:T(8,128)}, u32[]{:S(2)}) copy-start(f32[64,96]{1,0:T(8,128)} %constant.32.clone) | copy-start | bytes 73732
  6.7 7.9 %copy-start.4 = (s32[6,1024]{1,0:T(8,128)S(1)}, s32[6,1024]{1,0:T(8,128)}, u32[]{:S(2)}) copy-start(s32[6,1024]{1,0:T(8,128)} %param.14) | copy-start | bytes 73732
  7.8 8.1 %collective-permute-start = (f32[16,512]{0,1:T(8,128)S(1)}, f32[16,512]{0,1:T(8,128)S(1)}, u32[]{:S(2)}, u32[]{:S(2)}) collective-permute-start(f32[16,512]{0,1:T(8,128)S(1)} %get-tuple-element.21), channel_id=1, source_target_pairs={{0,1},{1,2},{2,3},{3,4},{4,5},{5,6},{6,7},{7,0},{8,9},{9,10},{10,1... | collective-permute-start | bytes 98312 | tf_op jit(solution)/shard_map/ppermute | solution.py:28
  9.1 9.9 %collective-permute-start.1 = (f32[16,512]{0,1:T(8,128)S(1)}, f32[16,512]{0,1:T(8,128)S(1)}, u32[]{:S(2)}, u32[]{:S(2)}) collective-permute-start(f32[16,512]{0,1:T(8,128)S(1)} %get-tuple-element.22), channel_id=1, source_target_pairs={{0,7},{1,0},{2,1},{3,2},{4,3},{5,4},{6,5},{7,6},{8,15},{9,8},{10,9... | collective-permute-start | bytes 98312 | tf_op jit(solution)/shard_map/ppermute | solution.py:28
  41.2 6.9 %collective-permute-start.2 = (f32[16,512]{0,1:T(8,128)S(1)}, f32[16,512]{0,1:T(8,128)S(1)}, u32[]{:S(2)}, u32[]{:S(2)}) collective-permute-start(f32[16,512]{0,1:T(8,128)S(1)} %get-tuple-element.19), channel_id=1, source_target_pairs={{0,1},{1,2},{2,3},{3,4},{4,5},{5,6},{6,7},{7,0},{8,9},{9,10},{10,1... | collective-permute-start | bytes 98312 | tf_op jit(solution)/shard_map/ppermute | solution.py:28
  41.6 9.0 %collective-permute-start.3 = (f32[16,512]{0,1:T(8,128)S(1)}, f32[16,512]{0,1:T(8,128)S(1)}, u32[]{:S(2)}, u32[]{:S(2)}) collective-permute-start(f32[16,512]{0,1:T(8,128)S(1)} %get-tuple-element.20), channel_id=1, source_target_pairs={{0,7},{1,0},{2,1},{3,2},{4,3},{5,4},{6,5},{7,6},{8,15},{9,8},{10,9... | collective-permute-start | bytes 98312 | tf_op jit(solution)/shard_map/ppermute | solution.py:28
  72.9 6.4 %collective-permute-start.4 = (f32[16,512]{0,1:T(8,128)S(1)}, f32[16,512]{0,1:T(8,128)S(1)}, u32[]{:S(2)}, u32[]{:S(2)}) collective-permute-start(f32[16,512]{0,1:T(8,128)S(1)} %get-tuple-element.17), channel_id=1, source_target_pairs={{0,1},{1,2},{2,3},{3,4},{4,5},{5,6},{6,7},{7,0},{8,9},{9,10},{10,1... | collective-permute-start | bytes 98312 | tf_op jit(solution)/shard_map/ppermute | solution.py:28
  73.2 8.5 %collective-permute-start.5 = (f32[16,512]{0,1:T(8,128)S(1)}, f32[16,512]{0,1:T(8,128)S(1)}, u32[]{:S(2)}, u32[]{:S(2)}) collective-permute-start(f32[16,512]{0,1:T(8,128)S(1)} %get-tuple-element.18), channel_id=1, source_target_pairs={{0,7},{1,0},{2,1},{3,2},{4,3},{5,4},{6,5},{7,6},{8,15},{9,8},{10,9... | collective-permute-start | bytes 98312 | tf_op jit(solution)/shard_map/ppermute | solution.py:28
  82.7 18.6 %copy-start.1 = (f32[1,64,1024]{2,1,0:T(8,128)S(1)}, f32[1,64,1024]{2,1,0:T(8,128)}, u32[]{:S(2)}) copy-start(f32[1,64,1024]{2,1,0:T(8,128)} %param.10) | copy-start | bytes 786436
  103.4 11.9 %collective-permute-start.6 = (f32[64,256]{0,1:T(8,128)S(1)}, f32[64,256]{0,1:T(8,128)S(1)}, u32[]{:S(2)}, u32[]{:S(2)}) collective-permute-start(f32[64,256]{0,1:T(8,128)S(1)} %get-tuple-element.13), channel_id=1, source_target_pairs={{0,8},{8,16},{16,24},{24,32},{32,40},{40,48},{48,56},{56,64},{64,7... | collective-permute-start | bytes 196616 | tf_op jit(solution)/shard_map/ppermute | solution.py:23
  105.5 13.9 %collective-permute-start.11 = (f32[64,256]{0,1:T(8,128)S(1)}, f32[64,256]{0,1:T(8,128)S(1)}, u32[]{:S(2)}, u32[]{:S(2)}) collective-permute-start(f32[64,256]{0,1:T(8,128)S(1)} %get-tuple-element.16), channel_id=1, source_target_pairs={{0,8},{8,16},{16,24},{24,32},{32,40},{40,48},{48,56},{56,64},{64,7... | collective-permute-start | bytes 196616 | tf_op jit(solution)/shard_map/ppermute | solution.py:23
  109.4 15.3 %collective-permute-start.16 = (f32[64,256]{0,1:T(8,128)S(1)}, f32[64,256]{0,1:T(8,128)S(1)}, u32[]{:S(2)}, u32[]{:S(2)}) collective-permute-start(f32[64,256]{0,1:T(8,128)S(1)} %get-tuple-element.15), channel_id=1, source_target_pairs={{0,8},{8,16},{16,24},{24,32},{32,40},{40,48},{48,56},{56,64},{64,7... | collective-permute-start | bytes 196616 | tf_op jit(solution)/shard_map/ppermute | solution.py:23
  111.3 16.6 %collective-permute-start.21 = (f32[64,256]{0,1:T(8,128)S(1)}, f32[64,256]{0,1:T(8,128)S(1)}, u32[]{:S(2)}, u32[]{:S(2)}) collective-permute-start(f32[64,256]{0,1:T(8,128)S(1)} %get-tuple-element.14), channel_id=1, source_target_pairs={{0,8},{8,16},{16,24},{24,32},{32,40},{40,48},{48,56},{56,64},{64,7... | collective-permute-start | bytes 196616 | tf_op jit(solution)/shard_map/ppermute | solution.py:23
  115.5 15.6 %collective-permute-start.7 = (f32[64,256]{0,1:T(8,128)S(1)}, f32[64,256]{0,1:T(8,128)S(1)}, u32[]{:S(2)}, u32[]{:S(2)}) collective-permute-start(f32[64,256]{0,1:T(8,128)S(1)} %fusion.3), channel_id=1, source_target_pairs={{0,16},{8,24},{16,32},{24,40},{32,48},{40,56},{48,64},{56,72},{64,... | collective-permute-start | bytes 196616 | tf_op jit(solution)/shard_map/ppermute | solution.py:23
  119.7 14.1 %collective-permute-start.12 = (f32[64,256]{0,1:T(8,128)S(1)}, f32[64,256]{0,1:T(8,128)S(1)}, u32[]{:S(2)}, u32[]{:S(2)}) collective-permute-start(f32[64,256]{0,1:T(8,128)S(1)} %fusion.2), channel_id=1, source_target_pairs={{0,16},{8,24},{16,32},{24,40},{32,48},{40,56},{48,64},{56,72},{64,... | collective-permute-start | bytes 196616 | tf_op jit(solution)/shard_map/ppermute | solution.py:23
  125.0 11.0 %collective-permute-start.17 = (f32[64,256]{0,1:T(8,128)S(1)}, f32[64,256]{0,1:T(8,128)S(1)}, u32[]{:S(2)}, u32[]{:S(2)}) collective-permute-start(f32[64,256]{0,1:T(8,128)S(1)} %fusion.1), channel_id=1, source_target_pairs={{0,16},{8,24},{16,32},{24,40},{32,48},{40,56},{48,64},{56,72},{64,... | collective-permute-start | bytes 196616 | tf_op jit(solution)/shard_map/ppermute | solution.py:23
  128.2 10.5 %collective-permute-start.22 = (f32[64,256]{0,1:T(8,128)S(1)}, f32[64,256]{0,1:T(8,128)S(1)}, u32[]{:S(2)}, u32[]{:S(2)}) collective-permute-start(f32[64,256]{0,1:T(8,128)S(1)} %fusion), channel_id=1, source_target_pairs={{0,16},{8,24},{16,32},{24,40},{32,48},{40,56},{48,64},{56,72},{64,... | collective-permute-start | bytes 196616 | tf_op jit(solution)/shard_map/ppermute | solution.py:23
  131.4 19.6 %collective-permute-start.8 = (f32[64,256]{0,1:T(8,128)S(1)}, f32[64,256]{0,1:T(8,128)S(1)}, u32[]{:S(2)}, u32[]{:S(2)}) collective-permute-start(f32[64,256]{0,1:T(8,128)S(1)} %convolution_add_fusion.15), channel_id=1, source_target_pairs={{0,32},{8,40},{16,48},{24,56},{32,64},{40,72},{48,80},{56,88},{64,... | collective-permute-start | bytes 196616 | tf_op jit(solution)/shard_map/ppermute | solution.py:23
  134.1 23.2 %collective-permute-start.13 = (f32[64,256]{0,1:T(8,128)S(1)}, f32[64,256]{0,1:T(8,128)S(1)}, u32[]{:S(2)}, u32[]{:S(2)}) collective-permute-start(f32[64,256]{0,1:T(8,128)S(1)} %convolution_add_fusion.11), channel_id=1, source_target_pairs={{0,32},{8,40},{16,48},{24,56},{32,64},{40,72},{48,80},{56,88},{64,... | collective-permute-start | bytes 196616 | tf_op jit(solution)/shard_map/ppermute | solution.py:23
  136.3 23.8 %collective-permute-start.18 = (f32[64,256]{0,1:T(8,128)S(1)}, f32[64,256]{0,1:T(8,128)S(1)}, u32[]{:S(2)}, u32[]{:S(2)}) collective-permute-start(f32[64,256]{0,1:T(8,128)S(1)} %convolution_add_fusion.7), channel_id=1, source_target_pairs={{0,32},{8,40},{16,48},{24,56},{32,64},{40,72},{48,80},{56,88},{64,... | collective-permute-start | bytes 196616 | tf_op jit(solution)/shard_map/ppermute | solution.py:23
  138.9 24.7 %collective-permute-start.23 = (f32[64,256]{0,1:T(8,128)S(1)}, f32[64,256]{0,1:T(8,128)S(1)}, u32[]{:S(2)}, u32[]{:S(2)}) collective-permute-start(f32[64,256]{0,1:T(8,128)S(1)} %convolution_add_fusion.3), channel_id=1, source_target_pairs={{0,32},{8,40},{16,48},{24,56},{32,64},{40,72},{48,80},{56,88},{64,... | collective-permute-start | bytes 196616 | tf_op jit(solution)/shard_map/ppermute | solution.py:23
  151.3 24.2 %collective-permute-start.9 = (f32[64,256]{0,1:T(8,128)S(1)}, f32[64,256]{0,1:T(8,128)S(1)}, u32[]{:S(2)}, u32[]{:S(2)}) collective-permute-start(f32[64,256]{0,1:T(8,128)S(1)} %convolution_add_fusion.14), channel_id=1, source_target_pairs={{0,64},{8,72},{16,80},{24,88},{32,96},{40,104},{48,112},{56,120},{... | collective-permute-start | bytes 196616 | tf_op jit(solution)/shard_map/ppermute | solution.py:23
  157.6 19.6 %collective-permute-start.14 = (f32[64,256]{0,1:T(8,128)S(1)}, f32[64,256]{0,1:T(8,128)S(1)}, u32[]{:S(2)}, u32[]{:S(2)}) collective-permute-start(f32[64,256]{0,1:T(8,128)S(1)} %convolution_add_fusion.10), channel_id=1, source_target_pairs={{0,64},{8,72},{16,80},{24,88},{32,96},{40,104},{48,112},{56,120},{... | collective-permute-start | bytes 196616 | tf_op jit(solution)/shard_map/ppermute | solution.py:23
  160.4 23.4 %collective-permute-start.19 = (f32[64,256]{0,1:T(8,128)S(1)}, f32[64,256]{0,1:T(8,128)S(1)}, u32[]{:S(2)}, u32[]{:S(2)}) collective-permute-start(f32[64,256]{0,1:T(8,128)S(1)} %convolution_add_fusion.6), channel_id=1, source_target_pairs={{0,64},{8,72},{16,80},{24,88},{32,96},{40,104},{48,112},{56,120},{... | collective-permute-start | bytes 196616 | tf_op jit(solution)/shard_map/ppermute | solution.py:23
  163.9 21.5 %collective-permute-start.24 = (f32[64,256]{0,1:T(8,128)S(1)}, f32[64,256]{0,1:T(8,128)S(1)}, u32[]{:S(2)}, u32[]{:S(2)}) collective-permute-start(f32[64,256]{0,1:T(8,128)S(1)} %convolution_add_fusion.2), channel_id=1, source_target_pairs={{0,64},{8,72},{16,80},{24,88},{32,96},{40,104},{48,112},{56,120},{... | collective-permute-start | bytes 196616 | tf_op jit(solution)/shard_map/ppermute | solution.py:23
  175.8 11.6 %collective-permute-start.10 = (f32[64,256]{0,1:T(8,128)S(1)}, f32[64,256]{0,1:T(8,128)S(1)}, u32[]{:S(2)}, u32[]{:S(2)}) collective-permute-start(f32[64,256]{0,1:T(8,128)S(1)} %convolution_add_fusion.13), channel_id=1, source_target_pairs={{0,128},{8,136},{16,144},{24,152},{32,160},{40,168},{48,176},{56,1... | collective-permute-start | bytes 196616 | tf_op jit(solution)/shard_map/ppermute | solution.py:23
  177.4 11.6 %collective-permute-start.15 = (f32[64,256]{0,1:T(8,128)S(1)}, f32[64,256]{0,1:T(8,128)S(1)}, u32[]{:S(2)}, u32[]{:S(2)}) collective-permute-start(f32[64,256]{0,1:T(8,128)S(1)} %convolution_add_fusion.9), channel_id=1, source_target_pairs={{0,128},{8,136},{16,144},{24,152},{32,160},{40,168},{48,176},{56,1... | collective-permute-start | bytes 196616 | tf_op jit(solution)/shard_map/ppermute | solution.py:23
  184.0 9.2 %collective-permute-start.20 = (f32[64,256]{0,1:T(8,128)S(1)}, f32[64,256]{0,1:T(8,128)S(1)}, u32[]{:S(2)}, u32[]{:S(2)}) collective-permute-start(f32[64,256]{0,1:T(8,128)S(1)} %convolution_add_fusion.5), channel_id=1, source_target_pairs={{0,128},{8,136},{16,144},{24,152},{32,160},{40,168},{48,176},{56,1... | collective-permute-start | bytes 196616 | tf_op jit(solution)/shard_map/ppermute | solution.py:23
  185.6 9.0 %collective-permute-start.25 = (f32[64,256]{0,1:T(8,128)S(1)}, f32[64,256]{0,1:T(8,128)S(1)}, u32[]{:S(2)}, u32[]{:S(2)}) collective-permute-start(f32[64,256]{0,1:T(8,128)S(1)} %convolution_add_fusion.1), channel_id=1, source_target_pairs={{0,128},{8,136},{16,144},{24,152},{32,160},{40,168},{48,176},{56,1... | collective-permute-start | bytes 196616 | tf_op jit(solution)/shard_map/ppermute | solution.py:23

commit v6 on v5

--- a/solution.py
+++ b/solution.py
@@ -11,7 +11,6 @@
 STEPS = 3
 LANES = 128
 UNROLL = 8
-SCAN_PIECES = 4
 
 
 time_step = 0.05
@@ -204,19 +203,38 @@
     defect = fine_state - coarse_start
     is_first = lax.axis_index("tm") == 0
     total = jnp.where(is_first, coarse_start + defect, defect)
-    power = coarse
-    offset = 1
+    return scan_over_time(total, coarse)[None]
+
+
+def scan_over_time(total, coarse):
     peers = lax.axis_size("tm")
-    while offset < peers:
-        pieces = jnp.split(total, SCAN_PIECES, axis=1)
-        arrived = [from_behind(piece, "tm", offset) for piece in pieces]
-        total = jnp.concatenate(
-            [piece + product(power, got) for piece, got in zip(pieces, arrived)], axis=1
-        )
-        offset *= 2
-        if offset < peers:
+    core = lax.axis_index("tm") % 2
+    partner = [(i, i ^ 1) for i in range(peers)]
+    half = total.shape[1] // 2
+    low, high = total[:, :half], total[:, half:]
+    got = lax.ppermute(jnp.where(core == 0, high, low), "tm", partner)
+    keep = jnp.where(core == 0, low, high)
+    first = jnp.where(core == 0, keep, got)
+    second = jnp.where(core == 0, got, keep)
+    aggregate = product(coarse, first) + second
+    square = product(coarse, coarse)
+    before = from_behind(aggregate, "tm", 2)
+    power = square
+    shift = 1
+    while shift < peers // 2:
+        before = before + product(power, from_behind(before, "tm", 2 * shift))
+        shift *= 2
+        if shift < peers // 2:
             power = product(power, power)
-    return total[None]
+    end_first = product(coarse, before) + first
+    end_second = product(square, before) + aggregate
+    mine = jnp.where(core == 0, end_first, end_second)
+    got = lax.ppermute(jnp.where(core == 0, end_second, end_first), "tm", partner)
+    return jnp.where(
+        core == 0,
+        jnp.concatenate([mine, got], axis=1),
+        jnp.concatenate([got, mine], axis=1),
+    )
 
 
 def solution(mesh):

time: 197 us -> 185 us (0.939)
  starting transfers between devices: 73.6 us -> 17.4 us
  waiting for transfers between devices: 35.9 us -> 83.9 us
  matrix products: 8.12 us -> 5.43 us
    ppermute x20 -> x5, starting transfers between devices: 67.3 us -> 10.9 us  [from_behind(): return lax.ppermute(shard, axis, pairs)]
    ppermute x20 -> x5, waiting for transfers between devices: 18.4 us -> 62.9 us  [from_behind(): return lax.ppermute(shard, axis, pairs)]
    ppermute x0 -> x2, waiting for transfers between devices: none -> 3.04 us  [the longest x1 1.52 us: scan_over_time(): got = lax.ppermute(jnp.where(core == 0, high, low), 'tm', partner)]
    dot_general x26 -> x13, matrix products: 8.12 us -> 5.43 us  [product(): jnp.dot(matrix, vector, precision=lax.Precision.HIGHEST, preferred_elemen...]
  transfers between devices with their start and end apart: 26 -> 13, of which waited for: 15 -> 13; matrix products, arithmetic and copies ran while one was open for 5% -> 3% of each run, Pallas kernels for 0% -> 0%
where the time goes in v6:
time: 185 us
  waiting for transfers between devices  83.9 us (45%)
  Pallas kernels  62.2 us (34%)
  starting transfers between devices  17.4 us (9%)
  local copies, waits for them, and re-layouts  9.99 us (5%)
  other arithmetic  5.55 us (3%)
  matrix products  5.43 us (3%)
    ppermute x5, waiting for transfers between devices, from_behind(): return lax.ppermute(shard, axis, pairs)  62.9 us
    pallas_call x3, Pallas kernels, fused_step(): pl.pallas_call(functools.partial(fused_kernel, with_send), out_shape=tupl...  58.9 us
    ppermute x6, waiting for transfers between devices, ring(): lax.ppermute(shard, axis, [(i, (i + by) % peers) for i in range(peers)])  18 us
    ppermute x5, starting transfers between devices, from_behind(): return lax.ppermute(shard, axis, pairs)  10.9 us
    ppermute x6, starting transfers between devices, ring(): lax.ppermute(shard, axis, [(i, (i + by) % peers) for i in range(peers)])  6.31 us
    dot_general x13, matrix products, product(): jnp.dot(matrix, vector, precision=lax.Precision.HIGHEST, preferred_elemen...  5.43 us
  transfers between devices with their start and end apart: 13, of which 13 were waited for; matrix products, arithmetic and copies ran while one was open for 3% of the time, Pallas kernels for 0%

profile of v6, /device:TPU:22, one launch (start us, length us, event | category | flops | bytes accessed | tf_op | source)
XLA Modules:
  0.0 184.7 jit_solution(4059048823938586450)
XLA Ops:
  0.0 1.2 copy.24
  1.2 0.7 constant_dynamic-update-slice_fusion
  1.9 0.7 constant_dynamic-update-slice_fusion.1.idx_ref.send_ref
  2.6 0.8 pad.32.table_ref.state_ref
  3.4 3.3 %shard_map.100 = f32[1024,128]{1,0:T(8,128)} custom-call(s32[1024]{0:T(1024)} %copy-done.7, f32[1024,128]{1,0:T(8,128)} %pad.32.table_ref.state_ref), custom_call_target="tpu_custom_call" | custom-call | tf_op jit(solution)/shard_map/pallas_call | solution.py:85
  6.7 1.2 slice_bitcast_fusion.2
  7.9 1.3 collective-permute-start
  9.1 0.8 collective-permute-start.1
  10.1 2.7 %compare_convert_fusion.mask_ref = f32[6,1024,128]{2,1,0:T(8,128)} fusion(s32[128]{0:T(128)S(1)} %and_select_fusion, s32[6,1024]{1,0:T(8,128)S(1)} %copy-done.3), kind=kLoop, calls=%fused_computation | loop fusion | flops 1572864 | bytes 3170816 | tf_op jit(solution)/shard_map/convert_element_type | solution.py:178
  13.0 0.8 pad.35.spread_ref
  13.8 0.6 pad.36.folded_ref
  14.5 0.6 reshape.76.idx_ref
  15.1 0.9 collective-permute-done
  16.0 3.0 %collective-permute-done.1 = f32[16,512]{0,1:T(8,128)S(1)} collective-permute-done((f32[16,512]{0,1:T(8,128)S(1)}, f32[16,512]{0,1:T(8,128)S(1)}, u32[]{:S(2)}, u32[]{:S(2)}) %collective-permute-start.1) | collective-permute-done | bytes 32800 | tf_op jit(solution)/shard_map/ppermute | solution.py:27
  19.0 0.9 select_maximum_fusion.2.halo_ref
  20.0 20.1 %shard_map.101 = (f32[1024,128]{1,0:T(8,128)}, f32[1024,128]{1,0:T(8,128)}) custom-call(s32[6144]{0:T(1024)} %reshape.76.idx_ref, s32[1024]{0:T(1024)} %copy-done.7, f32[1024,128]{1,0:T(8,128)} %pad.32.table_ref.state_ref, f32[1024,128]{1,0:T(8,128)} %select_maximum_fusion.2.halo_ref, f32[6,1024,128]{2,1,0:T(8,128)} %compare_convert_fusion.mask_ref, ...), custom_call_target="tpu_custom_call" | custom-call | flops 2617245696 | bytes 6029312 | tf_op jit(solution)/shard_map/pallas_call | solution.py:151
  40.1 1.2 slice_bitcast_fusion.6
  41.6 1.7 collective-permute-start.3
  43.4 4.8 %collective-permute-done.2 = f32[16,512]{0,1:T(8,128)S(1)} collective-permute-done((f32[16,512]{0,1:T(8,128)S(1)}, f32[16,512]{0,1:T(8,128)S(1)}, u32[]{:S(2)}, u32[]{:S(2)}) %collective-permute-start.2) | collective-permute-done | bytes 32800 | tf_op jit(solution)/shard_map/ppermute | solution.py:27
  48.2 2.4 %collective-permute-done.3 = f32[16,512]{0,1:T(8,128)S(1)} collective-permute-done((f32[16,512]{0,1:T(8,128)S(1)}, f32[16,512]{0,1:T(8,128)S(1)}, u32[]{:S(2)}, u32[]{:S(2)}) %collective-permute-start.3) | collective-permute-done | bytes 32800 | tf_op jit(solution)/shard_map/ppermute | solution.py:27
  50.6 0.9 select_maximum_fusion.1.halo_ref
  51.6 20.2 %shard_map.102 = (f32[1024,128]{1,0:T(8,128)}, f32[1024,128]{1,0:T(8,128)}) custom-call(s32[6144]{0:T(1024)} %reshape.76.idx_ref, s32[1024]{0:T(1024)} %copy-done.7, f32[1024,128]{1,0:T(8,128)} %get-tuple-element.9.state_ref, f32[1024,128]{1,0:T(8,128)} %select_maximum_fusion.1.halo_ref, f32[6,1024,128]{2,1,0:T(8,128)} %compare_convert_fusion.mask_ref, ...), custom_call_target="tpu_custom_call" | custom-call | flops 2617245696 | bytes 6029312 | tf_op jit(solution)/shard_map/pallas_call | solution.py:151
  71.7 1.2 slice_bitcast_fusion.4
  73.2 1.7 collective-permute-start.5
  75.0 4.3 %collective-permute-done.4 = f32[16,512]{0,1:T(8,128)S(1)} collective-permute-done((f32[16,512]{0,1:T(8,128)S(1)}, f32[16,512]{0,1:T(8,128)S(1)}, u32[]{:S(2)}, u32[]{:S(2)}) %collective-permute-start.4) | collective-permute-done | bytes 32800 | tf_op jit(solution)/shard_map/ppermute | solution.py:27
  79.3 2.4 %collective-permute-done.5 = f32[16,512]{0,1:T(8,128)S(1)} collective-permute-done((f32[16,512]{0,1:T(8,128)S(1)}, f32[16,512]{0,1:T(8,128)S(1)}, u32[]{:S(2)}, u32[]{:S(2)}) %collective-permute-start.5) | collective-permute-done | bytes 32800 | tf_op jit(solution)/shard_map/ppermute | solution.py:27
  81.8 0.9 select_maximum_fusion.halo_ref
  82.7 18.6 %shard_map.103 = f32[1024,128]{1,0:T(8,128)} custom-call(s32[6144]{0:T(1024)} %reshape.76.idx_ref, s32[1024]{0:T(1024)} %copy-done.7, f32[1024,128]{1,0:T(8,128)} %get-tuple-element.11.state_ref, f32[1024,128]{1,0:T(8,128)} %select_maximum_fusion.halo_ref, f32[6,1024,128]{2,1,0:T(8,128)} %compare_convert_fusion.mask_ref, ...), custom_call_target="tpu_custom_call" | custom-call | flops 2617245696 | bytes 6029312 | tf_op jit(solution)/shard_map/pallas_call | solution.py:151
  101.3 2.0 %add_select_fusion = f32[64,1024]{0,1:T(8,128)S(1)} fusion(f32[1024,128]{1,0:T(8,128)} %shard_map.103, f32[64,64]{1,0:T(8,128)S(1)} %copy-done, f32[1,64,1024]{2,1,0:T(8,128)S(1)} %copy-done.1, pred[]{:T(512)S(6)} %eq.13), kind=kOutput, calls=%fused_computation.11 | convolution fusion | flops 50528256 | bytes 802817 | tf_op jit(solution)/shard_map/dot_general | solution.py:31
  103.5 1.5 collective-permute-done.6
  105.0 0.4 fusion.1
  105.4 3.8 %collective-permute-start.7 = (f32[64,512]{0,1:T(8,128)S(1)}, f32[64,512]{0,1:T(8,128)S(1)}, u32[]{:S(2)}, u32[]{:S(2)}) collective-permute-start(f32[64,512]{0,1:T(8,128)S(1)} %fusion.1), channel_id=1, source_target_pairs={{0,16},{8,24},{16,32},{24,40},{32,48},{40,56},{48,64},{56,72},{64,... | collective-permute-start | bytes 393224 | tf_op jit(solution)/shard_map/ppermute | solution.py:22
  109.2 10.6 %collective-permute-done.7 = f32[64,512]{0,1:T(8,128)S(1)} collective-permute-done((f32[64,512]{0,1:T(8,128)S(1)}, f32[64,512]{0,1:T(8,128)S(1)}, u32[]{:S(2)}, u32[]{:S(2)}) %collective-permute-start.7) | collective-permute-done | bytes 131104 | tf_op jit(solution)/shard_map/ppermute | solution.py:22
  119.8 1.9 %collective-permute-start.8 = (f32[64,512]{0,1:T(8,128)S(1)}, f32[64,512]{0,1:T(8,128)S(1)}, u32[]{:S(2)}, u32[]{:S(2)}) collective-permute-start(f32[64,512]{0,1:T(8,128)S(1)} %collective-permute-done.7), channel_id=1, source_target_pairs={{0,16},{8,24},{16,32},{24,40},{32,48},{40,56},{48,64},{56,72},{64,... | collective-permute-start | bytes 393224 | tf_op jit(solution)/shard_map/ppermute | solution.py:22
  121.9 11.2 %collective-permute-done.8 = f32[64,512]{0,1:T(8,128)S(1)} collective-permute-done((f32[64,512]{0,1:T(8,128)S(1)}, f32[64,512]{0,1:T(8,128)S(1)}, u32[]{:S(2)}, u32[]{:S(2)}) %collective-permute-start.8) | collective-permute-done | bytes 131104 | tf_op jit(solution)/shard_map/ppermute | solution.py:22
  133.1 0.4 convolution_add_fusion.4
  133.5 1.9 %collective-permute-start.9 = (f32[64,512]{0,1:T(8,128)S(1)}, f32[64,512]{0,1:T(8,128)S(1)}, u32[]{:S(2)}, u32[]{:S(2)}) collective-permute-start(f32[64,512]{0,1:T(8,128)S(1)} %convolution_add_fusion.4), channel_id=1, source_target_pairs={{0,32},{8,40},{16,48},{24,56},{32,64},{40,72},{48,80},{56,88},{64,... | collective-permute-start | bytes 393224 | tf_op jit(solution)/shard_map/ppermute | solution.py:22
  135.6 14.4 %collective-permute-done.9 = f32[64,512]{0,1:T(8,128)S(1)} collective-permute-done((f32[64,512]{0,1:T(8,128)S(1)}, f32[64,512]{0,1:T(8,128)S(1)}, u32[]{:S(2)}, u32[]{:S(2)}) %collective-permute-start.9) | collective-permute-done | bytes 131104 | tf_op jit(solution)/shard_map/ppermute | solution.py:22
  150.0 0.4 convolution_add_fusion.3
  150.4 1.9 %collective-permute-start.10 = (f32[64,512]{0,1:T(8,128)S(1)}, f32[64,512]{0,1:T(8,128)S(1)}, u32[]{:S(2)}, u32[]{:S(2)}) collective-permute-start(f32[64,512]{0,1:T(8,128)S(1)} %convolution_add_fusion.3), channel_id=1, source_target_pairs={{0,64},{8,72},{16,80},{24,88},{32,96},{40,104},{48,112},{56,120},{... | collective-permute-start | bytes 393224 | tf_op jit(solution)/shard_map/ppermute | solution.py:22
  152.5 16.5 %collective-permute-done.10 = f32[64,512]{0,1:T(8,128)S(1)} collective-permute-done((f32[64,512]{0,1:T(8,128)S(1)}, f32[64,512]{0,1:T(8,128)S(1)}, u32[]{:S(2)}, u32[]{:S(2)}) %collective-permute-start.10) | collective-permute-done | bytes 131104 | tf_op jit(solution)/shard_map/ppermute | solution.py:22
  169.0 0.4 convolution_add_fusion.2
  169.3 1.3 collective-permute-start.11
  170.8 10.2 %collective-permute-done.11 = f32[64,512]{0,1:T(8,128)S(1)} collective-permute-done((f32[64,512]{0,1:T(8,128)S(1)}, f32[64,512]{0,1:T(8,128)S(1)}, u32[]{:S(2)}, u32[]{:S(2)}) %collective-permute-start.11) | collective-permute-done | bytes 131104 | tf_op jit(solution)/shard_map/ppermute | solution.py:22
  181.4 0.4 convolution_add_fusion
  181.7 0.4 select_bitcast_fusion
  182.2 1.5 collective-permute-done.12
  183.8 0.9 copy.36
  (33 shorter events, 2.4 us)
Async XLA Ops:
  0.0 101.3 %copy-start = (f32[64,64]{1,0:T(8,128)S(1)}, f32[64,64]{1,0:T(8,128)}, u32[]{:S(2)}) copy-start(f32[64,64]{1,0:T(8,128)} %param.13) | copy-start | bytes 49156
  0.0 10.0 %copy-start.5 = (f32[64,64]{1,0:T(8,128)S(1)}, f32[64,64]{1,0:T(8,128)}, u32[]{:S(2)}) copy-start(f32[64,64]{1,0:T(8,128)} %param.11) | copy-start | bytes 49156
  0.0 10.0 %copy-start.3 = (s32[6,1024]{1,0:T(8,128)S(1)}, s32[6,1024]{1,0:T(8,128)}, u32[]{:S(2)}) copy-start(s32[6,1024]{1,0:T(8,128)} %param.15) | copy-start | bytes 73732
  2.6 0.9 copy-start.7
  2.6 10.1 %copy-start.2 = (f32[64,96]{1,0:T(8,128)S(1)}, f32[64,96]{1,0:T(8,128)}, u32[]{:S(2)}) copy-start(f32[64,96]{1,0:T(8,128)} %param.12) | copy-start | bytes 73732
  2.6 10.1 %copy-start.6 = (f32[64,96]{1,0:T(8,128)S(1)}, f32[64,96]{1,0:T(8,128)}, u32[]{:S(2)}) copy-start(f32[64,96]{1,0:T(8,128)} %constant.43.clone) | copy-start | bytes 73732
  6.7 7.8 %copy-start.4 = (s32[6,1024]{1,0:T(8,128)S(1)}, s32[6,1024]{1,0:T(8,128)}, u32[]{:S(2)}) copy-start(s32[6,1024]{1,0:T(8,128)} %param.14) | copy-start | bytes 73732
  7.9 8.1 %collective-permute-start = (f32[16,512]{0,1:T(8,128)S(1)}, f32[16,512]{0,1:T(8,128)S(1)}, u32[]{:S(2)}, u32[]{:S(2)}) collective-permute-start(f32[16,512]{0,1:T(8,128)S(1)} %get-tuple-element.19), channel_id=1, source_target_pairs={{0,1},{1,2},{2,3},{3,4},{4,5},{5,6},{6,7},{7,0},{8,9},{9,10},{10,1... | collective-permute-start | bytes 98312 | tf_op jit(solution)/shard_map/ppermute | solution.py:27
  9.1 9.9 %collective-permute-start.1 = (f32[16,512]{0,1:T(8,128)S(1)}, f32[16,512]{0,1:T(8,128)S(1)}, u32[]{:S(2)}, u32[]{:S(2)}) collective-permute-start(f32[16,512]{0,1:T(8,128)S(1)} %get-tuple-element.20), channel_id=1, source_target_pairs={{0,7},{1,0},{2,1},{3,2},{4,3},{5,4},{6,5},{7,6},{8,15},{9,8},{10,9... | collective-permute-start | bytes 98312 | tf_op jit(solution)/shard_map/ppermute | solution.py:27
  41.3 6.9 %collective-permute-start.2 = (f32[16,512]{0,1:T(8,128)S(1)}, f32[16,512]{0,1:T(8,128)S(1)}, u32[]{:S(2)}, u32[]{:S(2)}) collective-permute-start(f32[16,512]{0,1:T(8,128)S(1)} %get-tuple-element.17), channel_id=1, source_target_pairs={{0,1},{1,2},{2,3},{3,4},{4,5},{5,6},{6,7},{7,0},{8,9},{9,10},{10,1... | collective-permute-start | bytes 98312 | tf_op jit(solution)/shard_map/ppermute | solution.py:27
  41.6 9.0 %collective-permute-start.3 = (f32[16,512]{0,1:T(8,128)S(1)}, f32[16,512]{0,1:T(8,128)S(1)}, u32[]{:S(2)}, u32[]{:S(2)}) collective-permute-start(f32[16,512]{0,1:T(8,128)S(1)} %get-tuple-element.18), channel_id=1, source_target_pairs={{0,7},{1,0},{2,1},{3,2},{4,3},{5,4},{6,5},{7,6},{8,15},{9,8},{10,9... | collective-permute-start | bytes 98312 | tf_op jit(solution)/shard_map/ppermute | solution.py:27
  72.9 6.4 %collective-permute-start.4 = (f32[16,512]{0,1:T(8,128)S(1)}, f32[16,512]{0,1:T(8,128)S(1)}, u32[]{:S(2)}, u32[]{:S(2)}) collective-permute-start(f32[16,512]{0,1:T(8,128)S(1)} %get-tuple-element.15), channel_id=1, source_target_pairs={{0,1},{1,2},{2,3},{3,4},{4,5},{5,6},{6,7},{7,0},{8,9},{9,10},{10,1... | collective-permute-start | bytes 98312 | tf_op jit(solution)/shard_map/ppermute | solution.py:27
  73.2 8.5 %collective-permute-start.5 = (f32[16,512]{0,1:T(8,128)S(1)}, f32[16,512]{0,1:T(8,128)S(1)}, u32[]{:S(2)}, u32[]{:S(2)}) collective-permute-start(f32[16,512]{0,1:T(8,128)S(1)} %get-tuple-element.16), channel_id=1, source_target_pairs={{0,7},{1,0},{2,1},{3,2},{4,3},{5,4},{6,5},{7,6},{8,15},{9,8},{10,9... | collective-permute-start | bytes 98312 | tf_op jit(solution)/shard_map/ppermute | solution.py:27
  82.7 18.6 %copy-start.1 = (f32[1,64,1024]{2,1,0:T(8,128)S(1)}, f32[1,64,1024]{2,1,0:T(8,128)}, u32[]{:S(2)}) copy-start(f32[1,64,1024]{2,1,0:T(8,128)} %param.10) | copy-start | bytes 786436
  103.4 1.6 collective-permute-start.6
  105.4 14.4 %collective-permute-start.7 = (f32[64,512]{0,1:T(8,128)S(1)}, f32[64,512]{0,1:T(8,128)S(1)}, u32[]{:S(2)}, u32[]{:S(2)}) collective-permute-start(f32[64,512]{0,1:T(8,128)S(1)} %fusion.1), channel_id=1, source_target_pairs={{0,16},{8,24},{16,32},{24,40},{32,48},{40,56},{48,64},{56,72},{64,... | collective-permute-start | bytes 393224 | tf_op jit(solution)/shard_map/ppermute | solution.py:22
  119.8 13.3 %collective-permute-start.8 = (f32[64,512]{0,1:T(8,128)S(1)}, f32[64,512]{0,1:T(8,128)S(1)}, u32[]{:S(2)}, u32[]{:S(2)}) collective-permute-start(f32[64,512]{0,1:T(8,128)S(1)} %collective-permute-done.7), channel_id=1, source_target_pairs={{0,16},{8,24},{16,32},{24,40},{32,48},{40,56},{48,64},{56,72},{64,... | collective-permute-start | bytes 393224 | tf_op jit(solution)/shard_map/ppermute | solution.py:22
  133.5 16.5 %collective-permute-start.9 = (f32[64,512]{0,1:T(8,128)S(1)}, f32[64,512]{0,1:T(8,128)S(1)}, u32[]{:S(2)}, u32[]{:S(2)}) collective-permute-start(f32[64,512]{0,1:T(8,128)S(1)} %convolution_add_fusion.4), channel_id=1, source_target_pairs={{0,32},{8,40},{16,48},{24,56},{32,64},{40,72},{48,80},{56,88},{64,... | collective-permute-start | bytes 393224 | tf_op jit(solution)/shard_map/ppermute | solution.py:22
  150.4 18.6 %collective-permute-start.10 = (f32[64,512]{0,1:T(8,128)S(1)}, f32[64,512]{0,1:T(8,128)S(1)}, u32[]{:S(2)}, u32[]{:S(2)}) collective-permute-start(f32[64,512]{0,1:T(8,128)S(1)} %convolution_add_fusion.3), channel_id=1, source_target_pairs={{0,64},{8,72},{16,80},{24,88},{32,96},{40,104},{48,112},{56,120},{... | collective-permute-start | bytes 393224 | tf_op jit(solution)/shard_map/ppermute | solution.py:22
  169.3 11.6 %collective-permute-start.11 = (f32[64,512]{0,1:T(8,128)S(1)}, f32[64,512]{0,1:T(8,128)S(1)}, u32[]{:S(2)}, u32[]{:S(2)}) collective-permute-start(f32[64,512]{0,1:T(8,128)S(1)} %convolution_add_fusion.2), channel_id=1, source_target_pairs={{0,128},{8,136},{16,144},{24,152},{32,160},{40,168},{48,176},{56,1... | collective-permute-start | bytes 393224 | tf_op jit(solution)/shard_map/ppermute | solution.py:22
  182.1 1.6 collective-permute-start.12

commit v7 on v6

--- a/solution.py
+++ b/solution.py
@@ -93,6 +93,25 @@
     )(idx, table)
 
 
+def split_three(x):
+    high = x.astype(jnp.bfloat16)
+    rest = x - high.astype(jnp.float32)
+    middle = rest.astype(jnp.bfloat16)
+    low = (rest - middle.astype(jnp.float32)).astype(jnp.bfloat16)
+    return high, middle, low
+
+
+def bf16_dot(a, b):
+    return jnp.dot(a, b, preferred_element_type=jnp.float32)
+
+
+def three_pass_dot(a, b):
+    a_parts, b_parts = split_three(a), split_three(b)
+    return bf16_dot(a_parts[0], b_parts[0]) + (
+        bf16_dot(a_parts[0], b_parts[1]) + bf16_dot(a_parts[1], b_parts[0])
+    )
+
+
 def fused_kernel(with_send, idx_ref, send_ref, state_ref, halo_ref, mask_ref, pick_ref,
                  spread_ref, folded_ref, out_ref, *rest):
     if with_send:
@@ -113,15 +132,12 @@
     state = state_ref[...]
     lifted = jnp.zeros_like(state)
     for face in range(6):
-        turned = jnp.dot(
-            beside[face * elements:(face + 1) * elements, :], pick_ref[face],
-            precision=lax.Precision.HIGHEST, preferred_element_type=jnp.float32,
+        parts = split_three(beside[face * elements:(face + 1) * elements, :])
+        turned = (bf16_dot(parts[0], pick_ref[face]) + bf16_dot(parts[1], pick_ref[face])) + (
+            bf16_dot(parts[2], pick_ref[face])
         )
         chosen = jnp.where(mask_ref[face] > 0.5, turned, 0.0)
-        lifted = lifted + jnp.dot(
-            chosen, spread_ref[face],
-            precision=lax.Precision.HIGHEST, preferred_element_type=jnp.float32,
-        )
+        lifted = lifted + three_pass_dot(chosen, spread_ref[face])
     own = jnp.dot(
         state, folded_ref[...], precision=lax.Precision.HIGHEST,
         preferred_element_type=jnp.float32,
@@ -164,7 +180,7 @@
 
 def shards(start_state, stiffness, lifting, coarse, neighbor, orientation, send_low, send_high):
     pick_np, own_np = selection_tables()
-    pick = jnp.asarray(pick_np)
+    pick = jnp.asarray(pick_np, dtype=jnp.bfloat16)
     own = jnp.asarray(own_np)
     lift_t = lifting.T.reshape(6, 16, 64)
     spread = jnp.broadcast_to(lift_t[:, None], (6, 8, 16, 64)).reshape(6, LANES, 64)

time: 185 us -> 176 us (0.951)
  Pallas kernels: 62.2 us -> 52.3 us
    pallas_call x3, Pallas kernels: 58.9 us -> 49 us  [fused_step(): pl.pallas_call(functools.partial(fused_kernel, with_send), out_shape=tupl...]
where the time goes in v7:
time: 176 us; the launch traced here: 175 us
  waiting for transfers between devices  83.9 us (48%)
  Pallas kernels  52.3 us (30%)
  starting transfers between devices  17.5 us (10%)
  local copies, waits for them, and re-layouts  9.99 us (6%)
  other arithmetic  5.55 us (3%)
  matrix products  5.44 us (3%)
    ppermute x5, waiting for transfers between devices, from_behind(): return lax.ppermute(shard, axis, pairs)  62.9 us
    pallas_call x3, Pallas kernels, fused_step(): pl.pallas_call(functools.partial(fused_kernel, with_send), out_shape=tupl...  49 us
    ppermute x6, waiting for transfers between devices, ring(): lax.ppermute(shard, axis, [(i, (i + by) % peers) for i in range(peers)])  17.9 us
    ppermute x5, starting transfers between devices, from_behind(): return lax.ppermute(shard, axis, pairs)  10.9 us
    ppermute x6, starting transfers between devices, ring(): lax.ppermute(shard, axis, [(i, (i + by) % peers) for i in range(peers)])  6.49 us
    dot_general x13, matrix products, product(): jnp.dot(matrix, vector, precision=lax.Precision.HIGHEST, preferred_elemen...  5.44 us
  transfers between devices with their start and end apart: 13, of which 13 were waited for; matrix products, arithmetic and copies ran while one was open for 3% of the time, Pallas kernels for 0%

profile of v7, /device:TPU:22, one launch (start us, length us, event | category | flops | bytes accessed | tf_op | source)
XLA Modules:
  0.0 174.9 jit_solution(12112950304801032996)
XLA Ops:
  0.0 1.2 copy.24
  1.2 0.7 constant_dynamic-update-slice_fusion
  1.9 0.7 constant_dynamic-update-slice_fusion.1.idx_ref.send_ref
  2.6 0.8 pad.32.table_ref.state_ref
  3.4 3.3 %shard_map.100 = f32[1024,128]{1,0:T(8,128)} custom-call(s32[1024]{0:T(1024)} %copy-done.7, f32[1024,128]{1,0:T(8,128)} %pad.32.table_ref.state_ref), custom_call_target="tpu_custom_call" | custom-call | tf_op jit(solution)/shard_map/pallas_call | solution.py:85
  6.7 1.2 slice_bitcast_fusion.2
  7.9 1.3 collective-permute-start
  9.1 0.8 collective-permute-start.1
  10.1 2.7 %compare_convert_fusion.mask_ref = f32[6,1024,128]{2,1,0:T(8,128)} fusion(s32[128]{0:T(128)S(1)} %and_select_fusion, s32[6,1024]{1,0:T(8,128)S(1)} %copy-done.3), kind=kLoop, calls=%fused_computation | loop fusion | flops 1572864 | bytes 3170816 | tf_op jit(solution)/shard_map/convert_element_type | solution.py:194
  13.0 0.8 pad.35.spread_ref
  13.8 0.6 pad.36.folded_ref
  14.5 0.6 reshape.76.idx_ref
  15.1 0.9 collective-permute-done
  16.0 3.0 %collective-permute-done.1 = f32[16,512]{0,1:T(8,128)S(1)} collective-permute-done((f32[16,512]{0,1:T(8,128)S(1)}, f32[16,512]{0,1:T(8,128)S(1)}, u32[]{:S(2)}, u32[]{:S(2)}) %collective-permute-start.1) | collective-permute-done | bytes 32800 | tf_op jit(solution)/shard_map/ppermute | solution.py:27
  19.0 0.9 select_maximum_fusion.2.halo_ref
  20.0 16.8 %shard_map.101 = (f32[1024,128]{1,0:T(8,128)}, f32[1024,128]{1,0:T(8,128)}) custom-call(s32[6144]{0:T(1024)} %reshape.76.idx_ref, s32[1024]{0:T(1024)} %copy-done.7, f32[1024,128]{1,0:T(8,128)} %pad.32.table_ref.state_ref, f32[1024,128]{1,0:T(8,128)} %select_maximum_fusion.2.halo_ref, f32[6,1024,128]{2,1,0:T(8,128)} %compare_convert_fusion.mask_ref, ...), custom_call_target="tpu_custom_call" | custom-call | flops 2617245696 | bytes 6029312 | tf_op jit(solution)/shard_map/pallas_call | solution.py:167
  36.8 1.2 slice_bitcast_fusion.6
  38.3 1.7 collective-permute-start.3
  40.1 4.8 %collective-permute-done.2 = f32[16,512]{0,1:T(8,128)S(1)} collective-permute-done((f32[16,512]{0,1:T(8,128)S(1)}, f32[16,512]{0,1:T(8,128)S(1)}, u32[]{:S(2)}, u32[]{:S(2)}) %collective-permute-start.2) | collective-permute-done | bytes 32800 | tf_op jit(solution)/shard_map/ppermute | solution.py:27
  44.9 2.4 %collective-permute-done.3 = f32[16,512]{0,1:T(8,128)S(1)} collective-permute-done((f32[16,512]{0,1:T(8,128)S(1)}, f32[16,512]{0,1:T(8,128)S(1)}, u32[]{:S(2)}, u32[]{:S(2)}) %collective-permute-start.3) | collective-permute-done | bytes 32800 | tf_op jit(solution)/shard_map/ppermute | solution.py:27
  47.3 0.9 select_maximum_fusion.1.halo_ref
  48.3 16.9 %shard_map.102 = (f32[1024,128]{1,0:T(8,128)}, f32[1024,128]{1,0:T(8,128)}) custom-call(s32[6144]{0:T(1024)} %reshape.76.idx_ref, s32[1024]{0:T(1024)} %copy-done.7, f32[1024,128]{1,0:T(8,128)} %get-tuple-element.9.state_ref, f32[1024,128]{1,0:T(8,128)} %select_maximum_fusion.1.halo_ref, f32[6,1024,128]{2,1,0:T(8,128)} %compare_convert_fusion.mask_ref, ...), custom_call_target="tpu_custom_call" | custom-call | flops 2617245696 | bytes 6029312 | tf_op jit(solution)/shard_map/pallas_call | solution.py:167
  65.1 1.2 slice_bitcast_fusion.4
  66.3 0.5 collective-permute-start.4
  66.8 1.7 collective-permute-start.5
  68.6 4.3 %collective-permute-done.4 = f32[16,512]{0,1:T(8,128)S(1)} collective-permute-done((f32[16,512]{0,1:T(8,128)S(1)}, f32[16,512]{0,1:T(8,128)S(1)}, u32[]{:S(2)}, u32[]{:S(2)}) %collective-permute-start.4) | collective-permute-done | bytes 32800 | tf_op jit(solution)/shard_map/ppermute | solution.py:27
  72.9 2.4 %collective-permute-done.5 = f32[16,512]{0,1:T(8,128)S(1)} collective-permute-done((f32[16,512]{0,1:T(8,128)S(1)}, f32[16,512]{0,1:T(8,128)S(1)}, u32[]{:S(2)}, u32[]{:S(2)}) %collective-permute-start.5) | collective-permute-done | bytes 32800 | tf_op jit(solution)/shard_map/ppermute | solution.py:27
  75.3 0.9 select_maximum_fusion.halo_ref
  76.2 15.3 %shard_map.103 = f32[1024,128]{1,0:T(8,128)} custom-call(s32[6144]{0:T(1024)} %reshape.76.idx_ref, s32[1024]{0:T(1024)} %copy-done.7, f32[1024,128]{1,0:T(8,128)} %get-tuple-element.11.state_ref, f32[1024,128]{1,0:T(8,128)} %select_maximum_fusion.halo_ref, f32[6,1024,128]{2,1,0:T(8,128)} %compare_convert_fusion.mask_ref, ...), custom_call_target="tpu_custom_call" | custom-call | flops 2617245696 | bytes 6029312 | tf_op jit(solution)/shard_map/pallas_call | solution.py:167
  91.5 2.0 %add_select_fusion = f32[64,1024]{0,1:T(8,128)S(1)} fusion(f32[1024,128]{1,0:T(8,128)} %shard_map.103, f32[64,64]{1,0:T(8,128)S(1)} %copy-done, f32[1,64,1024]{2,1,0:T(8,128)S(1)} %copy-done.1, pred[]{:T(512)S(6)} %eq.13), kind=kOutput, calls=%fused_computation.11 | convolution fusion | flops 50528256 | bytes 802817 | tf_op jit(solution)/shard_map/dot_general | solution.py:31
  93.7 1.5 collective-permute-done.6
  95.6 3.8 %collective-permute-start.7 = (f32[64,512]{0,1:T(8,128)S(1)}, f32[64,512]{0,1:T(8,128)S(1)}, u32[]{:S(2)}, u32[]{:S(2)}) collective-permute-start(f32[64,512]{0,1:T(8,128)S(1)} %fusion.1), channel_id=1, source_target_pairs={{0,16},{8,24},{16,32},{24,40},{32,48},{40,56},{48,64},{56,72},{64,... | collective-permute-start | bytes 393224 | tf_op jit(solution)/shard_map/ppermute | solution.py:22
  99.5 10.6 %collective-permute-done.7 = f32[64,512]{0,1:T(8,128)S(1)} collective-permute-done((f32[64,512]{0,1:T(8,128)S(1)}, f32[64,512]{0,1:T(8,128)S(1)}, u32[]{:S(2)}, u32[]{:S(2)}) %collective-permute-start.7) | collective-permute-done | bytes 131104 | tf_op jit(solution)/shard_map/ppermute | solution.py:22
  110.1 1.9 %collective-permute-start.8 = (f32[64,512]{0,1:T(8,128)S(1)}, f32[64,512]{0,1:T(8,128)S(1)}, u32[]{:S(2)}, u32[]{:S(2)}) collective-permute-start(f32[64,512]{0,1:T(8,128)S(1)} %collective-permute-done.7), channel_id=1, source_target_pairs={{0,16},{8,24},{16,32},{24,40},{32,48},{40,56},{48,64},{56,72},{64,... | collective-permute-start | bytes 393224 | tf_op jit(solution)/shard_map/ppermute | solution.py:22
  112.1 11.2 %collective-permute-done.8 = f32[64,512]{0,1:T(8,128)S(1)} collective-permute-done((f32[64,512]{0,1:T(8,128)S(1)}, f32[64,512]{0,1:T(8,128)S(1)}, u32[]{:S(2)}, u32[]{:S(2)}) %collective-permute-start.8) | collective-permute-done | bytes 131104 | tf_op jit(solution)/shard_map/ppermute | solution.py:22
  123.4 0.4 convolution_add_fusion.4
  123.8 1.9 %collective-permute-start.9 = (f32[64,512]{0,1:T(8,128)S(1)}, f32[64,512]{0,1:T(8,128)S(1)}, u32[]{:S(2)}, u32[]{:S(2)}) collective-permute-start(f32[64,512]{0,1:T(8,128)S(1)} %convolution_add_fusion.4), channel_id=1, source_target_pairs={{0,32},{8,40},{16,48},{24,56},{32,64},{40,72},{48,80},{56,88},{64,... | collective-permute-start | bytes 393224 | tf_op jit(solution)/shard_map/ppermute | solution.py:22
  125.9 14.4 %collective-permute-done.9 = f32[64,512]{0,1:T(8,128)S(1)} collective-permute-done((f32[64,512]{0,1:T(8,128)S(1)}, f32[64,512]{0,1:T(8,128)S(1)}, u32[]{:S(2)}, u32[]{:S(2)}) %collective-permute-start.9) | collective-permute-done | bytes 131104 | tf_op jit(solution)/shard_map/ppermute | solution.py:22
  140.3 0.4 convolution_add_fusion.3
  140.6 1.9 %collective-permute-start.10 = (f32[64,512]{0,1:T(8,128)S(1)}, f32[64,512]{0,1:T(8,128)S(1)}, u32[]{:S(2)}, u32[]{:S(2)}) collective-permute-start(f32[64,512]{0,1:T(8,128)S(1)} %convolution_add_fusion.3), channel_id=1, source_target_pairs={{0,64},{8,72},{16,80},{24,88},{32,96},{40,104},{48,112},{56,120},{... | collective-permute-start | bytes 393224 | tf_op jit(solution)/shard_map/ppermute | solution.py:22
  142.7 16.5 %collective-permute-done.10 = f32[64,512]{0,1:T(8,128)S(1)} collective-permute-done((f32[64,512]{0,1:T(8,128)S(1)}, f32[64,512]{0,1:T(8,128)S(1)}, u32[]{:S(2)}, u32[]{:S(2)}) %collective-permute-start.10) | collective-permute-done | bytes 131104 | tf_op jit(solution)/shard_map/ppermute | solution.py:22
  159.2 0.4 convolution_add_fusion.2
  159.6 1.3 collective-permute-start.11
  161.1 10.2 %collective-permute-done.11 = f32[64,512]{0,1:T(8,128)S(1)} collective-permute-done((f32[64,512]{0,1:T(8,128)S(1)}, f32[64,512]{0,1:T(8,128)S(1)}, u32[]{:S(2)}, u32[]{:S(2)}) %collective-permute-start.11) | collective-permute-done | bytes 131104 | tf_op jit(solution)/shard_map/ppermute | solution.py:22
  171.6 0.4 convolution_add_fusion
  172.0 0.4 select_bitcast_fusion
  172.4 1.5 collective-permute-done.12
  174.0 0.9 copy.36
  (33 shorter events, 2.4 us)
Async XLA Ops:
  0.0 91.5 %copy-start = (f32[64,64]{1,0:T(8,128)S(1)}, f32[64,64]{1,0:T(8,128)}, u32[]{:S(2)}) copy-start(f32[64,64]{1,0:T(8,128)} %param.13) | copy-start | bytes 49156
  0.0 10.0 %copy-start.5 = (f32[64,64]{1,0:T(8,128)S(1)}, f32[64,64]{1,0:T(8,128)}, u32[]{:S(2)}) copy-start(f32[64,64]{1,0:T(8,128)} %param.11) | copy-start | bytes 49156
  0.0 10.0 %copy-start.3 = (s32[6,1024]{1,0:T(8,128)S(1)}, s32[6,1024]{1,0:T(8,128)}, u32[]{:S(2)}) copy-start(s32[6,1024]{1,0:T(8,128)} %param.15) | copy-start | bytes 73732
  2.6 0.9 copy-start.7
  2.6 10.1 %copy-start.2 = (f32[64,96]{1,0:T(8,128)S(1)}, f32[64,96]{1,0:T(8,128)}, u32[]{:S(2)}) copy-start(f32[64,96]{1,0:T(8,128)} %param.12) | copy-start | bytes 73732
  2.6 10.1 %copy-start.6 = (f32[64,96]{1,0:T(8,128)S(1)}, f32[64,96]{1,0:T(8,128)}, u32[]{:S(2)}) copy-start(f32[64,96]{1,0:T(8,128)} %constant.43.clone) | copy-start | bytes 73732
  6.7 7.8 %copy-start.4 = (s32[6,1024]{1,0:T(8,128)S(1)}, s32[6,1024]{1,0:T(8,128)}, u32[]{:S(2)}) copy-start(s32[6,1024]{1,0:T(8,128)} %param.14) | copy-start | bytes 73732
  7.9 8.1 %collective-permute-start = (f32[16,512]{0,1:T(8,128)S(1)}, f32[16,512]{0,1:T(8,128)S(1)}, u32[]{:S(2)}, u32[]{:S(2)}) collective-permute-start(f32[16,512]{0,1:T(8,128)S(1)} %get-tuple-element.19), channel_id=1, source_target_pairs={{0,1},{1,2},{2,3},{3,4},{4,5},{5,6},{6,7},{7,0},{8,9},{9,10},{10,1... | collective-permute-start | bytes 98312 | tf_op jit(solution)/shard_map/ppermute | solution.py:27
  9.1 9.9 %collective-permute-start.1 = (f32[16,512]{0,1:T(8,128)S(1)}, f32[16,512]{0,1:T(8,128)S(1)}, u32[]{:S(2)}, u32[]{:S(2)}) collective-permute-start(f32[16,512]{0,1:T(8,128)S(1)} %get-tuple-element.20), channel_id=1, source_target_pairs={{0,7},{1,0},{2,1},{3,2},{4,3},{5,4},{6,5},{7,6},{8,15},{9,8},{10,9... | collective-permute-start | bytes 98312 | tf_op jit(solution)/shard_map/ppermute | solution.py:27
  37.9 6.9 %collective-permute-start.2 = (f32[16,512]{0,1:T(8,128)S(1)}, f32[16,512]{0,1:T(8,128)S(1)}, u32[]{:S(2)}, u32[]{:S(2)}) collective-permute-start(f32[16,512]{0,1:T(8,128)S(1)} %get-tuple-element.17), channel_id=1, source_target_pairs={{0,1},{1,2},{2,3},{3,4},{4,5},{5,6},{6,7},{7,0},{8,9},{9,10},{10,1... | collective-permute-start | bytes 98312 | tf_op jit(solution)/shard_map/ppermute | solution.py:27
  38.3 9.0 %collective-permute-start.3 = (f32[16,512]{0,1:T(8,128)S(1)}, f32[16,512]{0,1:T(8,128)S(1)}, u32[]{:S(2)}, u32[]{:S(2)}) collective-permute-start(f32[16,512]{0,1:T(8,128)S(1)} %get-tuple-element.18), channel_id=1, source_target_pairs={{0,7},{1,0},{2,1},{3,2},{4,3},{5,4},{6,5},{7,6},{8,15},{9,8},{10,9... | collective-permute-start | bytes 98312 | tf_op jit(solution)/shard_map/ppermute | solution.py:27
  66.3 6.6 %collective-permute-start.4 = (f32[16,512]{0,1:T(8,128)S(1)}, f32[16,512]{0,1:T(8,128)S(1)}, u32[]{:S(2)}, u32[]{:S(2)}) collective-permute-start(f32[16,512]{0,1:T(8,128)S(1)} %get-tuple-element.15), channel_id=1, source_target_pairs={{0,1},{1,2},{2,3},{3,4},{4,5},{5,6},{6,7},{7,0},{8,9},{9,10},{10,1... | collective-permute-start | bytes 98312 | tf_op jit(solution)/shard_map/ppermute | solution.py:27
  66.8 8.5 %collective-permute-start.5 = (f32[16,512]{0,1:T(8,128)S(1)}, f32[16,512]{0,1:T(8,128)S(1)}, u32[]{:S(2)}, u32[]{:S(2)}) collective-permute-start(f32[16,512]{0,1:T(8,128)S(1)} %get-tuple-element.16), channel_id=1, source_target_pairs={{0,7},{1,0},{2,1},{3,2},{4,3},{5,4},{6,5},{7,6},{8,15},{9,8},{10,9... | collective-permute-start | bytes 98312 | tf_op jit(solution)/shard_map/ppermute | solution.py:27
  76.2 15.3 %copy-start.1 = (f32[1,64,1024]{2,1,0:T(8,128)S(1)}, f32[1,64,1024]{2,1,0:T(8,128)}, u32[]{:S(2)}) copy-start(f32[1,64,1024]{2,1,0:T(8,128)} %param.10) | copy-start | bytes 786436
  93.6 1.6 collective-permute-start.6
  95.6 14.4 %collective-permute-start.7 = (f32[64,512]{0,1:T(8,128)S(1)}, f32[64,512]{0,1:T(8,128)S(1)}, u32[]{:S(2)}, u32[]{:S(2)}) collective-permute-start(f32[64,512]{0,1:T(8,128)S(1)} %fusion.1), channel_id=1, source_target_pairs={{0,16},{8,24},{16,32},{24,40},{32,48},{40,56},{48,64},{56,72},{64,... | collective-permute-start | bytes 393224 | tf_op jit(solution)/shard_map/ppermute | solution.py:22
  110.1 13.3 %collective-permute-start.8 = (f32[64,512]{0,1:T(8,128)S(1)}, f32[64,512]{0,1:T(8,128)S(1)}, u32[]{:S(2)}, u32[]{:S(2)}) collective-permute-start(f32[64,512]{0,1:T(8,128)S(1)} %collective-permute-done.7), channel_id=1, source_target_pairs={{0,16},{8,24},{16,32},{24,40},{32,48},{40,56},{48,64},{56,72},{64,... | collective-permute-start | bytes 393224 | tf_op jit(solution)/shard_map/ppermute | solution.py:22
  123.8 16.5 %collective-permute-start.9 = (f32[64,512]{0,1:T(8,128)S(1)}, f32[64,512]{0,1:T(8,128)S(1)}, u32[]{:S(2)}, u32[]{:S(2)}) collective-permute-start(f32[64,512]{0,1:T(8,128)S(1)} %convolution_add_fusion.4), channel_id=1, source_target_pairs={{0,32},{8,40},{16,48},{24,56},{32,64},{40,72},{48,80},{56,88},{64,... | collective-permute-start | bytes 393224 | tf_op jit(solution)/shard_map/ppermute | solution.py:22
  140.6 18.6 %collective-permute-start.10 = (f32[64,512]{0,1:T(8,128)S(1)}, f32[64,512]{0,1:T(8,128)S(1)}, u32[]{:S(2)}, u32[]{:S(2)}) collective-permute-start(f32[64,512]{0,1:T(8,128)S(1)} %convolution_add_fusion.3), channel_id=1, source_target_pairs={{0,64},{8,72},{16,80},{24,88},{32,96},{40,104},{48,112},{56,120},{... | collective-permute-start | bytes 393224 | tf_op jit(solution)/shard_map/ppermute | solution.py:22
  159.6 11.6 %collective-permute-start.11 = (f32[64,512]{0,1:T(8,128)S(1)}, f32[64,512]{0,1:T(8,128)S(1)}, u32[]{:S(2)}, u32[]{:S(2)}) collective-permute-start(f32[64,512]{0,1:T(8,128)S(1)} %convolution_add_fusion.2), channel_id=1, source_target_pairs={{0,128},{8,136},{16,144},{24,152},{32,160},{40,168},{48,176},{56,1... | collective-permute-start | bytes 393224 | tf_op jit(solution)/shard_map/ppermute | solution.py:22
  172.3 1.6 collective-permute-start.12

commit v8 on v7

--- a/solution.py
+++ b/solution.py
@@ -112,8 +112,39 @@
     )
 
 
-def fused_kernel(with_send, idx_ref, send_ref, state_ref, halo_ref, mask_ref, pick_ref,
-                 spread_ref, folded_ref, out_ref, *rest):
+def gather_into(idx_ref, table, beside):
+    def gather(step, carry):
+        for u in range(UNROLL):
+            row = step * UNROLL + u
+            beside[pl.ds(row, 1), :] = table[pl.ds(idx_ref[row], 1), :]
+        return carry
+
+    lax.fori_loop(0, beside.shape[0] // UNROLL, gather, 0)
+
+
+def lift_faces(beside, mask_ref, pick_ref, spread_ref, elements, lifted):
+    for face in range(pick_ref.shape[0]):
+        parts = split_three(beside[face * elements:(face + 1) * elements, :])
+        turned = (bf16_dot(parts[0], pick_ref[face]) + bf16_dot(parts[1], pick_ref[face])) + (
+            bf16_dot(parts[2], pick_ref[face])
+        )
+        chosen = jnp.where(mask_ref[face] > 0.5, turned, 0.0)
+        lifted = lifted + three_pass_dot(chosen, spread_ref[face])
+    return lifted
+
+
+def near_kernel(idx_ref, state_ref, mask_ref, pick_ref, spread_ref, folded_ref, out_ref, beside):
+    elements = state_ref.shape[0]
+    gather_into(idx_ref, state_ref, beside)
+    own = jnp.dot(
+        state_ref[...], folded_ref[...], precision=lax.Precision.HIGHEST,
+        preferred_element_type=jnp.float32,
+    )
+    out_ref[...] = lift_faces(beside, mask_ref, pick_ref, spread_ref, elements, own)
+
+
+def far_kernel(with_send, idx_ref, send_ref, state_ref, halo_ref, partial_ref, mask_ref,
+               pick_ref, spread_ref, out_ref, *rest):
     if with_send:
         sent_ref, table, beside = rest
     else:
@@ -121,28 +152,10 @@
     elements = state_ref.shape[0]
     table[0:elements, :] = state_ref[...]
     table[elements:, :] = halo_ref[...]
-
-    def gather(step, carry):
-        for u in range(UNROLL):
-            row = step * UNROLL + u
-            beside[pl.ds(row, 1), :] = table[pl.ds(idx_ref[row], 1), :]
-        return carry
-
-    lax.fori_loop(0, beside.shape[0] // UNROLL, gather, 0)
+    gather_into(idx_ref, table, beside)
     state = state_ref[...]
-    lifted = jnp.zeros_like(state)
-    for face in range(6):
-        parts = split_three(beside[face * elements:(face + 1) * elements, :])
-        turned = (bf16_dot(parts[0], pick_ref[face]) + bf16_dot(parts[1], pick_ref[face])) + (
-            bf16_dot(parts[2], pick_ref[face])
-        )
-        chosen = jnp.where(mask_ref[face] > 0.5, turned, 0.0)
-        lifted = lifted + three_pass_dot(chosen, spread_ref[face])
-    own = jnp.dot(
-        state, folded_ref[...], precision=lax.Precision.HIGHEST,
-        preferred_element_type=jnp.float32,
-    )
-    rate = own + lifted + state - state * state * state
+    lifted = lift_faces(beside, mask_ref, pick_ref, spread_ref, elements, partial_ref[...])
+    rate = lifted + state - state * state * state
     out_ref[...] = state + time_step * rate
     if with_send:
         def send(step, carry):
@@ -154,7 +167,23 @@
         lax.fori_loop(0, sent_ref.shape[0] // UNROLL, send, 0)
 
 
-def fused_step(state, halo, mask, pick, spread, folded, nbr_rows, send_rows, with_send):
+def near_part(state, mask, pick, spread, folded, rows):
+    elements, lanes = state.shape
+    vmem = pl.BlockSpec(memory_space=pltpu.VMEM)
+    faces = pick.shape[0]
+    flops = 2 * 6 * faces * elements * lanes * (2 * lanes) + 2 * 6 * elements * lanes * lanes
+    moved = 4 * (2 * elements * lanes + mask.size + pick.size + spread.size)
+    return pl.pallas_call(
+        near_kernel,
+        out_shape=jax.ShapeDtypeStruct((elements, lanes), state.dtype),
+        in_specs=[pl.BlockSpec(memory_space=pltpu.SMEM)] + [vmem] * 5,
+        out_specs=vmem,
+        scratch_shapes=[pltpu.VMEM((rows.shape[0], lanes), jnp.float32)],
+        cost_estimate=pl.CostEstimate(flops=flops, transcendentals=0, bytes_accessed=moved),
+    )(rows, state, mask, pick, spread, folded)
+
+
+def far_part(state, halo, partial, mask, pick, spread, rows, send_rows, with_send):
     elements, lanes = state.shape
     block = jax.ShapeDtypeStruct((elements, lanes), state.dtype)
     shapes = [block]
@@ -162,20 +191,20 @@
         shapes.append(jax.ShapeDtypeStruct((send_rows.shape[0], lanes), state.dtype))
     vmem = pl.BlockSpec(memory_space=pltpu.VMEM)
     smem = pl.BlockSpec(memory_space=pltpu.SMEM)
-    flops = 2 * 6 * 6 * elements * lanes * (2 * lanes) + 2 * 6 * elements * lanes * lanes
-    moved = 4 * (4 * elements * lanes + mask.size + pick.size + spread.size)
-    result = pl.pallas_call(
-        functools.partial(fused_kernel, with_send),
+    faces = pick.shape[0]
+    flops = 2 * 6 * faces * elements * lanes * (2 * lanes)
+    moved = 4 * (5 * elements * lanes + mask.size + pick.size + spread.size)
+    return pl.pallas_call(
+        functools.partial(far_kernel, with_send),
         out_shape=tuple(shapes),
         in_specs=[smem, smem] + [vmem] * 6,
         out_specs=tuple([vmem] * len(shapes)),
         scratch_shapes=[
             pltpu.VMEM((elements + halo.shape[0], lanes), jnp.float32),
-            pltpu.VMEM((nbr_rows.shape[0], lanes), jnp.float32),
+            pltpu.VMEM((rows.shape[0], lanes), jnp.float32),
         ],
         cost_estimate=pl.CostEstimate(flops=flops, transcendentals=0, bytes_accessed=moved),
-    )(nbr_rows, send_rows, state, halo, mask, pick, spread, folded)
-    return result
+    )(rows, send_rows, state, halo, partial, mask, pick, spread)
 
 
 def shards(start_state, stiffness, lifting, coarse, neighbor, orientation, send_low, send_high):
@@ -187,7 +216,8 @@
     folded = stiffness.T - product(own, lifting.T)
     lane_code = jnp.arange(LANES, dtype=jnp.int32) // 16
     mask = orientation[:, :, None] == lane_code[None, None, :]
-    nbr_rows = neighbor.reshape(-1)
+    far_rows = neighbor[:2].reshape(-1)
+    near_rows = neighbor[2:].reshape(-1)
     send_rows = jnp.concatenate([send_low, send_high])
     spread = jnp.pad(spread, ((0, 0), (0, 0), (0, LANES - 64)))
     folded = jnp.pad(folded, ((0, LANES - 64), (0, LANES - 64)))
@@ -200,6 +230,7 @@
     for step_id in range(STEPS):
         before = ring(sent[half:, 48:64].T, "space", 1)
         after = ring(sent[:half, 0:16].T, "space", -1)
+        partial = near_part(state, mask[2:], pick[2:], spread[2:], folded, near_rows)
         halo = jnp.concatenate(
             [
                 jnp.pad(before.T, ((0, 0), (48, LANES - 64))),
@@ -208,8 +239,8 @@
             axis=0,
         )
         with_send = step_id < STEPS - 1
-        result = fused_step(
-            state, halo, mask, pick, spread, folded, nbr_rows, send_rows, with_send
+        result = far_part(
+            state, halo, partial, mask[:2], pick[:2], spread[:2], far_rows, send_rows, with_send
         )
         state = result[0]
         if with_send:

time: 176 us -> 176 us (level)
  the two profiles are of different devices: /device:TPU:22 before, /device:TPU:25 now
where the time goes in v8:
time: 176 us
  waiting for transfers between devices  64.9 us (37%)
  Pallas kernels  58.5 us (33%)
  starting transfers between devices  25.5 us (14%)
  local copies, waits for them, and re-layouts  16 us (9%)
  matrix products  5.43 us (3%)
  other arithmetic  4.82 us (3%)
    ppermute x5, waiting for transfers between devices, from_behind(): return lax.ppermute(shard, axis, pairs)  62.6 us
    pallas_call x3, Pallas kernels, near_part(): pl.pallas_call(near_kernel, out_shape=jax.ShapeDtypeStruct((elements, lan...  32.1 us
    pallas_call x3, Pallas kernels, far_part(): pl.pallas_call(functools.partial(far_kernel, with_send), out_shape=tuple(...  23.1 us
    ppermute x6, starting transfers between devices, ring(): lax.ppermute(shard, axis, [(i, (i + by) % peers) for i in range(peers)])  10.9 us
    ppermute x5, starting transfers between devices, from_behind(): return lax.ppermute(shard, axis, pairs)  10.8 us
    dot_general x13, matrix products, product(): jnp.dot(matrix, vector, precision=lax.Precision.HIGHEST, preferred_elemen...  5.43 us
    transpose x3, local copies, waits for them, and re-layouts, shards(): before = ring(sent[half:, 48:64].T, 'space', 1)  4.17 us
    unnamed x26, local copies, waits for them, and re-layouts  3.98 us
  transfers between devices with their start and end apart: 13, of which 7 were waited for; matrix products, arithmetic and copies ran while one was open for 5% of the time, Pallas kernels for 18%

profile of v8, /device:TPU:25, one launch (start us, length us, event | category | flops | bytes accessed | tf_op | source)
XLA Modules:
  0.0 175.6 jit_solution(15468179720297305257)
XLA Ops:
  0.1 1.2 copy.24
  1.2 0.7 constant_dynamic-update-slice_fusion
  1.9 0.7 constant_dynamic-update-slice_fusion.1.idx_ref.send_ref
  2.6 0.8 pad.32.table_ref.state_ref
  3.4 3.3 %shard_map.100 = f32[1024,128]{1,0:T(8,128)} custom-call(s32[1024]{0:T(1024)} %copy-done.8, f32[1024,128]{1,0:T(8,128)} %pad.32.table_ref.state_ref), custom_call_target="tpu_custom_call" | custom-call | tf_op jit(solution)/shard_map/pallas_call | solution.py:85
  6.7 1.9 %slice_bitcast_fusion.2 = (f32[16,512]{0,1:T(8,128)}, f32[16,512]{0,1:T(8,128)S(1)}) fusion(f32[1024,128]{1,0:T(8,128)} %shard_map.100), kind=kLoop, calls=%fused_computation.22 | loop fusion | bytes 131072 | tf_op jit(solution)/shard_map/transpose | solution.py:231
  8.6 1.2 collective-permute-start
  9.8 2.4 %collective-permute-start.1 = (f32[16,512]{0,1:T(8,128)S(1)}, f32[16,512]{0,1:T(8,128)}, u32[]{:S(2)}, u32[]{:S(2)}) collective-permute-start(f32[16,512]{0,1:T(8,128)S(1)} %get-tuple-element.20), channel_id=1, source_target_pairs={{0,7},{1,0},{2,1},{3,2},{4,3},{5,4},{6,5},{7,6},{8,15},{9,8},{10,9... | collective-permute-start | bytes 98312 | tf_op jit(solution)/shard_map/ppermute | solution.py:27
  12.2 0.6 copy.49
  13.2 0.6 pad.36.folded_ref
  13.8 0.7 copy-done.1
  14.6 0.7 pad_slice_fusion.1.spread_ref
  15.3 0.9 compare_convert_fusion
  16.2 1.5 slice.82.mask_ref
  17.6 10.7 %shard_map.101.partial_ref = f32[1024,128]{1,0:T(8,128)} custom-call(s32[4096]{0:T(1024)} %bitcast.95, f32[1024,128]{1,0:T(8,128)} %pad.32.table_ref.state_ref, f32[4,1024,128]{2,1,0:T(8,128)} %slice.82.mask_ref, bf16[4,128,128]{2,1,0:T(8,128)(2,1)} %constant.63.pick_ref, f32[4,128,128]{2,1,0:T(8,128)} %pad_slice_fusion.1.spread_ref, f32[128,128]{1,0:T(8,128)} %pad.36.folded_ref), custom_call_target="tpu_custom_call" | custom-call | flops 1811939328 | bytes 3670016 | tf_op jit(solution)/shard_map/pallas_call | solution.py:176
  28.3 1.6 pad_slice_fusion.spread_ref
  29.9 1.1 slice.83.mask_ref
  31.0 0.6 copy.50
  31.6 2.0 %select_maximum_fusion.2.halo_ref = f32[1024,128]{1,0:T(8,128)} fusion(f32[512,16]{1,0:T(8,128)} %bitcast.5, f32[512,16]{1,0:T(8,128)} %bitcast.3), kind=kLoop, calls=%fused_computation.15 | loop fusion | flops 655360 | bytes 589824 | tf_op jit(solution)/shard_map/concatenate | solution.py:234
  33.5 8.2 %shard_map.102 = (f32[1024,128]{1,0:T(8,128)}, f32[1024,128]{1,0:T(8,128)}) custom-call(s32[2048]{0:T(1024)} %bitcast.92, s32[1024]{0:T(1024)} %copy-done.8, f32[1024,128]{1,0:T(8,128)} %pad.32.table_ref.state_ref, f32[1024,128]{1,0:T(8,128)} %select_maximum_fusion.2.halo_ref, f32[1024,128]{1,0:T(8,128)} %shard_map.101.partial_ref, ...), custom_call_target="tpu_custom_call" | custom-call | flops 805306368 | bytes 3932160 | tf_op jit(solution)/shard_map/pallas_call | solution.py:197
  41.8 1.2 slice_bitcast_fusion.6
  43.0 3.6 %collective-permute-start.3 = (f32[16,512]{0,1:T(8,128)S(1)}, f32[16,512]{0,1:T(8,128)S(1)}, u32[]{:S(2)}, u32[]{:S(2)}) collective-permute-start(f32[16,512]{0,1:T(8,128)S(1)} %get-tuple-element.18), channel_id=1, source_target_pairs={{0,7},{1,0},{2,1},{3,2},{4,3},{5,4},{6,5},{7,6},{8,15},{9,8},{10,9... | collective-permute-start | bytes 98312 | tf_op jit(solution)/shard_map/ppermute | solution.py:27
  46.6 10.7 %shard_map.103.partial_ref = f32[1024,128]{1,0:T(8,128)} custom-call(s32[4096]{0:T(1024)} %bitcast.96, f32[1024,128]{1,0:T(8,128)} %get-tuple-element.9.state_ref, f32[4,1024,128]{2,1,0:T(8,128)} %slice.82.mask_ref, bf16[4,128,128]{2,1,0:T(8,128)(2,1)} %constant.63.pick_ref, f32[4,128,128]{2,1,0:T(8,128)} %pad_slice_fusion.1.spread_ref, ...), custom_call_target="tpu_custom_call" | custom-call | flops 1811939328 | bytes 3670016 | tf_op jit(solution)/shard_map/pallas_call | solution.py:176
  57.3 0.9 select_maximum_fusion.1.halo_ref
  58.2 8.2 %shard_map.104 = (f32[1024,128]{1,0:T(8,128)}, f32[1024,128]{1,0:T(8,128)}) custom-call(s32[2048]{0:T(1024)} %bitcast.93, s32[1024]{0:T(1024)} %copy-done.8, f32[1024,128]{1,0:T(8,128)} %get-tuple-element.9.state_ref, f32[1024,128]{1,0:T(8,128)} %select_maximum_fusion.1.halo_ref, f32[1024,128]{1,0:T(8,128)} %shard_map.103.partial_ref, ...), custom_call_target="tpu_custom_call" | custom-call | flops 805306368 | bytes 3932160 | tf_op jit(solution)/shard_map/pallas_call | solution.py:197
  66.5 1.2 slice_bitcast_fusion.4
  67.7 3.6 %collective-permute-start.5 = (f32[16,512]{0,1:T(8,128)S(1)}, f32[16,512]{0,1:T(8,128)S(1)}, u32[]{:S(2)}, u32[]{:S(2)}) collective-permute-start(f32[16,512]{0,1:T(8,128)S(1)} %get-tuple-element.16), channel_id=1, source_target_pairs={{0,7},{1,0},{2,1},{3,2},{4,3},{5,4},{6,5},{7,6},{8,15},{9,8},{10,9... | collective-permute-start | bytes 98312 | tf_op jit(solution)/shard_map/ppermute | solution.py:27
  71.3 10.7 %shard_map.105.partial_ref = f32[1024,128]{1,0:T(8,128)} custom-call(s32[4096]{0:T(1024)} %bitcast.97, f32[1024,128]{1,0:T(8,128)} %get-tuple-element.11.state_ref, f32[4,1024,128]{2,1,0:T(8,128)} %slice.82.mask_ref, bf16[4,128,128]{2,1,0:T(8,128)(2,1)} %constant.63.pick_ref, f32[4,128,128]{2,1,0:T(8,128)} %pad_slice_fusion.1.spread_ref, ...), custom_call_target="tpu_custom_call" | custom-call | flops 1811939328 | bytes 3670016 | tf_op jit(solution)/shard_map/pallas_call | solution.py:176
  82.0 1.0 select_maximum_fusion.halo_ref
  82.9 6.7 %shard_map.106 = f32[1024,128]{1,0:T(8,128)} custom-call(s32[2048]{0:T(1024)} %bitcast.94, s32[1024]{0:T(1024)} %copy-done.8, f32[1024,128]{1,0:T(8,128)} %get-tuple-element.11.state_ref, f32[1024,128]{1,0:T(8,128)} %select_maximum_fusion.halo_ref, f32[1024,128]{1,0:T(8,128)} %shard_map.105.partial_ref, f32[2,1024,128]{2,1,0:T(8,128)} %slice.83.mask_ref, ...), custom_call_target="tpu_custom_call" | custom-call | flops 805306368 | bytes 3932160 | tf_op jit(solution)/shard_map/pallas_call | solution.py:197
  89.6 2.0 %add_select_fusion = f32[64,1024]{0,1:T(8,128)S(1)} fusion(f32[1024,128]{1,0:T(8,128)} %shard_map.106, f32[64,64]{1,0:T(8,128)S(1)} %copy-done, f32[1,64,1024]{2,1,0:T(8,128)S(1)} %copy-done.2, pred[]{:T(512)S(6)} %eq.13), kind=kOutput, calls=%fused_computation.11 | convolution fusion | flops 50528256 | bytes 802817 | tf_op jit(solution)/shard_map/dot_general | solution.py:31
  91.7 2.4 %collective-permute-start.6 = (f32[64,512]{0,1:T(8,128)S(1)}, f32[64,512]{0,1:T(8,128)S(1)}, u32[]{:S(2)}, u32[]{:S(2)}) collective-permute-start(f32[64,512]{0,1:T(8,128)S(1)} %slice_select_fusion), channel_id=1, source_target_pairs={{0,8},{8,0},{16,24},{24,16},{32,40},{40,32},{48,56},{56,48},{64,72... | collective-permute-start | bytes 393224 | tf_op jit(solution)/shard_map/ppermute | solution.py:262
  94.1 1.2 collective-permute-done.6
  95.7 3.6 %collective-permute-start.7 = (f32[64,512]{0,1:T(8,128)S(1)}, f32[64,512]{0,1:T(8,128)S(1)}, u32[]{:S(2)}, u32[]{:S(2)}) collective-permute-start(f32[64,512]{0,1:T(8,128)S(1)} %fusion.1), channel_id=1, source_target_pairs={{0,16},{8,24},{16,32},{24,40},{32,48},{40,56},{48,64},{56,72},{64,... | collective-permute-start | bytes 393224 | tf_op jit(solution)/shard_map/ppermute | solution.py:22
  99.2 11.0 %collective-permute-done.7 = f32[64,512]{0,1:T(8,128)S(1)} collective-permute-done((f32[64,512]{0,1:T(8,128)S(1)}, f32[64,512]{0,1:T(8,128)S(1)}, u32[]{:S(2)}, u32[]{:S(2)}) %collective-permute-start.7) | collective-permute-done | bytes 131104 | tf_op jit(solution)/shard_map/ppermute | solution.py:22
  110.2 1.9 %collective-permute-start.8 = (f32[64,512]{0,1:T(8,128)S(1)}, f32[64,512]{0,1:T(8,128)S(1)}, u32[]{:S(2)}, u32[]{:S(2)}) collective-permute-start(f32[64,512]{0,1:T(8,128)S(1)} %collective-permute-done.7), channel_id=1, source_target_pairs={{0,16},{8,24},{16,32},{24,40},{32,48},{40,56},{48,64},{56,72},{64,... | collective-permute-start | bytes 393224 | tf_op jit(solution)/shard_map/ppermute | solution.py:22
  112.3 10.3 %collective-permute-done.8 = f32[64,512]{0,1:T(8,128)S(1)} collective-permute-done((f32[64,512]{0,1:T(8,128)S(1)}, f32[64,512]{0,1:T(8,128)S(1)}, u32[]{:S(2)}, u32[]{:S(2)}) %collective-permute-start.8) | collective-permute-done | bytes 131104 | tf_op jit(solution)/shard_map/ppermute | solution.py:22
  123.0 2.1 %collective-permute-start.9 = (f32[64,512]{0,1:T(8,128)S(1)}, f32[64,512]{0,1:T(8,128)S(1)}, u32[]{:S(2)}, u32[]{:S(2)}) collective-permute-start(f32[64,512]{0,1:T(8,128)S(1)} %convolution_add_fusion.4), channel_id=1, source_target_pairs={{0,32},{8,40},{16,48},{24,56},{32,64},{40,72},{48,80},{56,88},{64,... | collective-permute-start | bytes 393224 | tf_op jit(solution)/shard_map/ppermute | solution.py:22
  125.3 15.5 %collective-permute-done.9 = f32[64,512]{0,1:T(8,128)S(1)} collective-permute-done((f32[64,512]{0,1:T(8,128)S(1)}, f32[64,512]{0,1:T(8,128)S(1)}, u32[]{:S(2)}, u32[]{:S(2)}) %collective-permute-start.9) | collective-permute-done | bytes 131104 | tf_op jit(solution)/shard_map/ppermute | solution.py:22
  140.8 0.4 convolution_add_fusion.3
  141.2 1.9 %collective-permute-start.10 = (f32[64,512]{0,1:T(8,128)S(1)}, f32[64,512]{0,1:T(8,128)S(1)}, u32[]{:S(2)}, u32[]{:S(2)}) collective-permute-start(f32[64,512]{0,1:T(8,128)S(1)} %convolution_add_fusion.3), channel_id=1, source_target_pairs={{0,64},{8,72},{16,80},{24,88},{32,96},{40,104},{48,112},{56,120},{... | collective-permute-start | bytes 393224 | tf_op jit(solution)/shard_map/ppermute | solution.py:22
  143.3 16.5 %collective-permute-done.10 = f32[64,512]{0,1:T(8,128)S(1)} collective-permute-done((f32[64,512]{0,1:T(8,128)S(1)}, f32[64,512]{0,1:T(8,128)S(1)}, u32[]{:S(2)}, u32[]{:S(2)}) %collective-permute-start.10) | collective-permute-done | bytes 131104 | tf_op jit(solution)/shard_map/ppermute | solution.py:22
  160.1 1.3 collective-permute-start.11
  161.6 9.3 %collective-permute-done.11 = f32[64,512]{0,1:T(8,128)S(1)} collective-permute-done((f32[64,512]{0,1:T(8,128)S(1)}, f32[64,512]{0,1:T(8,128)S(1)}, u32[]{:S(2)}, u32[]{:S(2)}) %collective-permute-start.11) | collective-permute-done | bytes 131104 | tf_op jit(solution)/shard_map/ppermute | solution.py:22
  171.6 0.4 select_bitcast_fusion
  172.0 1.4 collective-permute-start.12
  173.4 1.2 collective-permute-done.12
  174.7 0.9 copy.36
  (44 shorter events, 3.2 us)
Async XLA Ops:
  0.0 89.6 %copy-start = (f32[64,64]{1,0:T(8,128)S(1)}, f32[64,64]{1,0:T(8,128)}, u32[]{:S(2)}) copy-start(f32[64,64]{1,0:T(8,128)} %param.13) | copy-start | bytes 49156
  0.0 13.0 %copy-start.6 = (f32[64,96]{1,0:T(8,128)S(1)}, f32[64,96]{1,0:T(8,128)}, u32[]{:S(2)}) copy-start(f32[64,96]{1,0:T(8,128)} %constant.43.clone) | copy-start | bytes 73732
  0.0 12.2 %copy-start.7 = (s32[6,1024]{1,0:T(8,128)S(1)}, s32[6,1024]{1,0:T(8,128)}, u32[]{:S(2)}) copy-start(s32[6,1024]{1,0:T(8,128)} %param.14) | copy-start | bytes 73732
  0.0 12.8 %copy-start.5 = (f32[64,64]{1,0:T(8,128)S(1)}, f32[64,64]{1,0:T(8,128)}, u32[]{:S(2)}) copy-start(f32[64,64]{1,0:T(8,128)} %param.11) | copy-start | bytes 49156
  0.0 12.8 %copy-start.3 = (f32[64,96]{1,0:T(8,128)S(1)}, f32[64,96]{1,0:T(8,128)}, u32[]{:S(2)}) copy-start(f32[64,96]{1,0:T(8,128)} %param.12) | copy-start | bytes 73732
  0.0 15.3 %copy-start.4 = (s32[6,1024]{1,0:T(8,128)S(1)}, s32[6,1024]{1,0:T(8,128)}, u32[]{:S(2)}) copy-start(s32[6,1024]{1,0:T(8,128)} %param.15) | copy-start | bytes 73732
  2.6 0.8 copy-start.8
  8.6 23.0 %collective-permute-start = (f32[16,512]{0,1:T(8,128)}, f32[16,512]{0,1:T(8,128)}, u32[]{:S(2)}, u32[]{:S(2)}) collective-permute-start(f32[16,512]{0,1:T(8,128)} %get-tuple-element.19), channel_id=1, source_target_pairs={{0,1},{1,2},{2,3},{3,4},{4,5},{5,6},{6,7},{7,0},{8,9},{9,10},{10,1... | collective-permute-start | bytes 98312 | tf_op jit(solution)/shard_map/ppermute | solution.py:27
  9.8 21.8 %collective-permute-start.1 = (f32[16,512]{0,1:T(8,128)S(1)}, f32[16,512]{0,1:T(8,128)}, u32[]{:S(2)}, u32[]{:S(2)}) collective-permute-start(f32[16,512]{0,1:T(8,128)S(1)} %get-tuple-element.20), channel_id=1, source_target_pairs={{0,7},{1,0},{2,1},{3,2},{4,3},{5,4},{6,5},{7,6},{8,15},{9,8},{10,9... | collective-permute-start | bytes 98312 | tf_op jit(solution)/shard_map/ppermute | solution.py:27
  13.8 0.7 copy-start.1
  42.9 14.4 %collective-permute-start.2 = (f32[16,512]{0,1:T(8,128)S(1)}, f32[16,512]{0,1:T(8,128)S(1)}, u32[]{:S(2)}, u32[]{:S(2)}) collective-permute-start(f32[16,512]{0,1:T(8,128)S(1)} %get-tuple-element.17), channel_id=1, source_target_pairs={{0,1},{1,2},{2,3},{3,4},{4,5},{5,6},{6,7},{7,0},{8,9},{9,10},{10,1... | collective-permute-start | bytes 98312 | tf_op jit(solution)/shard_map/ppermute | solution.py:27
  43.0 14.3 %collective-permute-start.3 = (f32[16,512]{0,1:T(8,128)S(1)}, f32[16,512]{0,1:T(8,128)S(1)}, u32[]{:S(2)}, u32[]{:S(2)}) collective-permute-start(f32[16,512]{0,1:T(8,128)S(1)} %get-tuple-element.18), channel_id=1, source_target_pairs={{0,7},{1,0},{2,1},{3,2},{4,3},{5,4},{6,5},{7,6},{8,15},{9,8},{10,9... | collective-permute-start | bytes 98312 | tf_op jit(solution)/shard_map/ppermute | solution.py:27
  67.6 14.4 %collective-permute-start.4 = (f32[16,512]{0,1:T(8,128)S(1)}, f32[16,512]{0,1:T(8,128)S(1)}, u32[]{:S(2)}, u32[]{:S(2)}) collective-permute-start(f32[16,512]{0,1:T(8,128)S(1)} %get-tuple-element.15), channel_id=1, source_target_pairs={{0,1},{1,2},{2,3},{3,4},{4,5},{5,6},{6,7},{7,0},{8,9},{9,10},{10,1... | collective-permute-start | bytes 98312 | tf_op jit(solution)/shard_map/ppermute | solution.py:27
  67.7 14.3 %collective-permute-start.5 = (f32[16,512]{0,1:T(8,128)S(1)}, f32[16,512]{0,1:T(8,128)S(1)}, u32[]{:S(2)}, u32[]{:S(2)}) collective-permute-start(f32[16,512]{0,1:T(8,128)S(1)} %get-tuple-element.16), channel_id=1, source_target_pairs={{0,7},{1,0},{2,1},{3,2},{4,3},{5,4},{6,5},{7,6},{8,15},{9,8},{10,9... | collective-permute-start | bytes 98312 | tf_op jit(solution)/shard_map/ppermute | solution.py:27
  82.0 7.6 %copy-start.2 = (f32[1,64,1024]{2,1,0:T(8,128)S(1)}, f32[1,64,1024]{2,1,0:T(8,128)}, u32[]{:S(2)}) copy-start(f32[1,64,1024]{2,1,0:T(8,128)} %param.10) | copy-start | bytes 786436
  91.7 3.6 %collective-permute-start.6 = (f32[64,512]{0,1:T(8,128)S(1)}, f32[64,512]{0,1:T(8,128)S(1)}, u32[]{:S(2)}, u32[]{:S(2)}) collective-permute-start(f32[64,512]{0,1:T(8,128)S(1)} %slice_select_fusion), channel_id=1, source_target_pairs={{0,8},{8,0},{16,24},{24,16},{32,40},{40,32},{48,56},{56,48},{64,72... | collective-permute-start | bytes 393224 | tf_op jit(solution)/shard_map/ppermute | solution.py:262
  95.7 14.5 %collective-permute-start.7 = (f32[64,512]{0,1:T(8,128)S(1)}, f32[64,512]{0,1:T(8,128)S(1)}, u32[]{:S(2)}, u32[]{:S(2)}) collective-permute-start(f32[64,512]{0,1:T(8,128)S(1)} %fusion.1), channel_id=1, source_target_pairs={{0,16},{8,24},{16,32},{24,40},{32,48},{40,56},{48,64},{56,72},{64,... | collective-permute-start | bytes 393224 | tf_op jit(solution)/shard_map/ppermute | solution.py:22
  110.2 12.4 %collective-permute-start.8 = (f32[64,512]{0,1:T(8,128)S(1)}, f32[64,512]{0,1:T(8,128)S(1)}, u32[]{:S(2)}, u32[]{:S(2)}) collective-permute-start(f32[64,512]{0,1:T(8,128)S(1)} %collective-permute-done.7), channel_id=1, source_target_pairs={{0,16},{8,24},{16,32},{24,40},{32,48},{40,56},{48,64},{56,72},{64,... | collective-permute-start | bytes 393224 | tf_op jit(solution)/shard_map/ppermute | solution.py:22
  123.0 17.8 %collective-permute-start.9 = (f32[64,512]{0,1:T(8,128)S(1)}, f32[64,512]{0,1:T(8,128)S(1)}, u32[]{:S(2)}, u32[]{:S(2)}) collective-permute-start(f32[64,512]{0,1:T(8,128)S(1)} %convolution_add_fusion.4), channel_id=1, source_target_pairs={{0,32},{8,40},{16,48},{24,56},{32,64},{40,72},{48,80},{56,88},{64,... | collective-permute-start | bytes 393224 | tf_op jit(solution)/shard_map/ppermute | solution.py:22
  141.2 18.6 %collective-permute-start.10 = (f32[64,512]{0,1:T(8,128)S(1)}, f32[64,512]{0,1:T(8,128)S(1)}, u32[]{:S(2)}, u32[]{:S(2)}) collective-permute-start(f32[64,512]{0,1:T(8,128)S(1)} %convolution_add_fusion.3), channel_id=1, source_target_pairs={{0,64},{8,72},{16,80},{24,88},{32,96},{40,104},{48,112},{56,120},{... | collective-permute-start | bytes 393224 | tf_op jit(solution)/shard_map/ppermute | solution.py:22
  160.1 10.8 %collective-permute-start.11 = (f32[64,512]{0,1:T(8,128)S(1)}, f32[64,512]{0,1:T(8,128)S(1)}, u32[]{:S(2)}, u32[]{:S(2)}) collective-permute-start(f32[64,512]{0,1:T(8,128)S(1)} %convolution_add_fusion.2), channel_id=1, source_target_pairs={{0,128},{8,136},{16,144},{24,152},{32,160},{40,168},{48,176},{56,1... | collective-permute-start | bytes 393224 | tf_op jit(solution)/shard_map/ppermute | solution.py:22
  172.0 2.6 %collective-permute-start.12 = (f32[64,512]{0,1:T(8,128)S(1)}, f32[64,512]{0,1:T(8,128)S(1)}, u32[]{:S(2)}, u32[]{:S(2)}) collective-permute-start(f32[64,512]{0,1:T(8,128)S(1)} %get-tuple-element.14), channel_id=1, source_target_pairs={{0,8},{8,0},{16,24},{24,16},{32,40},{40,32},{48,56},{56,48},{64,72... | collective-permute-start | bytes 393224 | tf_op jit(solution)/shard_map/ppermute | solution.py:279

commit v9 on v7

--- a/solution.py
+++ b/solution.py
@@ -131,12 +131,13 @@
     lax.fori_loop(0, beside.shape[0] // UNROLL, gather, 0)
     state = state_ref[...]
     lifted = jnp.zeros_like(state)
+    lane_code = lax.broadcasted_iota(jnp.int32, state.shape, 1) // 16
     for face in range(6):
         parts = split_three(beside[face * elements:(face + 1) * elements, :])
         turned = (bf16_dot(parts[0], pick_ref[face]) + bf16_dot(parts[1], pick_ref[face])) + (
             bf16_dot(parts[2], pick_ref[face])
         )
-        chosen = jnp.where(mask_ref[face] > 0.5, turned, 0.0)
+        chosen = jnp.where(mask_ref[face] == lane_code, turned, 0.0)
         lifted = lifted + three_pass_dot(chosen, spread_ref[face])
     own = jnp.dot(
         state, folded_ref[...], precision=lax.Precision.HIGHEST,
@@ -185,13 +186,11 @@
     lift_t = lifting.T.reshape(6, 16, 64)
     spread = jnp.broadcast_to(lift_t[:, None], (6, 8, 16, 64)).reshape(6, LANES, 64)
     folded = stiffness.T - product(own, lifting.T)
-    lane_code = jnp.arange(LANES, dtype=jnp.int32) // 16
-    mask = orientation[:, :, None] == lane_code[None, None, :]
+    mask = orientation[:, :, None]
     nbr_rows = neighbor.reshape(-1)
     send_rows = jnp.concatenate([send_low, send_high])
     spread = jnp.pad(spread, ((0, 0), (0, 0), (0, LANES - 64)))
     folded = jnp.pad(folded, ((0, LANES - 64), (0, LANES - 64)))
-    mask = mask.astype(jnp.float32)
 
     state_start = start_state[0]
     state = jnp.pad(state_start.T, ((0, 0), (0, LANES - state_start.shape[0])))

time: 176 us -> 176 us (level)
  other arithmetic: 5.55 us -> 2.89 us
  local copies, waits for them, and re-layouts: 9.99 us -> 12.2 us
    convert_element_type x1 -> x0, other arithmetic: 2.66 us -> none  [shards(): mask = mask.astype(jnp.float32)]
    broadcast_in_dim x0 -> x1, local copies, waits for them, and re-layouts: none -> 2.21 us  [shards(): mask = orientation[:, :, None]]
where the time goes in v9:
time: 176 us; the launch traced here: 175 us
  waiting for transfers between devices  84.3 us (48%)
  Pallas kernels  52.2 us (30%)
  starting transfers between devices  17.5 us (10%)
  local copies, waits for them, and re-layouts  12.2 us (7%)
  matrix products  5.42 us (3%)
  other arithmetic  2.89 us (2%)
    ppermute x5, waiting for transfers between devices, from_behind(): return lax.ppermute(shard, axis, pairs)  62.9 us
    pallas_call x3, Pallas kernels, fused_step(): pl.pallas_call(functools.partial(fused_kernel, with_send), out_shape=tupl...  49 us
    ppermute x6, waiting for transfers between devices, ring(): lax.ppermute(shard, axis, [(i, (i + by) % peers) for i in range(peers)])  18.4 us
    ppermute x5, starting transfers between devices, from_behind(): return lax.ppermute(shard, axis, pairs)  10.9 us
    ppermute x6, starting transfers between devices, ring(): lax.ppermute(shard, axis, [(i, (i + by) % peers) for i in range(peers)])  6.49 us
    dot_general x13, matrix products, product(): jnp.dot(matrix, vector, precision=lax.Precision.HIGHEST, preferred_elemen...  5.42 us
  transfers between devices with their start and end apart: 13, of which 13 were waited for; matrix products, arithmetic and copies ran while one was open for 3% of the time, Pallas kernels for 0%

profile of v9, /device:TPU:22, one launch (start us, length us, event | category | flops | bytes accessed | tf_op | source)
XLA Modules:
  0.0 174.9 jit_solution(4745220186229363334)
XLA Ops:
  0.0 1.2 copy.24
  1.2 0.7 constant_dynamic-update-slice_fusion
  1.9 0.7 constant_dynamic-update-slice_fusion.1.idx_ref.send_ref
  2.6 0.8 pad.32.table_ref.state_ref
  3.4 3.3 %shard_map.100 = f32[1024,128]{1,0:T(8,128)} custom-call(s32[1024]{0:T(1024)} %copy-done.7, f32[1024,128]{1,0:T(8,128)} %pad.32.table_ref.state_ref), custom_call_target="tpu_custom_call" | custom-call | tf_op jit(solution)/shard_map/pallas_call | solution.py:85
  6.7 1.2 slice_bitcast_fusion.2
  7.9 1.3 collective-permute-start
  9.2 0.8 collective-permute-start.1
  10.4 2.2 %copy.27.mask_ref = s32[6,1024,1]{2,1,0:T(8,128)} copy(s32[6,1024,1]{1,0,2:T(8,128)S(1)} %bitcast.84) | data formatting | bytes 49152 | tf_op jit(solution)/shard_map/broadcast_in_dim | solution.py:189
  12.6 0.8 pad.35.spread_ref
  13.4 0.6 pad.36.folded_ref
  14.0 0.6 reshape.62.idx_ref
  14.7 1.3 collective-permute-done
  16.0 3.0 %collective-permute-done.1 = f32[16,512]{0,1:T(8,128)S(1)} collective-permute-done((f32[16,512]{0,1:T(8,128)S(1)}, f32[16,512]{0,1:T(8,128)S(1)}, u32[]{:S(2)}, u32[]{:S(2)}) %collective-permute-start.1) | collective-permute-done | bytes 32800 | tf_op jit(solution)/shard_map/ppermute | solution.py:27
  19.0 0.9 select_maximum_fusion.2.halo_ref
  20.0 16.8 %shard_map.101 = (f32[1024,128]{1,0:T(8,128)}, f32[1024,128]{1,0:T(8,128)}) custom-call(s32[6144]{0:T(1024)} %reshape.62.idx_ref, s32[1024]{0:T(1024)} %copy-done.7, f32[1024,128]{1,0:T(8,128)} %pad.32.table_ref.state_ref, f32[1024,128]{1,0:T(8,128)} %select_maximum_fusion.2.halo_ref, s32[6,1024,1]{2,1,0:T(8,128)} %copy.27.mask_ref, ...), custom_call_target="tpu_custom_call" | custom-call | flops 2617245696 | bytes 2908160 | tf_op jit(solution)/shard_map/pallas_call | solution.py:168
  36.8 1.2 slice_bitcast_fusion.6
  38.0 0.4 collective-permute-start.2
  38.3 1.7 collective-permute-start.3
  40.1 4.8 %collective-permute-done.2 = f32[16,512]{0,1:T(8,128)S(1)} collective-permute-done((f32[16,512]{0,1:T(8,128)S(1)}, f32[16,512]{0,1:T(8,128)S(1)}, u32[]{:S(2)}, u32[]{:S(2)}) %collective-permute-start.2) | collective-permute-done | bytes 32800 | tf_op jit(solution)/shard_map/ppermute | solution.py:27
  44.9 2.4 %collective-permute-done.3 = f32[16,512]{0,1:T(8,128)S(1)} collective-permute-done((f32[16,512]{0,1:T(8,128)S(1)}, f32[16,512]{0,1:T(8,128)S(1)}, u32[]{:S(2)}, u32[]{:S(2)}) %collective-permute-start.3) | collective-permute-done | bytes 32800 | tf_op jit(solution)/shard_map/ppermute | solution.py:27
  47.3 0.9 select_maximum_fusion.1.halo_ref
  48.3 16.8 %shard_map.102 = (f32[1024,128]{1,0:T(8,128)}, f32[1024,128]{1,0:T(8,128)}) custom-call(s32[6144]{0:T(1024)} %reshape.62.idx_ref, s32[1024]{0:T(1024)} %copy-done.7, f32[1024,128]{1,0:T(8,128)} %get-tuple-element.9.state_ref, f32[1024,128]{1,0:T(8,128)} %select_maximum_fusion.1.halo_ref, s32[6,1024,1]{2,1,0:T(8,128)} %copy.27.mask_ref, ...), custom_call_target="tpu_custom_call" | custom-call | flops 2617245696 | bytes 2908160 | tf_op jit(solution)/shard_map/pallas_call | solution.py:168
  65.1 1.2 slice_bitcast_fusion.4
  66.3 0.5 collective-permute-start.4
  66.8 1.7 collective-permute-start.5
  68.5 4.3 %collective-permute-done.4 = f32[16,512]{0,1:T(8,128)S(1)} collective-permute-done((f32[16,512]{0,1:T(8,128)S(1)}, f32[16,512]{0,1:T(8,128)S(1)}, u32[]{:S(2)}, u32[]{:S(2)}) %collective-permute-start.4) | collective-permute-done | bytes 32800 | tf_op jit(solution)/shard_map/ppermute | solution.py:27
  72.9 2.4 %collective-permute-done.5 = f32[16,512]{0,1:T(8,128)S(1)} collective-permute-done((f32[16,512]{0,1:T(8,128)S(1)}, f32[16,512]{0,1:T(8,128)S(1)}, u32[]{:S(2)}, u32[]{:S(2)}) %collective-permute-start.5) | collective-permute-done | bytes 32800 | tf_op jit(solution)/shard_map/ppermute | solution.py:27
  75.3 0.9 select_maximum_fusion.halo_ref
  76.2 15.3 %shard_map.103 = f32[1024,128]{1,0:T(8,128)} custom-call(s32[6144]{0:T(1024)} %reshape.62.idx_ref, s32[1024]{0:T(1024)} %copy-done.7, f32[1024,128]{1,0:T(8,128)} %get-tuple-element.11.state_ref, f32[1024,128]{1,0:T(8,128)} %select_maximum_fusion.halo_ref, s32[6,1024,1]{2,1,0:T(8,128)} %copy.27.mask_ref, bf16[6,128,128]{2,1,0:T(8,128)(2,1)} %constant.26.clone.pick_ref, ...), custom_call_target="tpu_custom_call" | custom-call | flops 2617245696 | bytes 2908160 | tf_op jit(solution)/shard_map/pallas_call | solution.py:168
  91.5 2.0 %add_select_fusion = f32[64,1024]{0,1:T(8,128)S(1)} fusion(f32[1024,128]{1,0:T(8,128)} %shard_map.103, f32[64,64]{1,0:T(8,128)S(1)} %copy-done, f32[1,64,1024]{2,1,0:T(8,128)S(1)} %copy-done.1, pred[]{:T(512)S(6)} %eq.7), kind=kOutput, calls=%fused_computation.10 | convolution fusion | flops 50528256 | bytes 802817 | tf_op jit(solution)/shard_map/dot_general | solution.py:31
  93.7 1.5 collective-permute-done.6
  95.2 0.4 fusion.1
  95.6 3.8 %collective-permute-start.7 = (f32[64,512]{0,1:T(8,128)S(1)}, f32[64,512]{0,1:T(8,128)S(1)}, u32[]{:S(2)}, u32[]{:S(2)}) collective-permute-start(f32[64,512]{0,1:T(8,128)S(1)} %fusion.1), channel_id=1, source_target_pairs={{0,16},{8,24},{16,32},{24,40},{32,48},{40,56},{48,64},{56,72},{64,... | collective-permute-start | bytes 393224 | tf_op jit(solution)/shard_map/ppermute | solution.py:22
  99.4 10.6 %collective-permute-done.7 = f32[64,512]{0,1:T(8,128)S(1)} collective-permute-done((f32[64,512]{0,1:T(8,128)S(1)}, f32[64,512]{0,1:T(8,128)S(1)}, u32[]{:S(2)}, u32[]{:S(2)}) %collective-permute-start.7) | collective-permute-done | bytes 131104 | tf_op jit(solution)/shard_map/ppermute | solution.py:22
  110.0 1.9 %collective-permute-start.8 = (f32[64,512]{0,1:T(8,128)S(1)}, f32[64,512]{0,1:T(8,128)S(1)}, u32[]{:S(2)}, u32[]{:S(2)}) collective-permute-start(f32[64,512]{0,1:T(8,128)S(1)} %collective-permute-done.7), channel_id=1, source_target_pairs={{0,16},{8,24},{16,32},{24,40},{32,48},{40,56},{48,64},{56,72},{64,... | collective-permute-start | bytes 393224 | tf_op jit(solution)/shard_map/ppermute | solution.py:22
  112.1 11.2 %collective-permute-done.8 = f32[64,512]{0,1:T(8,128)S(1)} collective-permute-done((f32[64,512]{0,1:T(8,128)S(1)}, f32[64,512]{0,1:T(8,128)S(1)}, u32[]{:S(2)}, u32[]{:S(2)}) %collective-permute-start.8) | collective-permute-done | bytes 131104 | tf_op jit(solution)/shard_map/ppermute | solution.py:22
  123.4 0.4 convolution_add_fusion.4
  123.7 1.9 %collective-permute-start.9 = (f32[64,512]{0,1:T(8,128)S(1)}, f32[64,512]{0,1:T(8,128)S(1)}, u32[]{:S(2)}, u32[]{:S(2)}) collective-permute-start(f32[64,512]{0,1:T(8,128)S(1)} %convolution_add_fusion.4), channel_id=1, source_target_pairs={{0,32},{8,40},{16,48},{24,56},{32,64},{40,72},{48,80},{56,88},{64,... | collective-permute-start | bytes 393224 | tf_op jit(solution)/shard_map/ppermute | solution.py:22
  125.8 14.4 %collective-permute-done.9 = f32[64,512]{0,1:T(8,128)S(1)} collective-permute-done((f32[64,512]{0,1:T(8,128)S(1)}, f32[64,512]{0,1:T(8,128)S(1)}, u32[]{:S(2)}, u32[]{:S(2)}) %collective-permute-start.9) | collective-permute-done | bytes 131104 | tf_op jit(solution)/shard_map/ppermute | solution.py:22
  140.6 1.9 %collective-permute-start.10 = (f32[64,512]{0,1:T(8,128)S(1)}, f32[64,512]{0,1:T(8,128)S(1)}, u32[]{:S(2)}, u32[]{:S(2)}) collective-permute-start(f32[64,512]{0,1:T(8,128)S(1)} %convolution_add_fusion.3), channel_id=1, source_target_pairs={{0,64},{8,72},{16,80},{24,88},{32,96},{40,104},{48,112},{56,120},{... | collective-permute-start | bytes 393224 | tf_op jit(solution)/shard_map/ppermute | solution.py:22
  142.7 16.5 %collective-permute-done.10 = f32[64,512]{0,1:T(8,128)S(1)} collective-permute-done((f32[64,512]{0,1:T(8,128)S(1)}, f32[64,512]{0,1:T(8,128)S(1)}, u32[]{:S(2)}, u32[]{:S(2)}) %collective-permute-start.10) | collective-permute-done | bytes 131104 | tf_op jit(solution)/shard_map/ppermute | solution.py:22
  159.5 1.3 collective-permute-start.11
  161.0 10.2 %collective-permute-done.11 = f32[64,512]{0,1:T(8,128)S(1)} collective-permute-done((f32[64,512]{0,1:T(8,128)S(1)}, f32[64,512]{0,1:T(8,128)S(1)}, u32[]{:S(2)}, u32[]{:S(2)}) %collective-permute-start.11) | collective-permute-done | bytes 131104 | tf_op jit(solution)/shard_map/ppermute | solution.py:22
  171.5 0.4 convolution_add_fusion
  171.9 0.4 select_bitcast_fusion
  172.4 1.5 collective-permute-done.12
  174.0 0.9 copy.39
  (32 shorter events, 2.4 us)
Async XLA Ops:
  0.0 91.5 %copy-start = (f32[64,64]{1,0:T(8,128)S(1)}, f32[64,64]{1,0:T(8,128)}, u32[]{:S(2)}) copy-start(f32[64,64]{1,0:T(8,128)} %param.13) | copy-start | bytes 49156
  0.0 10.1 %copy-start.6 = (f32[64,96]{1,0:T(8,128)S(1)}, f32[64,96]{1,0:T(8,128)}, u32[]{:S(2)}) copy-start(f32[64,96]{1,0:T(8,128)} %constant.27.clone) | copy-start | bytes 73732
  0.0 10.0 %copy-start.5 = (f32[64,64]{1,0:T(8,128)S(1)}, f32[64,64]{1,0:T(8,128)}, u32[]{:S(2)}) copy-start(f32[64,64]{1,0:T(8,128)} %param.11) | copy-start | bytes 49156
  0.0 10.1 %copy-start.2 = (f32[64,96]{1,0:T(8,128)S(1)}, f32[64,96]{1,0:T(8,128)}, u32[]{:S(2)}) copy-start(f32[64,96]{1,0:T(8,128)} %param.12) | copy-start | bytes 73732
  0.0 10.3 %copy-start.3 = (s32[6,1024]{1,0:T(8,128)S(1)}, s32[6,1024]{1,0:T(8,128)}, u32[]{:S(2)}) copy-start(s32[6,1024]{1,0:T(8,128)} %param.15) | copy-start | bytes 73732
  2.6 0.8 copy-start.7
  6.7 7.3 %copy-start.4 = (s32[6,1024]{1,0:T(8,128)S(1)}, s32[6,1024]{1,0:T(8,128)}, u32[]{:S(2)}) copy-start(s32[6,1024]{1,0:T(8,128)} %param.14) | copy-start | bytes 73732
  7.9 8.1 %collective-permute-start = (f32[16,512]{0,1:T(8,128)S(1)}, f32[16,512]{0,1:T(8,128)S(1)}, u32[]{:S(2)}, u32[]{:S(2)}) collective-permute-start(f32[16,512]{0,1:T(8,128)S(1)} %get-tuple-element.19), channel_id=1, source_target_pairs={{0,1},{1,2},{2,3},{3,4},{4,5},{5,6},{6,7},{7,0},{8,9},{9,10},{10,1... | collective-permute-start | bytes 98312 | tf_op jit(solution)/shard_map/ppermute | solution.py:27
  9.2 9.9 %collective-permute-start.1 = (f32[16,512]{0,1:T(8,128)S(1)}, f32[16,512]{0,1:T(8,128)S(1)}, u32[]{:S(2)}, u32[]{:S(2)}) collective-permute-start(f32[16,512]{0,1:T(8,128)S(1)} %get-tuple-element.20), channel_id=1, source_target_pairs={{0,7},{1,0},{2,1},{3,2},{4,3},{5,4},{6,5},{7,6},{8,15},{9,8},{10,9... | collective-permute-start | bytes 98312 | tf_op jit(solution)/shard_map/ppermute | solution.py:27
  38.0 6.9 %collective-permute-start.2 = (f32[16,512]{0,1:T(8,128)S(1)}, f32[16,512]{0,1:T(8,128)S(1)}, u32[]{:S(2)}, u32[]{:S(2)}) collective-permute-start(f32[16,512]{0,1:T(8,128)S(1)} %get-tuple-element.17), channel_id=1, source_target_pairs={{0,1},{1,2},{2,3},{3,4},{4,5},{5,6},{6,7},{7,0},{8,9},{9,10},{10,1... | collective-permute-start | bytes 98312 | tf_op jit(solution)/shard_map/ppermute | solution.py:27
  38.3 9.0 %collective-permute-start.3 = (f32[16,512]{0,1:T(8,128)S(1)}, f32[16,512]{0,1:T(8,128)S(1)}, u32[]{:S(2)}, u32[]{:S(2)}) collective-permute-start(f32[16,512]{0,1:T(8,128)S(1)} %get-tuple-element.18), channel_id=1, source_target_pairs={{0,7},{1,0},{2,1},{3,2},{4,3},{5,4},{6,5},{7,6},{8,15},{9,8},{10,9... | collective-permute-start | bytes 98312 | tf_op jit(solution)/shard_map/ppermute | solution.py:27
  66.3 6.6 %collective-permute-start.4 = (f32[16,512]{0,1:T(8,128)S(1)}, f32[16,512]{0,1:T(8,128)S(1)}, u32[]{:S(2)}, u32[]{:S(2)}) collective-permute-start(f32[16,512]{0,1:T(8,128)S(1)} %get-tuple-element.15), channel_id=1, source_target_pairs={{0,1},{1,2},{2,3},{3,4},{4,5},{5,6},{6,7},{7,0},{8,9},{9,10},{10,1... | collective-permute-start | bytes 98312 | tf_op jit(solution)/shard_map/ppermute | solution.py:27
  66.8 8.5 %collective-permute-start.5 = (f32[16,512]{0,1:T(8,128)S(1)}, f32[16,512]{0,1:T(8,128)S(1)}, u32[]{:S(2)}, u32[]{:S(2)}) collective-permute-start(f32[16,512]{0,1:T(8,128)S(1)} %get-tuple-element.16), channel_id=1, source_target_pairs={{0,7},{1,0},{2,1},{3,2},{4,3},{5,4},{6,5},{7,6},{8,15},{9,8},{10,9... | collective-permute-start | bytes 98312 | tf_op jit(solution)/shard_map/ppermute | solution.py:27
  76.2 15.3 %copy-start.1 = (f32[1,64,1024]{2,1,0:T(8,128)S(1)}, f32[1,64,1024]{2,1,0:T(8,128)}, u32[]{:S(2)}) copy-start(f32[1,64,1024]{2,1,0:T(8,128)} %param.10) | copy-start | bytes 786436
  93.6 1.6 collective-permute-start.6
  95.6 14.4 %collective-permute-start.7 = (f32[64,512]{0,1:T(8,128)S(1)}, f32[64,512]{0,1:T(8,128)S(1)}, u32[]{:S(2)}, u32[]{:S(2)}) collective-permute-start(f32[64,512]{0,1:T(8,128)S(1)} %fusion.1), channel_id=1, source_target_pairs={{0,16},{8,24},{16,32},{24,40},{32,48},{40,56},{48,64},{56,72},{64,... | collective-permute-start | bytes 393224 | tf_op jit(solution)/shard_map/ppermute | solution.py:22
  110.0 13.3 %collective-permute-start.8 = (f32[64,512]{0,1:T(8,128)S(1)}, f32[64,512]{0,1:T(8,128)S(1)}, u32[]{:S(2)}, u32[]{:S(2)}) collective-permute-start(f32[64,512]{0,1:T(8,128)S(1)} %collective-permute-done.7), channel_id=1, source_target_pairs={{0,16},{8,24},{16,32},{24,40},{32,48},{40,56},{48,64},{56,72},{64,... | collective-permute-start | bytes 393224 | tf_op jit(solution)/shard_map/ppermute | solution.py:22
  123.7 16.5 %collective-permute-start.9 = (f32[64,512]{0,1:T(8,128)S(1)}, f32[64,512]{0,1:T(8,128)S(1)}, u32[]{:S(2)}, u32[]{:S(2)}) collective-permute-start(f32[64,512]{0,1:T(8,128)S(1)} %convolution_add_fusion.4), channel_id=1, source_target_pairs={{0,32},{8,40},{16,48},{24,56},{32,64},{40,72},{48,80},{56,88},{64,... | collective-permute-start | bytes 393224 | tf_op jit(solution)/shard_map/ppermute | solution.py:22
  140.6 18.6 %collective-permute-start.10 = (f32[64,512]{0,1:T(8,128)S(1)}, f32[64,512]{0,1:T(8,128)S(1)}, u32[]{:S(2)}, u32[]{:S(2)}) collective-permute-start(f32[64,512]{0,1:T(8,128)S(1)} %convolution_add_fusion.3), channel_id=1, source_target_pairs={{0,64},{8,72},{16,80},{24,88},{32,96},{40,104},{48,112},{56,120},{... | collective-permute-start | bytes 393224 | tf_op jit(solution)/shard_map/ppermute | solution.py:22
  159.5 11.6 %collective-permute-start.11 = (f32[64,512]{0,1:T(8,128)S(1)}, f32[64,512]{0,1:T(8,128)S(1)}, u32[]{:S(2)}, u32[]{:S(2)}) collective-permute-start(f32[64,512]{0,1:T(8,128)S(1)} %convolution_add_fusion.2), channel_id=1, source_target_pairs={{0,128},{8,136},{16,144},{24,152},{32,160},{40,168},{48,176},{56,1... | collective-permute-start | bytes 393224 | tf_op jit(solution)/shard_map/ppermute | solution.py:22
  172.3 1.6 collective-permute-start.12

commit v10 on v9

--- a/solution.py
+++ b/solution.py
@@ -10,7 +10,7 @@
 
 STEPS = 3
 LANES = 128
-UNROLL = 8
+UNROLL = 64
 
 
 time_step = 0.05

time: 176 us -> 165 us (0.938)
  Pallas kernels: 52.2 us -> 42.1 us
    pallas_call x3, Pallas kernels: 49 us -> 39.4 us  [fused_step(): pl.pallas_call(functools.partial(fused_kernel, with_send), out_shape=tupl...]
where the time goes in v10:
time: 165 us
  waiting for transfers between devices  84.3 us (51%)
  Pallas kernels  42.1 us (26%)
  starting transfers between devices  17.5 us (11%)
  local copies, waits for them, and re-layouts  12.2 us (7%)
  matrix products  5.43 us (3%)
  other arithmetic  2.89 us (2%)
    ppermute x5, waiting for transfers between devices, from_behind(): return lax.ppermute(shard, axis, pairs)  62.9 us
    pallas_call x3, Pallas kernels, fused_step(): pl.pallas_call(functools.partial(fused_kernel, with_send), out_shape=tupl...  39.4 us
    ppermute x6, waiting for transfers between devices, ring(): lax.ppermute(shard, axis, [(i, (i + by) % peers) for i in range(peers)])  18.4 us
    ppermute x5, starting transfers between devices, from_behind(): return lax.ppermute(shard, axis, pairs)  10.9 us
    ppermute x6, starting transfers between devices, ring(): lax.ppermute(shard, axis, [(i, (i + by) % peers) for i in range(peers)])  6.49 us
    dot_general x13, matrix products, product(): jnp.dot(matrix, vector, precision=lax.Precision.HIGHEST, preferred_elemen...  5.43 us
    transpose x3, local copies, waits for them, and re-layouts, shards(): before = ring(sent[half:, 48:64].T, 'space', 1)  3.46 us
  transfers between devices with their start and end apart: 13, of which 13 were waited for; matrix products, arithmetic and copies ran while one was open for 3% of the time, Pallas kernels for 0%

profile of v10, /device:TPU:22, one launch (start us, length us, event | category | flops | bytes accessed | tf_op | source)
XLA Modules:
  0.0 164.8 jit_solution(13867750565964279332)
XLA Ops:
  0.0 1.2 copy.24
  1.2 0.7 constant_dynamic-update-slice_fusion
  1.9 0.7 constant_dynamic-update-slice_fusion.1.idx_ref.send_ref
  2.6 0.8 pad.32.table_ref.state_ref
  3.4 2.7 %shard_map.100 = f32[1024,128]{1,0:T(8,128)} custom-call(s32[1024]{0:T(1024)} %copy-done.7, f32[1024,128]{1,0:T(8,128)} %pad.32.table_ref.state_ref), custom_call_target="tpu_custom_call" | custom-call | tf_op jit(solution)/shard_map/pallas_call | solution.py:85
  6.2 1.2 slice_bitcast_fusion.2
  7.3 1.3 collective-permute-start
  8.6 0.8 collective-permute-start.1
  9.8 2.2 %copy.27.mask_ref = s32[6,1024,1]{2,1,0:T(8,128)} copy(s32[6,1024,1]{1,0,2:T(8,128)S(1)} %bitcast.84) | data formatting | bytes 49152 | tf_op jit(solution)/shard_map/broadcast_in_dim | solution.py:189
  12.1 0.8 pad.35.spread_ref
  12.9 0.6 pad.36.folded_ref
  13.5 0.6 reshape.62.idx_ref
  14.1 1.3 collective-permute-done
  15.5 3.0 %collective-permute-done.1 = f32[16,512]{0,1:T(8,128)S(1)} collective-permute-done((f32[16,512]{0,1:T(8,128)S(1)}, f32[16,512]{0,1:T(8,128)S(1)}, u32[]{:S(2)}, u32[]{:S(2)}) %collective-permute-start.1) | collective-permute-done | bytes 32800 | tf_op jit(solution)/shard_map/ppermute | solution.py:27
  18.5 0.9 select_maximum_fusion.2.halo_ref
  19.4 13.5 %shard_map.101 = (f32[1024,128]{1,0:T(8,128)}, f32[1024,128]{1,0:T(8,128)}) custom-call(s32[6144]{0:T(1024)} %reshape.62.idx_ref, s32[1024]{0:T(1024)} %copy-done.7, f32[1024,128]{1,0:T(8,128)} %pad.32.table_ref.state_ref, f32[1024,128]{1,0:T(8,128)} %select_maximum_fusion.2.halo_ref, s32[6,1024,1]{2,1,0:T(8,128)} %copy.27.mask_ref, ...), custom_call_target="tpu_custom_call" | custom-call | flops 2617245696 | bytes 2908160 | tf_op jit(solution)/shard_map/pallas_call | solution.py:168
  32.9 1.2 slice_bitcast_fusion.6
  34.4 1.7 %collective-permute-start.3 = (f32[16,512]{0,1:T(8,128)S(1)}, f32[16,512]{0,1:T(8,128)S(1)}, u32[]{:S(2)}, u32[]{:S(2)}) collective-permute-start(f32[16,512]{0,1:T(8,128)S(1)} %get-tuple-element.18), channel_id=1, source_target_pairs={{0,7},{1,0},{2,1},{3,2},{4,3},{5,4},{6,5},{7,6},{8,15},{9,8},{10,9... | collective-permute-start | bytes 98312 | tf_op jit(solution)/shard_map/ppermute | solution.py:27
  36.2 4.8 %collective-permute-done.2 = f32[16,512]{0,1:T(8,128)S(1)} collective-permute-done((f32[16,512]{0,1:T(8,128)S(1)}, f32[16,512]{0,1:T(8,128)S(1)}, u32[]{:S(2)}, u32[]{:S(2)}) %collective-permute-start.2) | collective-permute-done | bytes 32800 | tf_op jit(solution)/shard_map/ppermute | solution.py:27
  41.0 2.4 %collective-permute-done.3 = f32[16,512]{0,1:T(8,128)S(1)} collective-permute-done((f32[16,512]{0,1:T(8,128)S(1)}, f32[16,512]{0,1:T(8,128)S(1)}, u32[]{:S(2)}, u32[]{:S(2)}) %collective-permute-start.3) | collective-permute-done | bytes 32800 | tf_op jit(solution)/shard_map/ppermute | solution.py:27
  43.4 0.9 select_maximum_fusion.1.halo_ref
  44.4 13.5 %shard_map.102 = (f32[1024,128]{1,0:T(8,128)}, f32[1024,128]{1,0:T(8,128)}) custom-call(s32[6144]{0:T(1024)} %reshape.62.idx_ref, s32[1024]{0:T(1024)} %copy-done.7, f32[1024,128]{1,0:T(8,128)} %get-tuple-element.9.state_ref, f32[1024,128]{1,0:T(8,128)} %select_maximum_fusion.1.halo_ref, s32[6,1024,1]{2,1,0:T(8,128)} %copy.27.mask_ref, ...), custom_call_target="tpu_custom_call" | custom-call | flops 2617245696 | bytes 2908160 | tf_op jit(solution)/shard_map/pallas_call | solution.py:168
  57.8 1.2 slice_bitcast_fusion.4
  59.0 0.5 collective-permute-start.4
  59.5 1.7 %collective-permute-start.5 = (f32[16,512]{0,1:T(8,128)S(1)}, f32[16,512]{0,1:T(8,128)S(1)}, u32[]{:S(2)}, u32[]{:S(2)}) collective-permute-start(f32[16,512]{0,1:T(8,128)S(1)} %get-tuple-element.16), channel_id=1, source_target_pairs={{0,7},{1,0},{2,1},{3,2},{4,3},{5,4},{6,5},{7,6},{8,15},{9,8},{10,9... | collective-permute-start | bytes 98312 | tf_op jit(solution)/shard_map/ppermute | solution.py:27
  61.3 4.3 %collective-permute-done.4 = f32[16,512]{0,1:T(8,128)S(1)} collective-permute-done((f32[16,512]{0,1:T(8,128)S(1)}, f32[16,512]{0,1:T(8,128)S(1)}, u32[]{:S(2)}, u32[]{:S(2)}) %collective-permute-start.4) | collective-permute-done | bytes 32800 | tf_op jit(solution)/shard_map/ppermute | solution.py:27
  65.6 2.4 %collective-permute-done.5 = f32[16,512]{0,1:T(8,128)S(1)} collective-permute-done((f32[16,512]{0,1:T(8,128)S(1)}, f32[16,512]{0,1:T(8,128)S(1)}, u32[]{:S(2)}, u32[]{:S(2)}) %collective-permute-start.5) | collective-permute-done | bytes 32800 | tf_op jit(solution)/shard_map/ppermute | solution.py:27
  68.0 0.9 select_maximum_fusion.halo_ref
  68.9 12.5 %shard_map.103 = f32[1024,128]{1,0:T(8,128)} custom-call(s32[6144]{0:T(1024)} %reshape.62.idx_ref, s32[1024]{0:T(1024)} %copy-done.7, f32[1024,128]{1,0:T(8,128)} %get-tuple-element.11.state_ref, f32[1024,128]{1,0:T(8,128)} %select_maximum_fusion.halo_ref, s32[6,1024,1]{2,1,0:T(8,128)} %copy.27.mask_ref, bf16[6,128,128]{2,1,0:T(8,128)(2,1)} %constant.26.clone.pick_ref, ...), custom_call_target="tpu_custom_call" | custom-call | flops 2617245696 | bytes 2908160 | tf_op jit(solution)/shard_map/pallas_call | solution.py:168
  81.4 2.0 %add_select_fusion = f32[64,1024]{0,1:T(8,128)S(1)} fusion(f32[1024,128]{1,0:T(8,128)} %shard_map.103, f32[64,64]{1,0:T(8,128)S(1)} %copy-done, f32[1,64,1024]{2,1,0:T(8,128)S(1)} %copy-done.1, pred[]{:T(512)S(6)} %eq.7), kind=kOutput, calls=%fused_computation.10 | convolution fusion | flops 50528256 | bytes 802817 | tf_op jit(solution)/shard_map/dot_general | solution.py:31
  83.6 1.5 collective-permute-done.6
  85.1 0.4 fusion.1
  85.5 3.8 %collective-permute-start.7 = (f32[64,512]{0,1:T(8,128)S(1)}, f32[64,512]{0,1:T(8,128)S(1)}, u32[]{:S(2)}, u32[]{:S(2)}) collective-permute-start(f32[64,512]{0,1:T(8,128)S(1)} %fusion.1), channel_id=1, source_target_pairs={{0,16},{8,24},{16,32},{24,40},{32,48},{40,56},{48,64},{56,72},{64,... | collective-permute-start | bytes 393224 | tf_op jit(solution)/shard_map/ppermute | solution.py:22
  89.3 10.6 %collective-permute-done.7 = f32[64,512]{0,1:T(8,128)S(1)} collective-permute-done((f32[64,512]{0,1:T(8,128)S(1)}, f32[64,512]{0,1:T(8,128)S(1)}, u32[]{:S(2)}, u32[]{:S(2)}) %collective-permute-start.7) | collective-permute-done | bytes 131104 | tf_op jit(solution)/shard_map/ppermute | solution.py:22
  99.9 1.9 %collective-permute-start.8 = (f32[64,512]{0,1:T(8,128)S(1)}, f32[64,512]{0,1:T(8,128)S(1)}, u32[]{:S(2)}, u32[]{:S(2)}) collective-permute-start(f32[64,512]{0,1:T(8,128)S(1)} %collective-permute-done.7), channel_id=1, source_target_pairs={{0,16},{8,24},{16,32},{24,40},{32,48},{40,56},{48,64},{56,72},{64,... | collective-permute-start | bytes 393224 | tf_op jit(solution)/shard_map/ppermute | solution.py:22
  102.0 11.2 %collective-permute-done.8 = f32[64,512]{0,1:T(8,128)S(1)} collective-permute-done((f32[64,512]{0,1:T(8,128)S(1)}, f32[64,512]{0,1:T(8,128)S(1)}, u32[]{:S(2)}, u32[]{:S(2)}) %collective-permute-start.8) | collective-permute-done | bytes 131104 | tf_op jit(solution)/shard_map/ppermute | solution.py:22
  113.6 1.9 %collective-permute-start.9 = (f32[64,512]{0,1:T(8,128)S(1)}, f32[64,512]{0,1:T(8,128)S(1)}, u32[]{:S(2)}, u32[]{:S(2)}) collective-permute-start(f32[64,512]{0,1:T(8,128)S(1)} %convolution_add_fusion.4), channel_id=1, source_target_pairs={{0,32},{8,40},{16,48},{24,56},{32,64},{40,72},{48,80},{56,88},{64,... | collective-permute-start | bytes 393224 | tf_op jit(solution)/shard_map/ppermute | solution.py:22
  115.7 14.4 %collective-permute-done.9 = f32[64,512]{0,1:T(8,128)S(1)} collective-permute-done((f32[64,512]{0,1:T(8,128)S(1)}, f32[64,512]{0,1:T(8,128)S(1)}, u32[]{:S(2)}, u32[]{:S(2)}) %collective-permute-start.9) | collective-permute-done | bytes 131104 | tf_op jit(solution)/shard_map/ppermute | solution.py:22
  130.2 0.4 convolution_add_fusion.3
  130.5 1.9 %collective-permute-start.10 = (f32[64,512]{0,1:T(8,128)S(1)}, f32[64,512]{0,1:T(8,128)S(1)}, u32[]{:S(2)}, u32[]{:S(2)}) collective-permute-start(f32[64,512]{0,1:T(8,128)S(1)} %convolution_add_fusion.3), channel_id=1, source_target_pairs={{0,64},{8,72},{16,80},{24,88},{32,96},{40,104},{48,112},{56,120},{... | collective-permute-start | bytes 393224 | tf_op jit(solution)/shard_map/ppermute | solution.py:22
  132.6 16.5 %collective-permute-done.10 = f32[64,512]{0,1:T(8,128)S(1)} collective-permute-done((f32[64,512]{0,1:T(8,128)S(1)}, f32[64,512]{0,1:T(8,128)S(1)}, u32[]{:S(2)}, u32[]{:S(2)}) %collective-permute-start.10) | collective-permute-done | bytes 131104 | tf_op jit(solution)/shard_map/ppermute | solution.py:22
  149.5 1.3 collective-permute-start.11
  150.9 10.2 %collective-permute-done.11 = f32[64,512]{0,1:T(8,128)S(1)} collective-permute-done((f32[64,512]{0,1:T(8,128)S(1)}, f32[64,512]{0,1:T(8,128)S(1)}, u32[]{:S(2)}, u32[]{:S(2)}) %collective-permute-start.11) | collective-permute-done | bytes 131104 | tf_op jit(solution)/shard_map/ppermute | solution.py:22
  161.1 0.4 convolution_add_fusion.1
  161.5 0.4 convolution_add_fusion
  161.8 0.4 select_bitcast_fusion
  162.3 1.5 collective-permute-done.12
  163.9 0.9 copy.39
  (32 shorter events, 2.4 us)
Async XLA Ops:
  0.0 81.4 %copy-start = (f32[64,64]{1,0:T(8,128)S(1)}, f32[64,64]{1,0:T(8,128)}, u32[]{:S(2)}) copy-start(f32[64,64]{1,0:T(8,128)} %param.13) | copy-start | bytes 49156
  0.0 9.5 %copy-start.6 = (f32[64,96]{1,0:T(8,128)S(1)}, f32[64,96]{1,0:T(8,128)}, u32[]{:S(2)}) copy-start(f32[64,96]{1,0:T(8,128)} %constant.27.clone) | copy-start | bytes 73732
  0.0 9.4 %copy-start.5 = (f32[64,64]{1,0:T(8,128)S(1)}, f32[64,64]{1,0:T(8,128)}, u32[]{:S(2)}) copy-start(f32[64,64]{1,0:T(8,128)} %param.11) | copy-start | bytes 49156
  0.0 9.5 %copy-start.2 = (f32[64,96]{1,0:T(8,128)S(1)}, f32[64,96]{1,0:T(8,128)}, u32[]{:S(2)}) copy-start(f32[64,96]{1,0:T(8,128)} %param.12) | copy-start | bytes 73732
  0.0 9.8 %copy-start.3 = (s32[6,1024]{1,0:T(8,128)S(1)}, s32[6,1024]{1,0:T(8,128)}, u32[]{:S(2)}) copy-start(s32[6,1024]{1,0:T(8,128)} %param.15) | copy-start | bytes 73732
  2.6 0.8 copy-start.7
  6.2 7.3 %copy-start.4 = (s32[6,1024]{1,0:T(8,128)S(1)}, s32[6,1024]{1,0:T(8,128)}, u32[]{:S(2)}) copy-start(s32[6,1024]{1,0:T(8,128)} %param.14) | copy-start | bytes 73732
  7.3 8.1 %collective-permute-start = (f32[16,512]{0,1:T(8,128)S(1)}, f32[16,512]{0,1:T(8,128)S(1)}, u32[]{:S(2)}, u32[]{:S(2)}) collective-permute-start(f32[16,512]{0,1:T(8,128)S(1)} %get-tuple-element.19), channel_id=1, source_target_pairs={{0,1},{1,2},{2,3},{3,4},{4,5},{5,6},{6,7},{7,0},{8,9},{9,10},{10,1... | collective-permute-start | bytes 98312 | tf_op jit(solution)/shard_map/ppermute | solution.py:27
  8.6 9.9 %collective-permute-start.1 = (f32[16,512]{0,1:T(8,128)S(1)}, f32[16,512]{0,1:T(8,128)S(1)}, u32[]{:S(2)}, u32[]{:S(2)}) collective-permute-start(f32[16,512]{0,1:T(8,128)S(1)} %get-tuple-element.20), channel_id=1, source_target_pairs={{0,7},{1,0},{2,1},{3,2},{4,3},{5,4},{6,5},{7,6},{8,15},{9,8},{10,9... | collective-permute-start | bytes 98312 | tf_op jit(solution)/shard_map/ppermute | solution.py:27
  34.1 6.9 %collective-permute-start.2 = (f32[16,512]{0,1:T(8,128)S(1)}, f32[16,512]{0,1:T(8,128)S(1)}, u32[]{:S(2)}, u32[]{:S(2)}) collective-permute-start(f32[16,512]{0,1:T(8,128)S(1)} %get-tuple-element.17), channel_id=1, source_target_pairs={{0,1},{1,2},{2,3},{3,4},{4,5},{5,6},{6,7},{7,0},{8,9},{9,10},{10,1... | collective-permute-start | bytes 98312 | tf_op jit(solution)/shard_map/ppermute | solution.py:27
  34.4 9.0 %collective-permute-start.3 = (f32[16,512]{0,1:T(8,128)S(1)}, f32[16,512]{0,1:T(8,128)S(1)}, u32[]{:S(2)}, u32[]{:S(2)}) collective-permute-start(f32[16,512]{0,1:T(8,128)S(1)} %get-tuple-element.18), channel_id=1, source_target_pairs={{0,7},{1,0},{2,1},{3,2},{4,3},{5,4},{6,5},{7,6},{8,15},{9,8},{10,9... | collective-permute-start | bytes 98312 | tf_op jit(solution)/shard_map/ppermute | solution.py:27
  59.0 6.6 %collective-permute-start.4 = (f32[16,512]{0,1:T(8,128)S(1)}, f32[16,512]{0,1:T(8,128)S(1)}, u32[]{:S(2)}, u32[]{:S(2)}) collective-permute-start(f32[16,512]{0,1:T(8,128)S(1)} %get-tuple-element.15), channel_id=1, source_target_pairs={{0,1},{1,2},{2,3},{3,4},{4,5},{5,6},{6,7},{7,0},{8,9},{9,10},{10,1... | collective-permute-start | bytes 98312 | tf_op jit(solution)/shard_map/ppermute | solution.py:27
  59.5 8.5 %collective-permute-start.5 = (f32[16,512]{0,1:T(8,128)S(1)}, f32[16,512]{0,1:T(8,128)S(1)}, u32[]{:S(2)}, u32[]{:S(2)}) collective-permute-start(f32[16,512]{0,1:T(8,128)S(1)} %get-tuple-element.16), channel_id=1, source_target_pairs={{0,7},{1,0},{2,1},{3,2},{4,3},{5,4},{6,5},{7,6},{8,15},{9,8},{10,9... | collective-permute-start | bytes 98312 | tf_op jit(solution)/shard_map/ppermute | solution.py:27
  68.9 12.5 %copy-start.1 = (f32[1,64,1024]{2,1,0:T(8,128)S(1)}, f32[1,64,1024]{2,1,0:T(8,128)}, u32[]{:S(2)}) copy-start(f32[1,64,1024]{2,1,0:T(8,128)} %param.10) | copy-start | bytes 786436
  83.5 1.6 collective-permute-start.6
  85.5 14.4 %collective-permute-start.7 = (f32[64,512]{0,1:T(8,128)S(1)}, f32[64,512]{0,1:T(8,128)S(1)}, u32[]{:S(2)}, u32[]{:S(2)}) collective-permute-start(f32[64,512]{0,1:T(8,128)S(1)} %fusion.1), channel_id=1, source_target_pairs={{0,16},{8,24},{16,32},{24,40},{32,48},{40,56},{48,64},{56,72},{64,... | collective-permute-start | bytes 393224 | tf_op jit(solution)/shard_map/ppermute | solution.py:22
  99.9 13.3 %collective-permute-start.8 = (f32[64,512]{0,1:T(8,128)S(1)}, f32[64,512]{0,1:T(8,128)S(1)}, u32[]{:S(2)}, u32[]{:S(2)}) collective-permute-start(f32[64,512]{0,1:T(8,128)S(1)} %collective-permute-done.7), channel_id=1, source_target_pairs={{0,16},{8,24},{16,32},{24,40},{32,48},{40,56},{48,64},{56,72},{64,... | collective-permute-start | bytes 393224 | tf_op jit(solution)/shard_map/ppermute | solution.py:22
  113.6 16.5 %collective-permute-start.9 = (f32[64,512]{0,1:T(8,128)S(1)}, f32[64,512]{0,1:T(8,128)S(1)}, u32[]{:S(2)}, u32[]{:S(2)}) collective-permute-start(f32[64,512]{0,1:T(8,128)S(1)} %convolution_add_fusion.4), channel_id=1, source_target_pairs={{0,32},{8,40},{16,48},{24,56},{32,64},{40,72},{48,80},{56,88},{64,... | collective-permute-start | bytes 393224 | tf_op jit(solution)/shard_map/ppermute | solution.py:22
  130.5 18.6 %collective-permute-start.10 = (f32[64,512]{0,1:T(8,128)S(1)}, f32[64,512]{0,1:T(8,128)S(1)}, u32[]{:S(2)}, u32[]{:S(2)}) collective-permute-start(f32[64,512]{0,1:T(8,128)S(1)} %convolution_add_fusion.3), channel_id=1, source_target_pairs={{0,64},{8,72},{16,80},{24,88},{32,96},{40,104},{48,112},{56,120},{... | collective-permute-start | bytes 393224 | tf_op jit(solution)/shard_map/ppermute | solution.py:22
  149.5 11.6 %collective-permute-start.11 = (f32[64,512]{0,1:T(8,128)S(1)}, f32[64,512]{0,1:T(8,128)S(1)}, u32[]{:S(2)}, u32[]{:S(2)}) collective-permute-start(f32[64,512]{0,1:T(8,128)S(1)} %convolution_add_fusion.2), channel_id=1, source_target_pairs={{0,128},{8,136},{16,144},{24,152},{32,160},{40,168},{48,176},{56,1... | collective-permute-start | bytes 393224 | tf_op jit(solution)/shard_map/ppermute | solution.py:22
  162.2 1.6 collective-permute-start.12

commit v11 on v10

--- a/solution.py
+++ b/solution.py
@@ -139,10 +139,7 @@
         )
         chosen = jnp.where(mask_ref[face] == lane_code, turned, 0.0)
         lifted = lifted + three_pass_dot(chosen, spread_ref[face])
-    own = jnp.dot(
-        state, folded_ref[...], precision=lax.Precision.HIGHEST,
-        preferred_element_type=jnp.float32,
-    )
+    own = three_pass_dot(state, folded_ref[...])
     rate = own + lifted + state - state * state * state
     out_ref[...] = state + time_step * rate
     if with_send:

time: 165 us -> 164 us (level)
  no operation moved by 1% of the time
where the time goes in v11:
time: 164 us
  waiting for transfers between devices  84.3 us (51%)
  Pallas kernels  41.1 us (25%)
  starting transfers between devices  17.4 us (11%)
  local copies, waits for them, and re-layouts  12.2 us (7%)
  matrix products  5.42 us (3%)
  other arithmetic  2.89 us (2%)
    ppermute x5, waiting for transfers between devices, from_behind(): return lax.ppermute(shard, axis, pairs)  62.9 us
    pallas_call x3, Pallas kernels, fused_step(): pl.pallas_call(functools.partial(fused_kernel, with_send), out_shape=tupl...  38.4 us
    ppermute x6, waiting for transfers between devices, ring(): lax.ppermute(shard, axis, [(i, (i + by) % peers) for i in range(peers)])  18.4 us
    ppermute x5, starting transfers between devices, from_behind(): return lax.ppermute(shard, axis, pairs)  10.9 us
    ppermute x6, starting transfers between devices, ring(): lax.ppermute(shard, axis, [(i, (i + by) % peers) for i in range(peers)])  6.31 us
    dot_general x13, matrix products, product(): jnp.dot(matrix, vector, precision=lax.Precision.HIGHEST, preferred_elemen...  5.42 us
    transpose x3, local copies, waits for them, and re-layouts, shards(): before = ring(sent[half:, 48:64].T, 'space', 1)  3.46 us
  transfers between devices with their start and end apart: 13, of which 13 were waited for; matrix products, arithmetic and copies ran while one was open for 3% of the time, Pallas kernels for 0%

profile of v11, /device:TPU:22, one launch (start us, length us, event | category | flops | bytes accessed | tf_op | source)
XLA Modules:
  0.0 163.6 jit_solution(8949036088392747636)
XLA Ops:
  0.0 1.2 copy.24
  1.2 0.7 constant_dynamic-update-slice_fusion
  1.9 0.7 constant_dynamic-update-slice_fusion.1.idx_ref.send_ref
  2.6 0.8 pad.32.table_ref.state_ref
  3.4 2.7 %shard_map.100 = f32[1024,128]{1,0:T(8,128)} custom-call(s32[1024]{0:T(1024)} %copy-done.7, f32[1024,128]{1,0:T(8,128)} %pad.32.table_ref.state_ref), custom_call_target="tpu_custom_call" | custom-call | tf_op jit(solution)/shard_map/pallas_call | solution.py:85
  6.2 1.2 slice_bitcast_fusion.2
  7.3 1.3 collective-permute-start
  8.6 0.8 collective-permute-start.1
  9.8 2.2 %copy.27.mask_ref = s32[6,1024,1]{2,1,0:T(8,128)} copy(s32[6,1024,1]{1,0,2:T(8,128)S(1)} %bitcast.84) | data formatting | bytes 49152 | tf_op jit(solution)/shard_map/broadcast_in_dim | solution.py:186
  12.1 0.8 pad.35.spread_ref
  12.9 0.6 pad.36.folded_ref
  13.5 0.6 reshape.62.idx_ref
  14.1 1.3 collective-permute-done
  15.5 3.0 %collective-permute-done.1 = f32[16,512]{0,1:T(8,128)S(1)} collective-permute-done((f32[16,512]{0,1:T(8,128)S(1)}, f32[16,512]{0,1:T(8,128)S(1)}, u32[]{:S(2)}, u32[]{:S(2)}) %collective-permute-start.1) | collective-permute-done | bytes 32800 | tf_op jit(solution)/shard_map/ppermute | solution.py:27
  18.5 0.9 select_maximum_fusion.2.halo_ref
  19.4 13.1 %shard_map.101 = (f32[1024,128]{1,0:T(8,128)}, f32[1024,128]{1,0:T(8,128)}) custom-call(s32[6144]{0:T(1024)} %reshape.62.idx_ref, s32[1024]{0:T(1024)} %copy-done.7, f32[1024,128]{1,0:T(8,128)} %pad.32.table_ref.state_ref, f32[1024,128]{1,0:T(8,128)} %select_maximum_fusion.2.halo_ref, s32[6,1024,1]{2,1,0:T(8,128)} %copy.27.mask_ref, ...), custom_call_target="tpu_custom_call" | custom-call | flops 2617245696 | bytes 2908160 | tf_op jit(solution)/shard_map/pallas_call | solution.py:165
  32.6 1.2 slice_bitcast_fusion.6
  33.7 0.4 collective-permute-start.2
  34.1 1.7 %collective-permute-start.3 = (f32[16,512]{0,1:T(8,128)S(1)}, f32[16,512]{0,1:T(8,128)S(1)}, u32[]{:S(2)}, u32[]{:S(2)}) collective-permute-start(f32[16,512]{0,1:T(8,128)S(1)} %get-tuple-element.18), channel_id=1, source_target_pairs={{0,7},{1,0},{2,1},{3,2},{4,3},{5,4},{6,5},{7,6},{8,15},{9,8},{10,9... | collective-permute-start | bytes 98312 | tf_op jit(solution)/shard_map/ppermute | solution.py:27
  35.8 4.8 %collective-permute-done.2 = f32[16,512]{0,1:T(8,128)S(1)} collective-permute-done((f32[16,512]{0,1:T(8,128)S(1)}, f32[16,512]{0,1:T(8,128)S(1)}, u32[]{:S(2)}, u32[]{:S(2)}) %collective-permute-start.2) | collective-permute-done | bytes 32800 | tf_op jit(solution)/shard_map/ppermute | solution.py:27
  40.7 2.4 %collective-permute-done.3 = f32[16,512]{0,1:T(8,128)S(1)} collective-permute-done((f32[16,512]{0,1:T(8,128)S(1)}, f32[16,512]{0,1:T(8,128)S(1)}, u32[]{:S(2)}, u32[]{:S(2)}) %collective-permute-start.3) | collective-permute-done | bytes 32800 | tf_op jit(solution)/shard_map/ppermute | solution.py:27
  43.1 0.9 select_maximum_fusion.1.halo_ref
  44.0 13.1 %shard_map.102 = (f32[1024,128]{1,0:T(8,128)}, f32[1024,128]{1,0:T(8,128)}) custom-call(s32[6144]{0:T(1024)} %reshape.62.idx_ref, s32[1024]{0:T(1024)} %copy-done.7, f32[1024,128]{1,0:T(8,128)} %get-tuple-element.9.state_ref, f32[1024,128]{1,0:T(8,128)} %select_maximum_fusion.1.halo_ref, s32[6,1024,1]{2,1,0:T(8,128)} %copy.27.mask_ref, ...), custom_call_target="tpu_custom_call" | custom-call | flops 2617245696 | bytes 2908160 | tf_op jit(solution)/shard_map/pallas_call | solution.py:165
  57.2 1.2 slice_bitcast_fusion.4
  58.3 0.4 collective-permute-start.4
  58.7 1.7 %collective-permute-start.5 = (f32[16,512]{0,1:T(8,128)S(1)}, f32[16,512]{0,1:T(8,128)S(1)}, u32[]{:S(2)}, u32[]{:S(2)}) collective-permute-start(f32[16,512]{0,1:T(8,128)S(1)} %get-tuple-element.16), channel_id=1, source_target_pairs={{0,7},{1,0},{2,1},{3,2},{4,3},{5,4},{6,5},{7,6},{8,15},{9,8},{10,9... | collective-permute-start | bytes 98312 | tf_op jit(solution)/shard_map/ppermute | solution.py:27
  60.4 4.3 %collective-permute-done.4 = f32[16,512]{0,1:T(8,128)S(1)} collective-permute-done((f32[16,512]{0,1:T(8,128)S(1)}, f32[16,512]{0,1:T(8,128)S(1)}, u32[]{:S(2)}, u32[]{:S(2)}) %collective-permute-start.4) | collective-permute-done | bytes 32800 | tf_op jit(solution)/shard_map/ppermute | solution.py:27
  64.8 2.4 %collective-permute-done.5 = f32[16,512]{0,1:T(8,128)S(1)} collective-permute-done((f32[16,512]{0,1:T(8,128)S(1)}, f32[16,512]{0,1:T(8,128)S(1)}, u32[]{:S(2)}, u32[]{:S(2)}) %collective-permute-start.5) | collective-permute-done | bytes 32800 | tf_op jit(solution)/shard_map/ppermute | solution.py:27
  67.2 0.9 select_maximum_fusion.halo_ref
  68.1 12.1 %shard_map.103 = f32[1024,128]{1,0:T(8,128)} custom-call(s32[6144]{0:T(1024)} %reshape.62.idx_ref, s32[1024]{0:T(1024)} %copy-done.7, f32[1024,128]{1,0:T(8,128)} %get-tuple-element.11.state_ref, f32[1024,128]{1,0:T(8,128)} %select_maximum_fusion.halo_ref, s32[6,1024,1]{2,1,0:T(8,128)} %copy.27.mask_ref, bf16[6,128,128]{2,1,0:T(8,128)(2,1)} %constant.26.clone.pick_ref, ...), custom_call_target="tpu_custom_call" | custom-call | flops 2617245696 | bytes 2908160 | tf_op jit(solution)/shard_map/pallas_call | solution.py:165
  80.2 2.0 %add_select_fusion = f32[64,1024]{0,1:T(8,128)S(1)} fusion(f32[1024,128]{1,0:T(8,128)} %shard_map.103, f32[64,64]{1,0:T(8,128)S(1)} %copy-done, f32[1,64,1024]{2,1,0:T(8,128)S(1)} %copy-done.1, pred[]{:T(512)S(6)} %eq.7), kind=kOutput, calls=%fused_computation.10 | convolution fusion | flops 50528256 | bytes 802817 | tf_op jit(solution)/shard_map/dot_general | solution.py:31
  82.4 1.5 collective-permute-done.6
  83.9 0.4 fusion.1
  84.3 3.8 %collective-permute-start.7 = (f32[64,512]{0,1:T(8,128)S(1)}, f32[64,512]{0,1:T(8,128)S(1)}, u32[]{:S(2)}, u32[]{:S(2)}) collective-permute-start(f32[64,512]{0,1:T(8,128)S(1)} %fusion.1), channel_id=1, source_target_pairs={{0,16},{8,24},{16,32},{24,40},{32,48},{40,56},{48,64},{56,72},{64,... | collective-permute-start | bytes 393224 | tf_op jit(solution)/shard_map/ppermute | solution.py:22
  88.1 10.6 %collective-permute-done.7 = f32[64,512]{0,1:T(8,128)S(1)} collective-permute-done((f32[64,512]{0,1:T(8,128)S(1)}, f32[64,512]{0,1:T(8,128)S(1)}, u32[]{:S(2)}, u32[]{:S(2)}) %collective-permute-start.7) | collective-permute-done | bytes 131104 | tf_op jit(solution)/shard_map/ppermute | solution.py:22
  98.7 1.9 %collective-permute-start.8 = (f32[64,512]{0,1:T(8,128)S(1)}, f32[64,512]{0,1:T(8,128)S(1)}, u32[]{:S(2)}, u32[]{:S(2)}) collective-permute-start(f32[64,512]{0,1:T(8,128)S(1)} %collective-permute-done.7), channel_id=1, source_target_pairs={{0,16},{8,24},{16,32},{24,40},{32,48},{40,56},{48,64},{56,72},{64,... | collective-permute-start | bytes 393224 | tf_op jit(solution)/shard_map/ppermute | solution.py:22
  100.8 11.2 %collective-permute-done.8 = f32[64,512]{0,1:T(8,128)S(1)} collective-permute-done((f32[64,512]{0,1:T(8,128)S(1)}, f32[64,512]{0,1:T(8,128)S(1)}, u32[]{:S(2)}, u32[]{:S(2)}) %collective-permute-start.8) | collective-permute-done | bytes 131104 | tf_op jit(solution)/shard_map/ppermute | solution.py:22
  112.4 1.9 %collective-permute-start.9 = (f32[64,512]{0,1:T(8,128)S(1)}, f32[64,512]{0,1:T(8,128)S(1)}, u32[]{:S(2)}, u32[]{:S(2)}) collective-permute-start(f32[64,512]{0,1:T(8,128)S(1)} %convolution_add_fusion.4), channel_id=1, source_target_pairs={{0,32},{8,40},{16,48},{24,56},{32,64},{40,72},{48,80},{56,88},{64,... | collective-permute-start | bytes 393224 | tf_op jit(solution)/shard_map/ppermute | solution.py:22
  114.5 14.4 %collective-permute-done.9 = f32[64,512]{0,1:T(8,128)S(1)} collective-permute-done((f32[64,512]{0,1:T(8,128)S(1)}, f32[64,512]{0,1:T(8,128)S(1)}, u32[]{:S(2)}, u32[]{:S(2)}) %collective-permute-start.9) | collective-permute-done | bytes 131104 | tf_op jit(solution)/shard_map/ppermute | solution.py:22
  128.9 0.4 convolution_add_fusion.3
  129.3 1.9 %collective-permute-start.10 = (f32[64,512]{0,1:T(8,128)S(1)}, f32[64,512]{0,1:T(8,128)S(1)}, u32[]{:S(2)}, u32[]{:S(2)}) collective-permute-start(f32[64,512]{0,1:T(8,128)S(1)} %convolution_add_fusion.3), channel_id=1, source_target_pairs={{0,64},{8,72},{16,80},{24,88},{32,96},{40,104},{48,112},{56,120},{... | collective-permute-start | bytes 393224 | tf_op jit(solution)/shard_map/ppermute | solution.py:22
  131.4 16.5 %collective-permute-done.10 = f32[64,512]{0,1:T(8,128)S(1)} collective-permute-done((f32[64,512]{0,1:T(8,128)S(1)}, f32[64,512]{0,1:T(8,128)S(1)}, u32[]{:S(2)}, u32[]{:S(2)}) %collective-permute-start.10) | collective-permute-done | bytes 131104 | tf_op jit(solution)/shard_map/ppermute | solution.py:22
  148.2 1.3 collective-permute-start.11
  149.7 10.2 %collective-permute-done.11 = f32[64,512]{0,1:T(8,128)S(1)} collective-permute-done((f32[64,512]{0,1:T(8,128)S(1)}, f32[64,512]{0,1:T(8,128)S(1)}, u32[]{:S(2)}, u32[]{:S(2)}) %collective-permute-start.11) | collective-permute-done | bytes 131104 | tf_op jit(solution)/shard_map/ppermute | solution.py:22
  160.2 0.4 convolution_add_fusion
  160.6 0.4 select_bitcast_fusion
  161.1 1.5 collective-permute-done.12
  162.7 0.9 copy.39
  (32 shorter events, 2.4 us)
Async XLA Ops:
  0.0 80.2 %copy-start = (f32[64,64]{1,0:T(8,128)S(1)}, f32[64,64]{1,0:T(8,128)}, u32[]{:S(2)}) copy-start(f32[64,64]{1,0:T(8,128)} %param.13) | copy-start | bytes 49156
  0.0 9.5 %copy-start.6 = (f32[64,96]{1,0:T(8,128)S(1)}, f32[64,96]{1,0:T(8,128)}, u32[]{:S(2)}) copy-start(f32[64,96]{1,0:T(8,128)} %constant.27.clone) | copy-start | bytes 73732
  0.0 9.4 %copy-start.5 = (f32[64,64]{1,0:T(8,128)S(1)}, f32[64,64]{1,0:T(8,128)}, u32[]{:S(2)}) copy-start(f32[64,64]{1,0:T(8,128)} %param.11) | copy-start | bytes 49156
  0.0 9.5 %copy-start.2 = (f32[64,96]{1,0:T(8,128)S(1)}, f32[64,96]{1,0:T(8,128)}, u32[]{:S(2)}) copy-start(f32[64,96]{1,0:T(8,128)} %param.12) | copy-start | bytes 73732
  0.0 9.8 %copy-start.3 = (s32[6,1024]{1,0:T(8,128)S(1)}, s32[6,1024]{1,0:T(8,128)}, u32[]{:S(2)}) copy-start(s32[6,1024]{1,0:T(8,128)} %param.15) | copy-start | bytes 73732
  2.6 0.8 copy-start.7
  6.2 7.3 %copy-start.4 = (s32[6,1024]{1,0:T(8,128)S(1)}, s32[6,1024]{1,0:T(8,128)}, u32[]{:S(2)}) copy-start(s32[6,1024]{1,0:T(8,128)} %param.14) | copy-start | bytes 73732
  7.3 8.1 %collective-permute-start = (f32[16,512]{0,1:T(8,128)S(1)}, f32[16,512]{0,1:T(8,128)S(1)}, u32[]{:S(2)}, u32[]{:S(2)}) collective-permute-start(f32[16,512]{0,1:T(8,128)S(1)} %get-tuple-element.19), channel_id=1, source_target_pairs={{0,1},{1,2},{2,3},{3,4},{4,5},{5,6},{6,7},{7,0},{8,9},{9,10},{10,1... | collective-permute-start | bytes 98312 | tf_op jit(solution)/shard_map/ppermute | solution.py:27
  8.6 9.9 %collective-permute-start.1 = (f32[16,512]{0,1:T(8,128)S(1)}, f32[16,512]{0,1:T(8,128)S(1)}, u32[]{:S(2)}, u32[]{:S(2)}) collective-permute-start(f32[16,512]{0,1:T(8,128)S(1)} %get-tuple-element.20), channel_id=1, source_target_pairs={{0,7},{1,0},{2,1},{3,2},{4,3},{5,4},{6,5},{7,6},{8,15},{9,8},{10,9... | collective-permute-start | bytes 98312 | tf_op jit(solution)/shard_map/ppermute | solution.py:27
  33.7 6.9 %collective-permute-start.2 = (f32[16,512]{0,1:T(8,128)S(1)}, f32[16,512]{0,1:T(8,128)S(1)}, u32[]{:S(2)}, u32[]{:S(2)}) collective-permute-start(f32[16,512]{0,1:T(8,128)S(1)} %get-tuple-element.17), channel_id=1, source_target_pairs={{0,1},{1,2},{2,3},{3,4},{4,5},{5,6},{6,7},{7,0},{8,9},{9,10},{10,1... | collective-permute-start | bytes 98312 | tf_op jit(solution)/shard_map/ppermute | solution.py:27
  34.1 9.0 %collective-permute-start.3 = (f32[16,512]{0,1:T(8,128)S(1)}, f32[16,512]{0,1:T(8,128)S(1)}, u32[]{:S(2)}, u32[]{:S(2)}) collective-permute-start(f32[16,512]{0,1:T(8,128)S(1)} %get-tuple-element.18), channel_id=1, source_target_pairs={{0,7},{1,0},{2,1},{3,2},{4,3},{5,4},{6,5},{7,6},{8,15},{9,8},{10,9... | collective-permute-start | bytes 98312 | tf_op jit(solution)/shard_map/ppermute | solution.py:27
  58.3 6.4 %collective-permute-start.4 = (f32[16,512]{0,1:T(8,128)S(1)}, f32[16,512]{0,1:T(8,128)S(1)}, u32[]{:S(2)}, u32[]{:S(2)}) collective-permute-start(f32[16,512]{0,1:T(8,128)S(1)} %get-tuple-element.15), channel_id=1, source_target_pairs={{0,1},{1,2},{2,3},{3,4},{4,5},{5,6},{6,7},{7,0},{8,9},{9,10},{10,1... | collective-permute-start | bytes 98312 | tf_op jit(solution)/shard_map/ppermute | solution.py:27
  58.7 8.5 %collective-permute-start.5 = (f32[16,512]{0,1:T(8,128)S(1)}, f32[16,512]{0,1:T(8,128)S(1)}, u32[]{:S(2)}, u32[]{:S(2)}) collective-permute-start(f32[16,512]{0,1:T(8,128)S(1)} %get-tuple-element.16), channel_id=1, source_target_pairs={{0,7},{1,0},{2,1},{3,2},{4,3},{5,4},{6,5},{7,6},{8,15},{9,8},{10,9... | collective-permute-start | bytes 98312 | tf_op jit(solution)/shard_map/ppermute | solution.py:27
  68.1 12.1 %copy-start.1 = (f32[1,64,1024]{2,1,0:T(8,128)S(1)}, f32[1,64,1024]{2,1,0:T(8,128)}, u32[]{:S(2)}) copy-start(f32[1,64,1024]{2,1,0:T(8,128)} %param.10) | copy-start | bytes 786436
  82.3 1.6 collective-permute-start.6
  84.3 14.4 %collective-permute-start.7 = (f32[64,512]{0,1:T(8,128)S(1)}, f32[64,512]{0,1:T(8,128)S(1)}, u32[]{:S(2)}, u32[]{:S(2)}) collective-permute-start(f32[64,512]{0,1:T(8,128)S(1)} %fusion.1), channel_id=1, source_target_pairs={{0,16},{8,24},{16,32},{24,40},{32,48},{40,56},{48,64},{56,72},{64,... | collective-permute-start | bytes 393224 | tf_op jit(solution)/shard_map/ppermute | solution.py:22
  98.7 13.3 %collective-permute-start.8 = (f32[64,512]{0,1:T(8,128)S(1)}, f32[64,512]{0,1:T(8,128)S(1)}, u32[]{:S(2)}, u32[]{:S(2)}) collective-permute-start(f32[64,512]{0,1:T(8,128)S(1)} %collective-permute-done.7), channel_id=1, source_target_pairs={{0,16},{8,24},{16,32},{24,40},{32,48},{40,56},{48,64},{56,72},{64,... | collective-permute-start | bytes 393224 | tf_op jit(solution)/shard_map/ppermute | solution.py:22
  112.4 16.5 %collective-permute-start.9 = (f32[64,512]{0,1:T(8,128)S(1)}, f32[64,512]{0,1:T(8,128)S(1)}, u32[]{:S(2)}, u32[]{:S(2)}) collective-permute-start(f32[64,512]{0,1:T(8,128)S(1)} %convolution_add_fusion.4), channel_id=1, source_target_pairs={{0,32},{8,40},{16,48},{24,56},{32,64},{40,72},{48,80},{56,88},{64,... | collective-permute-start | bytes 393224 | tf_op jit(solution)/shard_map/ppermute | solution.py:22
  129.3 18.6 %collective-permute-start.10 = (f32[64,512]{0,1:T(8,128)S(1)}, f32[64,512]{0,1:T(8,128)S(1)}, u32[]{:S(2)}, u32[]{:S(2)}) collective-permute-start(f32[64,512]{0,1:T(8,128)S(1)} %convolution_add_fusion.3), channel_id=1, source_target_pairs={{0,64},{8,72},{16,80},{24,88},{32,96},{40,104},{48,112},{56,120},{... | collective-permute-start | bytes 393224 | tf_op jit(solution)/shard_map/ppermute | solution.py:22
  148.2 11.6 %collective-permute-start.11 = (f32[64,512]{0,1:T(8,128)S(1)}, f32[64,512]{0,1:T(8,128)S(1)}, u32[]{:S(2)}, u32[]{:S(2)}) collective-permute-start(f32[64,512]{0,1:T(8,128)S(1)} %convolution_add_fusion.2), channel_id=1, source_target_pairs={{0,128},{8,136},{16,144},{24,152},{32,160},{40,168},{48,176},{56,1... | collective-permute-start | bytes 393224 | tf_op jit(solution)/shard_map/ppermute | solution.py:22
  161.0 1.6 collective-permute-start.12

commit v12 on v11

--- a/solution.py
+++ b/solution.py
@@ -10,7 +10,7 @@
 
 STEPS = 3
 LANES = 128
-UNROLL = 64
+UNROLL = 128
 
 
 time_step = 0.05
@@ -30,6 +30,12 @@
 def product(matrix, vector):
     return jnp.dot(
         matrix, vector, precision=lax.Precision.HIGHEST, preferred_element_type=jnp.float32
+    )
+
+
+def quick_product(matrix, vector):
+    return jnp.dot(
+        matrix, vector, precision=lax.Precision.HIGH, preferred_element_type=jnp.float32
     )
 
 
@@ -228,18 +234,18 @@
     keep = jnp.where(core == 0, low, high)
     first = jnp.where(core == 0, keep, got)
     second = jnp.where(core == 0, got, keep)
-    aggregate = product(coarse, first) + second
+    aggregate = quick_product(coarse, first) + second
     square = product(coarse, coarse)
     before = from_behind(aggregate, "tm", 2)
     power = square
     shift = 1
     while shift < peers // 2:
-        before = before + product(power, from_behind(before, "tm", 2 * shift))
+        before = before + quick_product(power, from_behind(before, "tm", 2 * shift))
         shift *= 2
         if shift < peers // 2:
             power = product(power, power)
-    end_first = product(coarse, before) + first
-    end_second = product(square, before) + aggregate
+    end_first = quick_product(coarse, before) + first
+    end_second = quick_product(square, before) + aggregate
     mine = jnp.where(core == 0, end_first, end_second)
     got = lax.ppermute(jnp.where(core == 0, end_second, end_first), "tm", partner)
     return jnp.where(

time: 164 us -> 163 us (level)
    dot_general x13 -> x6, matrix products: 5.42 us -> 2.88 us  [product(): jnp.dot(matrix, vector, precision=lax.Precision.HIGHEST, preferred_elemen...]
    dot_general x0 -> x7, matrix products: none -> 1.82 us  [quick_product(): jnp.dot(matrix, vector, precision=lax.Precision.HIGH, preferred_element_t...]
where the time goes in v12:
time: 163 us; the launch traced here: 162 us
  waiting for transfers between devices  84.3 us (52%)
  Pallas kernels  40.4 us (25%)
  starting transfers between devices  17.5 us (11%)
  local copies, waits for them, and re-layouts  12.2 us (7%)
  matrix products  4.7 us (3%)
  other arithmetic  2.89 us (2%)
    ppermute x5, waiting for transfers between devices, from_behind(): return lax.ppermute(shard, axis, pairs)  62.9 us
    pallas_call x3, Pallas kernels, fused_step(): pl.pallas_call(functools.partial(fused_kernel, with_send), out_shape=tupl...  37.7 us
    ppermute x6, waiting for transfers between devices, ring(): lax.ppermute(shard, axis, [(i, (i + by) % peers) for i in range(peers)])  18.4 us
    ppermute x5, starting transfers between devices, from_behind(): return lax.ppermute(shard, axis, pairs)  10.9 us
    ppermute x6, starting transfers between devices, ring(): lax.ppermute(shard, axis, [(i, (i + by) % peers) for i in range(peers)])  6.49 us
    transpose x3, local copies, waits for them, and re-layouts, shards(): before = ring(sent[half:, 48:64].T, 'space', 1)  3.46 us
  transfers between devices with their start and end apart: 13, of which 13 were waited for; matrix products, arithmetic and copies ran while one was open for 3% of the time, Pallas kernels for 0%

profile of v12, /device:TPU:22, one launch (start us, length us, event | category | flops | bytes accessed | tf_op | source)
XLA Modules:
  0.0 162.3 jit_solution(3418668139953668243)
XLA Ops:
  0.0 1.2 copy.24
  1.2 0.7 constant_dynamic-update-slice_fusion
  1.9 0.7 constant_dynamic-update-slice_fusion.1.idx_ref.send_ref
  2.6 0.8 pad.32.table_ref.state_ref
  3.4 2.7 %shard_map.100 = f32[1024,128]{1,0:T(8,128)} custom-call(s32[1024]{0:T(1024)} %copy-done.7, f32[1024,128]{1,0:T(8,128)} %pad.32.table_ref.state_ref), custom_call_target="tpu_custom_call" | custom-call | tf_op jit(solution)/shard_map/pallas_call | solution.py:91
  6.1 1.2 slice_bitcast_fusion.2
  7.3 1.3 collective-permute-start
  8.6 0.8 collective-permute-start.1
  9.8 2.2 %copy.27.mask_ref = s32[6,1024,1]{2,1,0:T(8,128)} copy(s32[6,1024,1]{1,0,2:T(8,128)S(1)} %bitcast.84) | data formatting | bytes 49152 | tf_op jit(solution)/shard_map/broadcast_in_dim | solution.py:192
  12.0 0.8 pad.35.spread_ref
  12.8 0.6 pad.36.folded_ref
  13.5 0.6 reshape.62.idx_ref
  14.1 1.3 collective-permute-done
  15.4 3.0 %collective-permute-done.1 = f32[16,512]{0,1:T(8,128)S(1)} collective-permute-done((f32[16,512]{0,1:T(8,128)S(1)}, f32[16,512]{0,1:T(8,128)S(1)}, u32[]{:S(2)}, u32[]{:S(2)}) %collective-permute-start.1) | collective-permute-done | bytes 32800 | tf_op jit(solution)/shard_map/ppermute | solution.py:27
  18.5 0.9 select_maximum_fusion.2.halo_ref
  19.4 12.9 %shard_map.101 = (f32[1024,128]{1,0:T(8,128)}, f32[1024,128]{1,0:T(8,128)}) custom-call(s32[6144]{0:T(1024)} %reshape.62.idx_ref, s32[1024]{0:T(1024)} %copy-done.7, f32[1024,128]{1,0:T(8,128)} %pad.32.table_ref.state_ref, f32[1024,128]{1,0:T(8,128)} %select_maximum_fusion.2.halo_ref, s32[6,1024,1]{2,1,0:T(8,128)} %copy.27.mask_ref, ...), custom_call_target="tpu_custom_call" | custom-call | flops 2617245696 | bytes 2908160 | tf_op jit(solution)/shard_map/pallas_call | solution.py:171
  32.3 1.2 slice_bitcast_fusion.6
  33.4 0.4 collective-permute-start.2
  33.8 1.7 %collective-permute-start.3 = (f32[16,512]{0,1:T(8,128)S(1)}, f32[16,512]{0,1:T(8,128)S(1)}, u32[]{:S(2)}, u32[]{:S(2)}) collective-permute-start(f32[16,512]{0,1:T(8,128)S(1)} %get-tuple-element.18), channel_id=1, source_target_pairs={{0,7},{1,0},{2,1},{3,2},{4,3},{5,4},{6,5},{7,6},{8,15},{9,8},{10,9... | collective-permute-start | bytes 98312 | tf_op jit(solution)/shard_map/ppermute | solution.py:27
  35.5 4.8 %collective-permute-done.2 = f32[16,512]{0,1:T(8,128)S(1)} collective-permute-done((f32[16,512]{0,1:T(8,128)S(1)}, f32[16,512]{0,1:T(8,128)S(1)}, u32[]{:S(2)}, u32[]{:S(2)}) %collective-permute-start.2) | collective-permute-done | bytes 32800 | tf_op jit(solution)/shard_map/ppermute | solution.py:27
  40.4 2.4 %collective-permute-done.3 = f32[16,512]{0,1:T(8,128)S(1)} collective-permute-done((f32[16,512]{0,1:T(8,128)S(1)}, f32[16,512]{0,1:T(8,128)S(1)}, u32[]{:S(2)}, u32[]{:S(2)}) %collective-permute-start.3) | collective-permute-done | bytes 32800 | tf_op jit(solution)/shard_map/ppermute | solution.py:27
  42.8 0.9 select_maximum_fusion.1.halo_ref
  43.8 12.9 %shard_map.102 = (f32[1024,128]{1,0:T(8,128)}, f32[1024,128]{1,0:T(8,128)}) custom-call(s32[6144]{0:T(1024)} %reshape.62.idx_ref, s32[1024]{0:T(1024)} %copy-done.7, f32[1024,128]{1,0:T(8,128)} %get-tuple-element.9.state_ref, f32[1024,128]{1,0:T(8,128)} %select_maximum_fusion.1.halo_ref, s32[6,1024,1]{2,1,0:T(8,128)} %copy.27.mask_ref, ...), custom_call_target="tpu_custom_call" | custom-call | flops 2617245696 | bytes 2908160 | tf_op jit(solution)/shard_map/pallas_call | solution.py:171
  56.7 1.2 slice_bitcast_fusion.4
  57.8 0.5 collective-permute-start.4
  58.4 1.7 %collective-permute-start.5 = (f32[16,512]{0,1:T(8,128)S(1)}, f32[16,512]{0,1:T(8,128)S(1)}, u32[]{:S(2)}, u32[]{:S(2)}) collective-permute-start(f32[16,512]{0,1:T(8,128)S(1)} %get-tuple-element.16), channel_id=1, source_target_pairs={{0,7},{1,0},{2,1},{3,2},{4,3},{5,4},{6,5},{7,6},{8,15},{9,8},{10,9... | collective-permute-start | bytes 98312 | tf_op jit(solution)/shard_map/ppermute | solution.py:27
  60.1 4.3 %collective-permute-done.4 = f32[16,512]{0,1:T(8,128)S(1)} collective-permute-done((f32[16,512]{0,1:T(8,128)S(1)}, f32[16,512]{0,1:T(8,128)S(1)}, u32[]{:S(2)}, u32[]{:S(2)}) %collective-permute-start.4) | collective-permute-done | bytes 32800 | tf_op jit(solution)/shard_map/ppermute | solution.py:27
  64.4 2.4 %collective-permute-done.5 = f32[16,512]{0,1:T(8,128)S(1)} collective-permute-done((f32[16,512]{0,1:T(8,128)S(1)}, f32[16,512]{0,1:T(8,128)S(1)}, u32[]{:S(2)}, u32[]{:S(2)}) %collective-permute-start.5) | collective-permute-done | bytes 32800 | tf_op jit(solution)/shard_map/ppermute | solution.py:27
  66.8 0.9 select_maximum_fusion.halo_ref
  67.8 11.9 %shard_map.103 = f32[1024,128]{1,0:T(8,128)} custom-call(s32[6144]{0:T(1024)} %reshape.62.idx_ref, s32[1024]{0:T(1024)} %copy-done.7, f32[1024,128]{1,0:T(8,128)} %get-tuple-element.11.state_ref, f32[1024,128]{1,0:T(8,128)} %select_maximum_fusion.halo_ref, s32[6,1024,1]{2,1,0:T(8,128)} %copy.27.mask_ref, bf16[6,128,128]{2,1,0:T(8,128)(2,1)} %constant.26.clone.pick_ref, ...), custom_call_target="tpu_custom_call" | custom-call | flops 2617245696 | bytes 2908160 | tf_op jit(solution)/shard_map/pallas_call | solution.py:171
  79.7 2.0 %add_select_fusion = f32[64,1024]{0,1:T(8,128)S(1)} fusion(f32[1024,128]{1,0:T(8,128)} %shard_map.103, f32[64,64]{1,0:T(8,128)S(1)} %copy-done, f32[1,64,1024]{2,1,0:T(8,128)S(1)} %copy-done.1, pred[]{:T(512)S(6)} %eq.7), kind=kOutput, calls=%fused_computation.10 | convolution fusion | flops 50528256 | bytes 802817 | tf_op jit(solution)/shard_map/dot_general | solution.py:31
  81.9 1.5 collective-permute-done.6
  83.4 0.3 fusion.1
  83.7 3.8 %collective-permute-start.7 = (f32[64,512]{0,1:T(8,128)S(1)}, f32[64,512]{0,1:T(8,128)S(1)}, u32[]{:S(2)}, u32[]{:S(2)}) collective-permute-start(f32[64,512]{0,1:T(8,128)S(1)} %fusion.1), channel_id=1, source_target_pairs={{0,16},{8,24},{16,32},{24,40},{32,48},{40,56},{48,64},{56,72},{64,... | collective-permute-start | bytes 393224 | tf_op jit(solution)/shard_map/ppermute | solution.py:22
  87.5 10.6 %collective-permute-done.7 = f32[64,512]{0,1:T(8,128)S(1)} collective-permute-done((f32[64,512]{0,1:T(8,128)S(1)}, f32[64,512]{0,1:T(8,128)S(1)}, u32[]{:S(2)}, u32[]{:S(2)}) %collective-permute-start.7) | collective-permute-done | bytes 131104 | tf_op jit(solution)/shard_map/ppermute | solution.py:22
  98.1 1.9 %collective-permute-start.8 = (f32[64,512]{0,1:T(8,128)S(1)}, f32[64,512]{0,1:T(8,128)S(1)}, u32[]{:S(2)}, u32[]{:S(2)}) collective-permute-start(f32[64,512]{0,1:T(8,128)S(1)} %collective-permute-done.7), channel_id=1, source_target_pairs={{0,16},{8,24},{16,32},{24,40},{32,48},{40,56},{48,64},{56,72},{64,... | collective-permute-start | bytes 393224 | tf_op jit(solution)/shard_map/ppermute | solution.py:22
  100.2 11.2 %collective-permute-done.8 = f32[64,512]{0,1:T(8,128)S(1)} collective-permute-done((f32[64,512]{0,1:T(8,128)S(1)}, f32[64,512]{0,1:T(8,128)S(1)}, u32[]{:S(2)}, u32[]{:S(2)}) %collective-permute-start.8) | collective-permute-done | bytes 131104 | tf_op jit(solution)/shard_map/ppermute | solution.py:22
  111.7 1.9 %collective-permute-start.9 = (f32[64,512]{0,1:T(8,128)S(1)}, f32[64,512]{0,1:T(8,128)S(1)}, u32[]{:S(2)}, u32[]{:S(2)}) collective-permute-start(f32[64,512]{0,1:T(8,128)S(1)} %convolution_add_fusion.4), channel_id=1, source_target_pairs={{0,32},{8,40},{16,48},{24,56},{32,64},{40,72},{48,80},{56,88},{64,... | collective-permute-start | bytes 393224 | tf_op jit(solution)/shard_map/ppermute | solution.py:22
  113.8 14.4 %collective-permute-done.9 = f32[64,512]{0,1:T(8,128)S(1)} collective-permute-done((f32[64,512]{0,1:T(8,128)S(1)}, f32[64,512]{0,1:T(8,128)S(1)}, u32[]{:S(2)}, u32[]{:S(2)}) %collective-permute-start.9) | collective-permute-done | bytes 131104 | tf_op jit(solution)/shard_map/ppermute | solution.py:22
  128.5 1.9 %collective-permute-start.10 = (f32[64,512]{0,1:T(8,128)S(1)}, f32[64,512]{0,1:T(8,128)S(1)}, u32[]{:S(2)}, u32[]{:S(2)}) collective-permute-start(f32[64,512]{0,1:T(8,128)S(1)} %convolution_add_fusion.3), channel_id=1, source_target_pairs={{0,64},{8,72},{16,80},{24,88},{32,96},{40,104},{48,112},{56,120},{... | collective-permute-start | bytes 393224 | tf_op jit(solution)/shard_map/ppermute | solution.py:22
  130.6 16.5 %collective-permute-done.10 = f32[64,512]{0,1:T(8,128)S(1)} collective-permute-done((f32[64,512]{0,1:T(8,128)S(1)}, f32[64,512]{0,1:T(8,128)S(1)}, u32[]{:S(2)}, u32[]{:S(2)}) %collective-permute-start.10) | collective-permute-done | bytes 131104 | tf_op jit(solution)/shard_map/ppermute | solution.py:22
  147.0 0.3 convolution_add_fusion.2
  147.3 1.3 collective-permute-start.11
  148.8 10.2 %collective-permute-done.11 = f32[64,512]{0,1:T(8,128)S(1)} collective-permute-done((f32[64,512]{0,1:T(8,128)S(1)}, f32[64,512]{0,1:T(8,128)S(1)}, u32[]{:S(2)}, u32[]{:S(2)}) %collective-permute-start.11) | collective-permute-done | bytes 131104 | tf_op jit(solution)/shard_map/ppermute | solution.py:22
  159.2 0.3 convolution_add_fusion
  159.5 0.3 select_bitcast_fusion
  159.8 1.5 collective-permute-done.12
  161.4 0.9 copy.39
  (32 shorter events, 2.1 us)
Async XLA Ops:
  0.0 79.7 %copy-start = (f32[64,64]{1,0:T(8,128)S(1)}, f32[64,64]{1,0:T(8,128)}, u32[]{:S(2)}) copy-start(f32[64,64]{1,0:T(8,128)} %param.13) | copy-start | bytes 49156
  0.0 9.5 %copy-start.6 = (f32[64,96]{1,0:T(8,128)S(1)}, f32[64,96]{1,0:T(8,128)}, u32[]{:S(2)}) copy-start(f32[64,96]{1,0:T(8,128)} %constant.27.clone) | copy-start | bytes 73732
  0.0 9.4 %copy-start.5 = (f32[64,64]{1,0:T(8,128)S(1)}, f32[64,64]{1,0:T(8,128)}, u32[]{:S(2)}) copy-start(f32[64,64]{1,0:T(8,128)} %param.11) | copy-start | bytes 49156
  0.0 9.5 %copy-start.2 = (f32[64,96]{1,0:T(8,128)S(1)}, f32[64,96]{1,0:T(8,128)}, u32[]{:S(2)}) copy-start(f32[64,96]{1,0:T(8,128)} %param.12) | copy-start | bytes 73732
  0.0 9.8 %copy-start.3 = (s32[6,1024]{1,0:T(8,128)S(1)}, s32[6,1024]{1,0:T(8,128)}, u32[]{:S(2)}) copy-start(s32[6,1024]{1,0:T(8,128)} %param.15) | copy-start | bytes 73732
  2.6 0.8 copy-start.7
  6.1 7.3 %copy-start.4 = (s32[6,1024]{1,0:T(8,128)S(1)}, s32[6,1024]{1,0:T(8,128)}, u32[]{:S(2)}) copy-start(s32[6,1024]{1,0:T(8,128)} %param.14) | copy-start | bytes 73732
  7.3 8.1 %collective-permute-start = (f32[16,512]{0,1:T(8,128)S(1)}, f32[16,512]{0,1:T(8,128)S(1)}, u32[]{:S(2)}, u32[]{:S(2)}) collective-permute-start(f32[16,512]{0,1:T(8,128)S(1)} %get-tuple-element.19), channel_id=1, source_target_pairs={{0,1},{1,2},{2,3},{3,4},{4,5},{5,6},{6,7},{7,0},{8,9},{9,10},{10,1... | collective-permute-start | bytes 98312 | tf_op jit(solution)/shard_map/ppermute | solution.py:27
  8.6 9.9 %collective-permute-start.1 = (f32[16,512]{0,1:T(8,128)S(1)}, f32[16,512]{0,1:T(8,128)S(1)}, u32[]{:S(2)}, u32[]{:S(2)}) collective-permute-start(f32[16,512]{0,1:T(8,128)S(1)} %get-tuple-element.20), channel_id=1, source_target_pairs={{0,7},{1,0},{2,1},{3,2},{4,3},{5,4},{6,5},{7,6},{8,15},{9,8},{10,9... | collective-permute-start | bytes 98312 | tf_op jit(solution)/shard_map/ppermute | solution.py:27
  33.4 6.9 %collective-permute-start.2 = (f32[16,512]{0,1:T(8,128)S(1)}, f32[16,512]{0,1:T(8,128)S(1)}, u32[]{:S(2)}, u32[]{:S(2)}) collective-permute-start(f32[16,512]{0,1:T(8,128)S(1)} %get-tuple-element.17), channel_id=1, source_target_pairs={{0,1},{1,2},{2,3},{3,4},{4,5},{5,6},{6,7},{7,0},{8,9},{9,10},{10,1... | collective-permute-start | bytes 98312 | tf_op jit(solution)/shard_map/ppermute | solution.py:27
  33.8 9.0 %collective-permute-start.3 = (f32[16,512]{0,1:T(8,128)S(1)}, f32[16,512]{0,1:T(8,128)S(1)}, u32[]{:S(2)}, u32[]{:S(2)}) collective-permute-start(f32[16,512]{0,1:T(8,128)S(1)} %get-tuple-element.18), channel_id=1, source_target_pairs={{0,7},{1,0},{2,1},{3,2},{4,3},{5,4},{6,5},{7,6},{8,15},{9,8},{10,9... | collective-permute-start | bytes 98312 | tf_op jit(solution)/shard_map/ppermute | solution.py:27
  57.8 6.6 %collective-permute-start.4 = (f32[16,512]{0,1:T(8,128)S(1)}, f32[16,512]{0,1:T(8,128)S(1)}, u32[]{:S(2)}, u32[]{:S(2)}) collective-permute-start(f32[16,512]{0,1:T(8,128)S(1)} %get-tuple-element.15), channel_id=1, source_target_pairs={{0,1},{1,2},{2,3},{3,4},{4,5},{5,6},{6,7},{7,0},{8,9},{9,10},{10,1... | collective-permute-start | bytes 98312 | tf_op jit(solution)/shard_map/ppermute | solution.py:27
  58.4 8.5 %collective-permute-start.5 = (f32[16,512]{0,1:T(8,128)S(1)}, f32[16,512]{0,1:T(8,128)S(1)}, u32[]{:S(2)}, u32[]{:S(2)}) collective-permute-start(f32[16,512]{0,1:T(8,128)S(1)} %get-tuple-element.16), channel_id=1, source_target_pairs={{0,7},{1,0},{2,1},{3,2},{4,3},{5,4},{6,5},{7,6},{8,15},{9,8},{10,9... | collective-permute-start | bytes 98312 | tf_op jit(solution)/shard_map/ppermute | solution.py:27
  67.8 11.9 %copy-start.1 = (f32[1,64,1024]{2,1,0:T(8,128)S(1)}, f32[1,64,1024]{2,1,0:T(8,128)}, u32[]{:S(2)}) copy-start(f32[1,64,1024]{2,1,0:T(8,128)} %param.10) | copy-start | bytes 786436
  81.8 1.6 collective-permute-start.6
  83.7 14.4 %collective-permute-start.7 = (f32[64,512]{0,1:T(8,128)S(1)}, f32[64,512]{0,1:T(8,128)S(1)}, u32[]{:S(2)}, u32[]{:S(2)}) collective-permute-start(f32[64,512]{0,1:T(8,128)S(1)} %fusion.1), channel_id=1, source_target_pairs={{0,16},{8,24},{16,32},{24,40},{32,48},{40,56},{48,64},{56,72},{64,... | collective-permute-start | bytes 393224 | tf_op jit(solution)/shard_map/ppermute | solution.py:22
  98.1 13.3 %collective-permute-start.8 = (f32[64,512]{0,1:T(8,128)S(1)}, f32[64,512]{0,1:T(8,128)S(1)}, u32[]{:S(2)}, u32[]{:S(2)}) collective-permute-start(f32[64,512]{0,1:T(8,128)S(1)} %collective-permute-done.7), channel_id=1, source_target_pairs={{0,16},{8,24},{16,32},{24,40},{32,48},{40,56},{48,64},{56,72},{64,... | collective-permute-start | bytes 393224 | tf_op jit(solution)/shard_map/ppermute | solution.py:22
  111.7 16.5 %collective-permute-start.9 = (f32[64,512]{0,1:T(8,128)S(1)}, f32[64,512]{0,1:T(8,128)S(1)}, u32[]{:S(2)}, u32[]{:S(2)}) collective-permute-start(f32[64,512]{0,1:T(8,128)S(1)} %convolution_add_fusion.4), channel_id=1, source_target_pairs={{0,32},{8,40},{16,48},{24,56},{32,64},{40,72},{48,80},{56,88},{64,... | collective-permute-start | bytes 393224 | tf_op jit(solution)/shard_map/ppermute | solution.py:22
  128.5 18.6 %collective-permute-start.10 = (f32[64,512]{0,1:T(8,128)S(1)}, f32[64,512]{0,1:T(8,128)S(1)}, u32[]{:S(2)}, u32[]{:S(2)}) collective-permute-start(f32[64,512]{0,1:T(8,128)S(1)} %convolution_add_fusion.3), channel_id=1, source_target_pairs={{0,64},{8,72},{16,80},{24,88},{32,96},{40,104},{48,112},{56,120},{... | collective-permute-start | bytes 393224 | tf_op jit(solution)/shard_map/ppermute | solution.py:22
  147.3 11.6 %collective-permute-start.11 = (f32[64,512]{0,1:T(8,128)S(1)}, f32[64,512]{0,1:T(8,128)S(1)}, u32[]{:S(2)}, u32[]{:S(2)}) collective-permute-start(f32[64,512]{0,1:T(8,128)S(1)} %convolution_add_fusion.2), channel_id=1, source_target_pairs={{0,128},{8,136},{16,144},{24,152},{32,160},{40,168},{48,176},{56,1... | collective-permute-start | bytes 393224 | tf_op jit(solution)/shard_map/ppermute | solution.py:22
  159.7 1.6 collective-permute-start.12

commit v13 on v11

--- a/solution.py
+++ b/solution.py
@@ -10,7 +10,7 @@
 
 STEPS = 3
 LANES = 128
-UNROLL = 64
+UNROLL = 128
 
 
 time_step = 0.05

time: 164 us -> 164 us (level)
  no operation moved by 1% of the time
where the time goes in v13:
time: 164 us; the launch traced here: 163 us
  waiting for transfers between devices  84.3 us (51%)
  Pallas kernels  40.4 us (25%)
  starting transfers between devices  17.5 us (11%)
  local copies, waits for them, and re-layouts  12.2 us (7%)
  matrix products  5.42 us (3%)
  other arithmetic  2.89 us (2%)
    ppermute x5, waiting for transfers between devices, from_behind(): return lax.ppermute(shard, axis, pairs)  62.9 us
    pallas_call x3, Pallas kernels, fused_step(): pl.pallas_call(functools.partial(fused_kernel, with_send), out_shape=tupl...  37.7 us
    ppermute x6, waiting for transfers between devices, ring(): lax.ppermute(shard, axis, [(i, (i + by) % peers) for i in range(peers)])  18.4 us
    ppermute x5, starting transfers between devices, from_behind(): return lax.ppermute(shard, axis, pairs)  10.9 us
    ppermute x6, starting transfers between devices, ring(): lax.ppermute(shard, axis, [(i, (i + by) % peers) for i in range(peers)])  6.49 us
    dot_general x13, matrix products, product(): jnp.dot(matrix, vector, precision=lax.Precision.HIGHEST, preferred_elemen...  5.42 us
    transpose x3, local copies, waits for them, and re-layouts, shards(): before = ring(sent[half:, 48:64].T, 'space', 1)  3.46 us
  transfers between devices with their start and end apart: 13, of which 13 were waited for; matrix products, arithmetic and copies ran while one was open for 3% of the time, Pallas kernels for 0%

profile of v13, /device:TPU:22, one launch (start us, length us, event | category | flops | bytes accessed | tf_op | source)
XLA Modules:
  0.0 163.0 jit_solution(3877327791933256865)
XLA Ops:
  0.0 1.2 copy.24
  1.2 0.7 constant_dynamic-update-slice_fusion
  1.9 0.7 constant_dynamic-update-slice_fusion.1.idx_ref.send_ref
  2.6 0.8 pad.32.table_ref.state_ref
  3.4 2.7 %shard_map.100 = f32[1024,128]{1,0:T(8,128)} custom-call(s32[1024]{0:T(1024)} %copy-done.7, f32[1024,128]{1,0:T(8,128)} %pad.32.table_ref.state_ref), custom_call_target="tpu_custom_call" | custom-call | tf_op jit(solution)/shard_map/pallas_call | solution.py:85
  6.1 1.2 slice_bitcast_fusion.2
  7.3 1.3 collective-permute-start
  8.6 0.8 collective-permute-start.1
  9.8 2.2 %copy.27.mask_ref = s32[6,1024,1]{2,1,0:T(8,128)} copy(s32[6,1024,1]{1,0,2:T(8,128)S(1)} %bitcast.84) | data formatting | bytes 49152 | tf_op jit(solution)/shard_map/broadcast_in_dim | solution.py:186
  12.0 0.8 pad.35.spread_ref
  12.8 0.6 pad.36.folded_ref
  13.5 0.6 reshape.62.idx_ref
  14.1 1.3 collective-permute-done
  15.4 3.0 %collective-permute-done.1 = f32[16,512]{0,1:T(8,128)S(1)} collective-permute-done((f32[16,512]{0,1:T(8,128)S(1)}, f32[16,512]{0,1:T(8,128)S(1)}, u32[]{:S(2)}, u32[]{:S(2)}) %collective-permute-start.1) | collective-permute-done | bytes 32800 | tf_op jit(solution)/shard_map/ppermute | solution.py:27
  18.5 0.9 select_maximum_fusion.2.halo_ref
  19.4 12.9 %shard_map.101 = (f32[1024,128]{1,0:T(8,128)}, f32[1024,128]{1,0:T(8,128)}) custom-call(s32[6144]{0:T(1024)} %reshape.62.idx_ref, s32[1024]{0:T(1024)} %copy-done.7, f32[1024,128]{1,0:T(8,128)} %pad.32.table_ref.state_ref, f32[1024,128]{1,0:T(8,128)} %select_maximum_fusion.2.halo_ref, s32[6,1024,1]{2,1,0:T(8,128)} %copy.27.mask_ref, ...), custom_call_target="tpu_custom_call" | custom-call | flops 2617245696 | bytes 2908160 | tf_op jit(solution)/shard_map/pallas_call | solution.py:165
  32.3 1.2 slice_bitcast_fusion.6
  33.4 0.4 collective-permute-start.2
  33.8 1.7 %collective-permute-start.3 = (f32[16,512]{0,1:T(8,128)S(1)}, f32[16,512]{0,1:T(8,128)S(1)}, u32[]{:S(2)}, u32[]{:S(2)}) collective-permute-start(f32[16,512]{0,1:T(8,128)S(1)} %get-tuple-element.18), channel_id=1, source_target_pairs={{0,7},{1,0},{2,1},{3,2},{4,3},{5,4},{6,5},{7,6},{8,15},{9,8},{10,9... | collective-permute-start | bytes 98312 | tf_op jit(solution)/shard_map/ppermute | solution.py:27
  35.5 4.8 %collective-permute-done.2 = f32[16,512]{0,1:T(8,128)S(1)} collective-permute-done((f32[16,512]{0,1:T(8,128)S(1)}, f32[16,512]{0,1:T(8,128)S(1)}, u32[]{:S(2)}, u32[]{:S(2)}) %collective-permute-start.2) | collective-permute-done | bytes 32800 | tf_op jit(solution)/shard_map/ppermute | solution.py:27
  40.4 2.4 %collective-permute-done.3 = f32[16,512]{0,1:T(8,128)S(1)} collective-permute-done((f32[16,512]{0,1:T(8,128)S(1)}, f32[16,512]{0,1:T(8,128)S(1)}, u32[]{:S(2)}, u32[]{:S(2)}) %collective-permute-start.3) | collective-permute-done | bytes 32800 | tf_op jit(solution)/shard_map/ppermute | solution.py:27
  42.8 0.9 select_maximum_fusion.1.halo_ref
  43.8 12.9 %shard_map.102 = (f32[1024,128]{1,0:T(8,128)}, f32[1024,128]{1,0:T(8,128)}) custom-call(s32[6144]{0:T(1024)} %reshape.62.idx_ref, s32[1024]{0:T(1024)} %copy-done.7, f32[1024,128]{1,0:T(8,128)} %get-tuple-element.9.state_ref, f32[1024,128]{1,0:T(8,128)} %select_maximum_fusion.1.halo_ref, s32[6,1024,1]{2,1,0:T(8,128)} %copy.27.mask_ref, ...), custom_call_target="tpu_custom_call" | custom-call | flops 2617245696 | bytes 2908160 | tf_op jit(solution)/shard_map/pallas_call | solution.py:165
  56.7 1.2 slice_bitcast_fusion.4
  57.8 0.5 collective-permute-start.4
  58.4 1.7 %collective-permute-start.5 = (f32[16,512]{0,1:T(8,128)S(1)}, f32[16,512]{0,1:T(8,128)S(1)}, u32[]{:S(2)}, u32[]{:S(2)}) collective-permute-start(f32[16,512]{0,1:T(8,128)S(1)} %get-tuple-element.16), channel_id=1, source_target_pairs={{0,7},{1,0},{2,1},{3,2},{4,3},{5,4},{6,5},{7,6},{8,15},{9,8},{10,9... | collective-permute-start | bytes 98312 | tf_op jit(solution)/shard_map/ppermute | solution.py:27
  60.1 4.3 %collective-permute-done.4 = f32[16,512]{0,1:T(8,128)S(1)} collective-permute-done((f32[16,512]{0,1:T(8,128)S(1)}, f32[16,512]{0,1:T(8,128)S(1)}, u32[]{:S(2)}, u32[]{:S(2)}) %collective-permute-start.4) | collective-permute-done | bytes 32800 | tf_op jit(solution)/shard_map/ppermute | solution.py:27
  64.4 2.4 %collective-permute-done.5 = f32[16,512]{0,1:T(8,128)S(1)} collective-permute-done((f32[16,512]{0,1:T(8,128)S(1)}, f32[16,512]{0,1:T(8,128)S(1)}, u32[]{:S(2)}, u32[]{:S(2)}) %collective-permute-start.5) | collective-permute-done | bytes 32800 | tf_op jit(solution)/shard_map/ppermute | solution.py:27
  66.8 0.9 select_maximum_fusion.halo_ref
  67.8 11.9 %shard_map.103 = f32[1024,128]{1,0:T(8,128)} custom-call(s32[6144]{0:T(1024)} %reshape.62.idx_ref, s32[1024]{0:T(1024)} %copy-done.7, f32[1024,128]{1,0:T(8,128)} %get-tuple-element.11.state_ref, f32[1024,128]{1,0:T(8,128)} %select_maximum_fusion.halo_ref, s32[6,1024,1]{2,1,0:T(8,128)} %copy.27.mask_ref, bf16[6,128,128]{2,1,0:T(8,128)(2,1)} %constant.26.clone.pick_ref, ...), custom_call_target="tpu_custom_call" | custom-call | flops 2617245696 | bytes 2908160 | tf_op jit(solution)/shard_map/pallas_call | solution.py:165
  79.7 2.0 %add_select_fusion = f32[64,1024]{0,1:T(8,128)S(1)} fusion(f32[1024,128]{1,0:T(8,128)} %shard_map.103, f32[64,64]{1,0:T(8,128)S(1)} %copy-done, f32[1,64,1024]{2,1,0:T(8,128)S(1)} %copy-done.1, pred[]{:T(512)S(6)} %eq.7), kind=kOutput, calls=%fused_computation.10 | convolution fusion | flops 50528256 | bytes 802817 | tf_op jit(solution)/shard_map/dot_general | solution.py:31
  81.9 1.5 collective-permute-done.6
  83.4 0.4 fusion.1
  83.8 3.8 %collective-permute-start.7 = (f32[64,512]{0,1:T(8,128)S(1)}, f32[64,512]{0,1:T(8,128)S(1)}, u32[]{:S(2)}, u32[]{:S(2)}) collective-permute-start(f32[64,512]{0,1:T(8,128)S(1)} %fusion.1), channel_id=1, source_target_pairs={{0,16},{8,24},{16,32},{24,40},{32,48},{40,56},{48,64},{56,72},{64,... | collective-permute-start | bytes 393224 | tf_op jit(solution)/shard_map/ppermute | solution.py:22
  87.6 10.6 %collective-permute-done.7 = f32[64,512]{0,1:T(8,128)S(1)} collective-permute-done((f32[64,512]{0,1:T(8,128)S(1)}, f32[64,512]{0,1:T(8,128)S(1)}, u32[]{:S(2)}, u32[]{:S(2)}) %collective-permute-start.7) | collective-permute-done | bytes 131104 | tf_op jit(solution)/shard_map/ppermute | solution.py:22
  98.2 1.9 %collective-permute-start.8 = (f32[64,512]{0,1:T(8,128)S(1)}, f32[64,512]{0,1:T(8,128)S(1)}, u32[]{:S(2)}, u32[]{:S(2)}) collective-permute-start(f32[64,512]{0,1:T(8,128)S(1)} %collective-permute-done.7), channel_id=1, source_target_pairs={{0,16},{8,24},{16,32},{24,40},{32,48},{40,56},{48,64},{56,72},{64,... | collective-permute-start | bytes 393224 | tf_op jit(solution)/shard_map/ppermute | solution.py:22
  100.3 11.2 %collective-permute-done.8 = f32[64,512]{0,1:T(8,128)S(1)} collective-permute-done((f32[64,512]{0,1:T(8,128)S(1)}, f32[64,512]{0,1:T(8,128)S(1)}, u32[]{:S(2)}, u32[]{:S(2)}) %collective-permute-start.8) | collective-permute-done | bytes 131104 | tf_op jit(solution)/shard_map/ppermute | solution.py:22
  111.9 1.9 %collective-permute-start.9 = (f32[64,512]{0,1:T(8,128)S(1)}, f32[64,512]{0,1:T(8,128)S(1)}, u32[]{:S(2)}, u32[]{:S(2)}) collective-permute-start(f32[64,512]{0,1:T(8,128)S(1)} %convolution_add_fusion.4), channel_id=1, source_target_pairs={{0,32},{8,40},{16,48},{24,56},{32,64},{40,72},{48,80},{56,88},{64,... | collective-permute-start | bytes 393224 | tf_op jit(solution)/shard_map/ppermute | solution.py:22
  114.0 14.4 %collective-permute-done.9 = f32[64,512]{0,1:T(8,128)S(1)} collective-permute-done((f32[64,512]{0,1:T(8,128)S(1)}, f32[64,512]{0,1:T(8,128)S(1)}, u32[]{:S(2)}, u32[]{:S(2)}) %collective-permute-start.9) | collective-permute-done | bytes 131104 | tf_op jit(solution)/shard_map/ppermute | solution.py:22
  128.4 0.4 convolution_add_fusion.3
  128.8 1.9 %collective-permute-start.10 = (f32[64,512]{0,1:T(8,128)S(1)}, f32[64,512]{0,1:T(8,128)S(1)}, u32[]{:S(2)}, u32[]{:S(2)}) collective-permute-start(f32[64,512]{0,1:T(8,128)S(1)} %convolution_add_fusion.3), channel_id=1, source_target_pairs={{0,64},{8,72},{16,80},{24,88},{32,96},{40,104},{48,112},{56,120},{... | collective-permute-start | bytes 393224 | tf_op jit(solution)/shard_map/ppermute | solution.py:22
  130.9 16.5 %collective-permute-done.10 = f32[64,512]{0,1:T(8,128)S(1)} collective-permute-done((f32[64,512]{0,1:T(8,128)S(1)}, f32[64,512]{0,1:T(8,128)S(1)}, u32[]{:S(2)}, u32[]{:S(2)}) %collective-permute-start.10) | collective-permute-done | bytes 131104 | tf_op jit(solution)/shard_map/ppermute | solution.py:22
  147.7 1.3 collective-permute-start.11
  149.2 10.2 %collective-permute-done.11 = f32[64,512]{0,1:T(8,128)S(1)} collective-permute-done((f32[64,512]{0,1:T(8,128)S(1)}, f32[64,512]{0,1:T(8,128)S(1)}, u32[]{:S(2)}, u32[]{:S(2)}) %collective-permute-start.11) | collective-permute-done | bytes 131104 | tf_op jit(solution)/shard_map/ppermute | solution.py:22
  159.7 0.4 convolution_add_fusion
  160.1 0.4 select_bitcast_fusion
  160.6 1.5 collective-permute-done.12
  162.2 0.9 copy.39
  (32 shorter events, 2.4 us)
Async XLA Ops:
  0.0 79.7 %copy-start = (f32[64,64]{1,0:T(8,128)S(1)}, f32[64,64]{1,0:T(8,128)}, u32[]{:S(2)}) copy-start(f32[64,64]{1,0:T(8,128)} %param.13) | copy-start | bytes 49156
  0.0 9.5 %copy-start.6 = (f32[64,96]{1,0:T(8,128)S(1)}, f32[64,96]{1,0:T(8,128)}, u32[]{:S(2)}) copy-start(f32[64,96]{1,0:T(8,128)} %constant.27.clone) | copy-start | bytes 73732
  0.0 9.4 %copy-start.5 = (f32[64,64]{1,0:T(8,128)S(1)}, f32[64,64]{1,0:T(8,128)}, u32[]{:S(2)}) copy-start(f32[64,64]{1,0:T(8,128)} %param.11) | copy-start | bytes 49156
  0.0 9.5 %copy-start.2 = (f32[64,96]{1,0:T(8,128)S(1)}, f32[64,96]{1,0:T(8,128)}, u32[]{:S(2)}) copy-start(f32[64,96]{1,0:T(8,128)} %param.12) | copy-start | bytes 73732
  0.0 9.8 %copy-start.3 = (s32[6,1024]{1,0:T(8,128)S(1)}, s32[6,1024]{1,0:T(8,128)}, u32[]{:S(2)}) copy-start(s32[6,1024]{1,0:T(8,128)} %param.15) | copy-start | bytes 73732
  2.6 0.8 copy-start.7
  6.1 7.3 %copy-start.4 = (s32[6,1024]{1,0:T(8,128)S(1)}, s32[6,1024]{1,0:T(8,128)}, u32[]{:S(2)}) copy-start(s32[6,1024]{1,0:T(8,128)} %param.14) | copy-start | bytes 73732
  7.3 8.1 %collective-permute-start = (f32[16,512]{0,1:T(8,128)S(1)}, f32[16,512]{0,1:T(8,128)S(1)}, u32[]{:S(2)}, u32[]{:S(2)}) collective-permute-start(f32[16,512]{0,1:T(8,128)S(1)} %get-tuple-element.19), channel_id=1, source_target_pairs={{0,1},{1,2},{2,3},{3,4},{4,5},{5,6},{6,7},{7,0},{8,9},{9,10},{10,1... | collective-permute-start | bytes 98312 | tf_op jit(solution)/shard_map/ppermute | solution.py:27
  8.6 9.9 %collective-permute-start.1 = (f32[16,512]{0,1:T(8,128)S(1)}, f32[16,512]{0,1:T(8,128)S(1)}, u32[]{:S(2)}, u32[]{:S(2)}) collective-permute-start(f32[16,512]{0,1:T(8,128)S(1)} %get-tuple-element.20), channel_id=1, source_target_pairs={{0,7},{1,0},{2,1},{3,2},{4,3},{5,4},{6,5},{7,6},{8,15},{9,8},{10,9... | collective-permute-start | bytes 98312 | tf_op jit(solution)/shard_map/ppermute | solution.py:27
  33.4 6.9 %collective-permute-start.2 = (f32[16,512]{0,1:T(8,128)S(1)}, f32[16,512]{0,1:T(8,128)S(1)}, u32[]{:S(2)}, u32[]{:S(2)}) collective-permute-start(f32[16,512]{0,1:T(8,128)S(1)} %get-tuple-element.17), channel_id=1, source_target_pairs={{0,1},{1,2},{2,3},{3,4},{4,5},{5,6},{6,7},{7,0},{8,9},{9,10},{10,1... | collective-permute-start | bytes 98312 | tf_op jit(solution)/shard_map/ppermute | solution.py:27
  33.8 9.0 %collective-permute-start.3 = (f32[16,512]{0,1:T(8,128)S(1)}, f32[16,512]{0,1:T(8,128)S(1)}, u32[]{:S(2)}, u32[]{:S(2)}) collective-permute-start(f32[16,512]{0,1:T(8,128)S(1)} %get-tuple-element.18), channel_id=1, source_target_pairs={{0,7},{1,0},{2,1},{3,2},{4,3},{5,4},{6,5},{7,6},{8,15},{9,8},{10,9... | collective-permute-start | bytes 98312 | tf_op jit(solution)/shard_map/ppermute | solution.py:27
  57.8 6.6 %collective-permute-start.4 = (f32[16,512]{0,1:T(8,128)S(1)}, f32[16,512]{0,1:T(8,128)S(1)}, u32[]{:S(2)}, u32[]{:S(2)}) collective-permute-start(f32[16,512]{0,1:T(8,128)S(1)} %get-tuple-element.15), channel_id=1, source_target_pairs={{0,1},{1,2},{2,3},{3,4},{4,5},{5,6},{6,7},{7,0},{8,9},{9,10},{10,1... | collective-permute-start | bytes 98312 | tf_op jit(solution)/shard_map/ppermute | solution.py:27
  58.4 8.5 %collective-permute-start.5 = (f32[16,512]{0,1:T(8,128)S(1)}, f32[16,512]{0,1:T(8,128)S(1)}, u32[]{:S(2)}, u32[]{:S(2)}) collective-permute-start(f32[16,512]{0,1:T(8,128)S(1)} %get-tuple-element.16), channel_id=1, source_target_pairs={{0,7},{1,0},{2,1},{3,2},{4,3},{5,4},{6,5},{7,6},{8,15},{9,8},{10,9... | collective-permute-start | bytes 98312 | tf_op jit(solution)/shard_map/ppermute | solution.py:27
  67.7 11.9 %copy-start.1 = (f32[1,64,1024]{2,1,0:T(8,128)S(1)}, f32[1,64,1024]{2,1,0:T(8,128)}, u32[]{:S(2)}) copy-start(f32[1,64,1024]{2,1,0:T(8,128)} %param.10) | copy-start | bytes 786436
  81.8 1.6 collective-permute-start.6
  83.8 14.4 %collective-permute-start.7 = (f32[64,512]{0,1:T(8,128)S(1)}, f32[64,512]{0,1:T(8,128)S(1)}, u32[]{:S(2)}, u32[]{:S(2)}) collective-permute-start(f32[64,512]{0,1:T(8,128)S(1)} %fusion.1), channel_id=1, source_target_pairs={{0,16},{8,24},{16,32},{24,40},{32,48},{40,56},{48,64},{56,72},{64,... | collective-permute-start | bytes 393224 | tf_op jit(solution)/shard_map/ppermute | solution.py:22
  98.2 13.3 %collective-permute-start.8 = (f32[64,512]{0,1:T(8,128)S(1)}, f32[64,512]{0,1:T(8,128)S(1)}, u32[]{:S(2)}, u32[]{:S(2)}) collective-permute-start(f32[64,512]{0,1:T(8,128)S(1)} %collective-permute-done.7), channel_id=1, source_target_pairs={{0,16},{8,24},{16,32},{24,40},{32,48},{40,56},{48,64},{56,72},{64,... | collective-permute-start | bytes 393224 | tf_op jit(solution)/shard_map/ppermute | solution.py:22
  111.9 16.5 %collective-permute-start.9 = (f32[64,512]{0,1:T(8,128)S(1)}, f32[64,512]{0,1:T(8,128)S(1)}, u32[]{:S(2)}, u32[]{:S(2)}) collective-permute-start(f32[64,512]{0,1:T(8,128)S(1)} %convolution_add_fusion.4), channel_id=1, source_target_pairs={{0,32},{8,40},{16,48},{24,56},{32,64},{40,72},{48,80},{56,88},{64,... | collective-permute-start | bytes 393224 | tf_op jit(solution)/shard_map/ppermute | solution.py:22
  128.8 18.6 %collective-permute-start.10 = (f32[64,512]{0,1:T(8,128)S(1)}, f32[64,512]{0,1:T(8,128)S(1)}, u32[]{:S(2)}, u32[]{:S(2)}) collective-permute-start(f32[64,512]{0,1:T(8,128)S(1)} %convolution_add_fusion.3), channel_id=1, source_target_pairs={{0,64},{8,72},{16,80},{24,88},{32,96},{40,104},{48,112},{56,120},{... | collective-permute-start | bytes 393224 | tf_op jit(solution)/shard_map/ppermute | solution.py:22
  147.7 11.6 %collective-permute-start.11 = (f32[64,512]{0,1:T(8,128)S(1)}, f32[64,512]{0,1:T(8,128)S(1)}, u32[]{:S(2)}, u32[]{:S(2)}) collective-permute-start(f32[64,512]{0,1:T(8,128)S(1)} %convolution_add_fusion.2), channel_id=1, source_target_pairs={{0,128},{8,136},{16,144},{24,152},{32,160},{40,168},{48,176},{56,1... | collective-permute-start | bytes 393224 | tf_op jit(solution)/shard_map/ppermute | solution.py:22
  160.5 1.6 collective-permute-start.12

commit v14 on v13

--- a/solution.py
+++ b/solution.py
@@ -10,7 +10,7 @@
 
 STEPS = 3
 LANES = 128
-UNROLL = 128
+UNROLL = 256
 
 
 time_step = 0.05

time: 164 us -> 163 us (level)
  no operation moved by 1% of the time
where the time goes in v14:
time: 163 us
  waiting for transfers between devices  84.3 us (52%)
  Pallas kernels  40 us (25%)
  starting transfers between devices  17.5 us (11%)
  local copies, waits for them, and re-layouts  12.2 us (7%)
  matrix products  5.43 us (3%)
  other arithmetic  2.89 us (2%)
    ppermute x5, waiting for transfers between devices, from_behind(): return lax.ppermute(shard, axis, pairs)  62.9 us
    pallas_call x3, Pallas kernels, fused_step(): pl.pallas_call(functools.partial(fused_kernel, with_send), out_shape=tupl...  37.4 us
    ppermute x6, waiting for transfers between devices, ring(): lax.ppermute(shard, axis, [(i, (i + by) % peers) for i in range(peers)])  18.4 us
    ppermute x5, starting transfers between devices, from_behind(): return lax.ppermute(shard, axis, pairs)  10.9 us
    ppermute x6, starting transfers between devices, ring(): lax.ppermute(shard, axis, [(i, (i + by) % peers) for i in range(peers)])  6.49 us
    dot_general x13, matrix products, product(): jnp.dot(matrix, vector, precision=lax.Precision.HIGHEST, preferred_elemen...  5.43 us
    transpose x3, local copies, waits for them, and re-layouts, shards(): before = ring(sent[half:, 48:64].T, 'space', 1)  3.46 us
  transfers between devices with their start and end apart: 13, of which 13 were waited for; matrix products, arithmetic and copies ran while one was open for 3% of the time, Pallas kernels for 0%

profile of v14, /device:TPU:22, one launch (start us, length us, event | category | flops | bytes accessed | tf_op | source)
XLA Modules:
  0.0 162.7 jit_solution(5526504520974912800)
XLA Ops:
  0.0 1.2 copy.24
  1.2 0.7 constant_dynamic-update-slice_fusion
  1.9 0.7 constant_dynamic-update-slice_fusion.1.idx_ref.send_ref
  2.6 0.8 pad.32.table_ref.state_ref
  3.4 2.7 %shard_map.100 = f32[1024,128]{1,0:T(8,128)} custom-call(s32[1024]{0:T(1024)} %copy-done.7, f32[1024,128]{1,0:T(8,128)} %pad.32.table_ref.state_ref), custom_call_target="tpu_custom_call" | custom-call | tf_op jit(solution)/shard_map/pallas_call | solution.py:85
  6.1 1.2 slice_bitcast_fusion.2
  7.3 1.3 collective-permute-start
  8.6 0.8 collective-permute-start.1
  9.8 2.2 %copy.27.mask_ref = s32[6,1024,1]{2,1,0:T(8,128)} copy(s32[6,1024,1]{1,0,2:T(8,128)S(1)} %bitcast.84) | data formatting | bytes 49152 | tf_op jit(solution)/shard_map/broadcast_in_dim | solution.py:186
  12.0 0.8 pad.35.spread_ref
  12.8 0.6 pad.36.folded_ref
  13.5 0.6 reshape.62.idx_ref
  14.1 1.3 collective-permute-done
  15.4 3.0 %collective-permute-done.1 = f32[16,512]{0,1:T(8,128)S(1)} collective-permute-done((f32[16,512]{0,1:T(8,128)S(1)}, f32[16,512]{0,1:T(8,128)S(1)}, u32[]{:S(2)}, u32[]{:S(2)}) %collective-permute-start.1) | collective-permute-done | bytes 32800 | tf_op jit(solution)/shard_map/ppermute | solution.py:27
  18.4 0.9 select_maximum_fusion.2.halo_ref
  19.4 12.8 %shard_map.101 = (f32[1024,128]{1,0:T(8,128)}, f32[1024,128]{1,0:T(8,128)}) custom-call(s32[6144]{0:T(1024)} %reshape.62.idx_ref, s32[1024]{0:T(1024)} %copy-done.7, f32[1024,128]{1,0:T(8,128)} %pad.32.table_ref.state_ref, f32[1024,128]{1,0:T(8,128)} %select_maximum_fusion.2.halo_ref, s32[6,1024,1]{2,1,0:T(8,128)} %copy.27.mask_ref, ...), custom_call_target="tpu_custom_call" | custom-call | flops 2617245696 | bytes 2908160 | tf_op jit(solution)/shard_map/pallas_call | solution.py:165
  32.1 1.2 slice_bitcast_fusion.6
  33.7 1.7 %collective-permute-start.3 = (f32[16,512]{0,1:T(8,128)S(1)}, f32[16,512]{0,1:T(8,128)S(1)}, u32[]{:S(2)}, u32[]{:S(2)}) collective-permute-start(f32[16,512]{0,1:T(8,128)S(1)} %get-tuple-element.18), channel_id=1, source_target_pairs={{0,7},{1,0},{2,1},{3,2},{4,3},{5,4},{6,5},{7,6},{8,15},{9,8},{10,9... | collective-permute-start | bytes 98312 | tf_op jit(solution)/shard_map/ppermute | solution.py:27
  35.4 4.8 %collective-permute-done.2 = f32[16,512]{0,1:T(8,128)S(1)} collective-permute-done((f32[16,512]{0,1:T(8,128)S(1)}, f32[16,512]{0,1:T(8,128)S(1)}, u32[]{:S(2)}, u32[]{:S(2)}) %collective-permute-start.2) | collective-permute-done | bytes 32800 | tf_op jit(solution)/shard_map/ppermute | solution.py:27
  40.2 2.4 %collective-permute-done.3 = f32[16,512]{0,1:T(8,128)S(1)} collective-permute-done((f32[16,512]{0,1:T(8,128)S(1)}, f32[16,512]{0,1:T(8,128)S(1)}, u32[]{:S(2)}, u32[]{:S(2)}) %collective-permute-start.3) | collective-permute-done | bytes 32800 | tf_op jit(solution)/shard_map/ppermute | solution.py:27
  42.7 0.9 select_maximum_fusion.1.halo_ref
  43.6 12.8 %shard_map.102 = (f32[1024,128]{1,0:T(8,128)}, f32[1024,128]{1,0:T(8,128)}) custom-call(s32[6144]{0:T(1024)} %reshape.62.idx_ref, s32[1024]{0:T(1024)} %copy-done.7, f32[1024,128]{1,0:T(8,128)} %get-tuple-element.9.state_ref, f32[1024,128]{1,0:T(8,128)} %select_maximum_fusion.1.halo_ref, s32[6,1024,1]{2,1,0:T(8,128)} %copy.27.mask_ref, ...), custom_call_target="tpu_custom_call" | custom-call | flops 2617245696 | bytes 2908160 | tf_op jit(solution)/shard_map/pallas_call | solution.py:165
  56.4 1.2 slice_bitcast_fusion.4
  57.6 0.5 collective-permute-start.4
  58.1 1.7 %collective-permute-start.5 = (f32[16,512]{0,1:T(8,128)S(1)}, f32[16,512]{0,1:T(8,128)S(1)}, u32[]{:S(2)}, u32[]{:S(2)}) collective-permute-start(f32[16,512]{0,1:T(8,128)S(1)} %get-tuple-element.16), channel_id=1, source_target_pairs={{0,7},{1,0},{2,1},{3,2},{4,3},{5,4},{6,5},{7,6},{8,15},{9,8},{10,9... | collective-permute-start | bytes 98312 | tf_op jit(solution)/shard_map/ppermute | solution.py:27
  59.8 4.3 %collective-permute-done.4 = f32[16,512]{0,1:T(8,128)S(1)} collective-permute-done((f32[16,512]{0,1:T(8,128)S(1)}, f32[16,512]{0,1:T(8,128)S(1)}, u32[]{:S(2)}, u32[]{:S(2)}) %collective-permute-start.4) | collective-permute-done | bytes 32800 | tf_op jit(solution)/shard_map/ppermute | solution.py:27
  64.2 2.4 %collective-permute-done.5 = f32[16,512]{0,1:T(8,128)S(1)} collective-permute-done((f32[16,512]{0,1:T(8,128)S(1)}, f32[16,512]{0,1:T(8,128)S(1)}, u32[]{:S(2)}, u32[]{:S(2)}) %collective-permute-start.5) | collective-permute-done | bytes 32800 | tf_op jit(solution)/shard_map/ppermute | solution.py:27
  66.6 0.9 select_maximum_fusion.halo_ref
  67.5 11.8 %shard_map.103 = f32[1024,128]{1,0:T(8,128)} custom-call(s32[6144]{0:T(1024)} %reshape.62.idx_ref, s32[1024]{0:T(1024)} %copy-done.7, f32[1024,128]{1,0:T(8,128)} %get-tuple-element.11.state_ref, f32[1024,128]{1,0:T(8,128)} %select_maximum_fusion.halo_ref, s32[6,1024,1]{2,1,0:T(8,128)} %copy.27.mask_ref, bf16[6,128,128]{2,1,0:T(8,128)(2,1)} %constant.26.clone.pick_ref, ...), custom_call_target="tpu_custom_call" | custom-call | flops 2617245696 | bytes 2908160 | tf_op jit(solution)/shard_map/pallas_call | solution.py:165
  79.3 2.0 %add_select_fusion = f32[64,1024]{0,1:T(8,128)S(1)} fusion(f32[1024,128]{1,0:T(8,128)} %shard_map.103, f32[64,64]{1,0:T(8,128)S(1)} %copy-done, f32[1,64,1024]{2,1,0:T(8,128)S(1)} %copy-done.1, pred[]{:T(512)S(6)} %eq.7), kind=kOutput, calls=%fused_computation.10 | convolution fusion | flops 50528256 | bytes 802817 | tf_op jit(solution)/shard_map/dot_general | solution.py:31
  81.5 1.5 collective-permute-done.6
  83.0 0.4 fusion.1
  83.4 3.8 %collective-permute-start.7 = (f32[64,512]{0,1:T(8,128)S(1)}, f32[64,512]{0,1:T(8,128)S(1)}, u32[]{:S(2)}, u32[]{:S(2)}) collective-permute-start(f32[64,512]{0,1:T(8,128)S(1)} %fusion.1), channel_id=1, source_target_pairs={{0,16},{8,24},{16,32},{24,40},{32,48},{40,56},{48,64},{56,72},{64,... | collective-permute-start | bytes 393224 | tf_op jit(solution)/shard_map/ppermute | solution.py:22
  87.2 10.6 %collective-permute-done.7 = f32[64,512]{0,1:T(8,128)S(1)} collective-permute-done((f32[64,512]{0,1:T(8,128)S(1)}, f32[64,512]{0,1:T(8,128)S(1)}, u32[]{:S(2)}, u32[]{:S(2)}) %collective-permute-start.7) | collective-permute-done | bytes 131104 | tf_op jit(solution)/shard_map/ppermute | solution.py:22
  97.8 1.9 %collective-permute-start.8 = (f32[64,512]{0,1:T(8,128)S(1)}, f32[64,512]{0,1:T(8,128)S(1)}, u32[]{:S(2)}, u32[]{:S(2)}) collective-permute-start(f32[64,512]{0,1:T(8,128)S(1)} %collective-permute-done.7), channel_id=1, source_target_pairs={{0,16},{8,24},{16,32},{24,40},{32,48},{40,56},{48,64},{56,72},{64,... | collective-permute-start | bytes 393224 | tf_op jit(solution)/shard_map/ppermute | solution.py:22
  99.9 11.2 %collective-permute-done.8 = f32[64,512]{0,1:T(8,128)S(1)} collective-permute-done((f32[64,512]{0,1:T(8,128)S(1)}, f32[64,512]{0,1:T(8,128)S(1)}, u32[]{:S(2)}, u32[]{:S(2)}) %collective-permute-start.8) | collective-permute-done | bytes 131104 | tf_op jit(solution)/shard_map/ppermute | solution.py:22
  111.2 0.4 convolution_add_fusion.4
  111.5 1.9 %collective-permute-start.9 = (f32[64,512]{0,1:T(8,128)S(1)}, f32[64,512]{0,1:T(8,128)S(1)}, u32[]{:S(2)}, u32[]{:S(2)}) collective-permute-start(f32[64,512]{0,1:T(8,128)S(1)} %convolution_add_fusion.4), channel_id=1, source_target_pairs={{0,32},{8,40},{16,48},{24,56},{32,64},{40,72},{48,80},{56,88},{64,... | collective-permute-start | bytes 393224 | tf_op jit(solution)/shard_map/ppermute | solution.py:22
  113.6 14.4 %collective-permute-done.9 = f32[64,512]{0,1:T(8,128)S(1)} collective-permute-done((f32[64,512]{0,1:T(8,128)S(1)}, f32[64,512]{0,1:T(8,128)S(1)}, u32[]{:S(2)}, u32[]{:S(2)}) %collective-permute-start.9) | collective-permute-done | bytes 131104 | tf_op jit(solution)/shard_map/ppermute | solution.py:22
  128.1 0.4 convolution_add_fusion.3
  128.4 1.9 %collective-permute-start.10 = (f32[64,512]{0,1:T(8,128)S(1)}, f32[64,512]{0,1:T(8,128)S(1)}, u32[]{:S(2)}, u32[]{:S(2)}) collective-permute-start(f32[64,512]{0,1:T(8,128)S(1)} %convolution_add_fusion.3), channel_id=1, source_target_pairs={{0,64},{8,72},{16,80},{24,88},{32,96},{40,104},{48,112},{56,120},{... | collective-permute-start | bytes 393224 | tf_op jit(solution)/shard_map/ppermute | solution.py:22
  130.5 16.5 %collective-permute-done.10 = f32[64,512]{0,1:T(8,128)S(1)} collective-permute-done((f32[64,512]{0,1:T(8,128)S(1)}, f32[64,512]{0,1:T(8,128)S(1)}, u32[]{:S(2)}, u32[]{:S(2)}) %collective-permute-start.10) | collective-permute-done | bytes 131104 | tf_op jit(solution)/shard_map/ppermute | solution.py:22
  147.4 1.3 collective-permute-start.11
  148.8 10.2 %collective-permute-done.11 = f32[64,512]{0,1:T(8,128)S(1)} collective-permute-done((f32[64,512]{0,1:T(8,128)S(1)}, f32[64,512]{0,1:T(8,128)S(1)}, u32[]{:S(2)}, u32[]{:S(2)}) %collective-permute-start.11) | collective-permute-done | bytes 131104 | tf_op jit(solution)/shard_map/ppermute | solution.py:22
  159.4 0.4 convolution_add_fusion
  159.7 0.4 select_bitcast_fusion
  160.2 1.5 collective-permute-done.12
  161.8 0.9 copy.39
  (32 shorter events, 2.4 us)
Async XLA Ops:
  0.0 79.3 %copy-start = (f32[64,64]{1,0:T(8,128)S(1)}, f32[64,64]{1,0:T(8,128)}, u32[]{:S(2)}) copy-start(f32[64,64]{1,0:T(8,128)} %param.13) | copy-start | bytes 49156
  0.0 9.5 %copy-start.6 = (f32[64,96]{1,0:T(8,128)S(1)}, f32[64,96]{1,0:T(8,128)}, u32[]{:S(2)}) copy-start(f32[64,96]{1,0:T(8,128)} %constant.27.clone) | copy-start | bytes 73732
  0.0 9.4 %copy-start.5 = (f32[64,64]{1,0:T(8,128)S(1)}, f32[64,64]{1,0:T(8,128)}, u32[]{:S(2)}) copy-start(f32[64,64]{1,0:T(8,128)} %param.11) | copy-start | bytes 49156
  0.0 9.5 %copy-start.2 = (f32[64,96]{1,0:T(8,128)S(1)}, f32[64,96]{1,0:T(8,128)}, u32[]{:S(2)}) copy-start(f32[64,96]{1,0:T(8,128)} %param.12) | copy-start | bytes 73732
  0.0 9.8 %copy-start.3 = (s32[6,1024]{1,0:T(8,128)S(1)}, s32[6,1024]{1,0:T(8,128)}, u32[]{:S(2)}) copy-start(s32[6,1024]{1,0:T(8,128)} %param.15) | copy-start | bytes 73732
  2.6 0.8 copy-start.7
  6.1 7.3 %copy-start.4 = (s32[6,1024]{1,0:T(8,128)S(1)}, s32[6,1024]{1,0:T(8,128)}, u32[]{:S(2)}) copy-start(s32[6,1024]{1,0:T(8,128)} %param.14) | copy-start | bytes 73732
  7.3 8.1 %collective-permute-start = (f32[16,512]{0,1:T(8,128)S(1)}, f32[16,512]{0,1:T(8,128)S(1)}, u32[]{:S(2)}, u32[]{:S(2)}) collective-permute-start(f32[16,512]{0,1:T(8,128)S(1)} %get-tuple-element.19), channel_id=1, source_target_pairs={{0,1},{1,2},{2,3},{3,4},{4,5},{5,6},{6,7},{7,0},{8,9},{9,10},{10,1... | collective-permute-start | bytes 98312 | tf_op jit(solution)/shard_map/ppermute | solution.py:27
  8.6 9.9 %collective-permute-start.1 = (f32[16,512]{0,1:T(8,128)S(1)}, f32[16,512]{0,1:T(8,128)S(1)}, u32[]{:S(2)}, u32[]{:S(2)}) collective-permute-start(f32[16,512]{0,1:T(8,128)S(1)} %get-tuple-element.20), channel_id=1, source_target_pairs={{0,7},{1,0},{2,1},{3,2},{4,3},{5,4},{6,5},{7,6},{8,15},{9,8},{10,9... | collective-permute-start | bytes 98312 | tf_op jit(solution)/shard_map/ppermute | solution.py:27
  33.3 6.9 %collective-permute-start.2 = (f32[16,512]{0,1:T(8,128)S(1)}, f32[16,512]{0,1:T(8,128)S(1)}, u32[]{:S(2)}, u32[]{:S(2)}) collective-permute-start(f32[16,512]{0,1:T(8,128)S(1)} %get-tuple-element.17), channel_id=1, source_target_pairs={{0,1},{1,2},{2,3},{3,4},{4,5},{5,6},{6,7},{7,0},{8,9},{9,10},{10,1... | collective-permute-start | bytes 98312 | tf_op jit(solution)/shard_map/ppermute | solution.py:27
  33.7 9.0 %collective-permute-start.3 = (f32[16,512]{0,1:T(8,128)S(1)}, f32[16,512]{0,1:T(8,128)S(1)}, u32[]{:S(2)}, u32[]{:S(2)}) collective-permute-start(f32[16,512]{0,1:T(8,128)S(1)} %get-tuple-element.18), channel_id=1, source_target_pairs={{0,7},{1,0},{2,1},{3,2},{4,3},{5,4},{6,5},{7,6},{8,15},{9,8},{10,9... | collective-permute-start | bytes 98312 | tf_op jit(solution)/shard_map/ppermute | solution.py:27
  57.6 6.6 %collective-permute-start.4 = (f32[16,512]{0,1:T(8,128)S(1)}, f32[16,512]{0,1:T(8,128)S(1)}, u32[]{:S(2)}, u32[]{:S(2)}) collective-permute-start(f32[16,512]{0,1:T(8,128)S(1)} %get-tuple-element.15), channel_id=1, source_target_pairs={{0,1},{1,2},{2,3},{3,4},{4,5},{5,6},{6,7},{7,0},{8,9},{9,10},{10,1... | collective-permute-start | bytes 98312 | tf_op jit(solution)/shard_map/ppermute | solution.py:27
  58.1 8.5 %collective-permute-start.5 = (f32[16,512]{0,1:T(8,128)S(1)}, f32[16,512]{0,1:T(8,128)S(1)}, u32[]{:S(2)}, u32[]{:S(2)}) collective-permute-start(f32[16,512]{0,1:T(8,128)S(1)} %get-tuple-element.16), channel_id=1, source_target_pairs={{0,7},{1,0},{2,1},{3,2},{4,3},{5,4},{6,5},{7,6},{8,15},{9,8},{10,9... | collective-permute-start | bytes 98312 | tf_op jit(solution)/shard_map/ppermute | solution.py:27
  67.5 11.8 %copy-start.1 = (f32[1,64,1024]{2,1,0:T(8,128)S(1)}, f32[1,64,1024]{2,1,0:T(8,128)}, u32[]{:S(2)}) copy-start(f32[1,64,1024]{2,1,0:T(8,128)} %param.10) | copy-start | bytes 786436
  81.4 1.6 collective-permute-start.6
  83.4 14.4 %collective-permute-start.7 = (f32[64,512]{0,1:T(8,128)S(1)}, f32[64,512]{0,1:T(8,128)S(1)}, u32[]{:S(2)}, u32[]{:S(2)}) collective-permute-start(f32[64,512]{0,1:T(8,128)S(1)} %fusion.1), channel_id=1, source_target_pairs={{0,16},{8,24},{16,32},{24,40},{32,48},{40,56},{48,64},{56,72},{64,... | collective-permute-start | bytes 393224 | tf_op jit(solution)/shard_map/ppermute | solution.py:22
  97.8 13.3 %collective-permute-start.8 = (f32[64,512]{0,1:T(8,128)S(1)}, f32[64,512]{0,1:T(8,128)S(1)}, u32[]{:S(2)}, u32[]{:S(2)}) collective-permute-start(f32[64,512]{0,1:T(8,128)S(1)} %collective-permute-done.7), channel_id=1, source_target_pairs={{0,16},{8,24},{16,32},{24,40},{32,48},{40,56},{48,64},{56,72},{64,... | collective-permute-start | bytes 393224 | tf_op jit(solution)/shard_map/ppermute | solution.py:22
  111.5 16.5 %collective-permute-start.9 = (f32[64,512]{0,1:T(8,128)S(1)}, f32[64,512]{0,1:T(8,128)S(1)}, u32[]{:S(2)}, u32[]{:S(2)}) collective-permute-start(f32[64,512]{0,1:T(8,128)S(1)} %convolution_add_fusion.4), channel_id=1, source_target_pairs={{0,32},{8,40},{16,48},{24,56},{32,64},{40,72},{48,80},{56,88},{64,... | collective-permute-start | bytes 393224 | tf_op jit(solution)/shard_map/ppermute | solution.py:22
  128.4 18.6 %collective-permute-start.10 = (f32[64,512]{0,1:T(8,128)S(1)}, f32[64,512]{0,1:T(8,128)S(1)}, u32[]{:S(2)}, u32[]{:S(2)}) collective-permute-start(f32[64,512]{0,1:T(8,128)S(1)} %convolution_add_fusion.3), channel_id=1, source_target_pairs={{0,64},{8,72},{16,80},{24,88},{32,96},{40,104},{48,112},{56,120},{... | collective-permute-start | bytes 393224 | tf_op jit(solution)/shard_map/ppermute | solution.py:22
  147.4 11.6 %collective-permute-start.11 = (f32[64,512]{0,1:T(8,128)S(1)}, f32[64,512]{0,1:T(8,128)S(1)}, u32[]{:S(2)}, u32[]{:S(2)}) collective-permute-start(f32[64,512]{0,1:T(8,128)S(1)} %convolution_add_fusion.2), channel_id=1, source_target_pairs={{0,128},{8,136},{16,144},{24,152},{32,160},{40,168},{48,176},{56,1... | collective-permute-start | bytes 393224 | tf_op jit(solution)/shard_map/ppermute | solution.py:22
  160.1 1.6 collective-permute-start.12

commit v15 on v14

--- a/solution.py
+++ b/solution.py
@@ -112,10 +112,19 @@
     )
 
 
+def exact_nt_select(select, rows):
+    parts = split_three(rows)
+    dims = (((1,), (1,)), ((), ()))
+    take = lambda part: lax.dot_general(
+        select, part, dims, preferred_element_type=jnp.float32
+    )
+    return (take(parts[0]) + take(parts[1])) + take(parts[2])
+
+
 def fused_kernel(with_send, idx_ref, send_ref, state_ref, halo_ref, mask_ref, pick_ref,
-                 spread_ref, folded_ref, out_ref, *rest):
+                 spread_ref, folded_ref, pick_low_ref, pick_high_ref, out_ref, *rest):
     if with_send:
-        sent_ref, table, beside = rest
+        low_ref, high_ref, table, beside, sent_rows = rest
     else:
         table, beside = rest
     elements = state_ref.shape[0]
@@ -146,18 +155,31 @@
         def send(step, carry):
             for u in range(UNROLL):
                 row = step * UNROLL + u
-                sent_ref[pl.ds(row, 1), :] = out_ref[pl.ds(send_ref[row], 1), :]
+                sent_rows[pl.ds(row, 1), :] = out_ref[pl.ds(send_ref[row], 1), :]
             return carry
 
-        lax.fori_loop(0, sent_ref.shape[0] // UNROLL, send, 0)
+        lax.fori_loop(0, sent_rows.shape[0] // UNROLL, send, 0)
+        half = sent_rows.shape[0] // 2
+        low_ref[...] = exact_nt_select(pick_low_ref[...], sent_rows[0:half, :])
+        high_ref[...] = exact_nt_select(pick_high_ref[...], sent_rows[half:, :])
 
 
 def fused_step(state, halo, mask, pick, spread, folded, nbr_rows, send_rows, with_send):
     elements, lanes = state.shape
     block = jax.ShapeDtypeStruct((elements, lanes), state.dtype)
     shapes = [block]
+    scratch = [
+        pltpu.VMEM((elements + halo.shape[0], lanes), jnp.float32),
+        pltpu.VMEM((nbr_rows.shape[0], lanes), jnp.float32),
+    ]
     if with_send:
-        shapes.append(jax.ShapeDtypeStruct((send_rows.shape[0], lanes), state.dtype))
+        trace = jax.ShapeDtypeStruct((16, send_rows.shape[0] // 2), state.dtype)
+        shapes += [trace, trace]
+        scratch.append(pltpu.VMEM((send_rows.shape[0], lanes), jnp.float32))
+    lane = jnp.arange(lanes)[None, :]
+    spot = jnp.arange(16)[:, None]
+    pick_low = (lane == spot).astype(jnp.bfloat16)
+    pick_high = (lane == spot + 48).astype(jnp.bfloat16)
     vmem = pl.BlockSpec(memory_space=pltpu.VMEM)
     smem = pl.BlockSpec(memory_space=pltpu.SMEM)
     flops = 2 * 6 * 6 * elements * lanes * (2 * lanes) + 2 * 6 * elements * lanes * lanes
@@ -165,14 +187,11 @@
     result = pl.pallas_call(
         functools.partial(fused_kernel, with_send),
         out_shape=tuple(shapes),
-        in_specs=[smem, smem] + [vmem] * 6,
+        in_specs=[smem, smem] + [vmem] * 8,
         out_specs=tuple([vmem] * len(shapes)),
-        scratch_shapes=[
-            pltpu.VMEM((elements + halo.shape[0], lanes), jnp.float32),
-            pltpu.VMEM((nbr_rows.shape[0], lanes), jnp.float32),
-        ],
+        scratch_shapes=scratch,
         cost_estimate=pl.CostEstimate(flops=flops, transcendentals=0, bytes_accessed=moved),
-    )(nbr_rows, send_rows, state, halo, mask, pick, spread, folded)
+    )(nbr_rows, send_rows, state, halo, mask, pick, spread, folded, pick_low, pick_high)
     return result
 
 
@@ -193,9 +212,10 @@
     state = jnp.pad(state_start.T, ((0, 0), (0, LANES - state_start.shape[0])))
     sent = gather_rows(state, send_rows)
     half = send_low.shape[0]
+    low_trace, high_trace = sent[:half, 0:16].T, sent[half:, 48:64].T
     for step_id in range(STEPS):
-        before = ring(sent[half:, 48:64].T, "space", 1)
-        after = ring(sent[:half, 0:16].T, "space", -1)
+        before = ring(high_trace, "space", 1)
+        after = ring(low_trace, "space", -1)
         halo = jnp.concatenate(
             [
                 jnp.pad(before.T, ((0, 0), (48, LANES - 64))),
@@ -209,7 +229,7 @@
         )
         state = result[0]
         if with_send:
-            sent = result[1]
+            low_trace, high_trace = result[1], result[2]
     fine_state = state[:, : state_start.shape[0]].T
     coarse_start = product(coarse, state_start)
     defect = fine_state - coarse_start

time: 163 us -> 165 us (1.012)
    pallas_call x0 -> x4, local copies, waits for them, and re-layouts: none -> 3.51 us  [fused_step(): pl.pallas_call(functools.partial(fused_kernel, with_send), out_shape=tupl...]
    transpose x3 -> x1, local copies, waits for them, and re-layouts: 3.46 us -> 1.16 us  [shards(): low_trace, high_trace = (sent[:half, 0:16].T, sent[half:, 48:64].T)]
  transfers between devices with their start and end apart: 13 -> 13, of which waited for: 13 -> 13; matrix products, arithmetic and copies ran while one was open for 3% -> 5% of each run, Pallas kernels for 0% -> 0%
where the time goes in v15:
time: 165 us; the launch traced here: 164 us
  waiting for transfers between devices  83.2 us (50%)
  Pallas kernels  40 us (24%)
  starting transfers between devices  17.9 us (11%)
  local copies, waits for them, and re-layouts  13.4 us (8%)
  matrix products  5.43 us (3%)
  other arithmetic  3.56 us (2%)
    ppermute x5, waiting for transfers between devices, from_behind(): return lax.ppermute(shard, axis, pairs)  62.7 us
    pallas_call x3, Pallas kernels, fused_step(): pl.pallas_call(functools.partial(fused_kernel, with_send), out_shape=tupl...  37.3 us
    ppermute x6, waiting for transfers between devices, ring(): lax.ppermute(shard, axis, [(i, (i + by) % peers) for i in range(peers)])  17.5 us
    ppermute x5, starting transfers between devices, from_behind(): return lax.ppermute(shard, axis, pairs)  11.1 us
    ppermute x6, starting transfers between devices, ring(): lax.ppermute(shard, axis, [(i, (i + by) % peers) for i in range(peers)])  6.64 us
    dot_general x13, matrix products, product(): jnp.dot(matrix, vector, precision=lax.Precision.HIGHEST, preferred_elemen...  5.43 us
    pallas_call x4, local copies, waits for them, and re-layouts, fused_step(): pl.pallas_call(functools.partial(fused_kernel, with_send), out_shape=tupl...  3.51 us
  transfers between devices with their start and end apart: 13, of which 13 were waited for; matrix products, arithmetic and copies ran while one was open for 5% of the time, Pallas kernels for 0%

profile of v15, /device:TPU:22, one launch (start us, length us, event | category | flops | bytes accessed | tf_op | source)
XLA Modules:
  0.0 163.8 jit_solution(6030529840242379425)
XLA Ops:
  0.0 1.2 copy.28
  1.2 0.7 constant_dynamic-update-slice_fusion
  1.9 0.7 constant_dynamic-update-slice_fusion.1.idx_ref.send_ref
  2.6 0.8 pad.32.table_ref.state_ref
  3.4 2.7 %shard_map.100 = f32[1024,128]{1,0:T(8,128)} custom-call(s32[1024]{0:T(1024)} %copy-done.7, f32[1024,128]{1,0:T(8,128)} %pad.32.table_ref.state_ref), custom_call_target="tpu_custom_call" | custom-call | tf_op jit(solution)/shard_map/pallas_call | solution.py:85
  6.1 1.2 slice_bitcast_fusion.2
  7.3 1.3 collective-permute-start
  8.6 0.8 collective-permute-start.1
  9.7 0.7 fusion.6
  10.4 2.2 %copy.31.mask_ref = s32[6,1024,1]{2,1,0:T(8,128)} copy(s32[6,1024,1]{1,0,2:T(8,128)S(1)} %bitcast.76) | data formatting | bytes 49152 | tf_op jit(solution)/shard_map/broadcast_in_dim | solution.py:205
  12.7 0.8 pad.35.spread_ref
  13.5 0.6 pad.36.folded_ref
  14.1 0.6 reshape.67.idx_ref
  14.7 0.7 collective-permute-done
  15.4 3.0 %collective-permute-done.1 = f32[16,512]{0,1:T(8,128)S(1)} collective-permute-done((f32[16,512]{0,1:T(8,128)S(1)}, f32[16,512]{0,1:T(8,128)S(1)}, u32[]{:S(2)}, u32[]{:S(2)}) %collective-permute-start.1) | collective-permute-done | bytes 32800 | tf_op jit(solution)/shard_map/ppermute | solution.py:27
  18.4 0.9 select_maximum_fusion.2.halo_ref
  19.4 12.8 %shard_map.101 = (f32[1024,128]{1,0:T(8,128)}, f32[16,512]{1,0:T(8,128)}, f32[16,512]{1,0:T(8,128)}) custom-call(s32[6144]{0:T(1024)} %reshape.67.idx_ref, s32[1024]{0:T(1024)} %copy-done.7, f32[1024,128]{1,0:T(8,128)} %pad.32.table_ref.state_ref, f32[1024,128]{1,0:T(8,128)} %select_maximum_fusion.2.halo_ref, s32[6,1024,1]{2,1,0:T(8,128)} %copy.31.mask_ref, ...), custom_call_target="tpu_custom_call" | custom-call | flops 2617245696 | bytes 2908160 | tf_op jit(solution)/shard_map/pallas_call | solution.py:187
  32.1 0.9 copy.32
  33.4 0.9 copy.33
  34.3 2.0 %collective-permute-start.3 = (f32[16,512]{0,1:T(8,128)S(1)}, f32[16,512]{0,1:T(8,128)S(1)}, u32[]{:S(2)}, u32[]{:S(2)}) collective-permute-start(f32[16,512]{0,1:T(8,128)S(1)} %copy.33), channel_id=1, source_target_pairs={{0,7},{1,0},{2,1},{3,2},{4,3},{5,4},{6,5},{7,6},{8,15},{9,8},{10,9... | collective-permute-start | bytes 98312 | tf_op jit(solution)/shard_map/ppermute | solution.py:27
  36.3 3.7 %collective-permute-done.2 = f32[16,512]{0,1:T(8,128)S(1)} collective-permute-done((f32[16,512]{0,1:T(8,128)S(1)}, f32[16,512]{0,1:T(8,128)S(1)}, u32[]{:S(2)}, u32[]{:S(2)}) %collective-permute-start.2) | collective-permute-done | bytes 32800 | tf_op jit(solution)/shard_map/ppermute | solution.py:27
  39.9 3.6 %collective-permute-done.3 = f32[16,512]{0,1:T(8,128)S(1)} collective-permute-done((f32[16,512]{0,1:T(8,128)S(1)}, f32[16,512]{0,1:T(8,128)S(1)}, u32[]{:S(2)}, u32[]{:S(2)}) %collective-permute-start.3) | collective-permute-done | bytes 32800 | tf_op jit(solution)/shard_map/ppermute | solution.py:27
  43.5 0.9 select_maximum_fusion.1.halo_ref
  44.5 12.8 %shard_map.102 = (f32[1024,128]{1,0:T(8,128)}, f32[16,512]{1,0:T(8,128)}, f32[16,512]{1,0:T(8,128)}) custom-call(s32[6144]{0:T(1024)} %reshape.67.idx_ref, s32[1024]{0:T(1024)} %copy-done.7, f32[1024,128]{1,0:T(8,128)} %get-tuple-element.11.state_ref, f32[1024,128]{1,0:T(8,128)} %select_maximum_fusion.1.halo_ref, s32[6,1024,1]{2,1,0:T(8,128)} %copy.31.mask_ref, ...), custom_call_target="tpu_custom_call" | custom-call | flops 2617245696 | bytes 2908160 | tf_op jit(solution)/shard_map/pallas_call | solution.py:187
  57.2 0.9 copy.35
  58.2 0.9 copy.36
  59.1 2.1 %collective-permute-start.5 = (f32[16,512]{0,1:T(8,128)S(1)}, f32[16,512]{0,1:T(8,128)S(1)}, u32[]{:S(2)}, u32[]{:S(2)}) collective-permute-start(f32[16,512]{0,1:T(8,128)S(1)} %copy.36), channel_id=1, source_target_pairs={{0,7},{1,0},{2,1},{3,2},{4,3},{5,4},{6,5},{7,6},{8,15},{9,8},{10,9... | collective-permute-start | bytes 98312 | tf_op jit(solution)/shard_map/ppermute | solution.py:27
  61.2 3.4 %collective-permute-done.4 = f32[16,512]{0,1:T(8,128)S(1)} collective-permute-done((f32[16,512]{0,1:T(8,128)S(1)}, f32[16,512]{0,1:T(8,128)S(1)}, u32[]{:S(2)}, u32[]{:S(2)}) %collective-permute-start.4) | collective-permute-done | bytes 32800 | tf_op jit(solution)/shard_map/ppermute | solution.py:27
  64.5 3.1 %collective-permute-done.5 = f32[16,512]{0,1:T(8,128)S(1)} collective-permute-done((f32[16,512]{0,1:T(8,128)S(1)}, f32[16,512]{0,1:T(8,128)S(1)}, u32[]{:S(2)}, u32[]{:S(2)}) %collective-permute-start.5) | collective-permute-done | bytes 32800 | tf_op jit(solution)/shard_map/ppermute | solution.py:27
  67.6 0.9 select_maximum_fusion.halo_ref
  68.6 11.8 %shard_map.103 = f32[1024,128]{1,0:T(8,128)} custom-call(s32[6144]{0:T(1024)} %reshape.67.idx_ref, s32[1024]{0:T(1024)} %copy-done.7, f32[1024,128]{1,0:T(8,128)} %get-tuple-element.14.state_ref, f32[1024,128]{1,0:T(8,128)} %select_maximum_fusion.halo_ref, s32[6,1024,1]{2,1,0:T(8,128)} %copy.31.mask_ref, bf16[6,128,128]{2,1,0:T(8,128)(2,1)} %constant.28.clone.pick_ref, ...), custom_call_target="tpu_custom_call" | custom-call | flops 2617245696 | bytes 2908160 | tf_op jit(solution)/shard_map/pallas_call | solution.py:187
  80.4 2.0 %add_select_fusion = f32[64,1024]{0,1:T(8,128)S(1)} fusion(f32[1024,128]{1,0:T(8,128)} %shard_map.103, f32[64,64]{1,0:T(8,128)S(1)} %copy-done, f32[1,64,1024]{2,1,0:T(8,128)S(1)} %copy-done.1, pred[]{:T(512)S(6)} %eq.42), kind=kOutput, calls=%fused_computation.10 | convolution fusion | flops 50528256 | bytes 802817 | tf_op jit(solution)/shard_map/dot_general | solution.py:31
  82.6 1.5 collective-permute-done.6
  84.1 0.4 fusion.1
  84.5 3.8 %collective-permute-start.7 = (f32[64,512]{0,1:T(8,128)S(1)}, f32[64,512]{0,1:T(8,128)S(1)}, u32[]{:S(2)}, u32[]{:S(2)}) collective-permute-start(f32[64,512]{0,1:T(8,128)S(1)} %fusion.1), channel_id=1, source_target_pairs={{0,16},{8,24},{16,32},{24,40},{32,48},{40,56},{48,64},{56,72},{64,... | collective-permute-start | bytes 393224 | tf_op jit(solution)/shard_map/ppermute | solution.py:22
  88.3 10.6 %collective-permute-done.7 = f32[64,512]{0,1:T(8,128)S(1)} collective-permute-done((f32[64,512]{0,1:T(8,128)S(1)}, f32[64,512]{0,1:T(8,128)S(1)}, u32[]{:S(2)}, u32[]{:S(2)}) %collective-permute-start.7) | collective-permute-done | bytes 131104 | tf_op jit(solution)/shard_map/ppermute | solution.py:22
  98.9 1.9 %collective-permute-start.8 = (f32[64,512]{0,1:T(8,128)S(1)}, f32[64,512]{0,1:T(8,128)S(1)}, u32[]{:S(2)}, u32[]{:S(2)}) collective-permute-start(f32[64,512]{0,1:T(8,128)S(1)} %collective-permute-done.7), channel_id=1, source_target_pairs={{0,16},{8,24},{16,32},{24,40},{32,48},{40,56},{48,64},{56,72},{64,... | collective-permute-start | bytes 393224 | tf_op jit(solution)/shard_map/ppermute | solution.py:22
  101.0 11.2 %collective-permute-done.8 = f32[64,512]{0,1:T(8,128)S(1)} collective-permute-done((f32[64,512]{0,1:T(8,128)S(1)}, f32[64,512]{0,1:T(8,128)S(1)}, u32[]{:S(2)}, u32[]{:S(2)}) %collective-permute-start.8) | collective-permute-done | bytes 131104 | tf_op jit(solution)/shard_map/ppermute | solution.py:22
  112.6 2.1 %collective-permute-start.9 = (f32[64,512]{0,1:T(8,128)S(1)}, f32[64,512]{0,1:T(8,128)S(1)}, u32[]{:S(2)}, u32[]{:S(2)}) collective-permute-start(f32[64,512]{0,1:T(8,128)S(1)} %convolution_add_fusion.4), channel_id=1, source_target_pairs={{0,32},{8,40},{16,48},{24,56},{32,64},{40,72},{48,80},{56,88},{64,... | collective-permute-start | bytes 393224 | tf_op jit(solution)/shard_map/ppermute | solution.py:22
  114.9 14.2 %collective-permute-done.9 = f32[64,512]{0,1:T(8,128)S(1)} collective-permute-done((f32[64,512]{0,1:T(8,128)S(1)}, f32[64,512]{0,1:T(8,128)S(1)}, u32[]{:S(2)}, u32[]{:S(2)}) %collective-permute-start.9) | collective-permute-done | bytes 131104 | tf_op jit(solution)/shard_map/ppermute | solution.py:22
  129.1 0.4 convolution_add_fusion.3
  129.5 1.9 %collective-permute-start.10 = (f32[64,512]{0,1:T(8,128)S(1)}, f32[64,512]{0,1:T(8,128)S(1)}, u32[]{:S(2)}, u32[]{:S(2)}) collective-permute-start(f32[64,512]{0,1:T(8,128)S(1)} %convolution_add_fusion.3), channel_id=1, source_target_pairs={{0,64},{8,72},{16,80},{24,88},{32,96},{40,104},{48,112},{56,120},{... | collective-permute-start | bytes 393224 | tf_op jit(solution)/shard_map/ppermute | solution.py:22
  131.6 16.5 %collective-permute-done.10 = f32[64,512]{0,1:T(8,128)S(1)} collective-permute-done((f32[64,512]{0,1:T(8,128)S(1)}, f32[64,512]{0,1:T(8,128)S(1)}, u32[]{:S(2)}, u32[]{:S(2)}) %collective-permute-start.10) | collective-permute-done | bytes 131104 | tf_op jit(solution)/shard_map/ppermute | solution.py:22
  148.5 1.3 collective-permute-start.11
  149.9 10.2 %collective-permute-done.11 = f32[64,512]{0,1:T(8,128)S(1)} collective-permute-done((f32[64,512]{0,1:T(8,128)S(1)}, f32[64,512]{0,1:T(8,128)S(1)}, u32[]{:S(2)}, u32[]{:S(2)}) %collective-permute-start.11) | collective-permute-done | bytes 131104 | tf_op jit(solution)/shard_map/ppermute | solution.py:22
  160.8 0.4 select_bitcast_fusion
  161.3 1.5 collective-permute-done.12
  162.9 0.9 copy.47
  (36 shorter events, 3.2 us)
Async XLA Ops:
  0.0 80.4 %copy-start = (f32[64,64]{1,0:T(8,128)S(1)}, f32[64,64]{1,0:T(8,128)}, u32[]{:S(2)}) copy-start(f32[64,64]{1,0:T(8,128)} %param.13) | copy-start | bytes 49156
  0.0 9.5 %copy-start.6 = (f32[64,96]{1,0:T(8,128)S(1)}, f32[64,96]{1,0:T(8,128)}, u32[]{:S(2)}) copy-start(f32[64,96]{1,0:T(8,128)} %constant.29.clone) | copy-start | bytes 73732
  0.0 9.4 %copy-start.5 = (f32[64,64]{1,0:T(8,128)S(1)}, f32[64,64]{1,0:T(8,128)}, u32[]{:S(2)}) copy-start(f32[64,64]{1,0:T(8,128)} %param.11) | copy-start | bytes 49156
  0.0 9.5 %copy-start.2 = (f32[64,96]{1,0:T(8,128)S(1)}, f32[64,96]{1,0:T(8,128)}, u32[]{:S(2)}) copy-start(f32[64,96]{1,0:T(8,128)} %param.12) | copy-start | bytes 73732
  0.0 10.4 %copy-start.3 = (s32[6,1024]{1,0:T(8,128)S(1)}, s32[6,1024]{1,0:T(8,128)}, u32[]{:S(2)}) copy-start(s32[6,1024]{1,0:T(8,128)} %param.15) | copy-start | bytes 73732
  2.6 0.8 copy-start.7
  6.1 8.0 %copy-start.4 = (s32[6,1024]{1,0:T(8,128)S(1)}, s32[6,1024]{1,0:T(8,128)}, u32[]{:S(2)}) copy-start(s32[6,1024]{1,0:T(8,128)} %param.14) | copy-start | bytes 73732
  7.3 8.1 %collective-permute-start = (f32[16,512]{0,1:T(8,128)S(1)}, f32[16,512]{0,1:T(8,128)S(1)}, u32[]{:S(2)}, u32[]{:S(2)}) collective-permute-start(f32[16,512]{0,1:T(8,128)S(1)} %get-tuple-element.19), channel_id=1, source_target_pairs={{0,1},{1,2},{2,3},{3,4},{4,5},{5,6},{6,7},{7,0},{8,9},{9,10},{10,1... | collective-permute-start | bytes 98312 | tf_op jit(solution)/shard_map/ppermute | solution.py:27
  8.6 9.9 %collective-permute-start.1 = (f32[16,512]{0,1:T(8,128)S(1)}, f32[16,512]{0,1:T(8,128)S(1)}, u32[]{:S(2)}, u32[]{:S(2)}) collective-permute-start(f32[16,512]{0,1:T(8,128)S(1)} %get-tuple-element.20), channel_id=1, source_target_pairs={{0,7},{1,0},{2,1},{3,2},{4,3},{5,4},{6,5},{7,6},{8,15},{9,8},{10,9... | collective-permute-start | bytes 98312 | tf_op jit(solution)/shard_map/ppermute | solution.py:27
  33.0 6.9 %collective-permute-start.2 = (f32[16,512]{0,1:T(8,128)S(1)}, f32[16,512]{0,1:T(8,128)S(1)}, u32[]{:S(2)}, u32[]{:S(2)}) collective-permute-start(f32[16,512]{0,1:T(8,128)S(1)} %copy.32), channel_id=1, source_target_pairs={{0,1},{1,2},{2,3},{3,4},{4,5},{5,6},{6,7},{7,0},{8,9},{9,10},{10,1... | collective-permute-start | bytes 98312 | tf_op jit(solution)/shard_map/ppermute | solution.py:27
  34.3 9.3 %collective-permute-start.3 = (f32[16,512]{0,1:T(8,128)S(1)}, f32[16,512]{0,1:T(8,128)S(1)}, u32[]{:S(2)}, u32[]{:S(2)}) collective-permute-start(f32[16,512]{0,1:T(8,128)S(1)} %copy.33), channel_id=1, source_target_pairs={{0,7},{1,0},{2,1},{3,2},{4,3},{5,4},{6,5},{7,6},{8,15},{9,8},{10,9... | collective-permute-start | bytes 98312 | tf_op jit(solution)/shard_map/ppermute | solution.py:27
  58.1 6.4 %collective-permute-start.4 = (f32[16,512]{0,1:T(8,128)S(1)}, f32[16,512]{0,1:T(8,128)S(1)}, u32[]{:S(2)}, u32[]{:S(2)}) collective-permute-start(f32[16,512]{0,1:T(8,128)S(1)} %copy.35), channel_id=1, source_target_pairs={{0,1},{1,2},{2,3},{3,4},{4,5},{5,6},{6,7},{7,0},{8,9},{9,10},{10,1... | collective-permute-start | bytes 98312 | tf_op jit(solution)/shard_map/ppermute | solution.py:27
  59.1 8.6 %collective-permute-start.5 = (f32[16,512]{0,1:T(8,128)S(1)}, f32[16,512]{0,1:T(8,128)S(1)}, u32[]{:S(2)}, u32[]{:S(2)}) collective-permute-start(f32[16,512]{0,1:T(8,128)S(1)} %copy.36), channel_id=1, source_target_pairs={{0,7},{1,0},{2,1},{3,2},{4,3},{5,4},{6,5},{7,6},{8,15},{9,8},{10,9... | collective-permute-start | bytes 98312 | tf_op jit(solution)/shard_map/ppermute | solution.py:27
  68.6 11.8 %copy-start.1 = (f32[1,64,1024]{2,1,0:T(8,128)S(1)}, f32[1,64,1024]{2,1,0:T(8,128)}, u32[]{:S(2)}) copy-start(f32[1,64,1024]{2,1,0:T(8,128)} %param.10) | copy-start | bytes 786436
  82.5 1.6 collective-permute-start.6
  84.5 14.4 %collective-permute-start.7 = (f32[64,512]{0,1:T(8,128)S(1)}, f32[64,512]{0,1:T(8,128)S(1)}, u32[]{:S(2)}, u32[]{:S(2)}) collective-permute-start(f32[64,512]{0,1:T(8,128)S(1)} %fusion.1), channel_id=1, source_target_pairs={{0,16},{8,24},{16,32},{24,40},{32,48},{40,56},{48,64},{56,72},{64,... | collective-permute-start | bytes 393224 | tf_op jit(solution)/shard_map/ppermute | solution.py:22
  98.9 13.3 %collective-permute-start.8 = (f32[64,512]{0,1:T(8,128)S(1)}, f32[64,512]{0,1:T(8,128)S(1)}, u32[]{:S(2)}, u32[]{:S(2)}) collective-permute-start(f32[64,512]{0,1:T(8,128)S(1)} %collective-permute-done.7), channel_id=1, source_target_pairs={{0,16},{8,24},{16,32},{24,40},{32,48},{40,56},{48,64},{56,72},{64,... | collective-permute-start | bytes 393224 | tf_op jit(solution)/shard_map/ppermute | solution.py:22
  112.6 16.5 %collective-permute-start.9 = (f32[64,512]{0,1:T(8,128)S(1)}, f32[64,512]{0,1:T(8,128)S(1)}, u32[]{:S(2)}, u32[]{:S(2)}) collective-permute-start(f32[64,512]{0,1:T(8,128)S(1)} %convolution_add_fusion.4), channel_id=1, source_target_pairs={{0,32},{8,40},{16,48},{24,56},{32,64},{40,72},{48,80},{56,88},{64,... | collective-permute-start | bytes 393224 | tf_op jit(solution)/shard_map/ppermute | solution.py:22
  129.5 18.6 %collective-permute-start.10 = (f32[64,512]{0,1:T(8,128)S(1)}, f32[64,512]{0,1:T(8,128)S(1)}, u32[]{:S(2)}, u32[]{:S(2)}) collective-permute-start(f32[64,512]{0,1:T(8,128)S(1)} %convolution_add_fusion.3), channel_id=1, source_target_pairs={{0,64},{8,72},{16,80},{24,88},{32,96},{40,104},{48,112},{56,120},{... | collective-permute-start | bytes 393224 | tf_op jit(solution)/shard_map/ppermute | solution.py:22
  148.5 11.6 %collective-permute-start.11 = (f32[64,512]{0,1:T(8,128)S(1)}, f32[64,512]{0,1:T(8,128)S(1)}, u32[]{:S(2)}, u32[]{:S(2)}) collective-permute-start(f32[64,512]{0,1:T(8,128)S(1)} %convolution_add_fusion.2), channel_id=1, source_target_pairs={{0,128},{8,136},{16,144},{24,152},{32,160},{40,168},{48,176},{56,1... | collective-permute-start | bytes 393224 | tf_op jit(solution)/shard_map/ppermute | solution.py:22
  161.2 1.6 collective-permute-start.12

commit v16 on v14

--- a/solution.py
+++ b/solution.py
@@ -71,26 +71,30 @@
     return pick, own
 
 
-def gather_kernel(idx_ref, table_ref, out_ref):
-    def body(step, carry):
-        for u in range(UNROLL):
-            row = step * UNROLL + u
-            out_ref[pl.ds(row, 1), :] = table_ref[pl.ds(idx_ref[row], 1), :]
-        return carry
-
-    lax.fori_loop(0, out_ref.shape[0] // UNROLL, body, 0)
-
-
-def gather_rows(table, idx):
+def gather_kernel(*refs):
+    table_ref, out_ref = refs[-2:]
+    start = 0
+    for idx_ref in refs[:-2]:
+        def body(step, carry, idx_ref=idx_ref, start=start):
+            for u in range(UNROLL):
+                row = step * UNROLL + u
+                out_ref[pl.ds(start + row, 1), :] = table_ref[pl.ds(idx_ref[row], 1), :]
+            return carry
+
+        lax.fori_loop(0, idx_ref.shape[0] // UNROLL, body, 0)
+        start += idx_ref.shape[0]
+
+
+def gather_rows(table, *idx):
     return pl.pallas_call(
         gather_kernel,
-        out_shape=jax.ShapeDtypeStruct((idx.shape[0], table.shape[1]), table.dtype),
+        out_shape=jax.ShapeDtypeStruct((sum(part.shape[0] for part in idx), table.shape[1]), table.dtype),
         in_specs=[
-            pl.BlockSpec(memory_space=pltpu.SMEM),
+            *[pl.BlockSpec(memory_space=pltpu.SMEM)] * len(idx),
             pl.BlockSpec(memory_space=pltpu.VMEM),
         ],
         out_specs=pl.BlockSpec(memory_space=pltpu.VMEM),
-    )(idx, table)
+    )(*idx, table)
 
 
 def split_three(x):
@@ -112,7 +116,7 @@
     )
 
 
-def fused_kernel(with_send, idx_ref, send_ref, state_ref, halo_ref, mask_ref, pick_ref,
+def fused_kernel(with_send, idx_ref, send_low_ref, send_high_ref, state_ref, halo_ref, mask_ref, pick_ref,
                  spread_ref, folded_ref, out_ref, *rest):
     if with_send:
         sent_ref, table, beside = rest
@@ -143,21 +147,26 @@
     rate = own + lifted + state - state * state * state
     out_ref[...] = state + time_step * rate
     if with_send:
-        def send(step, carry):
-            for u in range(UNROLL):
-                row = step * UNROLL + u
-                sent_ref[pl.ds(row, 1), :] = out_ref[pl.ds(send_ref[row], 1), :]
-            return carry
-
-        lax.fori_loop(0, sent_ref.shape[0] // UNROLL, send, 0)
-
-
-def fused_step(state, halo, mask, pick, spread, folded, nbr_rows, send_rows, with_send):
+        start = 0
+        for send_ref in (send_low_ref, send_high_ref):
+            def send(step, carry, send_ref=send_ref, start=start):
+                for u in range(UNROLL):
+                    row = step * UNROLL + u
+                    sent_ref[pl.ds(start + row, 1), :] = out_ref[pl.ds(send_ref[row], 1), :]
+                return carry
+
+            lax.fori_loop(0, send_ref.shape[0] // UNROLL, send, 0)
+            start += send_ref.shape[0]
+
+
+def fused_step(state, halo, mask, pick, spread, folded, nbr_rows, send_low, send_high,
+               with_send):
     elements, lanes = state.shape
     block = jax.ShapeDtypeStruct((elements, lanes), state.dtype)
     shapes = [block]
     if with_send:
-        shapes.append(jax.ShapeDtypeStruct((send_rows.shape[0], lanes), state.dtype))
+        rows = send_low.shape[0] + send_high.shape[0]
+        shapes.append(jax.ShapeDtypeStruct((rows, lanes), state.dtype))
     vmem = pl.BlockSpec(memory_space=pltpu.VMEM)
     smem = pl.BlockSpec(memory_space=pltpu.SMEM)
     flops = 2 * 6 * 6 * elements * lanes * (2 * lanes) + 2 * 6 * elements * lanes * lanes
@@ -165,14 +174,14 @@
     result = pl.pallas_call(
         functools.partial(fused_kernel, with_send),
         out_shape=tuple(shapes),
-        in_specs=[smem, smem] + [vmem] * 6,
+        in_specs=[smem, smem, smem] + [vmem] * 6,
         out_specs=tuple([vmem] * len(shapes)),
         scratch_shapes=[
             pltpu.VMEM((elements + halo.shape[0], lanes), jnp.float32),
             pltpu.VMEM((nbr_rows.shape[0], lanes), jnp.float32),
         ],
         cost_estimate=pl.CostEstimate(flops=flops, transcendentals=0, bytes_accessed=moved),
-    )(nbr_rows, send_rows, state, halo, mask, pick, spread, folded)
+    )(nbr_rows, send_low, send_high, state, halo, mask, pick, spread, folded)
     return result
 
 
@@ -185,13 +194,12 @@
     folded = stiffness.T - product(own, lifting.T)
     mask = orientation[:, :, None]
     nbr_rows = neighbor.reshape(-1)
-    send_rows = jnp.concatenate([send_low, send_high])
     spread = jnp.pad(spread, ((0, 0), (0, 0), (0, LANES - 64)))
     folded = jnp.pad(folded, ((0, LANES - 64), (0, LANES - 64)))
 
     state_start = start_state[0]
     state = jnp.pad(state_start.T, ((0, 0), (0, LANES - state_start.shape[0])))
-    sent = gather_rows(state, send_rows)
+    sent = gather_rows(state, send_low, send_high)
     half = send_low.shape[0]
     for step_id in range(STEPS):
         before = ring(sent[half:, 48:64].T, "space", 1)
@@ -205,7 +213,7 @@
         )
         with_send = step_id < STEPS - 1
         result = fused_step(
-            state, halo, mask, pick, spread, folded, nbr_rows, send_rows, with_send
+            state, halo, mask, pick, spread, folded, nbr_rows, send_low, send_high, with_send
         )
         state = result[0]
         if with_send:

time: 163 us -> 162 us (level)
  no operation moved by 1% of the time
where the time goes in v16:
time: 162 us; the launch traced here: 161 us
  waiting for transfers between devices  84.1 us (52%)
  Pallas kernels  40.1 us (25%)
  starting transfers between devices  17.6 us (11%)
  local copies, waits for them, and re-layouts  10.8 us (7%)
  matrix products  5.43 us (3%)
  other arithmetic  2.89 us (2%)
    ppermute x5, waiting for transfers between devices, from_behind(): return lax.ppermute(shard, axis, pairs)  62.7 us
    pallas_call x3, Pallas kernels, fused_step(): pl.pallas_call(functools.partial(fused_kernel, with_send), out_shape=tupl...  37.4 us
    ppermute x6, waiting for transfers between devices, ring(): lax.ppermute(shard, axis, [(i, (i + by) % peers) for i in range(peers)])  18.4 us
    ppermute x5, starting transfers between devices, from_behind(): return lax.ppermute(shard, axis, pairs)  11.1 us
    ppermute x6, starting transfers between devices, ring(): lax.ppermute(shard, axis, [(i, (i + by) % peers) for i in range(peers)])  6.31 us
    dot_general x13, matrix products, product(): jnp.dot(matrix, vector, precision=lax.Precision.HIGHEST, preferred_elemen...  5.43 us
    transpose x3, local copies, waits for them, and re-layouts, shards(): before = ring(sent[half:, 48:64].T, 'space', 1)  3.46 us
  transfers between devices with their start and end apart: 13, of which 13 were waited for; matrix products, arithmetic and copies ran while one was open for 3% of the time, Pallas kernels for 0%

profile of v16, /device:TPU:22, one launch (start us, length us, event | category | flops | bytes accessed | tf_op | source)
XLA Modules:
  0.0 161.2 jit_solution(410933322058498292)
XLA Ops:
  0.0 1.2 copy.24
  1.2 0.8 pad.32.refs_2_.state_ref
  2.1 2.7 %shard_map.100 = f32[1024,128]{1,0:T(8,128)} custom-call(s32[512]{0:T(512)} %send_low_ref.5, s32[512]{0:T(512)} %send_high_ref.5, f32[1024,128]{1,0:T(8,128)} %pad.32.refs_2_.state_ref), custom_call_target="tpu_custom_call" | custom-call | tf_op jit(solution)/shard_map/pallas_call | solution.py:89
  4.7 1.2 slice_bitcast_fusion.2
  5.9 1.3 collective-permute-start
  7.2 0.8 collective-permute-start.1
  8.4 2.2 %copy.27.mask_ref = s32[6,1024,1]{2,1,0:T(8,128)} copy(s32[6,1024,1]{1,0,2:T(8,128)S(1)} %bitcast.84) | data formatting | bytes 49152 | tf_op jit(solution)/shard_map/broadcast_in_dim | solution.py:195
  10.6 0.8 pad.35.spread_ref
  11.4 0.6 pad.36.folded_ref
  12.1 0.6 reshape.62.idx_ref
  12.7 1.4 collective-permute-done
  14.0 3.0 %collective-permute-done.1 = f32[16,512]{0,1:T(8,128)S(1)} collective-permute-done((f32[16,512]{0,1:T(8,128)S(1)}, f32[16,512]{0,1:T(8,128)S(1)}, u32[]{:S(2)}, u32[]{:S(2)}) %collective-permute-start.1) | collective-permute-done | bytes 32800 | tf_op jit(solution)/shard_map/ppermute | solution.py:27
  17.1 0.9 select_maximum_fusion.2.halo_ref
  18.0 12.8 %shard_map.101 = (f32[1024,128]{1,0:T(8,128)}, f32[1024,128]{1,0:T(8,128)}) custom-call(s32[6144]{0:T(1024)} %reshape.62.idx_ref, s32[512]{0:T(512)} %send_low_ref.5, s32[512]{0:T(512)} %send_high_ref.5, f32[1024,128]{1,0:T(8,128)} %pad.32.refs_2_.state_ref, f32[1024,128]{1,0:T(8,128)} %select_maximum_fusion.2.halo_ref, s32[6,1024,1]{2,1,0:T(8,128)} %copy.27.mask_ref, ...), custom_call_target="tpu_custom_call" | custom-call | flops 2617245696 | bytes 2908160 | tf_op jit(solution)/shard_map/pallas_call | solution.py:174
  30.8 1.2 slice_bitcast_fusion.6
  31.9 0.4 collective-permute-start.2
  32.3 1.7 %collective-permute-start.3 = (f32[16,512]{0,1:T(8,128)S(1)}, f32[16,512]{0,1:T(8,128)S(1)}, u32[]{:S(2)}, u32[]{:S(2)}) collective-permute-start(f32[16,512]{0,1:T(8,128)S(1)} %get-tuple-element.18), channel_id=1, source_target_pairs={{0,7},{1,0},{2,1},{3,2},{4,3},{5,4},{6,5},{7,6},{8,15},{9,8},{10,9... | collective-permute-start | bytes 98312 | tf_op jit(solution)/shard_map/ppermute | solution.py:27
  34.0 4.8 %collective-permute-done.2 = f32[16,512]{0,1:T(8,128)S(1)} collective-permute-done((f32[16,512]{0,1:T(8,128)S(1)}, f32[16,512]{0,1:T(8,128)S(1)}, u32[]{:S(2)}, u32[]{:S(2)}) %collective-permute-start.2) | collective-permute-done | bytes 32800 | tf_op jit(solution)/shard_map/ppermute | solution.py:27
  38.9 2.4 %collective-permute-done.3 = f32[16,512]{0,1:T(8,128)S(1)} collective-permute-done((f32[16,512]{0,1:T(8,128)S(1)}, f32[16,512]{0,1:T(8,128)S(1)}, u32[]{:S(2)}, u32[]{:S(2)}) %collective-permute-start.3) | collective-permute-done | bytes 32800 | tf_op jit(solution)/shard_map/ppermute | solution.py:27
  41.3 0.9 select_maximum_fusion.1.halo_ref
  42.2 12.8 %shard_map.102 = (f32[1024,128]{1,0:T(8,128)}, f32[1024,128]{1,0:T(8,128)}) custom-call(s32[6144]{0:T(1024)} %reshape.62.idx_ref, s32[512]{0:T(512)} %send_low_ref.5, s32[512]{0:T(512)} %send_high_ref.5, f32[1024,128]{1,0:T(8,128)} %get-tuple-element.9.state_ref, f32[1024,128]{1,0:T(8,128)} %select_maximum_fusion.1.halo_ref, s32[6,1024,1]{2,1,0:T(8,128)} %copy.27.mask_ref, ...), custom_call_target="tpu_custom_call" | custom-call | flops 2617245696 | bytes 2908160 | tf_op jit(solution)/shard_map/pallas_call | solution.py:174
  55.0 1.2 slice_bitcast_fusion.4
  56.6 1.7 %collective-permute-start.5 = (f32[16,512]{0,1:T(8,128)S(1)}, f32[16,512]{0,1:T(8,128)S(1)}, u32[]{:S(2)}, u32[]{:S(2)}) collective-permute-start(f32[16,512]{0,1:T(8,128)S(1)} %get-tuple-element.16), channel_id=1, source_target_pairs={{0,7},{1,0},{2,1},{3,2},{4,3},{5,4},{6,5},{7,6},{8,15},{9,8},{10,9... | collective-permute-start | bytes 98312 | tf_op jit(solution)/shard_map/ppermute | solution.py:27
  58.3 4.3 %collective-permute-done.4 = f32[16,512]{0,1:T(8,128)S(1)} collective-permute-done((f32[16,512]{0,1:T(8,128)S(1)}, f32[16,512]{0,1:T(8,128)S(1)}, u32[]{:S(2)}, u32[]{:S(2)}) %collective-permute-start.4) | collective-permute-done | bytes 32800 | tf_op jit(solution)/shard_map/ppermute | solution.py:27
  62.6 2.4 %collective-permute-done.5 = f32[16,512]{0,1:T(8,128)S(1)} collective-permute-done((f32[16,512]{0,1:T(8,128)S(1)}, f32[16,512]{0,1:T(8,128)S(1)}, u32[]{:S(2)}, u32[]{:S(2)}) %collective-permute-start.5) | collective-permute-done | bytes 32800 | tf_op jit(solution)/shard_map/ppermute | solution.py:27
  65.0 0.9 select_maximum_fusion.halo_ref
  66.0 11.8 %shard_map.103 = f32[1024,128]{1,0:T(8,128)} custom-call(s32[6144]{0:T(1024)} %reshape.62.idx_ref, s32[512]{0:T(512)} %send_low_ref.5, s32[512]{0:T(512)} %send_high_ref.5, f32[1024,128]{1,0:T(8,128)} %get-tuple-element.11.state_ref, f32[1024,128]{1,0:T(8,128)} %select_maximum_fusion.halo_ref, s32[6,1024,1]{2,1,0:T(8,128)} %copy.27.mask_ref, ...), custom_call_target="tpu_custom_call" | custom-call | flops 2617245696 | bytes 2908160 | tf_op jit(solution)/shard_map/pallas_call | solution.py:174
  77.8 2.0 %add_select_fusion = f32[64,1024]{0,1:T(8,128)S(1)} fusion(f32[1024,128]{1,0:T(8,128)} %shard_map.103, f32[64,64]{1,0:T(8,128)S(1)} %copy-done, f32[1,64,1024]{2,1,0:T(8,128)S(1)} %copy-done.1, pred[]{:T(512)S(6)} %eq.7), kind=kOutput, calls=%fused_computation.10 | convolution fusion | flops 50528256 | bytes 802817 | tf_op jit(solution)/shard_map/dot_general | solution.py:31
  80.0 1.5 collective-permute-done.6
  81.5 0.4 fusion.1
  81.9 3.8 %collective-permute-start.7 = (f32[64,512]{0,1:T(8,128)S(1)}, f32[64,512]{0,1:T(8,128)S(1)}, u32[]{:S(2)}, u32[]{:S(2)}) collective-permute-start(f32[64,512]{0,1:T(8,128)S(1)} %fusion.1), channel_id=1, source_target_pairs={{0,16},{8,24},{16,32},{24,40},{32,48},{40,56},{48,64},{56,72},{64,... | collective-permute-start | bytes 393224 | tf_op jit(solution)/shard_map/ppermute | solution.py:22
  85.7 10.6 %collective-permute-done.7 = f32[64,512]{0,1:T(8,128)S(1)} collective-permute-done((f32[64,512]{0,1:T(8,128)S(1)}, f32[64,512]{0,1:T(8,128)S(1)}, u32[]{:S(2)}, u32[]{:S(2)}) %collective-permute-start.7) | collective-permute-done | bytes 131104 | tf_op jit(solution)/shard_map/ppermute | solution.py:22
  96.3 1.9 %collective-permute-start.8 = (f32[64,512]{0,1:T(8,128)S(1)}, f32[64,512]{0,1:T(8,128)S(1)}, u32[]{:S(2)}, u32[]{:S(2)}) collective-permute-start(f32[64,512]{0,1:T(8,128)S(1)} %collective-permute-done.7), channel_id=1, source_target_pairs={{0,16},{8,24},{16,32},{24,40},{32,48},{40,56},{48,64},{56,72},{64,... | collective-permute-start | bytes 393224 | tf_op jit(solution)/shard_map/ppermute | solution.py:22
  98.4 11.2 %collective-permute-done.8 = f32[64,512]{0,1:T(8,128)S(1)} collective-permute-done((f32[64,512]{0,1:T(8,128)S(1)}, f32[64,512]{0,1:T(8,128)S(1)}, u32[]{:S(2)}, u32[]{:S(2)}) %collective-permute-start.8) | collective-permute-done | bytes 131104 | tf_op jit(solution)/shard_map/ppermute | solution.py:22
  109.6 0.4 convolution_add_fusion.4
  110.0 2.1 %collective-permute-start.9 = (f32[64,512]{0,1:T(8,128)S(1)}, f32[64,512]{0,1:T(8,128)S(1)}, u32[]{:S(2)}, u32[]{:S(2)}) collective-permute-start(f32[64,512]{0,1:T(8,128)S(1)} %convolution_add_fusion.4), channel_id=1, source_target_pairs={{0,32},{8,40},{16,48},{24,56},{32,64},{40,72},{48,80},{56,88},{64,... | collective-permute-start | bytes 393224 | tf_op jit(solution)/shard_map/ppermute | solution.py:22
  112.3 14.2 %collective-permute-done.9 = f32[64,512]{0,1:T(8,128)S(1)} collective-permute-done((f32[64,512]{0,1:T(8,128)S(1)}, f32[64,512]{0,1:T(8,128)S(1)}, u32[]{:S(2)}, u32[]{:S(2)}) %collective-permute-start.9) | collective-permute-done | bytes 131104 | tf_op jit(solution)/shard_map/ppermute | solution.py:22
  126.5 0.4 convolution_add_fusion.3
  126.9 1.9 %collective-permute-start.10 = (f32[64,512]{0,1:T(8,128)S(1)}, f32[64,512]{0,1:T(8,128)S(1)}, u32[]{:S(2)}, u32[]{:S(2)}) collective-permute-start(f32[64,512]{0,1:T(8,128)S(1)} %convolution_add_fusion.3), channel_id=1, source_target_pairs={{0,64},{8,72},{16,80},{24,88},{32,96},{40,104},{48,112},{56,120},{... | collective-permute-start | bytes 393224 | tf_op jit(solution)/shard_map/ppermute | solution.py:22
  129.0 16.5 %collective-permute-done.10 = f32[64,512]{0,1:T(8,128)S(1)} collective-permute-done((f32[64,512]{0,1:T(8,128)S(1)}, f32[64,512]{0,1:T(8,128)S(1)}, u32[]{:S(2)}, u32[]{:S(2)}) %collective-permute-start.10) | collective-permute-done | bytes 131104 | tf_op jit(solution)/shard_map/ppermute | solution.py:22
  145.5 0.4 convolution_add_fusion.2
  145.8 1.3 collective-permute-start.11
  147.3 10.2 %collective-permute-done.11 = f32[64,512]{0,1:T(8,128)S(1)} collective-permute-done((f32[64,512]{0,1:T(8,128)S(1)}, f32[64,512]{0,1:T(8,128)S(1)}, u32[]{:S(2)}, u32[]{:S(2)}) %collective-permute-start.11) | collective-permute-done | bytes 131104 | tf_op jit(solution)/shard_map/ppermute | solution.py:22
  157.5 0.4 convolution_add_fusion.1
  157.8 0.4 convolution_add_fusion
  158.2 0.4 select_bitcast_fusion
  158.7 1.5 collective-permute-done.12
  160.3 0.9 copy.39
  (27 shorter events, 1.7 us)
Async XLA Ops:
  0.0 77.8 %copy-start = (f32[64,64]{1,0:T(8,128)S(1)}, f32[64,64]{1,0:T(8,128)}, u32[]{:S(2)}) copy-start(f32[64,64]{1,0:T(8,128)} %param.13) | copy-start | bytes 49156
  0.0 8.1 %copy-start.6 = (f32[64,96]{1,0:T(8,128)S(1)}, f32[64,96]{1,0:T(8,128)}, u32[]{:S(2)}) copy-start(f32[64,96]{1,0:T(8,128)} %constant.27.clone) | copy-start | bytes 73732
  0.0 8.0 %copy-start.5 = (f32[64,64]{1,0:T(8,128)S(1)}, f32[64,64]{1,0:T(8,128)}, u32[]{:S(2)}) copy-start(f32[64,64]{1,0:T(8,128)} %param.11) | copy-start | bytes 49156
  0.0 8.1 %copy-start.2 = (f32[64,96]{1,0:T(8,128)S(1)}, f32[64,96]{1,0:T(8,128)}, u32[]{:S(2)}) copy-start(f32[64,96]{1,0:T(8,128)} %param.12) | copy-start | bytes 73732
  0.0 8.4 %copy-start.3 = (s32[6,1024]{1,0:T(8,128)S(1)}, s32[6,1024]{1,0:T(8,128)}, u32[]{:S(2)}) copy-start(s32[6,1024]{1,0:T(8,128)} %param.15) | copy-start | bytes 73732
  4.7 7.3 %copy-start.4 = (s32[6,1024]{1,0:T(8,128)S(1)}, s32[6,1024]{1,0:T(8,128)}, u32[]{:S(2)}) copy-start(s32[6,1024]{1,0:T(8,128)} %param.14) | copy-start | bytes 73732
  5.9 8.1 %collective-permute-start = (f32[16,512]{0,1:T(8,128)S(1)}, f32[16,512]{0,1:T(8,128)S(1)}, u32[]{:S(2)}, u32[]{:S(2)}) collective-permute-start(f32[16,512]{0,1:T(8,128)S(1)} %get-tuple-element.19), channel_id=1, source_target_pairs={{0,1},{1,2},{2,3},{3,4},{4,5},{5,6},{6,7},{7,0},{8,9},{9,10},{10,1... | collective-permute-start | bytes 98312 | tf_op jit(solution)/shard_map/ppermute | solution.py:27
  7.2 9.9 %collective-permute-start.1 = (f32[16,512]{0,1:T(8,128)S(1)}, f32[16,512]{0,1:T(8,128)S(1)}, u32[]{:S(2)}, u32[]{:S(2)}) collective-permute-start(f32[16,512]{0,1:T(8,128)S(1)} %get-tuple-element.20), channel_id=1, source_target_pairs={{0,7},{1,0},{2,1},{3,2},{4,3},{5,4},{6,5},{7,6},{8,15},{9,8},{10,9... | collective-permute-start | bytes 98312 | tf_op jit(solution)/shard_map/ppermute | solution.py:27
  31.9 6.9 %collective-permute-start.2 = (f32[16,512]{0,1:T(8,128)S(1)}, f32[16,512]{0,1:T(8,128)S(1)}, u32[]{:S(2)}, u32[]{:S(2)}) collective-permute-start(f32[16,512]{0,1:T(8,128)S(1)} %get-tuple-element.17), channel_id=1, source_target_pairs={{0,1},{1,2},{2,3},{3,4},{4,5},{5,6},{6,7},{7,0},{8,9},{9,10},{10,1... | collective-permute-start | bytes 98312 | tf_op jit(solution)/shard_map/ppermute | solution.py:27
  32.3 9.0 %collective-permute-start.3 = (f32[16,512]{0,1:T(8,128)S(1)}, f32[16,512]{0,1:T(8,128)S(1)}, u32[]{:S(2)}, u32[]{:S(2)}) collective-permute-start(f32[16,512]{0,1:T(8,128)S(1)} %get-tuple-element.18), channel_id=1, source_target_pairs={{0,7},{1,0},{2,1},{3,2},{4,3},{5,4},{6,5},{7,6},{8,15},{9,8},{10,9... | collective-permute-start | bytes 98312 | tf_op jit(solution)/shard_map/ppermute | solution.py:27
  56.2 6.4 %collective-permute-start.4 = (f32[16,512]{0,1:T(8,128)S(1)}, f32[16,512]{0,1:T(8,128)S(1)}, u32[]{:S(2)}, u32[]{:S(2)}) collective-permute-start(f32[16,512]{0,1:T(8,128)S(1)} %get-tuple-element.15), channel_id=1, source_target_pairs={{0,1},{1,2},{2,3},{3,4},{4,5},{5,6},{6,7},{7,0},{8,9},{9,10},{10,1... | collective-permute-start | bytes 98312 | tf_op jit(solution)/shard_map/ppermute | solution.py:27
  56.6 8.5 %collective-permute-start.5 = (f32[16,512]{0,1:T(8,128)S(1)}, f32[16,512]{0,1:T(8,128)S(1)}, u32[]{:S(2)}, u32[]{:S(2)}) collective-permute-start(f32[16,512]{0,1:T(8,128)S(1)} %get-tuple-element.16), channel_id=1, source_target_pairs={{0,7},{1,0},{2,1},{3,2},{4,3},{5,4},{6,5},{7,6},{8,15},{9,8},{10,9... | collective-permute-start | bytes 98312 | tf_op jit(solution)/shard_map/ppermute | solution.py:27
  66.0 11.8 %copy-start.1 = (f32[1,64,1024]{2,1,0:T(8,128)S(1)}, f32[1,64,1024]{2,1,0:T(8,128)}, u32[]{:S(2)}) copy-start(f32[1,64,1024]{2,1,0:T(8,128)} %param.10) | copy-start | bytes 786436
  79.9 1.6 %collective-permute-start.6 = (f32[64,512]{0,1:T(8,128)S(1)}, f32[64,512]{0,1:T(8,128)S(1)}, u32[]{:S(2)}, u32[]{:S(2)}) collective-permute-start(f32[64,512]{0,1:T(8,128)S(1)} %slice_select_fusion), channel_id=1, source_target_pairs={{0,8},{8,0},{16,24},{24,16},{32,40},{40,32},{48,56},{56,48},{64,72... | collective-permute-start | bytes 393224 | tf_op jit(solution)/shard_map/ppermute | solution.py:235
  81.9 14.4 %collective-permute-start.7 = (f32[64,512]{0,1:T(8,128)S(1)}, f32[64,512]{0,1:T(8,128)S(1)}, u32[]{:S(2)}, u32[]{:S(2)}) collective-permute-start(f32[64,512]{0,1:T(8,128)S(1)} %fusion.1), channel_id=1, source_target_pairs={{0,16},{8,24},{16,32},{24,40},{32,48},{40,56},{48,64},{56,72},{64,... | collective-permute-start | bytes 393224 | tf_op jit(solution)/shard_map/ppermute | solution.py:22
  96.3 13.3 %collective-permute-start.8 = (f32[64,512]{0,1:T(8,128)S(1)}, f32[64,512]{0,1:T(8,128)S(1)}, u32[]{:S(2)}, u32[]{:S(2)}) collective-permute-start(f32[64,512]{0,1:T(8,128)S(1)} %collective-permute-done.7), channel_id=1, source_target_pairs={{0,16},{8,24},{16,32},{24,40},{32,48},{40,56},{48,64},{56,72},{64,... | collective-permute-start | bytes 393224 | tf_op jit(solution)/shard_map/ppermute | solution.py:22
  110.0 16.5 %collective-permute-start.9 = (f32[64,512]{0,1:T(8,128)S(1)}, f32[64,512]{0,1:T(8,128)S(1)}, u32[]{:S(2)}, u32[]{:S(2)}) collective-permute-start(f32[64,512]{0,1:T(8,128)S(1)} %convolution_add_fusion.4), channel_id=1, source_target_pairs={{0,32},{8,40},{16,48},{24,56},{32,64},{40,72},{48,80},{56,88},{64,... | collective-permute-start | bytes 393224 | tf_op jit(solution)/shard_map/ppermute | solution.py:22
  126.9 18.6 %collective-permute-start.10 = (f32[64,512]{0,1:T(8,128)S(1)}, f32[64,512]{0,1:T(8,128)S(1)}, u32[]{:S(2)}, u32[]{:S(2)}) collective-permute-start(f32[64,512]{0,1:T(8,128)S(1)} %convolution_add_fusion.3), channel_id=1, source_target_pairs={{0,64},{8,72},{16,80},{24,88},{32,96},{40,104},{48,112},{56,120},{... | collective-permute-start | bytes 393224 | tf_op jit(solution)/shard_map/ppermute | solution.py:22
  145.8 11.6 %collective-permute-start.11 = (f32[64,512]{0,1:T(8,128)S(1)}, f32[64,512]{0,1:T(8,128)S(1)}, u32[]{:S(2)}, u32[]{:S(2)}) collective-permute-start(f32[64,512]{0,1:T(8,128)S(1)} %convolution_add_fusion.2), channel_id=1, source_target_pairs={{0,128},{8,136},{16,144},{24,152},{32,160},{40,168},{48,176},{56,1... | collective-permute-start | bytes 393224 | tf_op jit(solution)/shard_map/ppermute | solution.py:22
  158.6 1.6 %collective-permute-start.12 = (f32[64,512]{0,1:T(8,128)S(1)}, f32[64,512]{0,1:T(8,128)S(1)}, u32[]{:S(2)}, u32[]{:S(2)}) collective-permute-start(f32[64,512]{0,1:T(8,128)S(1)} %get-tuple-element.14), channel_id=1, source_target_pairs={{0,8},{8,0},{16,24},{24,16},{32,40},{40,32},{48,56},{56,48},{64,72... | collective-permute-start | bytes 393224 | tf_op jit(solution)/shard_map/ppermute | solution.py:252

commit v17 on v16

--- a/solution.py
+++ b/solution.py
@@ -231,9 +231,10 @@
     core = lax.axis_index("tm") % 2
     partner = [(i, i ^ 1) for i in range(peers)]
     half = total.shape[1] // 2
-    low, high = total[:, :half], total[:, half:]
-    got = lax.ppermute(jnp.where(core == 0, high, low), "tm", partner)
-    keep = jnp.where(core == 0, low, high)
+    keep = lax.dynamic_slice_in_dim(total, core * half, half, axis=1)
+    got = lax.ppermute(
+        lax.dynamic_slice_in_dim(total, (1 - core) * half, half, axis=1), "tm", partner
+    )
     first = jnp.where(core == 0, keep, got)
     second = jnp.where(core == 0, got, keep)
     aggregate = product(coarse, first) + second
@@ -250,11 +251,8 @@
     end_second = product(square, before) + aggregate
     mine = jnp.where(core == 0, end_first, end_second)
     got = lax.ppermute(jnp.where(core == 0, end_second, end_first), "tm", partner)
-    return jnp.where(
-        core == 0,
-        jnp.concatenate([mine, got], axis=1),
-        jnp.concatenate([got, mine], axis=1),
-    )
+    whole = jnp.concatenate([got, got], axis=1)
+    return lax.dynamic_update_slice_in_dim(whole, mine, core * half, axis=1)
 
 
 def solution(mesh):

time: 162 us -> 162 us (level)
  no operation moved by 1% of the time
where the time goes in v17:
time: 162 us; the launch traced here: 161 us
  waiting for transfers between devices  84.1 us (52%)
  Pallas kernels  40.1 us (25%)
  starting transfers between devices  17.6 us (11%)
  local copies, waits for them, and re-layouts  10.8 us (7%)
  matrix products  5.45 us (3%)
  other arithmetic  2.87 us (2%)
    ppermute x5, waiting for transfers between devices, from_behind(): return lax.ppermute(shard, axis, pairs)  62.6 us
    pallas_call x3, Pallas kernels, fused_step(): pl.pallas_call(functools.partial(fused_kernel, with_send), out_shape=tupl...  37.4 us
    ppermute x6, waiting for transfers between devices, ring(): lax.ppermute(shard, axis, [(i, (i + by) % peers) for i in range(peers)])  18.4 us
    ppermute x5, starting transfers between devices, from_behind(): return lax.ppermute(shard, axis, pairs)  11.1 us
    ppermute x6, starting transfers between devices, ring(): lax.ppermute(shard, axis, [(i, (i + by) % peers) for i in range(peers)])  6.31 us
    dot_general x13, matrix products, product(): jnp.dot(matrix, vector, precision=lax.Precision.HIGHEST, preferred_elemen...  5.45 us
    transpose x3, local copies, waits for them, and re-layouts, shards(): before = ring(sent[half:, 48:64].T, 'space', 1)  3.46 us
  transfers between devices with their start and end apart: 13, of which 13 were waited for; matrix products, arithmetic and copies ran while one was open for 3% of the time, Pallas kernels for 0%

profile of v17, /device:TPU:22, one launch (start us, length us, event | category | flops | bytes accessed | tf_op | source)
XLA Modules:
  0.0 161.2 jit_solution(944901158004135804)
XLA Ops:
  0.0 1.2 copy.24
  1.2 0.8 pad.32.refs_2_.state_ref
  2.1 2.7 %shard_map.100 = f32[1024,128]{1,0:T(8,128)} custom-call(s32[512]{0:T(512)} %send_low_ref.5, s32[512]{0:T(512)} %send_high_ref.5, f32[1024,128]{1,0:T(8,128)} %pad.32.refs_2_.state_ref), custom_call_target="tpu_custom_call" | custom-call | tf_op jit(solution)/shard_map/pallas_call | solution.py:89
  4.7 1.2 slice_bitcast_fusion.2
  5.9 1.3 collective-permute-start
  7.2 0.8 collective-permute-start.1
  8.4 2.2 %copy.27.mask_ref = s32[6,1024,1]{2,1,0:T(8,128)} copy(s32[6,1024,1]{1,0,2:T(8,128)S(1)} %bitcast.82) | data formatting | bytes 49152 | tf_op jit(solution)/shard_map/broadcast_in_dim | solution.py:195
  10.6 0.8 pad.35.spread_ref
  11.4 0.6 pad.36.folded_ref
  12.1 0.6 reshape.9.idx_ref
  12.7 1.4 collective-permute-done
  14.0 3.0 %collective-permute-done.1 = f32[16,512]{0,1:T(8,128)S(1)} collective-permute-done((f32[16,512]{0,1:T(8,128)S(1)}, f32[16,512]{0,1:T(8,128)S(1)}, u32[]{:S(2)}, u32[]{:S(2)}) %collective-permute-start.1) | collective-permute-done | bytes 32800 | tf_op jit(solution)/shard_map/ppermute | solution.py:27
  17.1 0.9 select_maximum_fusion.2.halo_ref
  18.0 12.8 %shard_map.101 = (f32[1024,128]{1,0:T(8,128)}, f32[1024,128]{1,0:T(8,128)}) custom-call(s32[6144]{0:T(1024)} %reshape.9.idx_ref, s32[512]{0:T(512)} %send_low_ref.5, s32[512]{0:T(512)} %send_high_ref.5, f32[1024,128]{1,0:T(8,128)} %pad.32.refs_2_.state_ref, f32[1024,128]{1,0:T(8,128)} %select_maximum_fusion.2.halo_ref, s32[6,1024,1]{2,1,0:T(8,128)} %copy.27.mask_ref, ...), custom_call_target="tpu_custom_call" | custom-call | flops 2617245696 | bytes 2908160 | tf_op jit(solution)/shard_map/pallas_call | solution.py:174
  30.8 1.2 slice_bitcast_fusion.6
  31.9 0.4 collective-permute-start.2
  32.3 1.7 %collective-permute-start.3 = (f32[16,512]{0,1:T(8,128)S(1)}, f32[16,512]{0,1:T(8,128)S(1)}, u32[]{:S(2)}, u32[]{:S(2)}) collective-permute-start(f32[16,512]{0,1:T(8,128)S(1)} %get-tuple-element.16), channel_id=1, source_target_pairs={{0,7},{1,0},{2,1},{3,2},{4,3},{5,4},{6,5},{7,6},{8,15},{9,8},{10,9... | collective-permute-start | bytes 98312 | tf_op jit(solution)/shard_map/ppermute | solution.py:27
  34.0 4.8 %collective-permute-done.2 = f32[16,512]{0,1:T(8,128)S(1)} collective-permute-done((f32[16,512]{0,1:T(8,128)S(1)}, f32[16,512]{0,1:T(8,128)S(1)}, u32[]{:S(2)}, u32[]{:S(2)}) %collective-permute-start.2) | collective-permute-done | bytes 32800 | tf_op jit(solution)/shard_map/ppermute | solution.py:27
  38.9 2.4 %collective-permute-done.3 = f32[16,512]{0,1:T(8,128)S(1)} collective-permute-done((f32[16,512]{0,1:T(8,128)S(1)}, f32[16,512]{0,1:T(8,128)S(1)}, u32[]{:S(2)}, u32[]{:S(2)}) %collective-permute-start.3) | collective-permute-done | bytes 32800 | tf_op jit(solution)/shard_map/ppermute | solution.py:27
  41.3 0.9 select_maximum_fusion.1.halo_ref
  42.2 12.8 %shard_map.102 = (f32[1024,128]{1,0:T(8,128)}, f32[1024,128]{1,0:T(8,128)}) custom-call(s32[6144]{0:T(1024)} %reshape.9.idx_ref, s32[512]{0:T(512)} %send_low_ref.5, s32[512]{0:T(512)} %send_high_ref.5, f32[1024,128]{1,0:T(8,128)} %get-tuple-element.9.state_ref, f32[1024,128]{1,0:T(8,128)} %select_maximum_fusion.1.halo_ref, s32[6,1024,1]{2,1,0:T(8,128)} %copy.27.mask_ref, ...), custom_call_target="tpu_custom_call" | custom-call | flops 2617245696 | bytes 2908160 | tf_op jit(solution)/shard_map/pallas_call | solution.py:174
  55.0 1.2 slice_bitcast_fusion.4
  56.6 1.7 %collective-permute-start.5 = (f32[16,512]{0,1:T(8,128)S(1)}, f32[16,512]{0,1:T(8,128)S(1)}, u32[]{:S(2)}, u32[]{:S(2)}) collective-permute-start(f32[16,512]{0,1:T(8,128)S(1)} %get-tuple-element.14), channel_id=1, source_target_pairs={{0,7},{1,0},{2,1},{3,2},{4,3},{5,4},{6,5},{7,6},{8,15},{9,8},{10,9... | collective-permute-start | bytes 98312 | tf_op jit(solution)/shard_map/ppermute | solution.py:27
  58.3 4.3 %collective-permute-done.4 = f32[16,512]{0,1:T(8,128)S(1)} collective-permute-done((f32[16,512]{0,1:T(8,128)S(1)}, f32[16,512]{0,1:T(8,128)S(1)}, u32[]{:S(2)}, u32[]{:S(2)}) %collective-permute-start.4) | collective-permute-done | bytes 32800 | tf_op jit(solution)/shard_map/ppermute | solution.py:27
  62.6 2.4 %collective-permute-done.5 = f32[16,512]{0,1:T(8,128)S(1)} collective-permute-done((f32[16,512]{0,1:T(8,128)S(1)}, f32[16,512]{0,1:T(8,128)S(1)}, u32[]{:S(2)}, u32[]{:S(2)}) %collective-permute-start.5) | collective-permute-done | bytes 32800 | tf_op jit(solution)/shard_map/ppermute | solution.py:27
  65.0 0.9 select_maximum_fusion.halo_ref
  66.0 11.8 %shard_map.103 = f32[1024,128]{1,0:T(8,128)} custom-call(s32[6144]{0:T(1024)} %reshape.9.idx_ref, s32[512]{0:T(512)} %send_low_ref.5, s32[512]{0:T(512)} %send_high_ref.5, f32[1024,128]{1,0:T(8,128)} %get-tuple-element.11.state_ref, f32[1024,128]{1,0:T(8,128)} %select_maximum_fusion.halo_ref, s32[6,1024,1]{2,1,0:T(8,128)} %copy.27.mask_ref, ...), custom_call_target="tpu_custom_call" | custom-call | flops 2617245696 | bytes 2908160 | tf_op jit(solution)/shard_map/pallas_call | solution.py:174
  77.8 2.0 %add_select_fusion = f32[64,1024]{0,1:T(8,128)S(1)} fusion(f32[1024,128]{1,0:T(8,128)} %shard_map.103, f32[64,64]{1,0:T(8,128)S(1)} %copy-done, f32[1,64,1024]{2,1,0:T(8,128)S(1)} %copy-done.1, pred[]{:T(512)S(6)} %eq.12), kind=kOutput, calls=%fused_computation.10 | convolution fusion | flops 50528256 | bytes 802817 | tf_op jit(solution)/shard_map/dot_general | solution.py:31
  80.0 1.5 collective-permute-done.6
  81.5 0.4 fusion.1
  81.9 3.8 %collective-permute-start.7 = (f32[64,512]{0,1:T(8,128)S(1)}, f32[64,512]{0,1:T(8,128)S(1)}, u32[]{:S(2)}, u32[]{:S(2)}) collective-permute-start(f32[64,512]{0,1:T(8,128)S(1)} %fusion.1), channel_id=1, source_target_pairs={{0,16},{8,24},{16,32},{24,40},{32,48},{40,56},{48,64},{56,72},{64,... | collective-permute-start | bytes 393224 | tf_op jit(solution)/shard_map/ppermute | solution.py:22
  85.7 10.6 %collective-permute-done.7 = f32[64,512]{0,1:T(8,128)S(1)} collective-permute-done((f32[64,512]{0,1:T(8,128)S(1)}, f32[64,512]{0,1:T(8,128)S(1)}, u32[]{:S(2)}, u32[]{:S(2)}) %collective-permute-start.7) | collective-permute-done | bytes 131104 | tf_op jit(solution)/shard_map/ppermute | solution.py:22
  96.3 1.9 %collective-permute-start.8 = (f32[64,512]{0,1:T(8,128)S(1)}, f32[64,512]{0,1:T(8,128)S(1)}, u32[]{:S(2)}, u32[]{:S(2)}) collective-permute-start(f32[64,512]{0,1:T(8,128)S(1)} %collective-permute-done.7), channel_id=1, source_target_pairs={{0,16},{8,24},{16,32},{24,40},{32,48},{40,56},{48,64},{56,72},{64,... | collective-permute-start | bytes 393224 | tf_op jit(solution)/shard_map/ppermute | solution.py:22
  98.4 11.2 %collective-permute-done.8 = f32[64,512]{0,1:T(8,128)S(1)} collective-permute-done((f32[64,512]{0,1:T(8,128)S(1)}, f32[64,512]{0,1:T(8,128)S(1)}, u32[]{:S(2)}, u32[]{:S(2)}) %collective-permute-start.8) | collective-permute-done | bytes 131104 | tf_op jit(solution)/shard_map/ppermute | solution.py:22
  109.6 0.4 convolution_add_fusion.4
  110.0 2.1 %collective-permute-start.9 = (f32[64,512]{0,1:T(8,128)S(1)}, f32[64,512]{0,1:T(8,128)S(1)}, u32[]{:S(2)}, u32[]{:S(2)}) collective-permute-start(f32[64,512]{0,1:T(8,128)S(1)} %convolution_add_fusion.4), channel_id=1, source_target_pairs={{0,32},{8,40},{16,48},{24,56},{32,64},{40,72},{48,80},{56,88},{64,... | collective-permute-start | bytes 393224 | tf_op jit(solution)/shard_map/ppermute | solution.py:22
  112.3 14.2 %collective-permute-done.9 = f32[64,512]{0,1:T(8,128)S(1)} collective-permute-done((f32[64,512]{0,1:T(8,128)S(1)}, f32[64,512]{0,1:T(8,128)S(1)}, u32[]{:S(2)}, u32[]{:S(2)}) %collective-permute-start.9) | collective-permute-done | bytes 131104 | tf_op jit(solution)/shard_map/ppermute | solution.py:22
  126.5 0.4 convolution_add_fusion.3
  126.9 1.9 %collective-permute-start.10 = (f32[64,512]{0,1:T(8,128)S(1)}, f32[64,512]{0,1:T(8,128)S(1)}, u32[]{:S(2)}, u32[]{:S(2)}) collective-permute-start(f32[64,512]{0,1:T(8,128)S(1)} %convolution_add_fusion.3), channel_id=1, source_target_pairs={{0,64},{8,72},{16,80},{24,88},{32,96},{40,104},{48,112},{56,120},{... | collective-permute-start | bytes 393224 | tf_op jit(solution)/shard_map/ppermute | solution.py:22
  129.0 16.5 %collective-permute-done.10 = f32[64,512]{0,1:T(8,128)S(1)} collective-permute-done((f32[64,512]{0,1:T(8,128)S(1)}, f32[64,512]{0,1:T(8,128)S(1)}, u32[]{:S(2)}, u32[]{:S(2)}) %collective-permute-start.10) | collective-permute-done | bytes 131104 | tf_op jit(solution)/shard_map/ppermute | solution.py:22
  145.4 0.4 convolution_add_fusion.2
  145.8 1.3 collective-permute-start.11
  147.3 10.2 %collective-permute-done.11 = f32[64,512]{0,1:T(8,128)S(1)} collective-permute-done((f32[64,512]{0,1:T(8,128)S(1)}, f32[64,512]{0,1:T(8,128)S(1)}, u32[]{:S(2)}, u32[]{:S(2)}) %collective-permute-start.11) | collective-permute-done | bytes 131104 | tf_op jit(solution)/shard_map/ppermute | solution.py:22
  157.4 0.4 convolution_add_fusion.1
  157.8 0.4 fusion
  158.2 0.4 broadcast_select_fusion
  158.7 1.5 collective-permute-done.12
  160.3 0.9 copy.39
  (28 shorter events, 1.7 us)
Async XLA Ops:
  0.0 77.8 %copy-start = (f32[64,64]{1,0:T(8,128)S(1)}, f32[64,64]{1,0:T(8,128)}, u32[]{:S(2)}) copy-start(f32[64,64]{1,0:T(8,128)} %param.13) | copy-start | bytes 49156
  0.0 8.1 %copy-start.6 = (f32[64,96]{1,0:T(8,128)S(1)}, f32[64,96]{1,0:T(8,128)}, u32[]{:S(2)}) copy-start(f32[64,96]{1,0:T(8,128)} %constant.33.clone) | copy-start | bytes 73732
  0.0 8.0 %copy-start.5 = (f32[64,64]{1,0:T(8,128)S(1)}, f32[64,64]{1,0:T(8,128)}, u32[]{:S(2)}) copy-start(f32[64,64]{1,0:T(8,128)} %param.11) | copy-start | bytes 49156
  0.0 8.1 %copy-start.2 = (f32[64,96]{1,0:T(8,128)S(1)}, f32[64,96]{1,0:T(8,128)}, u32[]{:S(2)}) copy-start(f32[64,96]{1,0:T(8,128)} %param.12) | copy-start | bytes 73732
  0.0 8.4 %copy-start.3 = (s32[6,1024]{1,0:T(8,128)S(1)}, s32[6,1024]{1,0:T(8,128)}, u32[]{:S(2)}) copy-start(s32[6,1024]{1,0:T(8,128)} %param.15) | copy-start | bytes 73732
  4.7 7.3 %copy-start.4 = (s32[6,1024]{1,0:T(8,128)S(1)}, s32[6,1024]{1,0:T(8,128)}, u32[]{:S(2)}) copy-start(s32[6,1024]{1,0:T(8,128)} %param.14) | copy-start | bytes 73732
  5.9 8.1 %collective-permute-start = (f32[16,512]{0,1:T(8,128)S(1)}, f32[16,512]{0,1:T(8,128)S(1)}, u32[]{:S(2)}, u32[]{:S(2)}) collective-permute-start(f32[16,512]{0,1:T(8,128)S(1)} %get-tuple-element.17), channel_id=1, source_target_pairs={{0,1},{1,2},{2,3},{3,4},{4,5},{5,6},{6,7},{7,0},{8,9},{9,10},{10,1... | collective-permute-start | bytes 98312 | tf_op jit(solution)/shard_map/ppermute | solution.py:27
  7.2 9.9 %collective-permute-start.1 = (f32[16,512]{0,1:T(8,128)S(1)}, f32[16,512]{0,1:T(8,128)S(1)}, u32[]{:S(2)}, u32[]{:S(2)}) collective-permute-start(f32[16,512]{0,1:T(8,128)S(1)} %get-tuple-element.18), channel_id=1, source_target_pairs={{0,7},{1,0},{2,1},{3,2},{4,3},{5,4},{6,5},{7,6},{8,15},{9,8},{10,9... | collective-permute-start | bytes 98312 | tf_op jit(solution)/shard_map/ppermute | solution.py:27
  31.9 6.9 %collective-permute-start.2 = (f32[16,512]{0,1:T(8,128)S(1)}, f32[16,512]{0,1:T(8,128)S(1)}, u32[]{:S(2)}, u32[]{:S(2)}) collective-permute-start(f32[16,512]{0,1:T(8,128)S(1)} %get-tuple-element.15), channel_id=1, source_target_pairs={{0,1},{1,2},{2,3},{3,4},{4,5},{5,6},{6,7},{7,0},{8,9},{9,10},{10,1... | collective-permute-start | bytes 98312 | tf_op jit(solution)/shard_map/ppermute | solution.py:27
  32.3 9.0 %collective-permute-start.3 = (f32[16,512]{0,1:T(8,128)S(1)}, f32[16,512]{0,1:T(8,128)S(1)}, u32[]{:S(2)}, u32[]{:S(2)}) collective-permute-start(f32[16,512]{0,1:T(8,128)S(1)} %get-tuple-element.16), channel_id=1, source_target_pairs={{0,7},{1,0},{2,1},{3,2},{4,3},{5,4},{6,5},{7,6},{8,15},{9,8},{10,9... | collective-permute-start | bytes 98312 | tf_op jit(solution)/shard_map/ppermute | solution.py:27
  56.2 6.4 %collective-permute-start.4 = (f32[16,512]{0,1:T(8,128)S(1)}, f32[16,512]{0,1:T(8,128)S(1)}, u32[]{:S(2)}, u32[]{:S(2)}) collective-permute-start(f32[16,512]{0,1:T(8,128)S(1)} %get-tuple-element.13), channel_id=1, source_target_pairs={{0,1},{1,2},{2,3},{3,4},{4,5},{5,6},{6,7},{7,0},{8,9},{9,10},{10,1... | collective-permute-start | bytes 98312 | tf_op jit(solution)/shard_map/ppermute | solution.py:27
  56.6 8.5 %collective-permute-start.5 = (f32[16,512]{0,1:T(8,128)S(1)}, f32[16,512]{0,1:T(8,128)S(1)}, u32[]{:S(2)}, u32[]{:S(2)}) collective-permute-start(f32[16,512]{0,1:T(8,128)S(1)} %get-tuple-element.14), channel_id=1, source_target_pairs={{0,7},{1,0},{2,1},{3,2},{4,3},{5,4},{6,5},{7,6},{8,15},{9,8},{10,9... | collective-permute-start | bytes 98312 | tf_op jit(solution)/shard_map/ppermute | solution.py:27
  66.0 11.8 %copy-start.1 = (f32[1,64,1024]{2,1,0:T(8,128)S(1)}, f32[1,64,1024]{2,1,0:T(8,128)}, u32[]{:S(2)}) copy-start(f32[1,64,1024]{2,1,0:T(8,128)} %param.10) | copy-start | bytes 786436
  79.9 1.6 %collective-permute-start.6 = (f32[64,512]{0,1:T(8,128)S(1)}, f32[64,512]{0,1:T(8,128)S(1)}, u32[]{:S(2)}, u32[]{:S(2)}) collective-permute-start(f32[64,512]{0,1:T(8,128)S(1)} %constant_dynamic-slice_fusion), channel_id=1, source_target_pairs={{0,8},{8,0},{16,24},{24,16},{32,40},{40,32},{48,56},{56,48},{64,72... | collective-permute-start | bytes 393224 | tf_op jit(solution)/shard_map/ppermute | solution.py:235
  81.9 14.4 %collective-permute-start.7 = (f32[64,512]{0,1:T(8,128)S(1)}, f32[64,512]{0,1:T(8,128)S(1)}, u32[]{:S(2)}, u32[]{:S(2)}) collective-permute-start(f32[64,512]{0,1:T(8,128)S(1)} %fusion.1), channel_id=1, source_target_pairs={{0,16},{8,24},{16,32},{24,40},{32,48},{40,56},{48,64},{56,72},{64,... | collective-permute-start | bytes 393224 | tf_op jit(solution)/shard_map/ppermute | solution.py:22
  96.3 13.3 %collective-permute-start.8 = (f32[64,512]{0,1:T(8,128)S(1)}, f32[64,512]{0,1:T(8,128)S(1)}, u32[]{:S(2)}, u32[]{:S(2)}) collective-permute-start(f32[64,512]{0,1:T(8,128)S(1)} %collective-permute-done.7), channel_id=1, source_target_pairs={{0,16},{8,24},{16,32},{24,40},{32,48},{40,56},{48,64},{56,72},{64,... | collective-permute-start | bytes 393224 | tf_op jit(solution)/shard_map/ppermute | solution.py:22
  110.0 16.5 %collective-permute-start.9 = (f32[64,512]{0,1:T(8,128)S(1)}, f32[64,512]{0,1:T(8,128)S(1)}, u32[]{:S(2)}, u32[]{:S(2)}) collective-permute-start(f32[64,512]{0,1:T(8,128)S(1)} %convolution_add_fusion.4), channel_id=1, source_target_pairs={{0,32},{8,40},{16,48},{24,56},{32,64},{40,72},{48,80},{56,88},{64,... | collective-permute-start | bytes 393224 | tf_op jit(solution)/shard_map/ppermute | solution.py:22
  126.9 18.6 %collective-permute-start.10 = (f32[64,512]{0,1:T(8,128)S(1)}, f32[64,512]{0,1:T(8,128)S(1)}, u32[]{:S(2)}, u32[]{:S(2)}) collective-permute-start(f32[64,512]{0,1:T(8,128)S(1)} %convolution_add_fusion.3), channel_id=1, source_target_pairs={{0,64},{8,72},{16,80},{24,88},{32,96},{40,104},{48,112},{56,120},{... | collective-permute-start | bytes 393224 | tf_op jit(solution)/shard_map/ppermute | solution.py:22
  145.8 11.6 %collective-permute-start.11 = (f32[64,512]{0,1:T(8,128)S(1)}, f32[64,512]{0,1:T(8,128)S(1)}, u32[]{:S(2)}, u32[]{:S(2)}) collective-permute-start(f32[64,512]{0,1:T(8,128)S(1)} %convolution_add_fusion.2), channel_id=1, source_target_pairs={{0,128},{8,136},{16,144},{24,152},{32,160},{40,168},{48,176},{56,1... | collective-permute-start | bytes 393224 | tf_op jit(solution)/shard_map/ppermute | solution.py:22
  158.6 1.6 %collective-permute-start.12 = (f32[64,512]{0,1:T(8,128)S(1)}, f32[64,512]{0,1:T(8,128)S(1)}, u32[]{:S(2)}, u32[]{:S(2)}) collective-permute-start(f32[64,512]{0,1:T(8,128)S(1)} %get-tuple-element.19), channel_id=1, source_target_pairs={{0,8},{8,0},{16,24},{24,16},{32,40},{40,32},{48,56},{56,48},{64,72... | collective-permute-start | bytes 393224 | tf_op jit(solution)/shard_map/ppermute | solution.py:253

commit v18 on v16

--- a/solution.py
+++ b/solution.py
@@ -116,7 +116,8 @@
     )
 
 
-def fused_kernel(with_send, idx_ref, send_low_ref, send_high_ref, state_ref, halo_ref, mask_ref, pick_ref,
+def fused_kernel(with_send, idx_ref, send_low_ref, send_high_ref, state_ref, low_halo_ref,
+                 high_halo_ref, mask_ref, pick_ref,
                  spread_ref, folded_ref, out_ref, *rest):
     if with_send:
         sent_ref, table, beside = rest
@@ -124,7 +125,10 @@
         table, beside = rest
     elements = state_ref.shape[0]
     table[0:elements, :] = state_ref[...]
-    table[elements:, :] = halo_ref[...]
+    table[elements:, :] = jnp.zeros((table.shape[0] - elements, table.shape[1]), jnp.float32)
+    rows = low_halo_ref.shape[0]
+    table[elements:elements + rows, 48:64] = low_halo_ref[...]
+    table[elements + rows:, 0:16] = high_halo_ref[...]
 
     def gather(step, carry):
         for u in range(UNROLL):
@@ -174,14 +178,14 @@
     result = pl.pallas_call(
         functools.partial(fused_kernel, with_send),
         out_shape=tuple(shapes),
-        in_specs=[smem, smem, smem] + [vmem] * 6,
+        in_specs=[smem, smem, smem] + [vmem] * 7,
         out_specs=tuple([vmem] * len(shapes)),
         scratch_shapes=[
-            pltpu.VMEM((elements + halo.shape[0], lanes), jnp.float32),
+            pltpu.VMEM((elements + 2 * halo[0].shape[0], lanes), jnp.float32),
             pltpu.VMEM((nbr_rows.shape[0], lanes), jnp.float32),
         ],
         cost_estimate=pl.CostEstimate(flops=flops, transcendentals=0, bytes_accessed=moved),
-    )(nbr_rows, send_low, send_high, state, halo, mask, pick, spread, folded)
+    )(nbr_rows, send_low, send_high, state, halo[0], halo[1], mask, pick, spread, folded)
     return result
 
 
@@ -204,13 +208,7 @@
     for step_id in range(STEPS):
         before = ring(sent[half:, 48:64].T, "space", 1)
         after = ring(sent[:half, 0:16].T, "space", -1)
-        halo = jnp.concatenate(
-            [
-                jnp.pad(before.T, ((0, 0), (48, LANES - 64))),
-                jnp.pad(after.T, ((0, 0), (0, LANES - 16))),
-            ],
-            axis=0,
-        )
+        halo = (before.T, after.T)
         with_send = step_id < STEPS - 1
         result = fused_step(
             state, halo, mask, pick, spread, folded, nbr_rows, send_low, send_high, with_send

time: 162 us -> 161 us (level)
  other arithmetic: 2.89 us -> 0.09 us
  local copies, waits for them, and re-layouts: 10.8 us -> 12.9 us
    concatenate x3 -> x0, other arithmetic: 2.8 us -> none  [shards(): jnp.concatenate([jnp.pad(before.T, ((0, 0), (48, LANES - 64))), jnp.pad(a...]
    unnamed x17 -> x29, local copies, waits for them, and re-layouts: 1.37 us -> 3.47 us
where the time goes in v18:
time: 161 us
  waiting for transfers between devices  84.3 us (52%)
  Pallas kernels  40.2 us (25%)
  starting transfers between devices  17.6 us (11%)
  local copies, waits for them, and re-layouts  12.9 us (8%)
  matrix products  5.44 us (3%)
    ppermute x5, waiting for transfers between devices, from_behind(): return lax.ppermute(shard, axis, pairs)  62.7 us
    pallas_call x3, Pallas kernels, fused_step(): pl.pallas_call(functools.partial(fused_kernel, with_send), out_shape=tupl...  37.5 us
    ppermute x6, waiting for transfers between devices, ring(): lax.ppermute(shard, axis, [(i, (i + by) % peers) for i in range(peers)])  18.6 us
    ppermute x5, starting transfers between devices, from_behind(): return lax.ppermute(shard, axis, pairs)  11.1 us
    ppermute x6, starting transfers between devices, ring(): lax.ppermute(shard, axis, [(i, (i + by) % peers) for i in range(peers)])  6.31 us
    dot_general x13, matrix products, product(): jnp.dot(matrix, vector, precision=lax.Precision.HIGHEST, preferred_elemen...  5.44 us
    unnamed x29, local copies, waits for them, and re-layouts  3.47 us
    transpose x3, local copies, waits for them, and re-layouts, shards(): after = ring(sent[:half, 0:16].T, 'space', -1)  3.46 us
  transfers between devices with their start and end apart: 13, of which 13 were waited for; matrix products, arithmetic and copies ran while one was open for 3% of the time, Pallas kernels for 0%

profile of v18, /device:TPU:22, one launch (start us, length us, event | category | flops | bytes accessed | tf_op | source)
XLA Modules:
  0.0 160.8 jit_solution(5407623688874789678)
XLA Ops:
  0.0 1.2 copy.24
  1.2 0.9 pad.12.refs_2_.state_ref
  2.1 2.7 %shard_map.100 = f32[1024,128]{1,0:T(8,128)} custom-call(s32[512]{0:T(512)} %send_low_ref.5, s32[512]{0:T(512)} %send_high_ref.5, f32[1024,128]{1,0:T(8,128)} %pad.12.refs_2_.state_ref), custom_call_target="tpu_custom_call" | custom-call | tf_op jit(solution)/shard_map/pallas_call | solution.py:89
  4.8 1.2 slice_bitcast_fusion.1
  5.9 1.3 collective-permute-start
  7.2 0.8 collective-permute-start.1
  8.4 2.2 %copy.27.mask_ref = s32[6,1024,1]{2,1,0:T(8,128)} copy(s32[6,1024,1]{1,0,2:T(8,128)S(1)} %bitcast.78) | data formatting | bytes 49152 | tf_op jit(solution)/shard_map/broadcast_in_dim | solution.py:199
  10.7 0.8 pad.13.spread_ref
  11.4 0.6 pad.14.folded_ref
  12.1 0.6 reshape.62.idx_ref
  12.7 1.4 collective-permute-done
  14.1 3.0 %collective-permute-done.1 = f32[16,512]{0,1:T(8,128)S(1)} collective-permute-done((f32[16,512]{0,1:T(8,128)S(1)}, f32[16,512]{0,1:T(8,128)S(1)}, u32[]{:S(2)}, u32[]{:S(2)}) %collective-permute-start.1) | collective-permute-done | bytes 32800 | tf_op jit(solution)/shard_map/ppermute | solution.py:27
  17.1 0.7 copy-done.10
  17.8 12.8 %shard_map.101 = (f32[1024,128]{1,0:T(8,128)}, f32[1024,128]{1,0:T(8,128)}) custom-call(s32[6144]{0:T(1024)} %reshape.62.idx_ref, s32[512]{0:T(512)} %send_low_ref.5, s32[512]{0:T(512)} %send_high_ref.5, f32[1024,128]{1,0:T(8,128)} %pad.12.refs_2_.state_ref, f32[512,16]{1,0:T(8,128)} %bitcast.81, f32[512,16]{1,0:T(8,128)} %bitcast.82, ...), custom_call_target="tpu_custom_call" | custom-call | flops 2617245696 | bytes 2908160 | tf_op jit(solution)/shard_map/pallas_call | solution.py:178
  30.6 1.2 slice_bitcast_fusion.5
  31.8 0.4 collective-permute-start.2
  32.2 1.7 %collective-permute-start.3 = (f32[16,512]{0,1:T(8,128)S(1)}, f32[16,512]{0,1:T(8,128)S(1)}, u32[]{:S(2)}, u32[]{:S(2)}) collective-permute-start(f32[16,512]{0,1:T(8,128)S(1)} %get-tuple-element.17), channel_id=1, source_target_pairs={{0,7},{1,0},{2,1},{3,2},{4,3},{5,4},{6,5},{7,6},{8,15},{9,8},{10,9... | collective-permute-start | bytes 98312 | tf_op jit(solution)/shard_map/ppermute | solution.py:27
  33.9 4.8 %collective-permute-done.2 = f32[16,512]{0,1:T(8,128)S(1)} collective-permute-done((f32[16,512]{0,1:T(8,128)S(1)}, f32[16,512]{0,1:T(8,128)S(1)}, u32[]{:S(2)}, u32[]{:S(2)}) %collective-permute-start.2) | collective-permute-done | bytes 32800 | tf_op jit(solution)/shard_map/ppermute | solution.py:27
  38.7 2.5 %collective-permute-done.3 = f32[16,512]{0,1:T(8,128)S(1)} collective-permute-done((f32[16,512]{0,1:T(8,128)S(1)}, f32[16,512]{0,1:T(8,128)S(1)}, u32[]{:S(2)}, u32[]{:S(2)}) %collective-permute-start.3) | collective-permute-done | bytes 32800 | tf_op jit(solution)/shard_map/ppermute | solution.py:27
  41.2 0.7 copy-done.12
  41.9 12.9 %shard_map.102 = (f32[1024,128]{1,0:T(8,128)}, f32[1024,128]{1,0:T(8,128)}) custom-call(s32[6144]{0:T(1024)} %reshape.62.idx_ref, s32[512]{0:T(512)} %send_low_ref.5, s32[512]{0:T(512)} %send_high_ref.5, f32[1024,128]{1,0:T(8,128)} %get-tuple-element.9.state_ref, f32[512,16]{1,0:T(8,128)} %bitcast.83, f32[512,16]{1,0:T(8,128)} %bitcast.84, ...), custom_call_target="tpu_custom_call" | custom-call | flops 2617245696 | bytes 2908160 | tf_op jit(solution)/shard_map/pallas_call | solution.py:178
  54.8 1.2 slice_bitcast_fusion.3
  55.9 0.4 collective-permute-start.4
  56.4 1.7 %collective-permute-start.5 = (f32[16,512]{0,1:T(8,128)S(1)}, f32[16,512]{0,1:T(8,128)S(1)}, u32[]{:S(2)}, u32[]{:S(2)}) collective-permute-start(f32[16,512]{0,1:T(8,128)S(1)} %get-tuple-element.15), channel_id=1, source_target_pairs={{0,7},{1,0},{2,1},{3,2},{4,3},{5,4},{6,5},{7,6},{8,15},{9,8},{10,9... | collective-permute-start | bytes 98312 | tf_op jit(solution)/shard_map/ppermute | solution.py:27
  58.0 4.3 %collective-permute-done.4 = f32[16,512]{0,1:T(8,128)S(1)} collective-permute-done((f32[16,512]{0,1:T(8,128)S(1)}, f32[16,512]{0,1:T(8,128)S(1)}, u32[]{:S(2)}, u32[]{:S(2)}) %collective-permute-start.4) | collective-permute-done | bytes 32800 | tf_op jit(solution)/shard_map/ppermute | solution.py:27
  62.4 2.5 %collective-permute-done.5 = f32[16,512]{0,1:T(8,128)S(1)} collective-permute-done((f32[16,512]{0,1:T(8,128)S(1)}, f32[16,512]{0,1:T(8,128)S(1)}, u32[]{:S(2)}, u32[]{:S(2)}) %collective-permute-start.5) | collective-permute-done | bytes 32800 | tf_op jit(solution)/shard_map/ppermute | solution.py:27
  64.9 0.7 copy-done.8
  65.6 11.9 %shard_map.103 = f32[1024,128]{1,0:T(8,128)} custom-call(s32[6144]{0:T(1024)} %reshape.62.idx_ref, s32[512]{0:T(512)} %send_low_ref.5, s32[512]{0:T(512)} %send_high_ref.5, f32[1024,128]{1,0:T(8,128)} %get-tuple-element.11.state_ref, f32[512,16]{1,0:T(8,128)} %bitcast.79, f32[512,16]{1,0:T(8,128)} %bitcast.80, s32[6,1024,1]{2,1,0:T(8,128)} %copy.27.mask_ref, ...), custom_call_target="tpu_custom_call" | custom-call | flops 2617245696 | bytes 2908160 | tf_op jit(solution)/shard_map/pallas_call | solution.py:178
  77.4 2.0 %add_select_fusion = f32[64,1024]{0,1:T(8,128)S(1)} fusion(f32[1024,128]{1,0:T(8,128)} %shard_map.103, f32[64,64]{1,0:T(8,128)S(1)} %copy-done, f32[1,64,1024]{2,1,0:T(8,128)S(1)} %copy-done.1, pred[]{:T(512)S(6)} %eq.7), kind=kOutput, calls=%fused_computation.10 | convolution fusion | flops 50528256 | bytes 802817 | tf_op jit(solution)/shard_map/dot_general | solution.py:31
  79.6 1.5 collective-permute-done.6
  81.2 0.4 fusion.1
  81.5 3.8 %collective-permute-start.7 = (f32[64,512]{0,1:T(8,128)S(1)}, f32[64,512]{0,1:T(8,128)S(1)}, u32[]{:S(2)}, u32[]{:S(2)}) collective-permute-start(f32[64,512]{0,1:T(8,128)S(1)} %fusion.1), channel_id=1, source_target_pairs={{0,16},{8,24},{16,32},{24,40},{32,48},{40,56},{48,64},{56,72},{64,... | collective-permute-start | bytes 393224 | tf_op jit(solution)/shard_map/ppermute | solution.py:22
  85.4 10.6 %collective-permute-done.7 = f32[64,512]{0,1:T(8,128)S(1)} collective-permute-done((f32[64,512]{0,1:T(8,128)S(1)}, f32[64,512]{0,1:T(8,128)S(1)}, u32[]{:S(2)}, u32[]{:S(2)}) %collective-permute-start.7) | collective-permute-done | bytes 131104 | tf_op jit(solution)/shard_map/ppermute | solution.py:22
  96.0 1.9 %collective-permute-start.8 = (f32[64,512]{0,1:T(8,128)S(1)}, f32[64,512]{0,1:T(8,128)S(1)}, u32[]{:S(2)}, u32[]{:S(2)}) collective-permute-start(f32[64,512]{0,1:T(8,128)S(1)} %collective-permute-done.7), channel_id=1, source_target_pairs={{0,16},{8,24},{16,32},{24,40},{32,48},{40,56},{48,64},{56,72},{64,... | collective-permute-start | bytes 393224 | tf_op jit(solution)/shard_map/ppermute | solution.py:22
  98.0 11.2 %collective-permute-done.8 = f32[64,512]{0,1:T(8,128)S(1)} collective-permute-done((f32[64,512]{0,1:T(8,128)S(1)}, f32[64,512]{0,1:T(8,128)S(1)}, u32[]{:S(2)}, u32[]{:S(2)}) %collective-permute-start.8) | collective-permute-done | bytes 131104 | tf_op jit(solution)/shard_map/ppermute | solution.py:22
  109.7 2.1 %collective-permute-start.9 = (f32[64,512]{0,1:T(8,128)S(1)}, f32[64,512]{0,1:T(8,128)S(1)}, u32[]{:S(2)}, u32[]{:S(2)}) collective-permute-start(f32[64,512]{0,1:T(8,128)S(1)} %convolution_add_fusion.4), channel_id=1, source_target_pairs={{0,32},{8,40},{16,48},{24,56},{32,64},{40,72},{48,80},{56,88},{64,... | collective-permute-start | bytes 393224 | tf_op jit(solution)/shard_map/ppermute | solution.py:22
  112.0 14.2 %collective-permute-done.9 = f32[64,512]{0,1:T(8,128)S(1)} collective-permute-done((f32[64,512]{0,1:T(8,128)S(1)}, f32[64,512]{0,1:T(8,128)S(1)}, u32[]{:S(2)}, u32[]{:S(2)}) %collective-permute-start.9) | collective-permute-done | bytes 131104 | tf_op jit(solution)/shard_map/ppermute | solution.py:22
  126.2 0.4 convolution_add_fusion.3
  126.5 1.9 %collective-permute-start.10 = (f32[64,512]{0,1:T(8,128)S(1)}, f32[64,512]{0,1:T(8,128)S(1)}, u32[]{:S(2)}, u32[]{:S(2)}) collective-permute-start(f32[64,512]{0,1:T(8,128)S(1)} %convolution_add_fusion.3), channel_id=1, source_target_pairs={{0,64},{8,72},{16,80},{24,88},{32,96},{40,104},{48,112},{56,120},{... | collective-permute-start | bytes 393224 | tf_op jit(solution)/shard_map/ppermute | solution.py:22
  128.6 16.5 %collective-permute-done.10 = f32[64,512]{0,1:T(8,128)S(1)} collective-permute-done((f32[64,512]{0,1:T(8,128)S(1)}, f32[64,512]{0,1:T(8,128)S(1)}, u32[]{:S(2)}, u32[]{:S(2)}) %collective-permute-start.10) | collective-permute-done | bytes 131104 | tf_op jit(solution)/shard_map/ppermute | solution.py:22
  145.1 0.4 convolution_add_fusion.2
  145.5 1.3 collective-permute-start.11
  146.9 10.2 %collective-permute-done.11 = f32[64,512]{0,1:T(8,128)S(1)} collective-permute-done((f32[64,512]{0,1:T(8,128)S(1)}, f32[64,512]{0,1:T(8,128)S(1)}, u32[]{:S(2)}, u32[]{:S(2)}) %collective-permute-start.11) | collective-permute-done | bytes 131104 | tf_op jit(solution)/shard_map/ppermute | solution.py:22
  157.1 0.4 convolution_add_fusion.1
  157.5 0.4 convolution_add_fusion
  157.9 0.4 select_bitcast_fusion
  158.3 1.5 collective-permute-done.12
  159.9 0.9 copy.39
  (36 shorter events, 1.7 us)
Async XLA Ops:
  0.0 77.4 %copy-start = (f32[64,64]{1,0:T(8,128)S(1)}, f32[64,64]{1,0:T(8,128)}, u32[]{:S(2)}) copy-start(f32[64,64]{1,0:T(8,128)} %param.13) | copy-start | bytes 49156
  0.0 8.1 %copy-start.6 = (f32[64,96]{1,0:T(8,128)S(1)}, f32[64,96]{1,0:T(8,128)}, u32[]{:S(2)}) copy-start(f32[64,96]{1,0:T(8,128)} %constant.27.clone) | copy-start | bytes 73732
  0.0 8.0 %copy-start.5 = (f32[64,64]{1,0:T(8,128)S(1)}, f32[64,64]{1,0:T(8,128)}, u32[]{:S(2)}) copy-start(f32[64,64]{1,0:T(8,128)} %param.11) | copy-start | bytes 49156
  0.0 8.1 %copy-start.2 = (f32[64,96]{1,0:T(8,128)S(1)}, f32[64,96]{1,0:T(8,128)}, u32[]{:S(2)}) copy-start(f32[64,96]{1,0:T(8,128)} %param.12) | copy-start | bytes 73732
  0.0 8.4 %copy-start.3 = (s32[6,1024]{1,0:T(8,128)S(1)}, s32[6,1024]{1,0:T(8,128)}, u32[]{:S(2)}) copy-start(s32[6,1024]{1,0:T(8,128)} %param.15) | copy-start | bytes 73732
  4.8 7.3 %copy-start.4 = (s32[6,1024]{1,0:T(8,128)S(1)}, s32[6,1024]{1,0:T(8,128)}, u32[]{:S(2)}) copy-start(s32[6,1024]{1,0:T(8,128)} %param.14) | copy-start | bytes 73732
  5.9 8.1 %collective-permute-start = (f32[16,512]{0,1:T(8,128)S(1)}, f32[16,512]{0,1:T(8,128)S(1)}, u32[]{:S(2)}, u32[]{:S(2)}) collective-permute-start(f32[16,512]{0,1:T(8,128)S(1)} %get-tuple-element.20), channel_id=1, source_target_pairs={{0,1},{1,2},{2,3},{3,4},{4,5},{5,6},{6,7},{7,0},{8,9},{9,10},{10,1... | collective-permute-start | bytes 98312 | tf_op jit(solution)/shard_map/ppermute | solution.py:27
  7.2 9.9 %collective-permute-start.1 = (f32[16,512]{0,1:T(8,128)S(1)}, f32[16,512]{0,1:T(8,128)S(1)}, u32[]{:S(2)}, u32[]{:S(2)}) collective-permute-start(f32[16,512]{0,1:T(8,128)S(1)} %get-tuple-element.19), channel_id=1, source_target_pairs={{0,7},{1,0},{2,1},{3,2},{4,3},{5,4},{6,5},{7,6},{8,15},{9,8},{10,9... | collective-permute-start | bytes 98312 | tf_op jit(solution)/shard_map/ppermute | solution.py:27
  14.1 3.0 %copy-start.9 = (f32[16,512]{0,1:T(8,128)}, f32[16,512]{0,1:T(8,128)S(1)}, u32[]{:S(2)}) copy-start(f32[16,512]{0,1:T(8,128)S(1)} %collective-permute-done) | copy-start | bytes 98308
  17.1 0.7 copy-start.10
  31.8 6.9 %collective-permute-start.2 = (f32[16,512]{0,1:T(8,128)S(1)}, f32[16,512]{0,1:T(8,128)S(1)}, u32[]{:S(2)}, u32[]{:S(2)}) collective-permute-start(f32[16,512]{0,1:T(8,128)S(1)} %get-tuple-element.18), channel_id=1, source_target_pairs={{0,1},{1,2},{2,3},{3,4},{4,5},{5,6},{6,7},{7,0},{8,9},{9,10},{10,1... | collective-permute-start | bytes 98312 | tf_op jit(solution)/shard_map/ppermute | solution.py:27
  32.2 9.0 %collective-permute-start.3 = (f32[16,512]{0,1:T(8,128)S(1)}, f32[16,512]{0,1:T(8,128)S(1)}, u32[]{:S(2)}, u32[]{:S(2)}) collective-permute-start(f32[16,512]{0,1:T(8,128)S(1)} %get-tuple-element.17), channel_id=1, source_target_pairs={{0,7},{1,0},{2,1},{3,2},{4,3},{5,4},{6,5},{7,6},{8,15},{9,8},{10,9... | collective-permute-start | bytes 98312 | tf_op jit(solution)/shard_map/ppermute | solution.py:27
  38.7 2.5 %copy-start.11 = (f32[16,512]{0,1:T(8,128)}, f32[16,512]{0,1:T(8,128)S(1)}, u32[]{:S(2)}) copy-start(f32[16,512]{0,1:T(8,128)S(1)} %collective-permute-done.2) | copy-start | bytes 98308
  41.2 0.7 copy-start.12
  55.9 6.4 %collective-permute-start.4 = (f32[16,512]{0,1:T(8,128)S(1)}, f32[16,512]{0,1:T(8,128)S(1)}, u32[]{:S(2)}, u32[]{:S(2)}) collective-permute-start(f32[16,512]{0,1:T(8,128)S(1)} %get-tuple-element.16), channel_id=1, source_target_pairs={{0,1},{1,2},{2,3},{3,4},{4,5},{5,6},{6,7},{7,0},{8,9},{9,10},{10,1... | collective-permute-start | bytes 98312 | tf_op jit(solution)/shard_map/ppermute | solution.py:27
  56.4 8.5 %collective-permute-start.5 = (f32[16,512]{0,1:T(8,128)S(1)}, f32[16,512]{0,1:T(8,128)S(1)}, u32[]{:S(2)}, u32[]{:S(2)}) collective-permute-start(f32[16,512]{0,1:T(8,128)S(1)} %get-tuple-element.15), channel_id=1, source_target_pairs={{0,7},{1,0},{2,1},{3,2},{4,3},{5,4},{6,5},{7,6},{8,15},{9,8},{10,9... | collective-permute-start | bytes 98312 | tf_op jit(solution)/shard_map/ppermute | solution.py:27
  62.4 2.5 %copy-start.7 = (f32[16,512]{0,1:T(8,128)}, f32[16,512]{0,1:T(8,128)S(1)}, u32[]{:S(2)}) copy-start(f32[16,512]{0,1:T(8,128)S(1)} %collective-permute-done.4) | copy-start | bytes 98308
  64.9 0.7 copy-start.8
  65.6 11.9 %copy-start.1 = (f32[1,64,1024]{2,1,0:T(8,128)S(1)}, f32[1,64,1024]{2,1,0:T(8,128)}, u32[]{:S(2)}) copy-start(f32[1,64,1024]{2,1,0:T(8,128)} %param.10) | copy-start | bytes 786436
  79.5 1.6 %collective-permute-start.6 = (f32[64,512]{0,1:T(8,128)S(1)}, f32[64,512]{0,1:T(8,128)S(1)}, u32[]{:S(2)}, u32[]{:S(2)}) collective-permute-start(f32[64,512]{0,1:T(8,128)S(1)} %slice_select_fusion), channel_id=1, source_target_pairs={{0,8},{8,0},{16,24},{24,16},{32,40},{40,32},{48,56},{56,48},{64,72... | collective-permute-start | bytes 393224 | tf_op jit(solution)/shard_map/ppermute | solution.py:233
  81.5 14.4 %collective-permute-start.7 = (f32[64,512]{0,1:T(8,128)S(1)}, f32[64,512]{0,1:T(8,128)S(1)}, u32[]{:S(2)}, u32[]{:S(2)}) collective-permute-start(f32[64,512]{0,1:T(8,128)S(1)} %fusion.1), channel_id=1, source_target_pairs={{0,16},{8,24},{16,32},{24,40},{32,48},{40,56},{48,64},{56,72},{64,... | collective-permute-start | bytes 393224 | tf_op jit(solution)/shard_map/ppermute | solution.py:22
  96.0 13.3 %collective-permute-start.8 = (f32[64,512]{0,1:T(8,128)S(1)}, f32[64,512]{0,1:T(8,128)S(1)}, u32[]{:S(2)}, u32[]{:S(2)}) collective-permute-start(f32[64,512]{0,1:T(8,128)S(1)} %collective-permute-done.7), channel_id=1, source_target_pairs={{0,16},{8,24},{16,32},{24,40},{32,48},{40,56},{48,64},{56,72},{64,... | collective-permute-start | bytes 393224 | tf_op jit(solution)/shard_map/ppermute | solution.py:22
  109.7 16.5 %collective-permute-start.9 = (f32[64,512]{0,1:T(8,128)S(1)}, f32[64,512]{0,1:T(8,128)S(1)}, u32[]{:S(2)}, u32[]{:S(2)}) collective-permute-start(f32[64,512]{0,1:T(8,128)S(1)} %convolution_add_fusion.4), channel_id=1, source_target_pairs={{0,32},{8,40},{16,48},{24,56},{32,64},{40,72},{48,80},{56,88},{64,... | collective-permute-start | bytes 393224 | tf_op jit(solution)/shard_map/ppermute | solution.py:22
  126.5 18.6 %collective-permute-start.10 = (f32[64,512]{0,1:T(8,128)S(1)}, f32[64,512]{0,1:T(8,128)S(1)}, u32[]{:S(2)}, u32[]{:S(2)}) collective-permute-start(f32[64,512]{0,1:T(8,128)S(1)} %convolution_add_fusion.3), channel_id=1, source_target_pairs={{0,64},{8,72},{16,80},{24,88},{32,96},{40,104},{48,112},{56,120},{... | collective-permute-start | bytes 393224 | tf_op jit(solution)/shard_map/ppermute | solution.py:22
  145.5 11.6 %collective-permute-start.11 = (f32[64,512]{0,1:T(8,128)S(1)}, f32[64,512]{0,1:T(8,128)S(1)}, u32[]{:S(2)}, u32[]{:S(2)}) collective-permute-start(f32[64,512]{0,1:T(8,128)S(1)} %convolution_add_fusion.2), channel_id=1, source_target_pairs={{0,128},{8,136},{16,144},{24,152},{32,160},{40,168},{48,176},{56,1... | collective-permute-start | bytes 393224 | tf_op jit(solution)/shard_map/ppermute | solution.py:22
  158.2 1.6 %collective-permute-start.12 = (f32[64,512]{0,1:T(8,128)S(1)}, f32[64,512]{0,1:T(8,128)S(1)}, u32[]{:S(2)}, u32[]{:S(2)}) collective-permute-start(f32[64,512]{0,1:T(8,128)S(1)} %get-tuple-element.14), channel_id=1, source_target_pairs={{0,8},{8,0},{16,24},{24,16},{32,40},{40,32},{48,56},{56,48},{64,72... | collective-permute-start | bytes 393224 | tf_op jit(solution)/shard_map/ppermute | solution.py:250

commit v19 on v18

--- a/solution.py
+++ b/solution.py
@@ -10,7 +10,7 @@
 
 STEPS = 3
 LANES = 128
-UNROLL = 256
+UNROLL = 512
 
 
 time_step = 0.05

time: 161 us -> 160 us (level)
  no operation moved by 1% of the time
where the time goes in v19:
time: 160 us; the launch traced here: 159 us
  waiting for transfers between devices  84.3 us (53%)
  Pallas kernels  38.9 us (24%)
  starting transfers between devices  17.6 us (11%)
  local copies, waits for them, and re-layouts  12.9 us (8%)
  matrix products  5.44 us (3%)
    ppermute x5, waiting for transfers between devices, from_behind(): return lax.ppermute(shard, axis, pairs)  62.7 us
    pallas_call x3, Pallas kernels, fused_step(): pl.pallas_call(functools.partial(fused_kernel, with_send), out_shape=tupl...  36.5 us
    ppermute x6, waiting for transfers between devices, ring(): lax.ppermute(shard, axis, [(i, (i + by) % peers) for i in range(peers)])  18.6 us
    ppermute x5, starting transfers between devices, from_behind(): return lax.ppermute(shard, axis, pairs)  11.1 us
    ppermute x6, starting transfers between devices, ring(): lax.ppermute(shard, axis, [(i, (i + by) % peers) for i in range(peers)])  6.31 us
    dot_general x13, matrix products, product(): jnp.dot(matrix, vector, precision=lax.Precision.HIGHEST, preferred_elemen...  5.44 us
    unnamed x29, local copies, waits for them, and re-layouts  3.47 us
    transpose x3, local copies, waits for them, and re-layouts, shards(): after = ring(sent[:half, 0:16].T, 'space', -1)  3.46 us
  transfers between devices with their start and end apart: 13, of which 13 were waited for; matrix products, arithmetic and copies ran while one was open for 3% of the time, Pallas kernels for 0%

profile of v19, /device:TPU:22, one launch (start us, length us, event | category | flops | bytes accessed | tf_op | source)
XLA Modules:
  0.0 159.5 jit_solution(4077212626431993526)
XLA Ops:
  0.0 1.2 copy.24
  1.2 0.9 pad.12.refs_2_.state_ref
  2.1 2.4 %shard_map.100 = f32[1024,128]{1,0:T(8,128)} custom-call(s32[512]{0:T(512)} %send_low_ref.5, s32[512]{0:T(512)} %send_high_ref.5, f32[1024,128]{1,0:T(8,128)} %pad.12.refs_2_.state_ref), custom_call_target="tpu_custom_call" | custom-call | tf_op jit(solution)/shard_map/pallas_call | solution.py:89
  4.5 1.2 slice_bitcast_fusion.1
  5.7 1.3 collective-permute-start
  6.9 0.8 collective-permute-start.1
  8.1 2.2 %copy.27.mask_ref = s32[6,1024,1]{2,1,0:T(8,128)} copy(s32[6,1024,1]{1,0,2:T(8,128)S(1)} %bitcast.78) | data formatting | bytes 49152 | tf_op jit(solution)/shard_map/broadcast_in_dim | solution.py:199
  10.4 0.8 pad.13.spread_ref
  11.1 0.6 pad.14.folded_ref
  11.8 0.6 reshape.62.idx_ref
  12.4 1.4 collective-permute-done
  13.8 3.0 %collective-permute-done.1 = f32[16,512]{0,1:T(8,128)S(1)} collective-permute-done((f32[16,512]{0,1:T(8,128)S(1)}, f32[16,512]{0,1:T(8,128)S(1)}, u32[]{:S(2)}, u32[]{:S(2)}) %collective-permute-start.1) | collective-permute-done | bytes 32800 | tf_op jit(solution)/shard_map/ppermute | solution.py:27
  16.8 0.7 copy-done.10
  17.5 12.3 %shard_map.101 = (f32[1024,128]{1,0:T(8,128)}, f32[1024,128]{1,0:T(8,128)}) custom-call(s32[6144]{0:T(1024)} %reshape.62.idx_ref, s32[512]{0:T(512)} %send_low_ref.5, s32[512]{0:T(512)} %send_high_ref.5, f32[1024,128]{1,0:T(8,128)} %pad.12.refs_2_.state_ref, f32[512,16]{1,0:T(8,128)} %bitcast.81, f32[512,16]{1,0:T(8,128)} %bitcast.82, ...), custom_call_target="tpu_custom_call" | custom-call | flops 2617245696 | bytes 2908160 | tf_op jit(solution)/shard_map/pallas_call | solution.py:178
  29.8 1.2 slice_bitcast_fusion.5
  31.0 0.4 collective-permute-start.2
  31.4 1.7 %collective-permute-start.3 = (f32[16,512]{0,1:T(8,128)S(1)}, f32[16,512]{0,1:T(8,128)S(1)}, u32[]{:S(2)}, u32[]{:S(2)}) collective-permute-start(f32[16,512]{0,1:T(8,128)S(1)} %get-tuple-element.17), channel_id=1, source_target_pairs={{0,7},{1,0},{2,1},{3,2},{4,3},{5,4},{6,5},{7,6},{8,15},{9,8},{10,9... | collective-permute-start | bytes 98312 | tf_op jit(solution)/shard_map/ppermute | solution.py:27
  33.1 4.8 %collective-permute-done.2 = f32[16,512]{0,1:T(8,128)S(1)} collective-permute-done((f32[16,512]{0,1:T(8,128)S(1)}, f32[16,512]{0,1:T(8,128)S(1)}, u32[]{:S(2)}, u32[]{:S(2)}) %collective-permute-start.2) | collective-permute-done | bytes 32800 | tf_op jit(solution)/shard_map/ppermute | solution.py:27
  37.9 2.5 %collective-permute-done.3 = f32[16,512]{0,1:T(8,128)S(1)} collective-permute-done((f32[16,512]{0,1:T(8,128)S(1)}, f32[16,512]{0,1:T(8,128)S(1)}, u32[]{:S(2)}, u32[]{:S(2)}) %collective-permute-start.3) | collective-permute-done | bytes 32800 | tf_op jit(solution)/shard_map/ppermute | solution.py:27
  40.4 0.7 copy-done.12
  41.1 12.3 %shard_map.102 = (f32[1024,128]{1,0:T(8,128)}, f32[1024,128]{1,0:T(8,128)}) custom-call(s32[6144]{0:T(1024)} %reshape.62.idx_ref, s32[512]{0:T(512)} %send_low_ref.5, s32[512]{0:T(512)} %send_high_ref.5, f32[1024,128]{1,0:T(8,128)} %get-tuple-element.9.state_ref, f32[512,16]{1,0:T(8,128)} %bitcast.83, f32[512,16]{1,0:T(8,128)} %bitcast.84, ...), custom_call_target="tpu_custom_call" | custom-call | flops 2617245696 | bytes 2908160 | tf_op jit(solution)/shard_map/pallas_call | solution.py:178
  53.5 1.2 slice_bitcast_fusion.3
  54.6 0.4 collective-permute-start.4
  55.1 1.7 %collective-permute-start.5 = (f32[16,512]{0,1:T(8,128)S(1)}, f32[16,512]{0,1:T(8,128)S(1)}, u32[]{:S(2)}, u32[]{:S(2)}) collective-permute-start(f32[16,512]{0,1:T(8,128)S(1)} %get-tuple-element.15), channel_id=1, source_target_pairs={{0,7},{1,0},{2,1},{3,2},{4,3},{5,4},{6,5},{7,6},{8,15},{9,8},{10,9... | collective-permute-start | bytes 98312 | tf_op jit(solution)/shard_map/ppermute | solution.py:27
  56.7 4.3 %collective-permute-done.4 = f32[16,512]{0,1:T(8,128)S(1)} collective-permute-done((f32[16,512]{0,1:T(8,128)S(1)}, f32[16,512]{0,1:T(8,128)S(1)}, u32[]{:S(2)}, u32[]{:S(2)}) %collective-permute-start.4) | collective-permute-done | bytes 32800 | tf_op jit(solution)/shard_map/ppermute | solution.py:27
  61.1 2.5 %collective-permute-done.5 = f32[16,512]{0,1:T(8,128)S(1)} collective-permute-done((f32[16,512]{0,1:T(8,128)S(1)}, f32[16,512]{0,1:T(8,128)S(1)}, u32[]{:S(2)}, u32[]{:S(2)}) %collective-permute-start.5) | collective-permute-done | bytes 32800 | tf_op jit(solution)/shard_map/ppermute | solution.py:27
  63.6 0.7 copy-done.8
  64.3 11.8 %shard_map.103 = f32[1024,128]{1,0:T(8,128)} custom-call(s32[6144]{0:T(1024)} %reshape.62.idx_ref, s32[512]{0:T(512)} %send_low_ref.5, s32[512]{0:T(512)} %send_high_ref.5, f32[1024,128]{1,0:T(8,128)} %get-tuple-element.11.state_ref, f32[512,16]{1,0:T(8,128)} %bitcast.79, f32[512,16]{1,0:T(8,128)} %bitcast.80, s32[6,1024,1]{2,1,0:T(8,128)} %copy.27.mask_ref, ...), custom_call_target="tpu_custom_call" | custom-call | flops 2617245696 | bytes 2908160 | tf_op jit(solution)/shard_map/pallas_call | solution.py:178
  76.1 2.0 %add_select_fusion = f32[64,1024]{0,1:T(8,128)S(1)} fusion(f32[1024,128]{1,0:T(8,128)} %shard_map.103, f32[64,64]{1,0:T(8,128)S(1)} %copy-done, f32[1,64,1024]{2,1,0:T(8,128)S(1)} %copy-done.1, pred[]{:T(512)S(6)} %eq.7), kind=kOutput, calls=%fused_computation.10 | convolution fusion | flops 50528256 | bytes 802817 | tf_op jit(solution)/shard_map/dot_general | solution.py:31
  78.3 1.5 collective-permute-done.6
  79.8 0.4 fusion.1
  80.2 3.8 %collective-permute-start.7 = (f32[64,512]{0,1:T(8,128)S(1)}, f32[64,512]{0,1:T(8,128)S(1)}, u32[]{:S(2)}, u32[]{:S(2)}) collective-permute-start(f32[64,512]{0,1:T(8,128)S(1)} %fusion.1), channel_id=1, source_target_pairs={{0,16},{8,24},{16,32},{24,40},{32,48},{40,56},{48,64},{56,72},{64,... | collective-permute-start | bytes 393224 | tf_op jit(solution)/shard_map/ppermute | solution.py:22
  84.0 10.6 %collective-permute-done.7 = f32[64,512]{0,1:T(8,128)S(1)} collective-permute-done((f32[64,512]{0,1:T(8,128)S(1)}, f32[64,512]{0,1:T(8,128)S(1)}, u32[]{:S(2)}, u32[]{:S(2)}) %collective-permute-start.7) | collective-permute-done | bytes 131104 | tf_op jit(solution)/shard_map/ppermute | solution.py:22
  94.6 2.1 %collective-permute-start.8 = (f32[64,512]{0,1:T(8,128)S(1)}, f32[64,512]{0,1:T(8,128)S(1)}, u32[]{:S(2)}, u32[]{:S(2)}) collective-permute-start(f32[64,512]{0,1:T(8,128)S(1)} %collective-permute-done.7), channel_id=1, source_target_pairs={{0,16},{8,24},{16,32},{24,40},{32,48},{40,56},{48,64},{56,72},{64,... | collective-permute-start | bytes 393224 | tf_op jit(solution)/shard_map/ppermute | solution.py:22
  96.9 11.0 %collective-permute-done.8 = f32[64,512]{0,1:T(8,128)S(1)} collective-permute-done((f32[64,512]{0,1:T(8,128)S(1)}, f32[64,512]{0,1:T(8,128)S(1)}, u32[]{:S(2)}, u32[]{:S(2)}) %collective-permute-start.8) | collective-permute-done | bytes 131104 | tf_op jit(solution)/shard_map/ppermute | solution.py:22
  108.3 1.9 %collective-permute-start.9 = (f32[64,512]{0,1:T(8,128)S(1)}, f32[64,512]{0,1:T(8,128)S(1)}, u32[]{:S(2)}, u32[]{:S(2)}) collective-permute-start(f32[64,512]{0,1:T(8,128)S(1)} %convolution_add_fusion.4), channel_id=1, source_target_pairs={{0,32},{8,40},{16,48},{24,56},{32,64},{40,72},{48,80},{56,88},{64,... | collective-permute-start | bytes 393224 | tf_op jit(solution)/shard_map/ppermute | solution.py:22
  110.4 14.4 %collective-permute-done.9 = f32[64,512]{0,1:T(8,128)S(1)} collective-permute-done((f32[64,512]{0,1:T(8,128)S(1)}, f32[64,512]{0,1:T(8,128)S(1)}, u32[]{:S(2)}, u32[]{:S(2)}) %collective-permute-start.9) | collective-permute-done | bytes 131104 | tf_op jit(solution)/shard_map/ppermute | solution.py:22
  124.8 0.4 convolution_add_fusion.3
  125.2 1.9 %collective-permute-start.10 = (f32[64,512]{0,1:T(8,128)S(1)}, f32[64,512]{0,1:T(8,128)S(1)}, u32[]{:S(2)}, u32[]{:S(2)}) collective-permute-start(f32[64,512]{0,1:T(8,128)S(1)} %convolution_add_fusion.3), channel_id=1, source_target_pairs={{0,64},{8,72},{16,80},{24,88},{32,96},{40,104},{48,112},{56,120},{... | collective-permute-start | bytes 393224 | tf_op jit(solution)/shard_map/ppermute | solution.py:22
  127.3 16.5 %collective-permute-done.10 = f32[64,512]{0,1:T(8,128)S(1)} collective-permute-done((f32[64,512]{0,1:T(8,128)S(1)}, f32[64,512]{0,1:T(8,128)S(1)}, u32[]{:S(2)}, u32[]{:S(2)}) %collective-permute-start.10) | collective-permute-done | bytes 131104 | tf_op jit(solution)/shard_map/ppermute | solution.py:22
  143.7 0.4 convolution_add_fusion.2
  144.1 1.3 collective-permute-start.11
  145.6 10.2 %collective-permute-done.11 = f32[64,512]{0,1:T(8,128)S(1)} collective-permute-done((f32[64,512]{0,1:T(8,128)S(1)}, f32[64,512]{0,1:T(8,128)S(1)}, u32[]{:S(2)}, u32[]{:S(2)}) %collective-permute-start.11) | collective-permute-done | bytes 131104 | tf_op jit(solution)/shard_map/ppermute | solution.py:22
  155.8 0.4 convolution_add_fusion.1
  156.1 0.4 convolution_add_fusion
  156.5 0.4 select_bitcast_fusion
  157.0 1.5 collective-permute-done.12
  158.6 0.9 copy.39
  (36 shorter events, 1.7 us)
Async XLA Ops:
  0.0 76.1 %copy-start = (f32[64,64]{1,0:T(8,128)S(1)}, f32[64,64]{1,0:T(8,128)}, u32[]{:S(2)}) copy-start(f32[64,64]{1,0:T(8,128)} %param.13) | copy-start | bytes 49156
  0.0 7.8 %copy-start.6 = (f32[64,96]{1,0:T(8,128)S(1)}, f32[64,96]{1,0:T(8,128)}, u32[]{:S(2)}) copy-start(f32[64,96]{1,0:T(8,128)} %constant.27.clone) | copy-start | bytes 73732
  0.0 7.8 %copy-start.5 = (f32[64,64]{1,0:T(8,128)S(1)}, f32[64,64]{1,0:T(8,128)}, u32[]{:S(2)}) copy-start(f32[64,64]{1,0:T(8,128)} %param.11) | copy-start | bytes 49156
  0.0 7.8 %copy-start.2 = (f32[64,96]{1,0:T(8,128)S(1)}, f32[64,96]{1,0:T(8,128)}, u32[]{:S(2)}) copy-start(f32[64,96]{1,0:T(8,128)} %param.12) | copy-start | bytes 73732
  0.0 8.1 %copy-start.3 = (s32[6,1024]{1,0:T(8,128)S(1)}, s32[6,1024]{1,0:T(8,128)}, u32[]{:S(2)}) copy-start(s32[6,1024]{1,0:T(8,128)} %param.15) | copy-start | bytes 73732
  4.5 7.3 %copy-start.4 = (s32[6,1024]{1,0:T(8,128)S(1)}, s32[6,1024]{1,0:T(8,128)}, u32[]{:S(2)}) copy-start(s32[6,1024]{1,0:T(8,128)} %param.14) | copy-start | bytes 73732
  5.7 8.1 %collective-permute-start = (f32[16,512]{0,1:T(8,128)S(1)}, f32[16,512]{0,1:T(8,128)S(1)}, u32[]{:S(2)}, u32[]{:S(2)}) collective-permute-start(f32[16,512]{0,1:T(8,128)S(1)} %get-tuple-element.20), channel_id=1, source_target_pairs={{0,1},{1,2},{2,3},{3,4},{4,5},{5,6},{6,7},{7,0},{8,9},{9,10},{10,1... | collective-permute-start | bytes 98312 | tf_op jit(solution)/shard_map/ppermute | solution.py:27
  6.9 9.9 %collective-permute-start.1 = (f32[16,512]{0,1:T(8,128)S(1)}, f32[16,512]{0,1:T(8,128)S(1)}, u32[]{:S(2)}, u32[]{:S(2)}) collective-permute-start(f32[16,512]{0,1:T(8,128)S(1)} %get-tuple-element.19), channel_id=1, source_target_pairs={{0,7},{1,0},{2,1},{3,2},{4,3},{5,4},{6,5},{7,6},{8,15},{9,8},{10,9... | collective-permute-start | bytes 98312 | tf_op jit(solution)/shard_map/ppermute | solution.py:27
  13.8 3.0 %copy-start.9 = (f32[16,512]{0,1:T(8,128)}, f32[16,512]{0,1:T(8,128)S(1)}, u32[]{:S(2)}) copy-start(f32[16,512]{0,1:T(8,128)S(1)} %collective-permute-done) | copy-start | bytes 98308
  16.8 0.7 copy-start.10
  31.0 6.9 %collective-permute-start.2 = (f32[16,512]{0,1:T(8,128)S(1)}, f32[16,512]{0,1:T(8,128)S(1)}, u32[]{:S(2)}, u32[]{:S(2)}) collective-permute-start(f32[16,512]{0,1:T(8,128)S(1)} %get-tuple-element.18), channel_id=1, source_target_pairs={{0,1},{1,2},{2,3},{3,4},{4,5},{5,6},{6,7},{7,0},{8,9},{9,10},{10,1... | collective-permute-start | bytes 98312 | tf_op jit(solution)/shard_map/ppermute | solution.py:27
  31.4 9.0 %collective-permute-start.3 = (f32[16,512]{0,1:T(8,128)S(1)}, f32[16,512]{0,1:T(8,128)S(1)}, u32[]{:S(2)}, u32[]{:S(2)}) collective-permute-start(f32[16,512]{0,1:T(8,128)S(1)} %get-tuple-element.17), channel_id=1, source_target_pairs={{0,7},{1,0},{2,1},{3,2},{4,3},{5,4},{6,5},{7,6},{8,15},{9,8},{10,9... | collective-permute-start | bytes 98312 | tf_op jit(solution)/shard_map/ppermute | solution.py:27
  37.9 2.5 %copy-start.11 = (f32[16,512]{0,1:T(8,128)}, f32[16,512]{0,1:T(8,128)S(1)}, u32[]{:S(2)}) copy-start(f32[16,512]{0,1:T(8,128)S(1)} %collective-permute-done.2) | copy-start | bytes 98308
  40.4 0.7 copy-start.12
  54.6 6.4 %collective-permute-start.4 = (f32[16,512]{0,1:T(8,128)S(1)}, f32[16,512]{0,1:T(8,128)S(1)}, u32[]{:S(2)}, u32[]{:S(2)}) collective-permute-start(f32[16,512]{0,1:T(8,128)S(1)} %get-tuple-element.16), channel_id=1, source_target_pairs={{0,1},{1,2},{2,3},{3,4},{4,5},{5,6},{6,7},{7,0},{8,9},{9,10},{10,1... | collective-permute-start | bytes 98312 | tf_op jit(solution)/shard_map/ppermute | solution.py:27
  55.1 8.5 %collective-permute-start.5 = (f32[16,512]{0,1:T(8,128)S(1)}, f32[16,512]{0,1:T(8,128)S(1)}, u32[]{:S(2)}, u32[]{:S(2)}) collective-permute-start(f32[16,512]{0,1:T(8,128)S(1)} %get-tuple-element.15), channel_id=1, source_target_pairs={{0,7},{1,0},{2,1},{3,2},{4,3},{5,4},{6,5},{7,6},{8,15},{9,8},{10,9... | collective-permute-start | bytes 98312 | tf_op jit(solution)/shard_map/ppermute | solution.py:27
  61.1 2.5 %copy-start.7 = (f32[16,512]{0,1:T(8,128)}, f32[16,512]{0,1:T(8,128)S(1)}, u32[]{:S(2)}) copy-start(f32[16,512]{0,1:T(8,128)S(1)} %collective-permute-done.4) | copy-start | bytes 98308
  63.5 0.7 copy-start.8
  64.3 11.8 %copy-start.1 = (f32[1,64,1024]{2,1,0:T(8,128)S(1)}, f32[1,64,1024]{2,1,0:T(8,128)}, u32[]{:S(2)}) copy-start(f32[1,64,1024]{2,1,0:T(8,128)} %param.10) | copy-start | bytes 786436
  78.2 1.6 %collective-permute-start.6 = (f32[64,512]{0,1:T(8,128)S(1)}, f32[64,512]{0,1:T(8,128)S(1)}, u32[]{:S(2)}, u32[]{:S(2)}) collective-permute-start(f32[64,512]{0,1:T(8,128)S(1)} %slice_select_fusion), channel_id=1, source_target_pairs={{0,8},{8,0},{16,24},{24,16},{32,40},{40,32},{48,56},{56,48},{64,72... | collective-permute-start | bytes 393224 | tf_op jit(solution)/shard_map/ppermute | solution.py:233
  80.2 14.4 %collective-permute-start.7 = (f32[64,512]{0,1:T(8,128)S(1)}, f32[64,512]{0,1:T(8,128)S(1)}, u32[]{:S(2)}, u32[]{:S(2)}) collective-permute-start(f32[64,512]{0,1:T(8,128)S(1)} %fusion.1), channel_id=1, source_target_pairs={{0,16},{8,24},{16,32},{24,40},{32,48},{40,56},{48,64},{56,72},{64,... | collective-permute-start | bytes 393224 | tf_op jit(solution)/shard_map/ppermute | solution.py:22
  94.6 13.3 %collective-permute-start.8 = (f32[64,512]{0,1:T(8,128)S(1)}, f32[64,512]{0,1:T(8,128)S(1)}, u32[]{:S(2)}, u32[]{:S(2)}) collective-permute-start(f32[64,512]{0,1:T(8,128)S(1)} %collective-permute-done.7), channel_id=1, source_target_pairs={{0,16},{8,24},{16,32},{24,40},{32,48},{40,56},{48,64},{56,72},{64,... | collective-permute-start | bytes 393224 | tf_op jit(solution)/shard_map/ppermute | solution.py:22
  108.3 16.5 %collective-permute-start.9 = (f32[64,512]{0,1:T(8,128)S(1)}, f32[64,512]{0,1:T(8,128)S(1)}, u32[]{:S(2)}, u32[]{:S(2)}) collective-permute-start(f32[64,512]{0,1:T(8,128)S(1)} %convolution_add_fusion.4), channel_id=1, source_target_pairs={{0,32},{8,40},{16,48},{24,56},{32,64},{40,72},{48,80},{56,88},{64,... | collective-permute-start | bytes 393224 | tf_op jit(solution)/shard_map/ppermute | solution.py:22
  125.2 18.6 %collective-permute-start.10 = (f32[64,512]{0,1:T(8,128)S(1)}, f32[64,512]{0,1:T(8,128)S(1)}, u32[]{:S(2)}, u32[]{:S(2)}) collective-permute-start(f32[64,512]{0,1:T(8,128)S(1)} %convolution_add_fusion.3), channel_id=1, source_target_pairs={{0,64},{8,72},{16,80},{24,88},{32,96},{40,104},{48,112},{56,120},{... | collective-permute-start | bytes 393224 | tf_op jit(solution)/shard_map/ppermute | solution.py:22
  144.1 11.6 %collective-permute-start.11 = (f32[64,512]{0,1:T(8,128)S(1)}, f32[64,512]{0,1:T(8,128)S(1)}, u32[]{:S(2)}, u32[]{:S(2)}) collective-permute-start(f32[64,512]{0,1:T(8,128)S(1)} %convolution_add_fusion.2), channel_id=1, source_target_pairs={{0,128},{8,136},{16,144},{24,152},{32,160},{40,168},{48,176},{56,1... | collective-permute-start | bytes 393224 | tf_op jit(solution)/shard_map/ppermute | solution.py:22
  156.9 1.6 %collective-permute-start.12 = (f32[64,512]{0,1:T(8,128)S(1)}, f32[64,512]{0,1:T(8,128)S(1)}, u32[]{:S(2)}, u32[]{:S(2)}) collective-permute-start(f32[64,512]{0,1:T(8,128)S(1)} %get-tuple-element.14), channel_id=1, source_target_pairs={{0,8},{8,0},{16,24},{24,16},{32,40},{40,32},{48,56},{56,48},{64,72... | collective-permute-start | bytes 393224 | tf_op jit(solution)/shard_map/ppermute | solution.py:250
